TPU v7x, 32 devices: a whole 2x2x4 slice. The times are simulated.
32 devices in a mesh: event: 4 (over y, x), region: 8 (over z, core).
Axes of the slice: x: 2, y: 2, z: 4, core: 2. Of those that a mesh axis runs over, the one named last changes fastest.
Arguments:
- queries_in: bfloat16 [4096, 512], P('event'), parts along dimension 0, may hold values from -144 to 144
- hits_in: bfloat16 [32768, 512], P(('event', 'region')), parts along dimension 0, may hold values from -6 to 6
- w_query: bfloat16 [512, 512], replicated, may hold values from -0.25 to 0.25
- w_key: bfloat16 [512, 512], replicated, may hold values from -0.25 to 0.25
- w_value: bfloat16 [512, 512], replicated, may hold values from -0.25 to 0.25
- w_out: bfloat16 [512, 512], replicated, may hold values from -0.25 to 0.25
- mask_list: int32 [32, 16], P('event'), parts along dimension 0, may hold values from 0 to 63, all different within a row
- grad_out: bfloat16 [4096, 512], P('event'), parts along dimension 0, may hold values from -6 to 6
Outputs:
- layer_out: bfloat16 [4096, 512], P('event'), parts along dimension 0
- grad_queries: bfloat16 [4096, 512], P('event'), parts along dimension 0
- grad_hits: bfloat16 [32768, 512], P(('event', 'region')), parts along dimension 0
- grad_wq: float32 [2048, 512], P('event'), parts along dimension 0
- grad_wk: float32 [2048, 512], P('event'), parts along dimension 0
- grad_wv: float32 [2048, 512], P('event'), parts along dimension 0
- grad_wo: float32 [2048, 512], P('event'), parts along dimension 0
There are 4 independent parts, one for each index of `event`. A program takes and returns all parts, laid end to end along the dimension named above; an argument that names none is the same for every part. Nothing has to cross between parts.
Inputs may be any that keep to these rules, and one draw needn't show every extreme that they name: `mask_list`: each row names 16 different hit blocks, and every hit block is named by some row.
All inputs are finite; a program needn't handle non-finite values.
Results may differ from a plain program's by a relative error of at most 0.04.
The roundings to bfloat16 on the way count: a program that leaves them out, or rounds other values in their place, can miss the bound.
Values may be sent and summed in bfloat16 or wider, within the bound.
No kernel may reach another device: no remote copies, remote signals or barrier semaphores. Data moves between devices by JAX's collectives and lax.ppermute only.
A program may use at most 192 MiB of HBM per device.

v0:
```python
import math

import jax
import jax.numpy as jnp
from jax import lax
from jax.sharding import PartitionSpec as P

HEADS = 8
BLOCK = 128
ROWS = 512


def merged(shard, axis, combine):
    everything = jax.tree.map(lambda part: lax.all_gather(part, axis), shard)
    initial = jax.tree.map(lambda part: part[0], everything)

    def lap(k, so_far):
        return combine(so_far, jax.tree.map(lambda part: part[k], everything))

    return lax.fori_loop(1, lax.axis_size(axis), lap, initial)


def split_heads(array):
    return array.reshape(array.shape[:-1] + (HEADS, array.shape[-1] // HEADS))


def merge_partials(first, second):
    numer_a, max_a, total_a = first
    numer_b, max_b, total_b = second
    peak = jnp.maximum(max_a, max_b)
    scale_a = jnp.exp(max_a - peak)
    scale_b = jnp.exp(max_b - peak)
    head_dim = numer_a.shape[-1] // max_a.shape[-1]
    numer = numer_a * jnp.repeat(scale_a, head_dim, axis=-1) + numer_b * jnp.repeat(
        scale_b, head_dim, axis=-1
    )
    return (numer, peak, total_a * scale_a + total_b * scale_b)


def on_device(queries_in, hits_in, w_query, w_key, w_value, w_out, mask_list, grad_out):
    f32 = jnp.float32
    bf16 = jnp.bfloat16
    regions = lax.axis_size("region")
    region_index = lax.axis_index("region")
    n_queries, width = queries_in.shape
    n_hits = hits_in.shape[0]
    head_dim = width // HEADS
    score_scale = 1.0 / math.sqrt(head_dim)
    hit_blocks = n_hits // BLOCK
    all_blocks = hit_blocks * regions
    groups = n_queries // ROWS
    blockmask = jnp.any(
        mask_list[:, :, None] == jnp.arange(all_blocks, dtype=jnp.int32)[None, None, :], axis=1
    )
    local_blocks = lax.dynamic_slice_in_dim(blockmask, region_index * hit_blocks, hit_blocks, 1)
    column_mask = jnp.repeat(local_blocks, BLOCK, axis=1)
    column_groups = column_mask.reshape(groups, ROWS // BLOCK, n_hits)
    query = jnp.dot(queries_in, w_query, preferred_element_type=f32).astype(bf16)
    keys = jnp.dot(hits_in, w_key, preferred_element_type=f32).astype(bf16)
    vals = jnp.dot(hits_in, w_value, preferred_element_type=f32).astype(bf16)
    key_heads = split_heads(keys)
    value_heads = split_heads(vals)
    query_groups = query.reshape(groups, ROWS, width)

    def group_scores(query_rows, block_rows):
        allowed = jnp.repeat(block_rows, BLOCK, axis=0)[:, None, :]
        scores = (
            jnp.einsum(
                "rhd,khd->rhk", split_heads(query_rows), key_heads, preferred_element_type=f32
            )
            * score_scale
        )
        return (allowed, scores)

    def forward_group(inputs):
        query_rows, block_rows = inputs
        allowed, scores = group_scores(query_rows, block_rows)
        masked = jnp.where(allowed, scores, -1e30)
        maxima = jnp.max(masked, axis=2)
        exponents = jnp.where(allowed, jnp.exp(masked - maxima[..., None]), 0.0)
        totals = jnp.sum(exponents, axis=2)
        numer = jnp.einsum(
            "rhk,khd->rhd", exponents.astype(bf16), value_heads, preferred_element_type=f32
        )
        return (numer.reshape(ROWS, width), maxima, totals)

    numer_parts, maxima_parts, totals_parts = lax.map(forward_group, (query_groups, column_groups))
    numer_local = numer_parts.reshape(n_queries, width)
    maxima_local = maxima_parts.reshape(n_queries, HEADS)
    totals_local = totals_parts.reshape(n_queries, HEADS)
    numer, peak, total = merged((numer_local, maxima_local, totals_local), "region", merge_partials)
    attended = (numer / jnp.repeat(total, head_dim, axis=-1)).astype(bf16)
    log_total = peak + jnp.log(total)
    layer_out = (
        queries_in.astype(f32) + jnp.dot(attended, w_out, preferred_element_type=f32)
    ).astype(bf16)
    grad_att = lax.dot_general(
        grad_out, w_out, (((1,), (1,)), ((), ())), preferred_element_type=f32
    ).astype(bf16)
    grad_wo = jnp.einsum("qa,qb->ab", attended, grad_out, preferred_element_type=f32)
    deltas = jnp.sum(split_heads(grad_att).astype(f32) * split_heads(attended).astype(f32), axis=2)

    def backward_group(running, inputs):
        key_grad, value_grad = running
        query_rows, grad_rows, log_rows_g, delta_rows, block_rows = inputs
        allowed, scores = group_scores(query_rows, block_rows)
        attn_probs = jnp.where(allowed, jnp.exp(scores - log_rows_g[..., None]), 0.0)
        grad_heads = split_heads(grad_rows)
        value_grad = value_grad + jnp.einsum(
            "rhk,rhd->khd", attn_probs.astype(bf16), grad_heads, preferred_element_type=f32
        )
        grad_probs = jnp.einsum("rhd,khd->rhk", grad_heads, value_heads, preferred_element_type=f32)
        grad_scores = (attn_probs * (grad_probs - delta_rows[..., None]) * score_scale).astype(bf16)
        query_grad = jnp.einsum(
            "rhk,khd->rhd", grad_scores, key_heads, preferred_element_type=f32
        ).reshape(ROWS, width)
        key_grad = key_grad + jnp.einsum(
            "rhk,rhd->khd", grad_scores, split_heads(query_rows), preferred_element_type=f32
        )
        return ((key_grad, value_grad), query_grad)

    zero_grad = jnp.zeros((n_hits, HEADS, head_dim), f32)
    inputs_back = (
        query_groups,
        grad_att.reshape(groups, ROWS, width),
        log_total.reshape(groups, ROWS, HEADS),
        deltas.reshape(groups, ROWS, HEADS),
        column_groups,
    )
    (key_grad, value_grad), query_grad_parts = lax.scan(
        backward_group, (zero_grad, zero_grad), inputs_back
    )
    keys_grad = key_grad.reshape(n_hits, width).astype(bf16)
    vals_grad = value_grad.reshape(n_hits, width).astype(bf16)
    query_grad_local = query_grad_parts.reshape(n_queries, width)
    wk_part = jnp.einsum("ka,kb->ab", hits_in, keys_grad, preferred_element_type=f32)
    wv_part = jnp.einsum("ka,kb->ab", hits_in, vals_grad, preferred_element_type=f32)
    query_grad_sum, grad_wk, grad_wv = (
        lax.psum(query_grad_local.astype(jnp.bfloat16), "region").astype(jnp.float32),
        lax.psum(wk_part.astype(jnp.bfloat16), "region").astype(jnp.float32),
        lax.psum(wv_part.astype(jnp.bfloat16), "region").astype(jnp.float32),
    )
    grad_q = query_grad_sum.astype(bf16)
    grad_wq = jnp.einsum("qa,qb->ab", queries_in, grad_q, preferred_element_type=f32)
    grad_queries = (
        grad_out.astype(f32)
        + lax.dot_general(grad_q, w_query, (((1,), (1,)), ((), ())), preferred_element_type=f32)
    ).astype(bf16)
    grad_hits = (
        lax.dot_general(keys_grad, w_key, (((1,), (1,)), ((), ())), preferred_element_type=f32)
        + lax.dot_general(vals_grad, w_value, (((1,), (1,)), ((), ())), preferred_element_type=f32)
    ).astype(bf16)
    return (layer_out, grad_queries, grad_hits, grad_wq, grad_wk, grad_wv, grad_wo)


def solution(mesh):
    in_specs = (
        P("event", None),
        P(("event", "region"), None),
        P(),
        P(),
        P(),
        P(),
        P("event", None),
        P("event", None),
    )
    out_specs = (
        P("event", None),
        P("event", None),
        P(("event", "region"), None),
        P("event", None),
        P("event", None),
        P("event", None),
        P("event", None),
    )
    return jax.shard_map(
        on_device, mesh=mesh, in_specs=in_specs, out_specs=out_specs, check_vma=False
    )
```

profile of v0, /device:TPU:0, one launch (start us, length us, event | category | flops | bytes accessed | tf_op | source)
XLA Modules:
  0.0 451.3 jit_solution(18154993885858315720)
XLA Ops:
  14.3 36.3 %while.51 = (s32[]{:T(128)}, f32[2,512,512]{2,1,0:T(8,128)}, f32[2,512,8]{1,2,0:T(8,128)S(1)}, f32[2,512,8]{1,2,0:T(8,128)S(1)}, pred[2,4,1024]{2,1,0:T(4,128)(4...) while((s32[]{:T(128)}, f32[2,512,512]{2,1,0:T(8,128)}, ...), condition=%wide.region_4.5_spmd.clone, body=%wide.region_1.4_spmd.sunk.clone | while | flops 1128259584 | bytes 65679496 | solution.py:87
  18.6 5.2 %fusion.118 = f32[512,8]{0,1:T(8,128)S(1)} fusion(f32[8,512,1024]{2,1,0:T(8,128)S(1)} %get-tuple-element.707, f32[512,8]{0,1:T(8,128)S(1)} %get-tuple-element.708, pred[512,1024]{1,0:T(8,128)(4,1)S(1)} %bitcast.250), kind=kLoop, calls=%fused_computation.5.clone.1.clone | loop fusion | flops 20967424 | bytes 17334272 | tf_op jit(solution)/shard_map/while/body/eval_jaxpr/reduce_sum | solution.py:81
  23.7 6.0 %fusion.117 = f32[8,512,64]{1,2,0:T(8,128)} fusion(bf16[1024,8,64]{0,2,1:T(8,128)(2,1)S(1)} %copy-done.23, f32[8,512,1024]{2,1,0:T(8,128)S(1)} %get-tuple-element.707, f32[512,8]{0,1:T(8,128)S(1)} %get-tuple-element.708, pred[512,1024]{1,0:T(8,128)(4,1)S(1)} %bitcast.251), kind=kOutput, calls=%fused_computation.7.clone.1.clone | convolution fusion | flops 557842432 | bytes 19415040 | tf_op jit(solution)/shard_map/while/body/eval_jaxpr/rhk,khd->rhd/dot_general | solution.py:82
  36.7 5.2 %fusion.118 = f32[512,8]{0,1:T(8,128)S(1)} fusion(f32[8,512,1024]{2,1,0:T(8,128)S(1)} %get-tuple-element.707, f32[512,8]{0,1:T(8,128)S(1)} %get-tuple-element.708, pred[512,1024]{1,0:T(8,128)(4,1)S(1)} %bitcast.250), kind=kLoop, calls=%fused_computation.5.clone.1.clone | loop fusion | flops 20967424 | bytes 17334272 | tf_op jit(solution)/shard_map/while/body/eval_jaxpr/reduce_sum | solution.py:81
  41.9 6.0 %fusion.117 = f32[8,512,64]{1,2,0:T(8,128)} fusion(bf16[1024,8,64]{0,2,1:T(8,128)(2,1)S(1)} %copy-done.23, f32[8,512,1024]{2,1,0:T(8,128)S(1)} %get-tuple-element.707, f32[512,8]{0,1:T(8,128)S(1)} %get-tuple-element.708, pred[512,1024]{1,0:T(8,128)(4,1)S(1)} %bitcast.251), kind=kOutput, calls=%fused_computation.7.clone.1.clone | convolution fusion | flops 557842432 | bytes 19415040 | tf_op jit(solution)/shard_map/while/body/eval_jaxpr/rhk,khd->rhd/dot_general | solution.py:82
  50.6 16.0 %all_gather.11 = f32[8,1024,8]{1,2,0:T(8,128)S(1)} all-gather(f32[1,1024,8]{1,2,0:T(8,128)S(1)} %bitcast.273), channel_id=1, replica_groups=mesh['event'=4,'region'=8] {'region'}, dimensions={0}, use_global_device_ids=true | all-gather | bytes 294912 | tf_op jit(solution)/shard_map/all_gather | solution.py:14
  66.6 19.4 %all_gather.10 = f32[8,1024,8]{1,2,0:T(8,128)} all-gather(f32[1,1024,8]{1,2,0:T(8,128)S(1)} %bitcast.274), channel_id=1, replica_groups=mesh['event'=4,'region'=8] {'region'}, dimensions={0}, use_global_device_ids=true | all-gather | bytes 294912 | tf_op jit(solution)/shard_map/all_gather | solution.py:14
  87.8 118.8 %all-gather.2.cloned.1.call-done = f32[8,1024,512]{2,1,0:T(8,128)} async-done(((f32[1,1024,512]{2,1,0:T(8,128)}), f32[8,1024,512]{2,1,0:T(8,128)}) %all-gather.2.cloned.1.call-update) | async-done | bytes 16777232 | tf_op jit(solution)/shard_map/all_gather | solution.py:14
  212.6 65.3 %while.52 = (s32[]{:T(128)}, f32[1024,512]{0,1:T(8,128)}, f32[1024,8]{0,1:T(8,128)S(1)}, f32[1024,8]{0,1:T(8,128)S(1)}, f32[8,1024,8]{1,2,0:T(8,128)}, /*index=5*/f32[8,1024,512]{2,1,0:T(8,128)}, f32[8,1024,8]{1,2,0:T(8,128)S(1)}) while((s32[]{:T(128)}, f32[1024,512]{0,1:T(8,128)}, f32[1024,8]{0,1:T(8,128)S(1)}, ...), condition=%wide.region_6.7_spmd.clone, body=%wide.region_5.6_spmd.sunk.clone | while | flops 1622021 | bytes 15007863 | solution.py:20
  213.4 3.2 constant_dynamic-slice_fusion.14
  218.5 3.4 fusion.120
  222.8 3.2 constant_dynamic-slice_fusion.14
  227.9 3.4 fusion.120
  237.2 3.4 fusion.120
  246.5 3.4 fusion.120
  255.8 3.4 fusion.120
  265.2 3.4 fusion.120
  269.4 3.2 constant_dynamic-slice_fusion.14
  274.5 3.4 fusion.120
  282.9 5.5 %convert_multiply_fusion = (f32[1024,512]{1,0:T(8,128)}, bf16[1024,512]{1,0:T(8,128)(2,1)}, bf16[1024,512]{1,0:T(8,128)(2,1)}) fusion(f32[1024,512]{1,0:T(8,128)} %copy.52, f32[1024,512]{1,0:T(8,128)} %copy.53, bf16[1024,512]{1,0:T(8,128)(2,1)} %param.21, bf16[512,512]{1,0:T(8,128)(2,1)} %param.19), kind=kOutput, calls=%fused_computation.52 | convolution fusion | flops 540016640 | bytes 9961472 | tf_op jit(solution)/shard_map/dot_general | solution.py:97
  290.5 74.4 %while.53 = (s32[]{:T(128)}, f32[1024,8,64]{0,2,1:T(8,128)}, f32[1024,8,64]{0,2,1:T(8,128)}, bf16[2,512,512]{2,1,0:T(8,128)(2,1)}, bf16[2,512,512]{1,2,0:T(8,128...) while((s32[]{:T(128)}, f32[1024,8,64]{0,2,1:T(8,128)}, ...), condition=%wide.region_9.10_spmd.clone.clone, body=%wide.region_8.9_spmd.clone.sunk.clone | while | flops 2732589056 | bytes 147517968 | solution.py:130
  296.2 3.7 fusion.131
  299.9 5.2 %bitcast_add_fusion.7 = f32[1024,8,64]{0,2,1:T(8,128)} fusion(f32[1024,8,64]{0,2,1:T(8,128)} %get-tuple-element.827, bf16[512,8,64]{0,2,1:T(8,128)(2,1)S(1)} %bitcast.260, f32[8,512,1024]{2,1,0:T(8,128)S(1)} %fusion.131, f32[512,8]{0,1:T(8,128)S(1)} %copy-done.15, pred[512,1024]{1,0:T(8,128)(4,1)S(1)} %bitcast.258, pred[]{:T(512)S(6)} %compare.4), kind=kOutput, calls=%fused_computation.38.clone.1.clone | convolution fusion | flops 554696704 | bytes 22036480 | tf_op jit(solution)/shard_map/while/body/eval_jaxpr/rhk,rhd->khd/dot_general | solution.py:109
  305.1 10.5 %fusion.132 = bf16[512,8,1024]{2,0,1:T(8,128)(2,1)} fusion(f32[8,512,1024]{2,1,0:T(8,128)S(1)} %fusion.131, bf16[512,8,64]{0,2,1:T(8,128)(2,1)} %bitcast.259, bf16[1024,8,64]{0,2,1:T(8,128)(2,1)} %get-tuple-element.845, f32[512,8]{0,1:T(8,128)} %get-tuple-element.754, f32[512,8]{0,1:T(8,128)} %get-tuple-element.755, ...), kind=kOutput, calls=%fused_computation.31.clone.1.clone | convolution fusion | flops 566231040 | bytes 27295744 | tf_op jit(solution)/shard_map/while/body/eval_jaxpr/rhd,khd->rhk/dot_general | solution.py:112
  315.6 6.4 %fusion.133 = bf16[8,512,64]{1,2,0:T(8,128)(2,1)S(1)} fusion(bf16[512,8,1024]{2,0,1:T(8,128)(2,1)} %fusion.132, bf16[1024,8,64]{0,2,1:T(8,128)(2,1)} %get-tuple-element.842), kind=kOutput, calls=%fused_computation.72.clone.1.clone | convolution fusion | flops 536870912 | bytes 9961472 | tf_op jit(solution)/shard_map/while/body/eval_jaxpr/rhk,khd->rhd/dot_general | solution.py:114
  331.9 3.7 fusion.131
  335.6 6.4 %bitcast_add_fusion.7 = f32[1024,8,64]{0,2,1:T(8,128)} fusion(f32[1024,8,64]{0,2,1:T(8,128)} %get-tuple-element.827, bf16[512,8,64]{0,2,1:T(8,128)(2,1)S(1)} %bitcast.260, f32[8,512,1024]{2,1,0:T(8,128)S(1)} %fusion.131, f32[512,8]{0,1:T(8,128)S(1)} %copy-done.15, pred[512,1024]{1,0:T(8,128)(4,1)S(1)} %bitcast.258, pred[]{:T(512)S(6)} %compare.4), kind=kOutput, calls=%fused_computation.38.clone.1.clone | convolution fusion | flops 554696704 | bytes 22036480 | tf_op jit(solution)/shard_map/while/body/eval_jaxpr/rhk,rhd->khd/dot_general | solution.py:109
  342.0 10.5 %fusion.132 = bf16[512,8,1024]{2,0,1:T(8,128)(2,1)} fusion(f32[8,512,1024]{2,1,0:T(8,128)S(1)} %fusion.131, bf16[512,8,64]{0,2,1:T(8,128)(2,1)} %bitcast.259, bf16[1024,8,64]{0,2,1:T(8,128)(2,1)} %get-tuple-element.845, f32[512,8]{0,1:T(8,128)} %get-tuple-element.754, f32[512,8]{0,1:T(8,128)} %get-tuple-element.755, ...), kind=kOutput, calls=%fused_computation.31.clone.1.clone | convolution fusion | flops 566231040 | bytes 27295744 | tf_op jit(solution)/shard_map/while/body/eval_jaxpr/rhd,khd->rhk/dot_general | solution.py:112
  352.6 6.4 %fusion.133 = bf16[8,512,64]{1,2,0:T(8,128)(2,1)S(1)} fusion(bf16[512,8,1024]{2,0,1:T(8,128)(2,1)} %fusion.132, bf16[1024,8,64]{0,2,1:T(8,128)(2,1)} %get-tuple-element.842), kind=kOutput, calls=%fused_computation.72.clone.1.clone | convolution fusion | flops 536870912 | bytes 9961472 | tf_op jit(solution)/shard_map/while/body/eval_jaxpr/rhk,khd->rhd/dot_general | solution.py:114
  359.0 4.6 %bitcast_add_fusion.6 = f32[1024,8,64]{0,2,1:T(8,128)} fusion(f32[1024,8,64]{0,2,1:T(8,128)} %get-tuple-element.826, bf16[512,8,64]{0,2,1:T(8,128)(2,1)S(1)} %bitcast.253, bf16[512,8,1024]{2,0,1:T(8,128)(2,1)S(1)} %copy-done.1, pred[]{:T(512)S(6)} %compare.4), kind=kOutput, calls=%fused_computation.39.clone.1.clone | convolution fusion | flops 537919488 | bytes 13107201 | tf_op jit(solution)/shard_map/while/body/eval_jaxpr/rhk,rhd->khd/dot_general | solution.py:117
  371.5 3.4 fusion.34
  379.1 56.1 %all-reduce.3.cloned.1.call-done = (bf16[512,512]{0,1:T(8,128)(2,1)}, bf16[512,512]{0,1:T(8,128)(2,1)}, bf16[1024,512]{1,0:T(8,128)(2,1)}) async-done(((bf16[512,512]{0,1:T(8,128)(2,1)}, bf16[512,512]{0,1:T(8,128)(2,1)}, bf16[1024,512]{1,0:T(8,128)(2,1)}), (bf16[512,512]{0,1:T(8,128)(2,1)}, bf16[512,512]{0,1:T(8,128)(2,1)}, bf16[1024,512]{1,0:T(8,128)(2,1)})) %all-reduce.3.cloned.1.call-update) | async-done | bytes 2097168 | tf_op jit(solution)/shard_map/psum | solution.py:140
  (165 shorter events, 104.0 us)
Async XLA Ops:
  7.2 4.6 %copy-start = (bf16[1024,512]{1,0:T(8,128)(2,1)S(1)}, bf16[1024,512]{1,0:T(8,128)(2,1)}, u32[]{:S(2)}) copy-start(bf16[1024,512]{1,0:T(8,128)(2,1)} %param.15) | copy-start | bytes 3145732
  7.2 4.6 %copy-start.9 = (bf16[512,512]{1,0:T(8,128)(2,1)S(1)}, bf16[512,512]{1,0:T(8,128)(2,1)}, u32[]{:S(2)}) copy-start(bf16[512,512]{1,0:T(8,128)(2,1)} %param.17) | copy-start | bytes 1572868
  7.2 5.3 %copy-start.11 = (bf16[512,512]{1,0:T(8,128)(2,1)S(1)}, bf16[512,512]{1,0:T(8,128)(2,1)}, u32[]{:S(2)}) copy-start(bf16[512,512]{1,0:T(8,128)(2,1)} %param.18) | copy-start | bytes 1572868
  7.2 199.4 %all-gather.2.cloned.1.call-start = ((), (), s32[]{:S(2)}) async-start(), calls=%async_computation | async-start | bytes 18874368 | tf_op jit(solution)/shard_map/all_gather | solution.py:14
  18.5 5.2 %copy-start.23 = (bf16[1024,8,64]{0,2,1:T(8,128)(2,1)S(1)}, bf16[1024,8,64]{0,2,1:T(8,128)(2,1)}, u32[]{:S(2)}) copy-start(bf16[1024,8,64]{0,2,1:T(8,128)(2,1)} %get-tuple-element.792) | copy-start | bytes 3145732 | tf_op jit(solution)/shard_map/while
  36.7 5.2 %copy-start.23 = (bf16[1024,8,64]{0,2,1:T(8,128)(2,1)S(1)}, bf16[1024,8,64]{0,2,1:T(8,128)(2,1)}, u32[]{:S(2)}) copy-start(bf16[1024,8,64]{0,2,1:T(8,128)(2,1)} %get-tuple-element.792) | copy-start | bytes 3145732 | tf_op jit(solution)/shard_map/while
  50.6 162.1 %copy-start.4 = (bf16[1024,8,64]{0,2,1:T(8,128)(2,1)}, bf16[1024,8,64]{0,2,1:T(8,128)(2,1)S(1)}, u32[]{:S(2)}) copy-start(bf16[1024,8,64]{0,2,1:T(8,128)(2,1)S(1)} %get-tuple-element.854) | copy-start | bytes 3145732
  50.6 384.7 %all-reduce.3.cloned.1.call-start = ((), (), s32[]{:S(2)}) async-start(), calls=%async_computation.1 | async-start | bytes 4194304 | tf_op jit(solution)/shard_map/psum | solution.py:140
  290.6 4.8 %copy-start.16 = (f32[2,512,8]{1,2,0:T(8,128)}, f32[2,512,8]{1,2,0:T(8,128)S(1)}, u32[]{:S(2)}) copy-start(f32[2,512,8]{1,2,0:T(8,128)S(1)} %get-tuple-element.846) | copy-start | bytes 98308 | tf_op jit(solution)/shard_map/while
  290.6 4.8 %copy-start.18 = (f32[2,512,8]{1,2,0:T(8,128)}, f32[2,512,8]{1,2,0:T(8,128)S(1)}, u32[]{:S(2)}) copy-start(f32[2,512,8]{1,2,0:T(8,128)S(1)} %get-tuple-element.843) | copy-start | bytes 98308 | tf_op jit(solution)/shard_map/while
  296.2 3.7 copy-start.5
  296.2 3.7 copy-start.6
  296.2 3.7 copy-start.15
  315.6 6.4 %copy-start.1 = (bf16[512,8,1024]{2,0,1:T(8,128)(2,1)S(1)}, bf16[512,8,1024]{2,0,1:T(8,128)(2,1)}, u32[]{:S(2)}) copy-start(bf16[512,8,1024]{2,0,1:T(8,128)(2,1)} %fusion.132) | copy-start | bytes 25165828 | tf_op jit(solution)/shard_map/while
  315.6 6.4 %copy-start.3 = (bf16[1,512,512]{1,2,0:T(8,128)(2,1)S(1)}, bf16[1,512,512]{1,2,0:T(8,128)(2,1)}, u32[]{:S(2)}) copy-start(bf16[1,512,512]{1,2,0:T(8,128)(2,1)} %copy-done.2) | copy-start | bytes 1572868 | tf_op jit(solution)/shard_map/while
  322.1 4.2 copy-start.17
  322.1 4.2 copy-start.19
  326.3 4.8 %copy-start.16 = (f32[2,512,8]{1,2,0:T(8,128)}, f32[2,512,8]{1,2,0:T(8,128)S(1)}, u32[]{:S(2)}) copy-start(f32[2,512,8]{1,2,0:T(8,128)S(1)} %get-tuple-element.846) | copy-start | bytes 98308 | tf_op jit(solution)/shard_map/while
  326.3 4.8 %copy-start.18 = (f32[2,512,8]{1,2,0:T(8,128)}, f32[2,512,8]{1,2,0:T(8,128)S(1)}, u32[]{:S(2)}) copy-start(f32[2,512,8]{1,2,0:T(8,128)S(1)} %get-tuple-element.843) | copy-start | bytes 98308 | tf_op jit(solution)/shard_map/while
  331.9 3.7 copy-start.5
  331.9 3.7 copy-start.6
  331.9 3.7 copy-start.15
  352.5 6.4 %copy-start.1 = (bf16[512,8,1024]{2,0,1:T(8,128)(2,1)S(1)}, bf16[512,8,1024]{2,0,1:T(8,128)(2,1)}, u32[]{:S(2)}) copy-start(bf16[512,8,1024]{2,0,1:T(8,128)(2,1)} %fusion.132) | copy-start | bytes 25165828 | tf_op jit(solution)/shard_map/while
  352.5 6.4 %copy-start.3 = (bf16[1,512,512]{1,2,0:T(8,128)(2,1)S(1)}, bf16[1,512,512]{1,2,0:T(8,128)(2,1)}, u32[]{:S(2)}) copy-start(bf16[1,512,512]{1,2,0:T(8,128)(2,1)} %copy-done.2) | copy-start | bytes 1572868 | tf_op jit(solution)/shard_map/while
  359.0 4.9 %copy-start.7 = (bf16[2,512,512]{2,1,0:T(8,128)(2,1)S(1)}, bf16[2,512,512]{2,1,0:T(8,128)(2,1)}, u32[]{:S(2)}) copy-start(bf16[2,512,512]{2,1,0:T(8,128)(2,1)} %get-tuple-element.828) | copy-start | bytes 3145732 | tf_op jit(solution)/shard_map/while
  359.0 5.9 %copy-start.17 = (f32[2,512,8]{1,2,0:T(8,128)S(1)}, f32[2,512,8]{1,2,0:T(8,128)}, u32[]{:S(2)}) copy-start(f32[2,512,8]{1,2,0:T(8,128)} %copy-done.16) | copy-start | bytes 98308 | tf_op jit(solution)/shard_map/while
  359.0 5.9 %copy-start.19 = (f32[2,512,8]{1,2,0:T(8,128)S(1)}, f32[2,512,8]{1,2,0:T(8,128)}, u32[]{:S(2)}) copy-start(f32[2,512,8]{1,2,0:T(8,128)} %copy-done.18) | copy-start | bytes 98308 | tf_op jit(solution)/shard_map/while
  371.5 4.2 copy-start.20
  371.5 4.2 copy-start.22
  371.5 4.2 copy-start.24
  435.2 5.6 %copy-start.14 = (bf16[512,512]{0,1:T(8,128)(2,1)S(1)}, bf16[512,512]{0,1:T(8,128)(2,1)}, u32[]{:S(2)}) copy-start(bf16[512,512]{0,1:T(8,128)(2,1)} %get-tuple-element.503) | copy-start | bytes 1572868
  435.2 6.7 %copy-start.13 = (bf16[512,512]{0,1:T(8,128)(2,1)S(1)}, bf16[512,512]{0,1:T(8,128)(2,1)}, u32[]{:S(2)}) copy-start(bf16[512,512]{0,1:T(8,128)(2,1)} %get-tuple-element.504) | copy-start | bytes 1572868
  (8 other events, 15.1 us)
Sparse Core Ops, SparseCore 0:
  50.7 155.8 all-gather.1
  371.6 63.6 all-reduce.2
where the time goes:
time: 453 us; the launch traced here: 451 us
  waiting for transfers between devices  175 us (39%)
  matrix products  105 us (23%)
  local copies, waits for them, and re-layouts  75.9 us (17%)
  other arithmetic  45.6 us (10%)
  blocking collectives  35.3 us (8%)
  between operations  14.3 us (3%)
    all_gather x1, waiting for transfers between devices, merged(): everything = jax.tree.map(lambda part: lax.all_gather(part, axis), shard)  119 us
    psum x1, waiting for transfers between devices, on_device(): lax.psum(wk_part.astype(jnp.bfloat16), 'region').astype(jnp.float32)  56.1 us
    dynamic_slice x14, local copies, waits for them, and re-layouts, lap(): return combine(so_far, jax.tree.map(lambda part: part[k], everything))  35.6 us
    all_gather x2, blocking collectives, merged(): everything = jax.tree.map(lambda part: lax.all_gather(part, axis), shard)  35.3 us
    add x7, other arithmetic, merge_partials(): numer_a * jnp.repeat(scale_a, head_dim, axis=-1)  24.1 us
    dot_general x2, matrix products, backward_group(): jnp.einsum('rhd,khd->rhk', grad_heads, value_heads, preferred_element_typ...  21 us
    dot_general x4, matrix products, group_scores(): jnp.einsum('rhd,khd->rhk', split_heads(query_rows), key_heads, preferred_...  13.4 us
    dot_general x2, matrix products, backward_group(): jnp.einsum('rhk,khd->rhd', grad_scores, key_heads, preferred_element_type...  12.8 us
  transfers between devices with their start and end apart: 2, of which 2 were waited for; matrix products, arithmetic and copies ran while one was open for 2% of the time, Pallas kernels for 0%

commit v1 on v0

v1 whole, which is shorter than its diff:
```python
import functools
import math

import jax
import jax.numpy as jnp
from jax import lax
from jax.experimental import pallas as pl
from jax.experimental.pallas import tpu as pltpu
from jax.sharding import PartitionSpec as P

HEADS = 8
BLOCK = 128
TQ = 256


def _fwd_kernel(q_ref, k_ref, v_ref, cm_ref, numer_ref, m_ref, l_ref, *, scale):
    q = q_ref[0]
    k = k_ref[0]
    v = v_ref[0]
    s = lax.dot_general(q, k, (((1,), (1,)), ((), ())), preferred_element_type=jnp.float32) * scale
    tq, nk = s.shape
    nb = tq // BLOCK
    s3 = s.reshape(nb, BLOCK, nk)
    allowed = cm_ref[...] > 0.5
    masked = jnp.where(allowed, s3, -1e30)
    mx = jnp.max(masked, axis=2, keepdims=True)
    e = jnp.where(allowed, jnp.exp(masked - mx), 0.0)
    tot = jnp.sum(e, axis=2, keepdims=True)
    numer = jnp.dot(
        e.reshape(tq, nk).astype(jnp.bfloat16), v, preferred_element_type=jnp.float32
    )
    numer_ref[0] = numer
    m_ref[0] = mx.reshape(tq, 1)
    l_ref[0] = tot.reshape(tq, 1)


def _bwd_kernel(q_ref, k_ref, v_ref, ga_ref, lt_ref, dl_ref, cm_ref, dq_ref, dk_ref, dv_ref, *, scale):
    i = pl.program_id(1)

    @pl.when(i == 0)
    def _():
        dk_ref[...] = jnp.zeros_like(dk_ref)
        dv_ref[...] = jnp.zeros_like(dv_ref)

    q = q_ref[0]
    k = k_ref[0]
    v = v_ref[0]
    ga = ga_ref[0]
    s = lax.dot_general(q, k, (((1,), (1,)), ((), ())), preferred_element_type=jnp.float32) * scale
    tq, nk = s.shape
    nb = tq // BLOCK
    s3 = s.reshape(nb, BLOCK, nk)
    allowed = cm_ref[...] > 0.5
    lt = lt_ref[0].reshape(nb, BLOCK, 1)
    p = jnp.where(allowed, jnp.exp(s3 - lt), 0.0).reshape(tq, nk)
    dv_ref[0] += lax.dot_general(
        p.astype(jnp.bfloat16), ga, (((0,), (0,)), ((), ())), preferred_element_type=jnp.float32
    )
    dp = lax.dot_general(ga, v, (((1,), (1,)), ((), ())), preferred_element_type=jnp.float32)
    ds = (p * (dp - dl_ref[0]) * scale).astype(jnp.bfloat16)
    dq_ref[0] = jnp.dot(ds, k, preferred_element_type=jnp.float32)
    dk_ref[0] += lax.dot_general(
        ds, q, (((0,), (0,)), ((), ())), preferred_element_type=jnp.float32
    )


def _forward(qT, kT, vT, cm, scale):
    heads, nq, hd = qT.shape
    nk = kT.shape[1]
    nb = TQ // BLOCK
    f32 = jnp.float32
    return pl.pallas_call(
        functools.partial(_fwd_kernel, scale=scale),
        grid=(heads, nq // TQ),
        in_specs=[
            pl.BlockSpec((1, TQ, hd), lambda h, i: (h, i, 0)),
            pl.BlockSpec((1, nk, hd), lambda h, i: (h, 0, 0)),
            pl.BlockSpec((1, nk, hd), lambda h, i: (h, 0, 0)),
            pl.BlockSpec((nb, 1, nk), lambda h, i: (i, 0, 0)),
        ],
        out_specs=[
            pl.BlockSpec((1, TQ, hd), lambda h, i: (h, i, 0)),
            pl.BlockSpec((1, TQ, 1), lambda h, i: (h, i, 0)),
            pl.BlockSpec((1, TQ, 1), lambda h, i: (h, i, 0)),
        ],
        out_shape=[
            jax.ShapeDtypeStruct((heads, nq, hd), f32),
            jax.ShapeDtypeStruct((heads, nq, 1), f32),
            jax.ShapeDtypeStruct((heads, nq, 1), f32),
        ],
    )(qT, kT, vT, cm)


def _backward(qT, kT, vT, gaT, lt, dl, cm, scale):
    heads, nq, hd = qT.shape
    nk = kT.shape[1]
    nb = TQ // BLOCK
    f32 = jnp.float32
    return pl.pallas_call(
        functools.partial(_bwd_kernel, scale=scale),
        grid=(heads, nq // TQ),
        in_specs=[
            pl.BlockSpec((1, TQ, hd), lambda h, i: (h, i, 0)),
            pl.BlockSpec((1, nk, hd), lambda h, i: (h, 0, 0)),
            pl.BlockSpec((1, nk, hd), lambda h, i: (h, 0, 0)),
            pl.BlockSpec((1, TQ, hd), lambda h, i: (h, i, 0)),
            pl.BlockSpec((1, TQ, 1), lambda h, i: (h, i, 0)),
            pl.BlockSpec((1, TQ, 1), lambda h, i: (h, i, 0)),
            pl.BlockSpec((nb, 1, nk), lambda h, i: (i, 0, 0)),
        ],
        out_specs=[
            pl.BlockSpec((1, TQ, hd), lambda h, i: (h, i, 0)),
            pl.BlockSpec((1, nk, hd), lambda h, i: (h, 0, 0)),
            pl.BlockSpec((1, nk, hd), lambda h, i: (h, 0, 0)),
        ],
        out_shape=[
            jax.ShapeDtypeStruct((heads, nq, hd), f32),
            jax.ShapeDtypeStruct((heads, nk, hd), f32),
            jax.ShapeDtypeStruct((heads, nk, hd), f32),
        ],
        compiler_params=pltpu.CompilerParams(dimension_semantics=("parallel", "arbitrary")),
    )(qT, kT, vT, gaT, lt, dl, cm)


def on_device(queries_in, hits_in, w_query, w_key, w_value, w_out, mask_list, grad_out):
    f32 = jnp.float32
    bf16 = jnp.bfloat16
    region_index = lax.axis_index("region")
    n_queries, width = queries_in.shape
    n_hits = hits_in.shape[0]
    head_dim = width // HEADS
    scale = 1.0 / math.sqrt(head_dim)
    hit_blocks = n_hits // BLOCK
    q_blocks = n_queries // BLOCK
    local_ids = region_index * hit_blocks + jnp.arange(hit_blocks, dtype=jnp.int32)
    blockmask = jnp.any(mask_list[:, :, None] == local_ids[None, None, :], axis=1)
    cm = jnp.repeat(blockmask.astype(f32), BLOCK, axis=1).reshape(q_blocks, 1, n_hits)

    def heads(x):
        return x.reshape(x.shape[0], HEADS, head_dim).transpose(1, 0, 2)

    def joined(x):
        return x.transpose(1, 0, 2).reshape(x.shape[1], width)

    query = jnp.dot(queries_in, w_query, preferred_element_type=f32).astype(bf16)
    keys = jnp.dot(hits_in, w_key, preferred_element_type=f32).astype(bf16)
    vals = jnp.dot(hits_in, w_value, preferred_element_type=f32).astype(bf16)
    qT, kT, vT = heads(query), heads(keys), heads(vals)

    numer_r, max_r, total_r = _forward(qT, kT, vT, cm, scale)
    peak = lax.pmax(max_r, "region")
    weight = jnp.exp(max_r - peak)
    numer, total = lax.psum((numer_r * weight, total_r * weight), "region")
    attended_h = (numer / total).astype(bf16)
    log_total = peak + jnp.log(total)
    attended = joined(attended_h)
    layer_out = (
        queries_in.astype(f32) + jnp.dot(attended, w_out, preferred_element_type=f32)
    ).astype(bf16)
    grad_att = lax.dot_general(
        grad_out, w_out, (((1,), (1,)), ((), ())), preferred_element_type=f32
    ).astype(bf16)
    grad_wo = jnp.einsum("qa,qb->ab", attended, grad_out, preferred_element_type=f32)
    gaT = heads(grad_att)
    deltas = jnp.sum(gaT.astype(f32) * attended_h.astype(f32), axis=2, keepdims=True)

    dq_r, dk, dv = _backward(qT, kT, vT, gaT, log_total, deltas, cm, scale)
    keys_grad = joined(dk).astype(bf16)
    vals_grad = joined(dv).astype(bf16)
    query_grad_local = joined(dq_r)
    wk_part = jnp.einsum("ka,kb->ab", hits_in, keys_grad, preferred_element_type=f32)
    wv_part = jnp.einsum("ka,kb->ab", hits_in, vals_grad, preferred_element_type=f32)
    query_grad_sum, grad_wk, grad_wv = lax.psum(
        (query_grad_local.astype(bf16), wk_part.astype(bf16), wv_part.astype(bf16)), "region"
    )
    grad_wk = grad_wk.astype(f32)
    grad_wv = grad_wv.astype(f32)
    grad_q = query_grad_sum
    grad_wq = jnp.einsum("qa,qb->ab", queries_in, grad_q, preferred_element_type=f32)
    grad_queries = (
        grad_out.astype(f32)
        + lax.dot_general(grad_q, w_query, (((1,), (1,)), ((), ())), preferred_element_type=f32)
    ).astype(bf16)
    grad_hits = (
        lax.dot_general(keys_grad, w_key, (((1,), (1,)), ((), ())), preferred_element_type=f32)
        + lax.dot_general(vals_grad, w_value, (((1,), (1,)), ((), ())), preferred_element_type=f32)
    ).astype(bf16)
    return (layer_out, grad_queries, grad_hits, grad_wq, grad_wk, grad_wv, grad_wo)


def solution(mesh):
    in_specs = (
        P("event", None),
        P(("event", "region"), None),
        P(),
        P(),
        P(),
        P(),
        P("event", None),
        P("event", None),
    )
    out_specs = (
        P("event", None),
        P("event", None),
        P(("event", "region"), None),
        P("event", None),
        P("event", None),
        P("event", None),
        P("event", None),
    )
    return jax.shard_map(
        on_device, mesh=mesh, in_specs=in_specs, out_specs=out_specs, check_vma=False
    )
```

time: 453 us -> 477 us (1.053)
  blocking collectives: 35.3 us -> 249 us
  waiting for transfers between devices: 175 us -> 58.4 us
  matrix products: 105 us -> 25.1 us
  Pallas kernels: 0 us -> 73 us
  local copies, waits for them, and re-layouts: 75.9 us -> 24.3 us
  other arithmetic: 45.6 us -> 31.3 us
    psum x0 -> x1, blocking collectives: none -> 158 us  [on_device(): numer, total = lax.psum((numer_r * weight, total_r * weight), 'region')]
    all_gather x1 -> x0, waiting for transfers between devices: 119 us -> none  [merged(): everything = jax.tree.map(lambda part: lax.all_gather(part, axis), shard)]
    pmax x0 -> x1, blocking collectives: none -> 90.6 us  [on_device(): peak = lax.pmax(max_r, 'region')]
    dot_general x14 -> x0, matrix products: 78.5 us -> none  [the longest x2 21 us: backward_group(): jnp.einsum('rhd,khd->rhk', grad_heads, value_heads, preferred_element_typ...]
    pallas_call x0 -> x2, Pallas kernels: none -> 73 us  [the longest x1 44.2 us: _backward(): pl.pallas_call(functools.partial(_bwd_kernel, scale=scale), grid=(heads,...]
    dynamic_slice x23 -> x0, local copies, waits for them, and re-layouts: 44.3 us -> none  [the longest x14 35.6 us: lap(): return combine(so_far, jax.tree.map(lambda part: part[k], everything))]
    all_gather x2 -> x0, blocking collectives: 35.3 us -> none  [merged(): everything = jax.tree.map(lambda part: lax.all_gather(part, axis), shard)]
    add x14 -> x1, other arithmetic: 29.6 us -> 0.01 us  [on_device(): region_index * hit_blocks + jnp.arange(hit_blocks, dtype=jnp.int32)]
  transfers between devices with their start and end apart: 2 -> 2, of which waited for: 2 -> 1; matrix products, arithmetic and copies ran while one was open for 2% -> 4% of each run, Pallas kernels for 0% -> 0%
where the time goes in v1:
time: 477 us; the launch traced here: 475 us
  blocking collectives  249 us (52%)
  Pallas kernels  73 us (15%)
  waiting for transfers between devices  58.4 us (12%)
  other arithmetic  31.3 us (7%)
  matrix products  25.1 us (5%)
  local copies, waits for them, and re-layouts  24.3 us (5%)
  between operations  14.2 us (3%)
    psum x1, blocking collectives, on_device(): numer, total = lax.psum((numer_r * weight, total_r * weight), 'region')  158 us
    pmax x1, blocking collectives, on_device(): peak = lax.pmax(max_r, 'region')  90.6 us
    psum x1, waiting for transfers between devices, on_device(): lax.psum((query_grad_local.astype(bf16), wk_part.astype(bf16), wv_part.as...  58.4 us
    pallas_call x1, Pallas kernels, _backward(): pl.pallas_call(functools.partial(_bwd_kernel, scale=scale), grid=(heads,...  44.2 us
    pallas_call x1, Pallas kernels, _forward(): pl.pallas_call(functools.partial(_fwd_kernel, scale=scale), grid=(heads,...  28.8 us
    mul x2, other arithmetic, on_device(): numer, total = lax.psum((numer_r * weight, total_r * weight), 'region')  10.9 us
  transfers between devices with their start and end apart: 2, of which 1 were waited for; matrix products, arithmetic and copies ran while one was open for 4% of the time, Pallas kernels for 0%

profile of v1, /device:TPU:0, one launch (start us, length us, event | category | flops | bytes accessed | tf_op | source)
XLA Modules:
  0.0 475.4 jit_solution(14059532281690368642)
XLA Ops:
  8.3 2.1 convolution_convert_fusion.3
  10.5 1.8 copy.30
  13.0 1.8 copy.31
  15.6 1.8 copy.32
  18.1 28.8 %shard_map.135 = (f32[8,1024,64]{2,1,0:T(8,128)}, f32[8,1024,1]{2,1,0:T(8,128)}, f32[8,1024,1]{2,1,0:T(8,128)}) custom-call(bf16[8,1024,64]{2,1,0:T(8,128)(2,1)} %bitcast.53, bf16[8,1024,64]{2,1,0:T(8,128)(2,1)} %bitcast.55, bf16[8,1024,64]{2,1,0:T(8,128)(2,1)} %bitcast.57, f32[8,1,1024]{2,1,0:T(1,128)} %bitcast.71), custom_call_target="tpu_custom_call" | custom-call | tf_op jit(solution)/shard_map/pallas_call | solution.py:72
  46.9 90.6 %pmax.7 = f32[8,1024,1]{2,1,0:T(8,128)} all-reduce(f32[8,1024,1]{2,1,0:T(8,128)} %get-tuple-element.14), channel_id=1, replica_groups=mesh['event'=4,'region'=8] {'region'}, use_global_device_ids=true, to_apply=%region_1.0 | all-reduce | flops 8192 | bytes 65536 | tf_op jit(solution)/shard_map/pmax | solution.py:151
  137.5 7.8 %fusion = (f32[8,1024,1]{2,1,0:T(8,128)}, f32[8,1024]{1,0:T(8,128)S(1)}) fusion(f32[8,1024,1]{2,1,0:T(8,128)} %get-tuple-element.15, f32[8,1024,1]{2,1,0:T(8,128)} %get-tuple-element.14, f32[8,1024,1]{2,1,0:T(8,128)} %pmax.7), kind=kLoop, calls=%fused_computation.11 | loop fusion | flops 16384 | bytes 163840 | tf_op jit(solution)/shard_map/mul | solution.py:153
  145.3 3.1 broadcast_multiply_fusion
  149.7 1.7 convolution_convert_fusion
  151.5 2.0 copy.34
  153.5 158.3 %psum.36 = f32[8,1024,1]{2,1,0:T(8,128)} all-reduce(f32[8,1024,1]{2,1,0:T(8,128)} %get-tuple-element.43), channel_id=1, replica_groups=mesh['event'=4,'region'=8] {'region'}, use_global_device_ids=true, to_apply=%region_3.0 | all-reduce | flops 8192 | bytes 65536 | tf_op jit(solution)/shard_map/psum | solution.py:153
  311.8 6.4 %log_add_fusion = (f32[8,1024,1]{2,1,0:T(8,128)}, f32[8,1024]{1,0:T(8,128)S(1)}) fusion(f32[8,1024,1]{2,1,0:T(8,128)} %pmax.7, f32[8,1024,1]{2,1,0:T(8,128)} %psum.36), kind=kLoop, calls=%fused_computation.1 | loop fusion | flops 8192 | bytes 131072 | tf_op jit(solution)/shard_map/add | solution.py:155
  318.2 4.9 %multiply_reduce_fusion = (f32[8,1024]{1,0:T(8,128)S(1)}, bf16[1024,8,64]{2,0,1:T(8,128)(2,1)}) fusion(bf16[1024,8,64]{2,0,1:T(8,128)(2,1)S(1)} %copy.34, f32[8,1024,64]{2,1,0:T(8,128)} %all-reduce.4.cloned.1.call-done, f32[8,1024]{1,0:T(8,128)S(1)} %get-tuple-element.48), kind=kLoop, calls=%fused_computation | loop fusion | flops 3137536 | bytes 4259840 | tf_op jit(solution)/shard_map/reduce_sum | solution.py:165
  323.2 2.7 copy.33
  325.9 2.6 copy.35.dl_ref
  328.5 44.2 %shard_map.136 = (f32[8,1024,64]{2,1,0:T(8,128)}, f32[8,1024,64]{2,1,0:T(8,128)}, f32[8,1024,64]{2,1,0:T(8,128)}) custom-call(bf16[8,1024,64]{2,1,0:T(8,128)(2,1)} %bitcast.54, bf16[8,1024,64]{2,1,0:T(8,128)(2,1)} %bitcast.56, bf16[8,1024,64]{2,1,0:T(8,128)(2,1)} %bitcast.58, bf16[8,1024,64]{2,1,0:T(8,128)(2,1)} %bitcast.59, ...), custom_call_target="tpu_custom_call" | custom-call | tf_op jit(solution)/shard_map/pallas_call | solution.py:99
  372.7 2.5 convert_bitcast_fusion.2
  375.2 1.6 copy.36
  376.8 5.5 %convert_bitcast_fusion = (bf16[1024,8,64]{2,0,1:T(8,128)(2,1)}, bf16[1024,8,64]{2,0,1:T(8,128)(2,1)S(1)}) fusion(f32[8,1024,64]{2,1,0:T(8,128)} %get-tuple-element.18, f32[8,1024,64]{2,1,0:T(8,128)} %get-tuple-element.17), kind=kLoop, calls=%fused_computation.5 | loop fusion | flops 1048576 | bytes 6291456 | tf_op jit(solution)/shard_map/convert_element_type | solution.py:169
  382.3 2.7 copy.38
  385.0 2.7 fusion.3
  387.8 1.6 copy.37
  389.4 2.9 fusion.2
  392.3 3.0 fusion.6
  395.3 1.9 fusion.5
  397.3 1.7 add_convert_fusion.2
  399.0 1.7 add_convert_fusion
  400.7 58.4 %all-reduce.6.cloned.1.call-done = (bf16[512,512]{0,1:T(8,128)(2,1)}, bf16[512,512]{0,1:T(8,128)(2,1)}, bf16[1024,512]{0,1:T(8,128)(2,1)}) async-done(((bf16[512,512]{0,1:T(8,128)(2,1)}, bf16[512,512]{0,1:T(8,128)(2,1)}, bf16[1024,512]{0,1:T(8,128)(2,1)}), (bf16[512,512]{0,1:T(8,128)(2,1)}, bf16[512,512]{0,1:T(8,128)(2,1)}, bf16[1024,512]{0,1:T(8,128)(2,1)})) %all-reduce.6.cloned.1.call-update) | async-done | bytes 2097168 | tf_op jit(solution)/shard_map/psum | solution.py:173
  459.1 2.3 convolution_bitcast_fusion
  461.4 3.4 add_convert_fusion.1
  464.9 1.2 copy.40
  467.2 1.3 copy.39
  (42 shorter events, 5.9 us)
Async XLA Ops:
  7.2 5.1 %copy-start = (bf16[1024,512]{1,0:T(8,128)(2,1)S(1)}, bf16[1024,512]{1,0:T(8,128)(2,1)}, u32[]{:S(2)}) copy-start(bf16[1024,512]{1,0:T(8,128)(2,1)} %param.9) | copy-start | bytes 3145732
  7.2 5.1 %copy-start.6 = (bf16[512,512]{1,0:T(8,128)(2,1)S(1)}, bf16[512,512]{1,0:T(8,128)(2,1)}, u32[]{:S(2)}) copy-start(bf16[512,512]{1,0:T(8,128)(2,1)} %param.11) | copy-start | bytes 1572868
  7.2 311.0 %all-reduce.4.cloned.1.call-start = ((), (), s32[]{:S(2)}) async-start(), calls=%async_computation | async-start | bytes 8388608 | tf_op jit(solution)/shard_map/psum | solution.py:153
  10.5 4.4 copy-start.7
  137.5 7.8 %copy-start.3 = (f32[8,1024,64]{2,1,0:T(8,128)S(1)}, f32[8,1024,64]{2,1,0:T(8,128)}, u32[]{:S(2)}) copy-start(f32[8,1024,64]{2,1,0:T(8,128)} %get-tuple-element.13) | copy-start | bytes 6291460
  148.4 1.2 copy-start.12
  148.4 1.4 copy-start.13
  148.4 310.7 %all-reduce.6.cloned.1.call-start = ((), (), s32[]{:S(2)}) async-start(), calls=%async_computation.1 | async-start | bytes 4194304 | tf_op jit(solution)/shard_map/psum | solution.py:173
  153.5 164.8 %copy-start.1 = (bf16[1024,8,64]{2,0,1:T(8,128)(2,1)}, bf16[1024,8,64]{2,0,1:T(8,128)(2,1)S(1)}, u32[]{:S(2)}) copy-start(bf16[1024,8,64]{2,0,1:T(8,128)(2,1)S(1)} %copy.34) | copy-start | bytes 3145732
  389.4 2.9 copy-start.5
  389.4 6.0 %copy-start.2 = (bf16[1024,8,64]{0,2,1:T(8,128)(2,1)S(1)}, bf16[1024,8,64]{0,2,1:T(8,128)(2,1)}, u32[]{:S(2)}) copy-start(bf16[1024,8,64]{0,2,1:T(8,128)(2,1)} %copy.37) | copy-start | bytes 3145732
  392.3 5.0 %copy-start.11 = (bf16[1024,512]{1,0:T(8,128)(2,1)S(1)}, bf16[1024,512]{1,0:T(8,128)(2,1)}, u32[]{:S(2)}) copy-start(bf16[1024,512]{1,0:T(8,128)(2,1)} %param.8) | copy-start | bytes 3145732
  392.3 5.0 %copy-start.14 = (bf16[512,512]{1,0:T(8,128)(2,1)S(1)}, bf16[512,512]{1,0:T(8,128)(2,1)}, u32[]{:S(2)}) copy-start(bf16[512,512]{1,0:T(8,128)(2,1)} %param.13) | copy-start | bytes 1572868
  395.3 3.7 copy-start.4
  395.3 3.7 copy-start.8
  459.1 5.8 %copy-start.10 = (bf16[512,512]{0,1:T(8,128)(2,1)S(1)}, bf16[512,512]{0,1:T(8,128)(2,1)}, u32[]{:S(2)}) copy-start(bf16[512,512]{0,1:T(8,128)(2,1)} %get-tuple-element.40) | copy-start | bytes 1572868
  459.1 7.0 %copy-start.9 = (bf16[512,512]{0,1:T(8,128)(2,1)S(1)}, bf16[512,512]{0,1:T(8,128)(2,1)}, u32[]{:S(2)}) copy-start(bf16[512,512]{0,1:T(8,128)(2,1)} %get-tuple-element.41) | copy-start | bytes 1572868
Sparse Core Ops, SparseCore 0:
  148.5 166.4 all-reduce.3
  392.4 66.6 all-reduce.5

commit v2 on v1

--- a/solution.py
+++ b/solution.py
@@ -148,12 +148,15 @@
     qT, kT, vT = heads(query), heads(keys), heads(vals)
 
     numer_r, max_r, total_r = _forward(qT, kT, vT, cm, scale)
+    max_r = max_r.reshape(HEADS, n_queries)
+    total_r = total_r.reshape(HEADS, n_queries)
     peak = lax.pmax(max_r, "region")
     weight = jnp.exp(max_r - peak)
-    numer, total = lax.psum((numer_r * weight, total_r * weight), "region")
-    attended_h = (numer / total).astype(bf16)
-    log_total = peak + jnp.log(total)
-    attended = joined(attended_h)
+    spread = jnp.repeat(weight.T, head_dim, axis=1)
+    numer, total = lax.psum((joined(numer_r) * spread, total_r * weight), "region")
+    attended = (numer / jnp.repeat(total.T, head_dim, axis=1)).astype(bf16)
+    log_total = (peak + jnp.log(total)).reshape(HEADS, n_queries, 1)
+    attended_h = heads(attended)
     layer_out = (
         queries_in.astype(f32) + jnp.dot(attended, w_out, preferred_element_type=f32)
     ).astype(bf16)

time: 477 us -> 309 us (0.65)
  blocking collectives: 249 us -> 57.3 us
  waiting for transfers between devices: 58.4 us -> 86.2 us
  local copies, waits for them, and re-layouts: 24.3 us -> 33.6 us
  other arithmetic: 31.3 us -> 23.2 us
  matrix products: 25.1 us -> 19.5 us
    psum x1, blocking collectives: 158 us -> 27 us  [on_device(): lax.psum((joined(numer_r) * spread, total_r * weight), 'region')]
    pmax x1, blocking collectives: 90.6 us -> 30.3 us  [on_device(): peak = lax.pmax(max_r, 'region')]
    psum x1, waiting for transfers between devices: 0.01 us -> 28.9 us  [on_device(): lax.psum((joined(numer_r) * spread, total_r * weight), 'region')]
    pallas_call x0 -> x2, other arithmetic: none -> 6.67 us  [_forward(): pl.pallas_call(functools.partial(_fwd_kernel, scale=scale), grid=(heads,...]
    mul x2, other arithmetic: 10.9 us -> 4.26 us  [the longest x1 4.24 us: on_device(): joined(numer_r) * spread]
    add x1 -> x0, other arithmetic: 6.43 us -> none  [on_device(): log_total = peak + jnp.log(total)]
  transfers between devices with their start and end apart: 2 -> 2, of which waited for: 1 -> 2; matrix products, arithmetic and copies ran while one was open for 4% -> 4% of each run, Pallas kernels for 0% -> 0%
where the time goes in v2:
time: 309 us; the launch traced here: 307 us
  waiting for transfers between devices  86.2 us (28%)
  Pallas kernels  72.9 us (24%)
  blocking collectives  57.3 us (19%)
  local copies, waits for them, and re-layouts  33.6 us (11%)
  other arithmetic  23.2 us (8%)
  matrix products  19.5 us (6%)
  between operations  14.2 us (5%)
    psum x1, waiting for transfers between devices, on_device(): lax.psum((query_grad_local.astype(bf16), wk_part.astype(bf16), wv_part.as...  57.3 us
    pallas_call x1, Pallas kernels, _backward(): pl.pallas_call(functools.partial(_bwd_kernel, scale=scale), grid=(heads,...  44.2 us
    pmax x1, blocking collectives, on_device(): peak = lax.pmax(max_r, 'region')  30.3 us
    psum x1, waiting for transfers between devices, on_device(): lax.psum((joined(numer_r) * spread, total_r * weight), 'region')  28.9 us
    pallas_call x1, Pallas kernels, _forward(): pl.pallas_call(functools.partial(_fwd_kernel, scale=scale), grid=(heads,...  28.8 us
    psum x1, blocking collectives, on_device(): lax.psum((joined(numer_r) * spread, total_r * weight), 'region')  27 us
    reshape x4, local copies, waits for them, and re-layouts, heads(): return x.reshape(x.shape[0], HEADS, head_dim).transpose(1, 0, 2)  7.47 us
    unnamed x47, local copies, waits for them, and re-layouts  7.12 us
  transfers between devices with their start and end apart: 2, of which 2 were waited for; matrix products, arithmetic and copies ran while one was open for 4% of the time, Pallas kernels for 0%

profile of v2, /device:TPU:0, one launch (start us, length us, event | category | flops | bytes accessed | tf_op | source)
XLA Modules:
  0.0 307.1 jit_solution(14997520382864589735)
XLA Ops:
  7.2 2.2 convolution_convert_fusion.3
  9.4 1.8 copy.33
  12.0 1.8 copy.34
  14.6 1.8 copy.35
  17.4 28.8 %shard_map.135 = (f32[8,1024,64]{2,1,0:T(8,128)}, f32[8,1024,1]{2,1,0:T(8,128)}, f32[8,1024,1]{2,1,0:T(8,128)}) custom-call(bf16[8,1024,64]{2,1,0:T(8,128)(2,1)} %bitcast.68, bf16[8,1024,64]{2,1,0:T(8,128)(2,1)} %bitcast.70, bf16[8,1024,64]{2,1,0:T(8,128)(2,1)} %bitcast.72, f32[8,1,1024]{2,1,0:T(1,128)} %bitcast.86), custom_call_target="tpu_custom_call" | custom-call | tf_op jit(solution)/shard_map/pallas_call | solution.py:72
  46.2 3.3 %reduce = f32[8,1024]{1,0:T(8,128)S(1)} reduce(f32[8,1024,1]{2,1,0:T(8,128)} %get-tuple-element.14, f32[]{:T(128)} %constant.10), dimensions={2}, to_apply=%get-tuple-element.14.reduce_sub_computation | reduce | bytes 65540 | tf_op jit(solution)/shard_map/pallas_call | solution.py:72
  49.5 30.3 %pmax.7 = f32[8,1024]{1,0:T(8,128)S(1)} all-reduce(f32[8,1024]{1,0:T(8,128)S(1)} %reduce), channel_id=1, replica_groups=mesh['event'=4,'region'=8] {'region'}, use_global_device_ids=true, to_apply=%region_1.0 | all-reduce | flops 8192 | bytes 65536 | tf_op jit(solution)/shard_map/pmax | solution.py:153
  79.8 3.3 %reduce.1 = f32[8,1024]{1,0:T(8,128)S(1)} reduce(f32[8,1024,1]{2,1,0:T(8,128)} %get-tuple-element.15, f32[]{:T(128)} %constant.10), dimensions={2}, to_apply=%get-tuple-element.15.reduce_sub_computation | reduce | bytes 65540 | tf_op jit(solution)/shard_map/pallas_call | solution.py:72
  83.2 4.2 %bitcast_multiply_fusion.1 = f32[1024,8,64]{2,0,1:T(8,128)} fusion(f32[8,1024,64]{2,1,0:T(8,128)} %get-tuple-element.13, f32[1024,8]{0,1:T(8,128)S(1)} %get-tuple-element.44), kind=kLoop, calls=%fused_computation.2 | loop fusion | flops 524288 | bytes 4227072 | tf_op jit(solution)/shard_map/mul | solution.py:156
  87.4 3.8 %copy.36 = f32[1024,8,64]{0,2,1:T(8,128)} copy(f32[1024,8,64]{2,0,1:T(8,128)} %bitcast_multiply_fusion.1) | data formatting | bytes 4194304 | tf_op jit(solution)/shard_map/mul | solution.py:156
  92.5 1.7 convolution_convert_fusion
  94.2 2.1 copy.37
  96.3 27.0 %psum.36 = f32[8,1024]{1,0:T(8,128)S(1)} all-reduce(f32[8,1024]{1,0:T(8,128)S(1)} %get-tuple-element.43), channel_id=1, replica_groups=mesh['event'=4,'region'=8] {'region'}, use_global_device_ids=true, to_apply=%region_3.0 | all-reduce | flops 8192 | bytes 65536 | tf_op jit(solution)/shard_map/psum | solution.py:156
  123.3 2.7 copy.39.lt_ref
  126.0 28.9 %all-reduce.4.cloned.1.call-done = f32[1024,512]{0,1:T(8,128)} async-done(((f32[1024,512]{0,1:T(8,128)}), f32[1024,512]{0,1:T(8,128)}) %all-reduce.4.cloned.1.call-update) | async-done | bytes 2097168 | tf_op jit(solution)/shard_map/psum | solution.py:156
  154.8 2.8 fusion.1
  157.7 3.4 %copy.38 = f32[1024,8,64]{2,0,1:T(8,128)} copy(bf16[1024,8,64]{0,2,1:T(8,128)(2,1)} %bitcast.76) | data formatting | bytes 3145728 | tf_op jit(solution)/shard_map/convert_element_type | solution.py:168
  161.0 3.3 %fusion = f32[8,1024]{1,0:T(8,128)S(1)} fusion(f32[1024,8,64]{2,0,1:T(8,128)} %copy.38, bf16[1024,8,64]{2,0,1:T(8,128)(2,1)S(1)} %copy.37), kind=kLoop, calls=%fused_computation.1 | loop fusion | flops 1564672 | bytes 3178496 | tf_op jit(solution)/shard_map/reduce_sum | solution.py:168
  164.4 2.7 copy.40.dl_ref
  167.0 44.2 %shard_map.136 = (f32[8,1024,64]{2,1,0:T(8,128)}, f32[8,1024,64]{2,1,0:T(8,128)}, f32[8,1024,64]{2,1,0:T(8,128)}) custom-call(bf16[8,1024,64]{2,1,0:T(8,128)(2,1)} %bitcast.69, bf16[8,1024,64]{2,1,0:T(8,128)(2,1)} %bitcast.71, bf16[8,1024,64]{2,1,0:T(8,128)(2,1)} %bitcast.73, bf16[8,1024,64]{2,1,0:T(8,128)(2,1)} %bitcast.74, f32[8,1024,1]{2,1,0:T(8,128)} %copy.39.lt_ref, ...), custom_call_target="tpu_custom_call" | custom-call | tf_op jit(solution)/shard_map/pallas_call | solution.py:99
  211.2 5.5 %convert_bitcast_fusion = (bf16[1024,8,64]{2,0,1:T(8,128)(2,1)S(1)}, bf16[1024,8,64]{2,0,1:T(8,128)(2,1)}) fusion(f32[8,1024,64]{2,1,0:T(8,128)} %get-tuple-element.18, f32[8,1024,64]{2,1,0:T(8,128)} %get-tuple-element.17), kind=kLoop, calls=%fused_computation.6 | loop fusion | flops 1048576 | bytes 6291456 | tf_op jit(solution)/shard_map/convert_element_type | solution.py:172
  216.7 2.7 copy.42
  219.4 1.6 copy.43
  221.0 2.9 fusion.2
  223.9 1.5 fusion.3
  225.8 1.6 copy.41
  228.9 1.7 fusion.7
  232.0 1.7 add_convert_fusion.2
  233.7 1.7 add_convert_fusion
  235.4 57.3 %all-reduce.6.cloned.1.call-done = (bf16[512,512]{0,1:T(8,128)(2,1)}, bf16[512,512]{0,1:T(8,128)(2,1)}, bf16[1024,512]{0,1:T(8,128)(2,1)}) async-done(((bf16[512,512]{0,1:T(8,128)(2,1)}, bf16[512,512]{0,1:T(8,128)(2,1)}, bf16[1024,512]{0,1:T(8,128)(2,1)}), (bf16[512,512]{0,1:T(8,128)(2,1)}, bf16[512,512]{0,1:T(8,128)(2,1)}, bf16[1024,512]{0,1:T(8,128)(2,1)})) %all-reduce.6.cloned.1.call-update) | async-done | bytes 2097168 | tf_op jit(solution)/shard_map/psum | solution.py:176
  292.7 2.1 convolution_bitcast_fusion
  294.8 1.7 add_convert_fusion.1
  (61 shorter events, 10.9 us)
Async XLA Ops:
  7.2 4.1 %copy-start = (bf16[1024,512]{1,0:T(8,128)(2,1)S(1)}, bf16[1024,512]{1,0:T(8,128)(2,1)}, u32[]{:S(2)}) copy-start(bf16[1024,512]{1,0:T(8,128)(2,1)} %param.9) | copy-start | bytes 3145732
  7.2 147.7 %all-reduce.4.cloned.1.call-start = ((), (), s32[]{:S(2)}) async-start(), calls=%async_computation | async-start | bytes 4194304 | tf_op jit(solution)/shard_map/psum | solution.py:156
  9.4 1.8 copy-start.7
  12.0 1.8 copy-start.9
  14.6 1.8 copy-start.13
  91.2 1.2 copy-start.15
  91.2 1.4 copy-start.19
  91.2 201.5 %all-reduce.6.cloned.1.call-start = ((), (), s32[]{:S(2)}) async-start(), calls=%async_computation.1 | async-start | bytes 4194304 | tf_op jit(solution)/shard_map/psum | solution.py:176
  96.3 64.7 %copy-start.1 = (bf16[1024,8,64]{2,0,1:T(8,128)(2,1)}, bf16[1024,8,64]{2,0,1:T(8,128)(2,1)S(1)}, u32[]{:S(2)}) copy-start(bf16[1024,8,64]{2,0,1:T(8,128)(2,1)S(1)} %copy.37) | copy-start | bytes 3145732
  221.0 2.9 copy-start.5
  221.0 4.4 %copy-start.4 = (f32[8,1024,64]{2,1,0:T(8,128)S(1)}, f32[8,1024,64]{2,1,0:T(8,128)}, u32[]{:S(2)}) copy-start(f32[8,1024,64]{2,1,0:T(8,128)} %get-tuple-element.16) | copy-start | bytes 6291460
  227.4 1.2 copy-start.2
  227.4 1.5 copy-start.16
  228.9 1.7 copy-start.3
  228.9 1.7 copy-start.8
  230.6 1.2 copy-start.14
  230.6 1.4 copy-start.20
  232.0 1.7 copy-start.6
  232.0 1.7 copy-start.10
  292.7 2.1 copy-start.17
  292.7 2.1 copy-start.18
  292.7 2.1 copy-start.21
  294.8 3.1 copy-start.12
  296.6 2.5 copy-start.11
Sparse Core Ops, SparseCore 0:
  91.3 63.4 all-reduce.3
  227.5 65.1 all-reduce.5

commit v3 on v2

--- a/solution.py
+++ b/solution.py
@@ -150,10 +150,12 @@
     numer_r, max_r, total_r = _forward(qT, kT, vT, cm, scale)
     max_r = max_r.reshape(HEADS, n_queries)
     total_r = total_r.reshape(HEADS, n_queries)
-    peak = lax.pmax(max_r, "region")
+    stats = lax.all_gather(jnp.concatenate([max_r, total_r], axis=0), "region")
+    peak = jnp.max(stats[:, :HEADS], axis=0)
+    total = jnp.sum(stats[:, HEADS:] * jnp.exp(stats[:, :HEADS] - peak[None]), axis=0)
     weight = jnp.exp(max_r - peak)
     spread = jnp.repeat(weight.T, head_dim, axis=1)
-    numer, total = lax.psum((joined(numer_r) * spread, total_r * weight), "region")
+    numer = lax.psum((joined(numer_r) * spread).astype(bf16), "region").astype(f32)
     attended = (numer / jnp.repeat(total.T, head_dim, axis=1)).astype(bf16)
     log_total = (peak + jnp.log(total)).reshape(HEADS, n_queries, 1)
     attended_h = heads(attended)

time: 309 us -> 288 us (0.932)
  blocking collectives: 57.3 us -> 16.5 us
  waiting for transfers between devices: 86.2 us -> 109 us
  local copies, waits for them, and re-layouts: 33.6 us -> 30.1 us
    pmax x1 -> x0, blocking collectives: 30.3 us -> none  [on_device(): peak = lax.pmax(max_r, 'region')]
    psum x1 -> x0, blocking collectives: 27 us -> none  [on_device(): lax.psum((joined(numer_r) * spread, total_r * weight), 'region')]
    psum x1, waiting for transfers between devices: 28.9 us -> 52.5 us  [on_device(): lax.psum((joined(numer_r) * spread).astype(bf16), 'region').astype(f32)]
    all_gather x0 -> x1, blocking collectives: none -> 16.5 us  [on_device(): stats = lax.all_gather(jnp.concatenate([max_r, total_r], axis=0), 'region')]
    mul x2 -> x0, other arithmetic: 4.26 us -> none  [the longest x1 4.24 us: on_device(): joined(numer_r) * spread]
    mul x1 -> x0, local copies, waits for them, and re-layouts: 3.77 us -> none  [on_device(): joined(numer_r) * spread]
    unnamed x47 -> x43, local copies, waits for them, and re-layouts: 7.12 us -> 5.86 us
  transfers between devices with their start and end apart: 2 -> 2, of which waited for: 2 -> 2; matrix products, arithmetic and copies ran while one was open for 4% -> 5% of each run, Pallas kernels for 0% -> 0%
where the time goes in v3:
time: 288 us; the launch traced here: 286 us
  waiting for transfers between devices  109 us (38%)
  Pallas kernels  72.9 us (25%)
  local copies, waits for them, and re-layouts  30.1 us (10%)
  other arithmetic  21.7 us (8%)
  matrix products  20.9 us (7%)
  blocking collectives  16.5 us (6%)
  between operations  14.2 us (5%)
    psum x1, waiting for transfers between devices, on_device(): lax.psum((query_grad_local.astype(bf16), wk_part.astype(bf16), wv_part.as...  56.7 us
    psum x1, waiting for transfers between devices, on_device(): lax.psum((joined(numer_r) * spread).astype(bf16), 'region').astype(f32)  52.5 us
    pallas_call x1, Pallas kernels, _backward(): pl.pallas_call(functools.partial(_bwd_kernel, scale=scale), grid=(heads,...  44.1 us
    pallas_call x1, Pallas kernels, _forward(): pl.pallas_call(functools.partial(_fwd_kernel, scale=scale), grid=(heads,...  28.8 us
    all_gather x1, blocking collectives, on_device(): stats = lax.all_gather(jnp.concatenate([max_r, total_r], axis=0), 'region')  16.5 us
    reshape x4, local copies, waits for them, and re-layouts, heads(): return x.reshape(x.shape[0], HEADS, head_dim).transpose(1, 0, 2)  7.43 us
    pallas_call x2, other arithmetic, _forward(): pl.pallas_call(functools.partial(_fwd_kernel, scale=scale), grid=(heads,...  6.68 us
    unnamed x43, local copies, waits for them, and re-layouts  5.86 us
  transfers between devices with their start and end apart: 2, of which 2 were waited for; matrix products, arithmetic and copies ran while one was open for 5% of the time, Pallas kernels for 0%

profile of v3, /device:TPU:0, one launch (start us, length us, event | category | flops | bytes accessed | tf_op | source)
XLA Modules:
  0.0 285.9 jit_solution(1182479879502760930)
XLA Ops:
  7.2 2.2 convolution_convert_fusion.3
  9.4 1.8 copy.33
  12.0 1.8 copy.34
  14.6 1.8 copy.35
  17.4 28.8 %shard_map.135 = (f32[8,1024,64]{2,1,0:T(8,128)}, f32[8,1024,1]{2,1,0:T(8,128)}, f32[8,1024,1]{2,1,0:T(8,128)}) custom-call(bf16[8,1024,64]{2,1,0:T(8,128)(2,1)} %bitcast.71, bf16[8,1024,64]{2,1,0:T(8,128)(2,1)} %bitcast.73, bf16[8,1024,64]{2,1,0:T(8,128)(2,1)} %bitcast.75, f32[8,1,1024]{2,1,0:T(1,128)} %bitcast.91), custom_call_target="tpu_custom_call" | custom-call | tf_op jit(solution)/shard_map/pallas_call | solution.py:72
  46.2 3.3 %reduce = f32[8,1024]{1,0:T(8,128)S(1)} reduce(f32[8,1024,1]{2,1,0:T(8,128)} %get-tuple-element.14, f32[]{:T(128)} %constant.12), dimensions={2}, to_apply=%get-tuple-element.14.reduce_sub_computation | reduce | bytes 65540 | tf_op jit(solution)/shard_map/pallas_call | solution.py:72
  49.5 3.3 %reduce.1 = f32[8,1024]{1,0:T(8,128)S(1)} reduce(f32[8,1024,1]{2,1,0:T(8,128)} %get-tuple-element.15, f32[]{:T(128)} %constant.12), dimensions={2}, to_apply=%get-tuple-element.15.reduce_sub_computation | reduce | bytes 65540 | tf_op jit(solution)/shard_map/pallas_call | solution.py:72
  52.9 16.5 %all-gather = f32[128,1024]{1,0:T(8,128)S(1)} all-gather(f32[16,1024]{1,0:T(8,128)S(1)} %pad_maximum_fusion), channel_id=2, replica_groups=mesh['event'=4,'region'=8] {'region'}, dimensions={0}, use_global_device_ids=true | all-gather | bytes 589824 | tf_op jit(solution)/shard_map/all_gather | solution.py:153
  69.5 2.9 %fusion.1 = bf16[1024,8,64]{2,0,1:T(8,128)(2,1)S(1)} fusion(f32[8,1024,64]{2,1,0:T(8,128)} %get-tuple-element.13, f32[1024,8]{0,1:T(8,128)S(1)} %get-tuple-element.44), kind=kLoop, calls=%fused_computation.3 | loop fusion | flops 1048576 | bytes 3178496 | tf_op jit(solution)/shard_map/convert_element_type | solution.py:158
  72.4 1.6 copy.36
  74.2 3.1 %convolution_convert_fusion = bf16[1024,512]{0,1:T(8,128)(2,1)} fusion(bf16[1024,512]{1,0:T(8,128)(2,1)} %param.15, bf16[512,512]{1,0:T(8,128)(2,1)} %param.13), kind=kOutput, calls=%fused_computation.12 | convolution fusion | flops 537395200 | bytes 2621440 | tf_op jit(solution)/shard_map/dot_general | solution.py:165
  77.3 2.0 copy.37
  79.3 2.6 copy.39.lt_ref
  82.0 52.5 %all-reduce.4.cloned.1.call-done = bf16[1024,512]{0,1:T(8,128)(2,1)} async-done(((bf16[1024,512]{0,1:T(8,128)(2,1)}), bf16[1024,512]{0,1:T(8,128)(2,1)}) %all-reduce.4.cloned.1.call-update) | async-done | bytes 1048592 | tf_op jit(solution)/shard_map/psum | solution.py:158
  134.5 2.5 fusion.2
  137.1 3.4 %copy.38 = f32[1024,8,64]{2,0,1:T(8,128)} copy(bf16[1024,8,64]{0,2,1:T(8,128)(2,1)} %bitcast.80) | data formatting | bytes 3145728 | tf_op jit(solution)/shard_map/convert_element_type | solution.py:170
  140.4 3.3 %fusion = f32[8,1024]{1,0:T(8,128)S(1)} fusion(f32[1024,8,64]{2,0,1:T(8,128)} %copy.38, bf16[1024,8,64]{2,0,1:T(8,128)(2,1)S(1)} %copy.37), kind=kLoop, calls=%fused_computation.1 | loop fusion | flops 1564672 | bytes 3178496 | tf_op jit(solution)/shard_map/reduce_sum | solution.py:170
  143.8 2.6 copy.40.dl_ref
  146.4 44.1 %shard_map.136 = (f32[8,1024,64]{2,1,0:T(8,128)}, f32[8,1024,64]{2,1,0:T(8,128)}, f32[8,1024,64]{2,1,0:T(8,128)}) custom-call(bf16[8,1024,64]{2,1,0:T(8,128)(2,1)} %bitcast.72, bf16[8,1024,64]{2,1,0:T(8,128)(2,1)} %bitcast.74, bf16[8,1024,64]{2,1,0:T(8,128)(2,1)} %bitcast.76, bf16[8,1024,64]{2,1,0:T(8,128)(2,1)} %bitcast.77, f32[8,1024,1]{2,1,0:T(8,128)} %copy.39.lt_ref, ...), custom_call_target="tpu_custom_call" | custom-call | tf_op jit(solution)/shard_map/pallas_call | solution.py:99
  190.6 5.5 %convert_bitcast_fusion = (bf16[1024,8,64]{2,0,1:T(8,128)(2,1)S(1)}, bf16[1024,8,64]{2,0,1:T(8,128)(2,1)}) fusion(f32[8,1024,64]{2,1,0:T(8,128)} %get-tuple-element.18, f32[8,1024,64]{2,1,0:T(8,128)} %get-tuple-element.17), kind=kLoop, calls=%fused_computation.7 | loop fusion | flops 1048576 | bytes 6291456 | tf_op jit(solution)/shard_map/convert_element_type | solution.py:174
  196.1 2.7 copy.42
  198.8 1.6 copy.43
  200.4 2.9 %fusion.3 = bf16[512,512]{0,1:T(8,128)(2,1)} fusion(bf16[1024,512]{0,1:T(8,128)(2,1)} %bitcast.78, bf16[1024,512]{1,0:T(8,128)(2,1)S(1)} %copy-done), kind=kOutput, calls=%fused_computation.19 | convolution fusion | flops 537133056 | bytes 2621440 | tf_op jit(solution)/shard_map/ka,kb->ab/dot_general | solution.py:176
  203.3 1.5 fusion.4
  205.1 1.6 copy.41
  208.3 1.7 fusion.7
  211.3 1.7 add_convert_fusion.2
  213.1 1.7 add_convert_fusion
  214.8 56.7 %all-reduce.6.cloned.1.call-done = (bf16[512,512]{0,1:T(8,128)(2,1)}, bf16[512,512]{0,1:T(8,128)(2,1)}, bf16[1024,512]{0,1:T(8,128)(2,1)}) async-done(((bf16[512,512]{0,1:T(8,128)(2,1)}, bf16[512,512]{0,1:T(8,128)(2,1)}, bf16[1024,512]{0,1:T(8,128)(2,1)}), (bf16[512,512]{0,1:T(8,128)(2,1)}, bf16[512,512]{0,1:T(8,128)(2,1)}, bf16[1024,512]{0,1:T(8,128)(2,1)})) %all-reduce.6.cloned.1.call-update) | async-done | bytes 2097168 | tf_op jit(solution)/shard_map/psum | solution.py:178
  271.5 2.1 convolution_bitcast_fusion
  273.6 1.7 add_convert_fusion.1
  275.4 1.3 copy.44
  (58 shorter events, 8.5 us)
Async XLA Ops:
  7.2 4.1 %copy-start = (bf16[1024,512]{1,0:T(8,128)(2,1)S(1)}, bf16[1024,512]{1,0:T(8,128)(2,1)}, u32[]{:S(2)}) copy-start(bf16[1024,512]{1,0:T(8,128)(2,1)} %param.9) | copy-start | bytes 3145732
  7.2 127.4 %all-reduce.4.cloned.1.call-start = ((), (), s32[]{:S(2)}) async-start(), calls=%async_computation | async-start | bytes 2097152 | tf_op jit(solution)/shard_map/psum | solution.py:158
  9.4 1.8 copy-start.7
  12.0 1.8 copy-start.9
  14.6 1.8 copy-start.13
  74.0 197.5 %all-reduce.6.cloned.1.call-start = ((), (), s32[]{:S(2)}) async-start(), calls=%async_computation.1 | async-start | bytes 4194304 | tf_op jit(solution)/shard_map/psum | solution.py:178
  79.3 61.1 %copy-start.1 = (bf16[1024,8,64]{2,0,1:T(8,128)(2,1)}, bf16[1024,8,64]{2,0,1:T(8,128)(2,1)S(1)}, u32[]{:S(2)}) copy-start(bf16[1024,8,64]{2,0,1:T(8,128)(2,1)S(1)} %copy.37) | copy-start | bytes 3145732
  200.4 2.9 %copy-start.5 = (bf16[1024,8,64]{0,2,1:T(8,128)(2,1)S(1)}, bf16[1024,8,64]{0,2,1:T(8,128)(2,1)}, u32[]{:S(2)}) copy-start(bf16[1024,8,64]{0,2,1:T(8,128)(2,1)} %copy.43) | copy-start | bytes 3145732
  200.4 4.4 %copy-start.4 = (f32[8,1024,64]{2,1,0:T(8,128)S(1)}, f32[8,1024,64]{2,1,0:T(8,128)}, u32[]{:S(2)}) copy-start(f32[8,1024,64]{2,1,0:T(8,128)} %get-tuple-element.16) | copy-start | bytes 6291460
  206.7 1.2 copy-start.3
  206.7 1.5 copy-start.15
  208.3 1.7 copy-start.2
  208.3 1.7 copy-start.8
  210.0 1.2 copy-start.14
  210.0 1.4 copy-start.18
  211.3 1.7 copy-start.6
  211.3 1.7 copy-start.10
  271.5 2.1 copy-start.16
  271.5 2.1 copy-start.17
  271.5 2.1 copy-start.19
  273.6 3.1 %copy-start.12 = (bf16[512,512]{0,1:T(8,128)(2,1)S(1)}, bf16[512,512]{0,1:T(8,128)(2,1)}, u32[]{:S(2)}) copy-start(bf16[512,512]{0,1:T(8,128)(2,1)} %get-tuple-element.40) | copy-start | bytes 1572868
  275.4 2.5 copy-start.11
Sparse Core Ops, SparseCore 0:
  74.1 60.3 all-reduce.3
  206.9 64.5 all-reduce.5

commit v4 on v1

--- a/solution.py
+++ b/solution.py
@@ -147,34 +147,94 @@
     vals = jnp.dot(hits_in, w_value, preferred_element_type=f32).astype(bf16)
     qT, kT, vT = heads(query), heads(keys), heads(vals)
 
+    regions = lax.axis_size("region")
     numer_r, max_r, total_r = _forward(qT, kT, vT, cm, scale)
-    peak = lax.pmax(max_r, "region")
-    weight = jnp.exp(max_r - peak)
-    numer, total = lax.psum((numer_r * weight, total_r * weight), "region")
-    attended_h = (numer / total).astype(bf16)
-    log_total = peak + jnp.log(total)
-    attended = joined(attended_h)
+    numer = joined(numer_r)
+    peak = max_r.reshape(HEADS, n_queries)
+    total = total_r.reshape(HEADS, n_queries)
+    rows = n_queries
+    base = 0
+    steps = []
+    k = 0
+    while (1 << k) < regions:
+        bit = (region_index >> k) & 1
+        half = rows // 2
+        pairs = [(i, i ^ (1 << k)) for i in range(regions)]
+        mine = (
+            lax.dynamic_slice_in_dim(numer, bit * half, half, 0),
+            lax.dynamic_slice_in_dim(peak, bit * half, half, 1),
+            lax.dynamic_slice_in_dim(total, bit * half, half, 1),
+        )
+        theirs = lax.ppermute(
+            (
+                lax.dynamic_slice_in_dim(numer, (1 - bit) * half, half, 0),
+                lax.dynamic_slice_in_dim(peak, (1 - bit) * half, half, 1),
+                lax.dynamic_slice_in_dim(total, (1 - bit) * half, half, 1),
+            ),
+            "region",
+            pairs,
+        )
+        top = jnp.maximum(mine[1], theirs[1])
+        scale_a = jnp.exp(mine[1] - top)
+        scale_b = jnp.exp(theirs[1] - top)
+        numer = mine[0] * jnp.repeat(scale_a.T, head_dim, axis=1) + theirs[0] * jnp.repeat(
+            scale_b.T, head_dim, axis=1
+        )
+        total = mine[2] * scale_a + theirs[2] * scale_b
+        peak = top
+        base = base + bit * half
+        steps.append((k, bit, half))
+        rows = half
+        k += 1
+    attended_part = (numer / jnp.repeat(total.T, head_dim, axis=1)).astype(bf16)
+    log_part = peak + jnp.log(total)
+    grad_att = lax.dot_general(
+        grad_out, w_out, (((1,), (1,)), ((), ())), preferred_element_type=f32
+    ).astype(bf16)
+    grad_att_part = lax.dynamic_slice_in_dim(grad_att, base, rows, 0)
+    delta_part = jnp.sum(
+        (grad_att_part.astype(f32) * attended_part.astype(f32)).reshape(rows, HEADS, head_dim),
+        axis=2,
+    ).T
+    gathered = (attended_part, jnp.concatenate([log_part, delta_part], axis=0))
+    for k, bit, half in reversed(steps):
+        pairs = [(i, i ^ (1 << k)) for i in range(regions)]
+        other = lax.ppermute(gathered, "region", pairs)
+        lo = jax.tree.map(lambda a, b: jnp.where(bit == 0, a, b), gathered, other)
+        hi = jax.tree.map(lambda a, b: jnp.where(bit == 0, b, a), gathered, other)
+        gathered = (
+            jnp.concatenate([lo[0], hi[0]], axis=0),
+            jnp.concatenate([lo[1], hi[1]], axis=1),
+        )
+    attended = gathered[0]
+    log_total = gathered[1][:HEADS].reshape(HEADS, n_queries, 1)
+    deltas = gathered[1][HEADS:].reshape(HEADS, n_queries, 1)
     layer_out = (
         queries_in.astype(f32) + jnp.dot(attended, w_out, preferred_element_type=f32)
     ).astype(bf16)
-    grad_att = lax.dot_general(
-        grad_out, w_out, (((1,), (1,)), ((), ())), preferred_element_type=f32
-    ).astype(bf16)
     grad_wo = jnp.einsum("qa,qb->ab", attended, grad_out, preferred_element_type=f32)
     gaT = heads(grad_att)
-    deltas = jnp.sum(gaT.astype(f32) * attended_h.astype(f32), axis=2, keepdims=True)
 
     dq_r, dk, dv = _backward(qT, kT, vT, gaT, log_total, deltas, cm, scale)
     keys_grad = joined(dk).astype(bf16)
     vals_grad = joined(dv).astype(bf16)
-    query_grad_local = joined(dq_r)
     wk_part = jnp.einsum("ka,kb->ab", hits_in, keys_grad, preferred_element_type=f32)
     wv_part = jnp.einsum("ka,kb->ab", hits_in, vals_grad, preferred_element_type=f32)
-    query_grad_sum, grad_wk, grad_wv = lax.psum(
-        (query_grad_local.astype(bf16), wk_part.astype(bf16), wv_part.astype(bf16)), "region"
-    )
-    grad_wk = grad_wk.astype(f32)
-    grad_wv = grad_wv.astype(f32)
+    summed = jnp.concatenate([joined(dq_r), wk_part, wv_part], axis=0)
+    for k, bit, half in steps:
+        half = summed.shape[0] // 2
+        pairs = [(i, i ^ (1 << k)) for i in range(regions)]
+        other = lax.ppermute(lax.dynamic_slice_in_dim(summed, (1 - bit) * half, half, 0), "region", pairs)
+        summed = lax.dynamic_slice_in_dim(summed, bit * half, half, 0) + other
+    for k, bit, half in reversed(steps):
+        pairs = [(i, i ^ (1 << k)) for i in range(regions)]
+        other = lax.ppermute(summed, "region", pairs)
+        summed = jnp.concatenate(
+            [jnp.where(bit == 0, summed, other), jnp.where(bit == 0, other, summed)], axis=0
+        )
+    query_grad_sum = summed[:n_queries].astype(bf16)
+    grad_wk = summed[n_queries : n_queries + width]
+    grad_wv = summed[n_queries + width :]
     grad_q = query_grad_sum
     grad_wq = jnp.einsum("qa,qb->ab", queries_in, grad_q, preferred_element_type=f32)
     grad_queries = (

time: 477 us -> 306 us (0.64)
  blocking collectives: 249 us -> 0 us
  waiting for transfers between devices: 58.4 us -> 134 us
  starting transfers between devices: 0.08 us -> 21.4 us
  local copies, waits for them, and re-layouts: 24.3 us -> 41.1 us
  other arithmetic: 31.3 us -> 16 us
  between operations: 14.2 us -> 1.17 us
  matrix products: 25.1 us -> 17.6 us
    psum x1 -> x0, blocking collectives: 158 us -> none  [on_device(): numer, total = lax.psum((numer_r * weight, total_r * weight), 'region')]
    ppermute x0 -> x21, waiting for transfers between devices: none -> 134 us  [the longest x3 52.2 us: on_device(): lax.ppermute(lax.dynamic_slice_in_dim(summed, (1 - bit) * half, half, 0),...]
    pmax x1 -> x0, blocking collectives: 90.6 us -> none  [on_device(): peak = lax.pmax(max_r, 'region')]
    psum x2 -> x0, waiting for transfers between devices: 58.4 us -> none  [the longest x1 58.4 us: on_device(): lax.psum((query_grad_local.astype(bf16), wk_part.astype(bf16), wv_part.as...]
    ppermute x0 -> x21, starting transfers between devices: none -> 21.4 us  [the longest x9 11.8 us: on_device(): lax.ppermute((lax.dynamic_slice_in_dim(numer, (1 - bit) * half, half, 0),...]
    mul x2 -> x0, other arithmetic: 10.9 us -> none  [on_device(): numer, total = lax.psum((numer_r * weight, total_r * weight), 'region')]
    dynamic_slice x0 -> x12, local copies, waits for them, and re-layouts: none -> 6.24 us  [the longest x1 3.52 us: on_device(): lax.dynamic_slice_in_dim(peak, bit * half, half, 1)]
    reshape x0 -> x2, local copies, waits for them, and re-layouts: none -> 5.33 us  [the longest x1 2.68 us: on_device(): log_total = gathered[1][:HEADS].reshape(HEADS, n_queries, 1)]
  transfers between devices with their start and end apart: 2 -> 21, of which waited for: 1 -> 11; matrix products, arithmetic and copies ran while one was open for 4% -> 5% of each run, Pallas kernels for 0% -> 0%
where the time goes in v4:
time: 306 us; the launch traced here: 304 us
  waiting for transfers between devices  134 us (44%)
  Pallas kernels  72.9 us (24%)
  local copies, waits for them, and re-layouts  41.1 us (13%)
  starting transfers between devices  21.4 us (7%)
  matrix products  17.6 us (6%)
  other arithmetic  16 us (5%)
    ppermute x3, waiting for transfers between devices, on_device(): lax.ppermute(lax.dynamic_slice_in_dim(summed, (1 - bit) * half, half, 0),...  52.2 us
    pallas_call x1, Pallas kernels, _backward(): pl.pallas_call(functools.partial(_bwd_kernel, scale=scale), grid=(heads,...  44.1 us
    ppermute x6, waiting for transfers between devices, on_device(): other = lax.ppermute(gathered, 'region', pairs)  35.9 us
    pallas_call x1, Pallas kernels, _forward(): pl.pallas_call(functools.partial(_fwd_kernel, scale=scale), grid=(heads,...  28.8 us
    ppermute x3, waiting for transfers between devices, on_device(): other = lax.ppermute(summed, 'region', pairs)  25.5 us
    ppermute x9, waiting for transfers between devices, on_device(): lax.ppermute((lax.dynamic_slice_in_dim(numer, (1 - bit) * half, half, 0),...  20.1 us
    ppermute x9, starting transfers between devices, on_device(): lax.ppermute((lax.dynamic_slice_in_dim(numer, (1 - bit) * half, half, 0),...  11.8 us
    unnamed x37, local copies, waits for them, and re-layouts  7.5 us
  transfers between devices with their start and end apart: 21, of which 11 were waited for; matrix products, arithmetic and copies ran while one was open for 5% of the time, Pallas kernels for 0%

profile of v4, /device:TPU:0, one launch (start us, length us, event | category | flops | bytes accessed | tf_op | source)
XLA Modules:
  0.0 303.9 jit_solution(15158226002005218659)
XLA Ops:
  1.7 2.1 convolution_convert_fusion.3
  3.9 1.8 copy.46
  6.5 1.9 copy.47
  11.6 28.8 %shard_map.135 = (f32[8,1024,64]{2,1,0:T(8,128)}, f32[8,1024,1]{2,1,0:T(8,128)}, f32[8,1024,1]{2,1,0:T(8,128)}) custom-call(bf16[8,1024,64]{2,1,0:T(8,128)(2,1)} %bitcast.101, bf16[8,1024,64]{2,1,0:T(8,128)(2,1)} %bitcast.103, bf16[8,1024,64]{2,1,0:T(8,128)(2,1)} %bitcast.105, f32[8,1,1024]{2,1,0:T(1,128)} %bitcast.121), custom_call_target="tpu_custom_call" | custom-call | tf_op jit(solution)/shard_map/pallas_call | solution.py:72
  40.4 2.8 copy.49
  44.8 3.5 %dynamic-slice_reduce_fusion.3 = (f32[8,512]{1,0:T(8,128)S(1)}, f32[8,512]{1,0:T(8,128)S(1)}) fusion(f32[8,1024,1]{2,1,0:T(8,128)} %get-tuple-element.14, s32[]{:T(128)S(6)} %select_n.162, s32[]{:T(128)S(6)} %select_n.163), kind=kLoop, calls=%fused_computation.12 | loop fusion | bytes 65544 | tf_op jit(solution)/shard_map/dynamic_slice | solution.py:165
  51.0 3.0 collective-permute-start.2
  55.7 2.0 collective-permute-start.3
  57.7 2.7 collective-permute-start.8
  60.7 8.9 %collective-permute-done.3 = f32[256,512]{0,1:T(8,128)S(1)} collective-permute-done((f32[256,512]{0,1:T(8,128)S(1)}, f32[256,512]{0,1:T(8,128)S(1)}, u32[]{:S(2)}, u32[]{:S(2)}) %collective-permute-start.3) | collective-permute-done | bytes 524320 | tf_op jit(solution)/shard_map/ppermute | solution.py:168
  69.8 2.6 collective-permute-start.5
  73.2 10.4 %collective-permute-done.5 = f32[128,512]{0,1:T(8,128)S(1)} collective-permute-done((f32[128,512]{0,1:T(8,128)S(1)}, f32[128,512]{0,1:T(8,128)S(1)}, u32[]{:S(2)}, u32[]{:S(2)}) %collective-permute-start.5) | collective-permute-done | bytes 262176 | tf_op jit(solution)/shard_map/ppermute | solution.py:168
  83.8 4.5 %collective-permute-done.12 = f32[16,128]{1,0:T(8,128)S(1)} collective-permute-done((f32[16,128]{1,0:T(8,128)S(1)}, f32[16,128]{1,0:T(8,128)S(1)}, u32[]{:S(2)}, u32[]{:S(2)}) %collective-permute-start.12) | collective-permute-done | bytes 8224 | tf_op jit(solution)/shard_map/ppermute | solution.py:202
  89.1 3.0 collective-permute-done.13
  94.1 2.7 copy.51.lt_ref
  96.7 2.7 copy.52.dl_ref
  99.4 44.1 %shard_map.136 = (f32[8,1024,64]{2,1,0:T(8,128)}, f32[8,1024,64]{2,1,0:T(8,128)}, f32[8,1024,64]{2,1,0:T(8,128)}) custom-call(bf16[8,1024,64]{2,1,0:T(8,128)(2,1)} %bitcast.102, bf16[8,1024,64]{2,1,0:T(8,128)(2,1)} %bitcast.104, bf16[8,1024,64]{2,1,0:T(8,128)(2,1)} %bitcast.106, bf16[8,1024,64]{2,1,0:T(8,128)(2,1)} %bitcast.110, f32[8,1024,1]{2,1,0:T(8,128)} %copy.51.lt_ref, ...), custom_call_target="tpu_custom_call" | custom-call | tf_op jit(solution)/shard_map/pallas_call | solution.py:99
  143.5 5.5 %convert_bitcast_fusion = (bf16[1024,8,64]{2,0,1:T(8,128)(2,1)S(1)}, bf16[1024,8,64]{2,0,1:T(8,128)(2,1)}) fusion(f32[8,1024,64]{2,1,0:T(8,128)} %get-tuple-element.18, f32[8,1024,64]{2,1,0:T(8,128)} %get-tuple-element.17), kind=kLoop, calls=%fused_computation.6 | loop fusion | flops 1048576 | bytes 6291456 | tf_op jit(solution)/shard_map/convert_element_type | solution.py:220
  149.0 2.7 copy.54
  151.7 3.0 convolution_bitcast_fusion.2
  154.7 2.5 copy.56
  158.8 2.0 convolution_bitcast_fusion.1
  162.1 2.9 copy.53
  169.1 3.9 %collective-permute-done.15 = f32[1024,512]{0,1:T(8,128)} collective-permute-done((f32[1024,512]{0,1:T(8,128)S(1)}, f32[1024,512]{0,1:T(8,128)}, u32[]{:S(2)}, u32[]{:S(2)}) %collective-permute-start.15) | collective-permute-done | bytes 2097184 | tf_op jit(solution)/shard_map/ppermute | solution.py:227
  173.0 2.6 dynamic-slice_add_fusion
  176.6 24.8 %collective-permute-done.16 = f32[512,512]{0,1:T(8,128)} collective-permute-done((f32[512,512]{0,1:T(8,128)S(1)}, f32[512,512]{0,1:T(8,128)}, u32[]{:S(2)}, u32[]{:S(2)}) %collective-permute-start.16) | collective-permute-done | bytes 1048608 | tf_op jit(solution)/shard_map/ppermute | solution.py:227
  202.8 2.0 collective-permute-start.17
  204.8 23.5 %collective-permute-done.17 = f32[256,512]{0,1:T(8,128)S(1)} collective-permute-done((f32[256,512]{0,1:T(8,128)S(1)}, f32[256,512]{0,1:T(8,128)S(1)}, u32[]{:S(2)}, u32[]{:S(2)}) %collective-permute-start.17) | collective-permute-done | bytes 524320 | tf_op jit(solution)/shard_map/ppermute | solution.py:227
  228.5 25.5 %collective-permute-done.18 = f32[256,512]{0,1:T(8,128)S(1)} collective-permute-done((f32[256,512]{0,1:T(8,128)S(1)}, f32[256,512]{0,1:T(8,128)S(1)}, u32[]{:S(2)}, u32[]{:S(2)}) %collective-permute-start.18) | collective-permute-done | bytes 524320 | tf_op jit(solution)/shard_map/ppermute | solution.py:231
  256.0 23.0 %collective-permute-done.9 = bf16[128,512]{0,1:T(8,128)(2,1)S(1)} collective-permute-done((bf16[128,512]{0,1:T(8,128)(2,1)S(1)}, bf16[128,512]{0,1:T(8,128)(2,1)S(1)}, u32[]{:S(2)}, u32[]{:S(2)}) %collective-permute-start.9) | collective-permute-done | bytes 131104 | tf_op jit(solution)/shard_map/ppermute | solution.py:202
  279.1 3.3 %collective-permute-start.10 = (bf16[256,512]{0,1:T(8,128)(2,1)S(1)}, bf16[256,512]{0,1:T(8,128)(2,1)S(1)}, u32[]{:S(2)}, u32[]{:S(2)}) collective-permute-start(bf16[256,512]{0,1:T(8,128)(2,1)S(1)} %pad_maximum_fusion.7), channel_id=1, source_target_pairs={{0,2},{1,3},{2,0},{3,1},{4,6},{5,7},{6,4},{7,5},{8,10},{9,11},{10,... | collective-permute-start | bytes 786440 | tf_op jit(solution)/shard_map/ppermute | solution.py:202
  282.8 5.5 %collective-permute-done.10 = bf16[256,512]{0,1:T(8,128)(2,1)S(1)} collective-permute-done((bf16[256,512]{0,1:T(8,128)(2,1)S(1)}, bf16[256,512]{0,1:T(8,128)(2,1)S(1)}, u32[]{:S(2)}, u32[]{:S(2)}) %collective-permute-start.10) | collective-permute-done | bytes 262176 | tf_op jit(solution)/shard_map/ppermute | solution.py:202
  (121 shorter events, 42.8 us)
Async XLA Ops:
  0.6 5.0 %copy-start = (bf16[1024,512]{1,0:T(8,128)(2,1)S(1)}, bf16[1024,512]{1,0:T(8,128)(2,1)}, u32[]{:S(2)}) copy-start(bf16[1024,512]{1,0:T(8,128)(2,1)} %param.9) | copy-start | bytes 3145732
  44.3 9.8 %collective-permute-start.1 = (f32[512,512]{0,1:T(8,128)}, f32[512,512]{0,1:T(8,128)}, u32[]{:S(2)}, u32[]{:S(2)}) collective-permute-start(f32[512,512]{0,1:T(8,128)} %constant_dynamic-slice_fusion.11), channel_id=1, source_target_pairs={{0,1},{1,0},{2,3},{3,2},{4,5},{5,4},{6,7},{7,6},{8,9},{9,8},{10,11... | collective-permute-start | bytes 3145736 | tf_op jit(solution)/shard_map/ppermute | solution.py:168
  44.8 3.6 %copy-start.4 = (f32[8,1024,1]{2,1,0:T(8,128)S(1)}, f32[8,1024,1]{2,1,0:T(8,128)}, u32[]{:S(2)}) copy-start(f32[8,1024,1]{2,1,0:T(8,128)} %get-tuple-element.15) | copy-start | bytes 98308
  48.3 1.8 collective-permute-start
  49.6 1.4 collective-permute-start.6
  51.0 6.7 %collective-permute-start.2 = (f32[8,256]{1,0:T(8,128)S(1)}, f32[8,256]{1,0:T(8,128)S(1)}, u32[]{:S(2)}, u32[]{:S(2)}) collective-permute-start(f32[8,256]{1,0:T(8,128)S(1)} %constant_dynamic-slice_fusion.10), channel_id=1, source_target_pairs={{0,2},{1,3},{2,0},{3,1},{4,6},{5,7},{6,4},{7,5},{8,10},{9,11},{10,... | collective-permute-start | bytes 24584 | tf_op jit(solution)/shard_map/ppermute | solution.py:168
  54.0 3.7 %collective-permute-start.7 = (f32[8,256]{1,0:T(8,128)S(1)}, f32[8,256]{1,0:T(8,128)S(1)}, u32[]{:S(2)}, u32[]{:S(2)}) collective-permute-start(f32[8,256]{1,0:T(8,128)S(1)} %constant_dynamic-slice_fusion.5), channel_id=1, source_target_pairs={{0,2},{1,3},{2,0},{3,1},{4,6},{5,7},{6,4},{7,5},{8,10},{9,11},{10,... | collective-permute-start | bytes 24584 | tf_op jit(solution)/shard_map/ppermute | solution.py:168
  55.6 16.8 %copy-start.12 = (bf16[1024,512]{1,0:T(8,128)(2,1)S(1)}, bf16[1024,512]{1,0:T(8,128)(2,1)}, u32[]{:S(2)}) copy-start(bf16[1024,512]{1,0:T(8,128)(2,1)} %param.15) | copy-start | bytes 3145732
  55.6 16.8 %copy-start.14 = (bf16[512,512]{1,0:T(8,128)(2,1)S(1)}, bf16[512,512]{1,0:T(8,128)(2,1)}, u32[]{:S(2)}) copy-start(bf16[512,512]{1,0:T(8,128)(2,1)} %param.13) | copy-start | bytes 1572868
  55.7 14.0 %collective-permute-start.3 = (f32[256,512]{0,1:T(8,128)S(1)}, f32[256,512]{0,1:T(8,128)S(1)}, u32[]{:S(2)}, u32[]{:S(2)}) collective-permute-start(f32[256,512]{0,1:T(8,128)S(1)} %constant_dynamic-slice_fusion.9), channel_id=1, source_target_pairs={{0,2},{1,3},{2,0},{3,1},{4,6},{5,7},{6,4},{7,5},{8,10},{9,11},{10,... | collective-permute-start | bytes 1572872 | tf_op jit(solution)/shard_map/ppermute | solution.py:168
  57.7 15.5 %collective-permute-start.8 = (f32[8,128]{1,0:T(8,128)S(1)}, f32[8,128]{1,0:T(8,128)S(1)}, u32[]{:S(2)}, u32[]{:S(2)}) collective-permute-start(f32[8,128]{1,0:T(8,128)S(1)} %constant_dynamic-slice_fusion.3), channel_id=1, source_target_pairs={{0,4},{1,5},{2,6},{3,7},{4,0},{5,1},{6,2},{7,3},{8,12},{9,13},{10,... | collective-permute-start | bytes 12296 | tf_op jit(solution)/shard_map/ppermute | solution.py:168
  60.3 12.8 %collective-permute-start.4 = (f32[8,128]{1,0:T(8,128)S(1)}, f32[8,128]{1,0:T(8,128)S(1)}, u32[]{:S(2)}, u32[]{:S(2)}) collective-permute-start(f32[8,128]{1,0:T(8,128)S(1)} %constant_dynamic-slice_fusion.7), channel_id=1, source_target_pairs={{0,4},{1,5},{2,6},{3,7},{4,0},{5,1},{6,2},{7,3},{8,12},{9,13},{10,... | collective-permute-start | bytes 12296 | tf_op jit(solution)/shard_map/ppermute | solution.py:168
  69.8 13.8 %collective-permute-start.5 = (f32[128,512]{0,1:T(8,128)S(1)}, f32[128,512]{0,1:T(8,128)S(1)}, u32[]{:S(2)}, u32[]{:S(2)}) collective-permute-start(f32[128,512]{0,1:T(8,128)S(1)} %constant_dynamic-slice_fusion.6), channel_id=1, source_target_pairs={{0,4},{1,5},{2,6},{3,7},{4,0},{5,1},{6,2},{7,3},{8,12},{9,13},{10,... | collective-permute-start | bytes 786440 | tf_op jit(solution)/shard_map/ppermute | solution.py:168
  83.7 4.6 %collective-permute-start.12 = (f32[16,128]{1,0:T(8,128)S(1)}, f32[16,128]{1,0:T(8,128)S(1)}, u32[]{:S(2)}, u32[]{:S(2)}) collective-permute-start(f32[16,128]{1,0:T(8,128)S(1)} %pad_maximum_fusion.11), channel_id=1, source_target_pairs={{0,4},{1,5},{2,6},{3,7},{4,0},{5,1},{6,2},{7,3},{8,12},{9,13},{10,... | collective-permute-start | bytes 24584 | tf_op jit(solution)/shard_map/ppermute | solution.py:202
  88.3 3.8 %collective-permute-start.13 = (f32[16,256]{1,0:T(8,128)S(1)}, f32[16,256]{1,0:T(8,128)S(1)}, u32[]{:S(2)}, u32[]{:S(2)}) collective-permute-start(f32[16,256]{1,0:T(8,128)S(1)} %pad_maximum_fusion.10), channel_id=1, source_target_pairs={{0,2},{1,3},{2,0},{3,1},{4,6},{5,7},{6,4},{7,5},{8,10},{9,11},{10,... | collective-permute-start | bytes 49160 | tf_op jit(solution)/shard_map/ppermute | solution.py:202
  92.1 1.9 collective-permute-start.14
  162.1 2.9 copy-start.6
  166.6 2.0 copy-start.2
  168.6 4.4 %collective-permute-start.15 = (f32[1024,512]{0,1:T(8,128)S(1)}, f32[1024,512]{0,1:T(8,128)}, u32[]{:S(2)}, u32[]{:S(2)}) collective-permute-start(f32[1024,512]{0,1:T(8,128)S(1)} %constant_dynamic-slice_fusion.2), channel_id=1, source_target_pairs={{0,1},{1,0},{2,3},{3,2},{4,5},{5,4},{6,7},{7,6},{8,9},{9,8},{10,11... | collective-permute-start | bytes 6291464 | tf_op jit(solution)/shard_map/ppermute | solution.py:227
  175.7 25.6 %collective-permute-start.16 = (f32[512,512]{0,1:T(8,128)S(1)}, f32[512,512]{0,1:T(8,128)}, u32[]{:S(2)}, u32[]{:S(2)}) collective-permute-start(f32[512,512]{0,1:T(8,128)S(1)} %constant_dynamic-slice_fusion.1), channel_id=1, source_target_pairs={{0,2},{1,3},{2,0},{3,1},{4,6},{5,7},{6,4},{7,5},{8,10},{9,11},{10,... | collective-permute-start | bytes 3145736 | tf_op jit(solution)/shard_map/ppermute | solution.py:227
  202.8 25.5 %collective-permute-start.17 = (f32[256,512]{0,1:T(8,128)S(1)}, f32[256,512]{0,1:T(8,128)S(1)}, u32[]{:S(2)}, u32[]{:S(2)}) collective-permute-start(f32[256,512]{0,1:T(8,128)S(1)} %constant_dynamic-slice_fusion), channel_id=1, source_target_pairs={{0,4},{1,5},{2,6},{3,7},{4,0},{5,1},{6,2},{7,3},{8,12},{9,13},{10,... | collective-permute-start | bytes 1572872 | tf_op jit(solution)/shard_map/ppermute | solution.py:227
  228.5 25.6 %collective-permute-start.18 = (f32[256,512]{0,1:T(8,128)S(1)}, f32[256,512]{0,1:T(8,128)S(1)}, u32[]{:S(2)}, u32[]{:S(2)}) collective-permute-start(f32[256,512]{0,1:T(8,128)S(1)} %dynamic-slice_add_fusion.2), channel_id=1, source_target_pairs={{0,4},{1,5},{2,6},{3,7},{4,0},{5,1},{6,2},{7,3},{8,12},{9,13},{10,... | collective-permute-start | bytes 1572872 | tf_op jit(solution)/shard_map/ppermute | solution.py:231
  254.2 28.1 %collective-permute-start.19 = (f32[512,512]{0,1:T(8,128)S(1)}, f32[512,512]{0,1:T(8,128)S(1)}, u32[]{:S(2)}, u32[]{:S(2)}) collective-permute-start(f32[512,512]{0,1:T(8,128)S(1)} %pad_maximum_fusion.3), channel_id=1, source_target_pairs={{0,2},{1,3},{2,0},{3,1},{4,6},{5,7},{6,4},{7,5},{8,10},{9,11},{10,... | collective-permute-start | bytes 3145736 | tf_op jit(solution)/shard_map/ppermute | solution.py:231
  254.3 24.7 %collective-permute-start.9 = (bf16[128,512]{0,1:T(8,128)(2,1)S(1)}, bf16[128,512]{0,1:T(8,128)(2,1)S(1)}, u32[]{:S(2)}, u32[]{:S(2)}) collective-permute-start(bf16[128,512]{0,1:T(8,128)(2,1)S(1)} %get-tuple-element.52), channel_id=1, source_target_pairs={{0,4},{1,5},{2,6},{3,7},{4,0},{5,1},{6,2},{7,3},{8,12},{9,13},{10,... | collective-permute-start | bytes 393224 | tf_op jit(solution)/shard_map/ppermute | solution.py:202
  279.1 9.2 %collective-permute-start.10 = (bf16[256,512]{0,1:T(8,128)(2,1)S(1)}, bf16[256,512]{0,1:T(8,128)(2,1)S(1)}, u32[]{:S(2)}, u32[]{:S(2)}) collective-permute-start(bf16[256,512]{0,1:T(8,128)(2,1)S(1)} %pad_maximum_fusion.7), channel_id=1, source_target_pairs={{0,2},{1,3},{2,0},{3,1},{4,6},{5,7},{6,4},{7,5},{8,10},{9,11},{10,... | collective-permute-start | bytes 786440 | tf_op jit(solution)/shard_map/ppermute | solution.py:202
  282.7 5.8 %copy-start.3 = (bf16[1024,8,64]{0,2,1:T(8,128)(2,1)S(1)}, bf16[1024,8,64]{0,2,1:T(8,128)(2,1)}, u32[]{:S(2)}) copy-start(bf16[1024,8,64]{0,2,1:T(8,128)(2,1)} %copy.54) | copy-start | bytes 3145732
  282.7 5.8 %copy-start.8 = (bf16[512,512]{1,0:T(8,128)(2,1)S(1)}, bf16[512,512]{1,0:T(8,128)(2,1)}, u32[]{:S(2)}) copy-start(bf16[512,512]{1,0:T(8,128)(2,1)} %param.11) | copy-start | bytes 1572868
  282.7 13.4 %collective-permute-start.20 = (f32[1024,512]{0,1:T(8,128)S(1)}, f32[1024,512]{0,1:T(8,128)S(1)}, u32[]{:S(2)}, u32[]{:S(2)}) collective-permute-start(f32[1024,512]{0,1:T(8,128)S(1)} %pad_maximum_fusion.1), channel_id=1, source_target_pairs={{0,1},{1,0},{2,3},{3,2},{4,5},{5,4},{6,7},{7,6},{8,9},{9,8},{10,11... | collective-permute-start | bytes 6291464 | tf_op jit(solution)/shard_map/ppermute | solution.py:231
  288.4 3.1 %collective-permute-start.11 = (bf16[512,512]{0,1:T(8,128)(2,1)S(1)}, bf16[512,512]{0,1:T(8,128)(2,1)S(1)}, u32[]{:S(2)}, u32[]{:S(2)}) collective-permute-start(bf16[512,512]{0,1:T(8,128)(2,1)S(1)} %pad_maximum_fusion.6), channel_id=1, source_target_pairs={{0,1},{1,0},{2,3},{3,2},{4,5},{5,4},{6,7},{7,6},{8,9},{9,8},{10,11... | collective-permute-start | bytes 1572872 | tf_op jit(solution)/shard_map/ppermute | solution.py:202
  291.7 2.7 copy-start.11
  291.7 2.7 copy-start.15
  301.3 2.6 copy-start.1
  (6 other events, 8.6 us)

commit v5 on v4

--- a/solution.py
+++ b/solution.py
@@ -220,21 +220,11 @@
     vals_grad = joined(dv).astype(bf16)
     wk_part = jnp.einsum("ka,kb->ab", hits_in, keys_grad, preferred_element_type=f32)
     wv_part = jnp.einsum("ka,kb->ab", hits_in, vals_grad, preferred_element_type=f32)
-    summed = jnp.concatenate([joined(dq_r), wk_part, wv_part], axis=0)
-    for k, bit, half in steps:
-        half = summed.shape[0] // 2
-        pairs = [(i, i ^ (1 << k)) for i in range(regions)]
-        other = lax.ppermute(lax.dynamic_slice_in_dim(summed, (1 - bit) * half, half, 0), "region", pairs)
-        summed = lax.dynamic_slice_in_dim(summed, bit * half, half, 0) + other
-    for k, bit, half in reversed(steps):
-        pairs = [(i, i ^ (1 << k)) for i in range(regions)]
-        other = lax.ppermute(summed, "region", pairs)
-        summed = jnp.concatenate(
-            [jnp.where(bit == 0, summed, other), jnp.where(bit == 0, other, summed)], axis=0
-        )
-    query_grad_sum = summed[:n_queries].astype(bf16)
-    grad_wk = summed[n_queries : n_queries + width]
-    grad_wv = summed[n_queries + width :]
+    query_grad_sum, grad_wk, grad_wv = lax.psum(
+        (joined(dq_r).astype(bf16), wk_part.astype(bf16), wv_part.astype(bf16)), "region"
+    )
+    grad_wk = grad_wk.astype(f32)
+    grad_wv = grad_wv.astype(f32)
     grad_q = query_grad_sum
     grad_wq = jnp.einsum("qa,qb->ab", queries_in, grad_q, preferred_element_type=f32)
     grad_queries = (

time: 306 us -> 252 us (0.82)
  waiting for transfers between devices: 134 us -> 83.7 us
  between operations: 1.17 us -> 14.5 us
  local copies, waits for them, and re-layouts: 41.1 us -> 33.2 us
  starting transfers between devices: 21.4 us -> 16.6 us
  other arithmetic: 16 us -> 11.4 us
    ppermute x6 -> x0, waiting for transfers between devices: 77.7 us -> none  [the longest x3 52.2 us: on_device(): lax.ppermute(lax.dynamic_slice_in_dim(summed, (1 - bit) * half, half, 0),...]
    psum x0 -> x1, waiting for transfers between devices: none -> 52.1 us  [on_device(): lax.psum((joined(dq_r).astype(bf16), wk_part.astype(bf16), wv_part.astype...]
    ppermute x6, waiting for transfers between devices: 35.9 us -> 11.5 us  [on_device(): other = lax.ppermute(gathered, 'region', pairs)]
    add x3 -> x0, other arithmetic: 4.13 us -> none  [on_device(): summed = lax.dynamic_slice_in_dim(summed, bit * half, half, 0) + other]
    dot_general x2 -> x0, local copies, waits for them, and re-layouts: 3.84 us -> none  [the longest x1 2.53 us: on_device(): jnp.einsum('ka,kb->ab', hits_in, keys_grad, preferred_element_type=f32)]
    ppermute x6 -> x0, starting transfers between devices: 3.54 us -> none  [the longest x3 3.33 us: on_device(): lax.ppermute(lax.dynamic_slice_in_dim(summed, (1 - bit) * half, half, 0),...]
    unnamed x37 -> x41, local copies, waits for them, and re-layouts: 7.5 us -> 5.23 us
  transfers between devices with their start and end apart: 21 -> 16, of which waited for: 11 -> 7; matrix products, arithmetic and copies ran while one was open for 5% -> 15% of each run, Pallas kernels for 0% -> 18%
where the time goes in v5:
time: 252 us; the launch traced here: 251 us
  waiting for transfers between devices  83.7 us (33%)
  Pallas kernels  72.9 us (29%)
  local copies, waits for them, and re-layouts  33.2 us (13%)
  matrix products  18.3 us (7%)
  starting transfers between devices  16.6 us (7%)
  between operations  14.5 us (6%)
  other arithmetic  11.4 us (5%)
    psum x1, waiting for transfers between devices, on_device(): lax.psum((joined(dq_r).astype(bf16), wk_part.astype(bf16), wv_part.astype...  52.1 us
    pallas_call x1, Pallas kernels, _backward(): pl.pallas_call(functools.partial(_bwd_kernel, scale=scale), grid=(heads,...  44.1 us
    pallas_call x1, Pallas kernels, _forward(): pl.pallas_call(functools.partial(_fwd_kernel, scale=scale), grid=(heads,...  28.8 us
    ppermute x9, waiting for transfers between devices, on_device(): lax.ppermute((lax.dynamic_slice_in_dim(numer, (1 - bit) * half, half, 0),...  20.2 us
    ppermute x9, starting transfers between devices, on_device(): lax.ppermute((lax.dynamic_slice_in_dim(numer, (1 - bit) * half, half, 0),...  11.8 us
    ppermute x6, waiting for transfers between devices, on_device(): other = lax.ppermute(gathered, 'region', pairs)  11.5 us
    reshape x4, local copies, waits for them, and re-layouts, heads(): return x.reshape(x.shape[0], HEADS, head_dim).transpose(1, 0, 2)  7.33 us
    convert_element_type x1, other arithmetic, on_device(): vals_grad = joined(dv).astype(bf16)  5.5 us
  transfers between devices with their start and end apart: 16, of which 7 were waited for; matrix products, arithmetic and copies ran while one was open for 15% of the time, Pallas kernels for 18%

profile of v5, /device:TPU:0, one launch (start us, length us, event | category | flops | bytes accessed | tf_op | source)
XLA Modules:
  0.0 250.5 jit_solution(14159375644577756380)
XLA Ops:
  8.3 2.1 convolution_convert_fusion.3
  10.4 1.8 copy.44
  13.0 1.9 copy.45
  15.7 1.8 copy.46
  18.2 28.8 %shard_map.135 = (f32[8,1024,64]{2,1,0:T(8,128)}, f32[8,1024,1]{2,1,0:T(8,128)}, f32[8,1024,1]{2,1,0:T(8,128)}) custom-call(bf16[8,1024,64]{2,1,0:T(8,128)(2,1)} %bitcast.102, bf16[8,1024,64]{2,1,0:T(8,128)(2,1)} %bitcast.104, bf16[8,1024,64]{2,1,0:T(8,128)(2,1)} %bitcast.106, f32[8,1,1024]{2,1,0:T(1,128)} %bitcast.121), custom_call_target="tpu_custom_call" | custom-call | tf_op jit(solution)/shard_map/pallas_call | solution.py:72
  47.0 2.8 %copy.47 = f32[1024,8,64]{0,2,1:T(8,128)S(1)} copy(f32[1024,8,64]{2,0,1:T(8,128)} %bitcast.114) | data formatting | bytes 4194304 | tf_op jit(solution)/shard_map/transpose | solution.py:143
  51.4 3.5 %dynamic-slice_reduce_fusion.3 = (f32[8,512]{1,0:T(8,128)S(1)}, f32[8,512]{1,0:T(8,128)S(1)}) fusion(f32[8,1024,1]{2,1,0:T(8,128)} %get-tuple-element.14, s32[]{:T(128)S(6)} %select_n.108, s32[]{:T(128)S(6)} %select_n.109), kind=kLoop, calls=%fused_computation.9 | loop fusion | bytes 65544 | tf_op jit(solution)/shard_map/dynamic_slice | solution.py:165
  57.6 3.0 %collective-permute-start.2 = (f32[8,256]{1,0:T(8,128)S(1)}, f32[8,256]{1,0:T(8,128)S(1)}, u32[]{:S(2)}, u32[]{:S(2)}) collective-permute-start(f32[8,256]{1,0:T(8,128)S(1)} %constant_dynamic-slice_fusion.7), channel_id=1, source_target_pairs={{0,2},{1,3},{2,0},{3,1},{4,6},{5,7},{6,4},{7,5},{8,10},{9,11},{10,... | collective-permute-start | bytes 24584 | tf_op jit(solution)/shard_map/ppermute | solution.py:168
  62.3 2.0 collective-permute-start.3
  64.3 2.6 %collective-permute-start.8 = (f32[8,128]{1,0:T(8,128)S(1)}, f32[8,128]{1,0:T(8,128)S(1)}, u32[]{:S(2)}, u32[]{:S(2)}) collective-permute-start(f32[8,128]{1,0:T(8,128)S(1)} %constant_dynamic-slice_fusion), channel_id=1, source_target_pairs={{0,4},{1,5},{2,6},{3,7},{4,0},{5,1},{6,2},{7,3},{8,12},{9,13},{10,... | collective-permute-start | bytes 12296 | tf_op jit(solution)/shard_map/ppermute | solution.py:168
  67.3 8.9 %collective-permute-done.3 = f32[256,512]{0,1:T(8,128)S(1)} collective-permute-done((f32[256,512]{0,1:T(8,128)S(1)}, f32[256,512]{0,1:T(8,128)S(1)}, u32[]{:S(2)}, u32[]{:S(2)}) %collective-permute-start.3) | collective-permute-done | bytes 524320 | tf_op jit(solution)/shard_map/ppermute | solution.py:168
  76.4 2.6 %collective-permute-start.5 = (f32[128,512]{0,1:T(8,128)S(1)}, f32[128,512]{0,1:T(8,128)S(1)}, u32[]{:S(2)}, u32[]{:S(2)}) collective-permute-start(f32[128,512]{0,1:T(8,128)S(1)} %constant_dynamic-slice_fusion.3), channel_id=1, source_target_pairs={{0,4},{1,5},{2,6},{3,7},{4,0},{5,1},{6,2},{7,3},{8,12},{9,13},{10,... | collective-permute-start | bytes 786440 | tf_op jit(solution)/shard_map/ppermute | solution.py:168
  79.8 10.4 %collective-permute-done.5 = f32[128,512]{0,1:T(8,128)S(1)} collective-permute-done((f32[128,512]{0,1:T(8,128)S(1)}, f32[128,512]{0,1:T(8,128)S(1)}, u32[]{:S(2)}, u32[]{:S(2)}) %collective-permute-start.5) | collective-permute-done | bytes 262176 | tf_op jit(solution)/shard_map/ppermute | solution.py:168
  90.4 4.5 %collective-permute-done.12 = f32[16,128]{1,0:T(8,128)S(1)} collective-permute-done((f32[16,128]{1,0:T(8,128)S(1)}, f32[16,128]{1,0:T(8,128)S(1)}, u32[]{:S(2)}, u32[]{:S(2)}) %collective-permute-start.12) | collective-permute-done | bytes 8224 | tf_op jit(solution)/shard_map/ppermute | solution.py:202
  95.7 3.0 %collective-permute-done.13 = f32[16,256]{1,0:T(8,128)S(1)} collective-permute-done((f32[16,256]{1,0:T(8,128)S(1)}, f32[16,256]{1,0:T(8,128)S(1)}, u32[]{:S(2)}, u32[]{:S(2)}) %collective-permute-start.13) | collective-permute-done | bytes 16416 | tf_op jit(solution)/shard_map/ppermute | solution.py:202
  98.8 1.8 copy.48
  100.6 1.6 collective-permute-start.9
  102.3 2.7 %copy.49.lt_ref = f32[8,1024,1]{2,1,0:T(8,128)} copy(f32[8,1024,1]{1,0,2:T(8,128)S(1)} %get-tuple-element.67) | data formatting | bytes 65536 | tf_op jit(solution)/shard_map/reshape | solution.py:210
  105.0 2.7 %copy.50.dl_ref = f32[8,1024,1]{2,1,0:T(8,128)} copy(f32[8,1024,1]{1,0,2:T(8,128)S(1)} %get-tuple-element.66) | data formatting | bytes 65536 | tf_op jit(solution)/shard_map/reshape | solution.py:211
  107.6 44.1 %shard_map.136 = (f32[8,1024,64]{2,1,0:T(8,128)}, f32[8,1024,64]{2,1,0:T(8,128)}, f32[8,1024,64]{2,1,0:T(8,128)}) custom-call(bf16[8,1024,64]{2,1,0:T(8,128)(2,1)} %bitcast.103, bf16[8,1024,64]{2,1,0:T(8,128)(2,1)} %bitcast.105, bf16[8,1024,64]{2,1,0:T(8,128)(2,1)} %bitcast.107, bf16[8,1024,64]{2,1,0:T(8,128)(2,1)} %bitcast.110, f32[8,1024,1]{2,1,0:T(8,128)} %copy.49.lt_ref, ...), custom_call_target="tpu_custom_call" | custom-call | tf_op jit(solution)/shard_map/pallas_call | solution.py:99
  151.8 5.5 %convert_bitcast_fusion = (bf16[1024,8,64]{2,0,1:T(8,128)(2,1)}, bf16[1024,8,64]{2,0,1:T(8,128)(2,1)S(1)}) fusion(f32[8,1024,64]{2,1,0:T(8,128)} %get-tuple-element.18, f32[8,1024,64]{2,1,0:T(8,128)} %get-tuple-element.17), kind=kLoop, calls=%fused_computation.1 | loop fusion | flops 1048576 | bytes 6291456 | tf_op jit(solution)/shard_map/convert_element_type | solution.py:220
  158.9 2.6 %convert_bitcast_fusion.2 = bf16[1024,8,64]{2,0,1:T(8,128)(2,1)S(1)} fusion(f32[8,1024,64]{2,1,0:T(8,128)} %get-tuple-element.16), kind=kLoop, calls=%fused_computation.4 | loop fusion | flops 524288 | bytes 3145728 | tf_op jit(solution)/shard_map/convert_element_type | solution.py:224
  163.0 2.7 %copy.53 = bf16[1024,8,64]{0,2,1:T(8,128)(2,1)} copy(bf16[1024,8,64]{2,0,1:T(8,128)(2,1)} %get-tuple-element.82) | data formatting | bytes 2097152 | tf_op jit(solution)/shard_map/convert_element_type | solution.py:220
  167.4 2.1 collective-permute-start.10
  169.4 2.7 %fusion.1 = bf16[512,512]{0,1:T(8,128)(2,1)} fusion(bf16[1024,512]{0,1:T(8,128)(2,1)} %bitcast.115, bf16[1024,512]{1,0:T(8,128)(2,1)S(1)} %copy-done), kind=kOutput, calls=%fused_computation.18 | convolution fusion | flops 537133056 | bytes 2621440 | tf_op jit(solution)/shard_map/ka,kb->ab/dot_general | solution.py:222
  172.2 3.9 %collective-permute-done.10 = bf16[256,512]{0,1:T(8,128)(2,1)S(1)} collective-permute-done((bf16[256,512]{0,1:T(8,128)(2,1)S(1)}, bf16[256,512]{0,1:T(8,128)(2,1)S(1)}, u32[]{:S(2)}, u32[]{:S(2)}) %collective-permute-start.10) | collective-permute-done | bytes 262176 | tf_op jit(solution)/shard_map/ppermute | solution.py:202
  177.6 1.7 add_convert_fusion
  180.6 1.7 fusion.3
  182.3 1.7 add_convert_fusion.2
  184.0 52.1 %all-reduce.3.cloned.1.call-done = (bf16[512,512]{0,1:T(8,128)(2,1)}, bf16[512,512]{0,1:T(8,128)(2,1)}, bf16[1024,512]{0,1:T(8,128)(2,1)}) async-done(((bf16[512,512]{0,1:T(8,128)(2,1)}, bf16[512,512]{0,1:T(8,128)(2,1)}, bf16[1024,512]{0,1:T(8,128)(2,1)}), (bf16[512,512]{0,1:T(8,128)(2,1)}, bf16[512,512]{0,1:T(8,128)(2,1)}, bf16[1024,512]{0,1:T(8,128)(2,1)})) %all-reduce.3.cloned.1.call-update) | async-done | bytes 2097168 | tf_op jit(solution)/shard_map/psum | solution.py:223
  236.1 2.1 convolution_bitcast_fusion
  238.3 1.7 add_convert_fusion.1
  (101 shorter events, 22.7 us)
Async XLA Ops:
  7.2 5.1 %copy-start = (bf16[1024,512]{1,0:T(8,128)(2,1)S(1)}, bf16[1024,512]{1,0:T(8,128)(2,1)}, u32[]{:S(2)}) copy-start(bf16[1024,512]{1,0:T(8,128)(2,1)} %param.9) | copy-start | bytes 3145732
  7.2 229.0 %all-reduce.3.cloned.1.call-start = ((), (), s32[]{:S(2)}) async-start(), calls=%async_computation | async-start | bytes 4194304 | tf_op jit(solution)/shard_map/psum | solution.py:223
  10.4 1.8 copy-start.5
  13.0 1.9 copy-start.7
  50.9 9.8 %collective-permute-start.1 = (f32[512,512]{0,1:T(8,128)}, f32[512,512]{0,1:T(8,128)}, u32[]{:S(2)}, u32[]{:S(2)}) collective-permute-start(f32[512,512]{0,1:T(8,128)} %constant_dynamic-slice_fusion.8), channel_id=1, source_target_pairs={{0,1},{1,0},{2,3},{3,2},{4,5},{5,4},{6,7},{7,6},{8,9},{9,8},{10,11... | collective-permute-start | bytes 3145736 | tf_op jit(solution)/shard_map/ppermute | solution.py:168
  51.4 3.6 %copy-start.3 = (f32[8,1024,1]{2,1,0:T(8,128)S(1)}, f32[8,1024,1]{2,1,0:T(8,128)}, u32[]{:S(2)}) copy-start(f32[8,1024,1]{2,1,0:T(8,128)} %get-tuple-element.15) | copy-start | bytes 98308
  54.9 1.8 collective-permute-start
  56.2 1.4 collective-permute-start.6
  57.6 6.7 %collective-permute-start.2 = (f32[8,256]{1,0:T(8,128)S(1)}, f32[8,256]{1,0:T(8,128)S(1)}, u32[]{:S(2)}, u32[]{:S(2)}) collective-permute-start(f32[8,256]{1,0:T(8,128)S(1)} %constant_dynamic-slice_fusion.7), channel_id=1, source_target_pairs={{0,2},{1,3},{2,0},{3,1},{4,6},{5,7},{6,4},{7,5},{8,10},{9,11},{10,... | collective-permute-start | bytes 24584 | tf_op jit(solution)/shard_map/ppermute | solution.py:168
  60.6 3.7 %collective-permute-start.7 = (f32[8,256]{1,0:T(8,128)S(1)}, f32[8,256]{1,0:T(8,128)S(1)}, u32[]{:S(2)}, u32[]{:S(2)}) collective-permute-start(f32[8,256]{1,0:T(8,128)S(1)} %constant_dynamic-slice_fusion.2), channel_id=1, source_target_pairs={{0,2},{1,3},{2,0},{3,1},{4,6},{5,7},{6,4},{7,5},{8,10},{9,11},{10,... | collective-permute-start | bytes 24584 | tf_op jit(solution)/shard_map/ppermute | solution.py:168
  62.2 16.8 %copy-start.12 = (bf16[1024,512]{1,0:T(8,128)(2,1)S(1)}, bf16[1024,512]{1,0:T(8,128)(2,1)}, u32[]{:S(2)}) copy-start(bf16[1024,512]{1,0:T(8,128)(2,1)} %param.15) | copy-start | bytes 3145732
  62.2 16.8 %copy-start.16 = (bf16[512,512]{1,0:T(8,128)(2,1)S(1)}, bf16[512,512]{1,0:T(8,128)(2,1)}, u32[]{:S(2)}) copy-start(bf16[512,512]{1,0:T(8,128)(2,1)} %param.13) | copy-start | bytes 1572868
  62.3 14.0 %collective-permute-start.3 = (f32[256,512]{0,1:T(8,128)S(1)}, f32[256,512]{0,1:T(8,128)S(1)}, u32[]{:S(2)}, u32[]{:S(2)}) collective-permute-start(f32[256,512]{0,1:T(8,128)S(1)} %constant_dynamic-slice_fusion.6), channel_id=1, source_target_pairs={{0,2},{1,3},{2,0},{3,1},{4,6},{5,7},{6,4},{7,5},{8,10},{9,11},{10,... | collective-permute-start | bytes 1572872 | tf_op jit(solution)/shard_map/ppermute | solution.py:168
  64.3 15.5 %collective-permute-start.8 = (f32[8,128]{1,0:T(8,128)S(1)}, f32[8,128]{1,0:T(8,128)S(1)}, u32[]{:S(2)}, u32[]{:S(2)}) collective-permute-start(f32[8,128]{1,0:T(8,128)S(1)} %constant_dynamic-slice_fusion), channel_id=1, source_target_pairs={{0,4},{1,5},{2,6},{3,7},{4,0},{5,1},{6,2},{7,3},{8,12},{9,13},{10,... | collective-permute-start | bytes 12296 | tf_op jit(solution)/shard_map/ppermute | solution.py:168
  66.9 12.8 %collective-permute-start.4 = (f32[8,128]{1,0:T(8,128)S(1)}, f32[8,128]{1,0:T(8,128)S(1)}, u32[]{:S(2)}, u32[]{:S(2)}) collective-permute-start(f32[8,128]{1,0:T(8,128)S(1)} %constant_dynamic-slice_fusion.4), channel_id=1, source_target_pairs={{0,4},{1,5},{2,6},{3,7},{4,0},{5,1},{6,2},{7,3},{8,12},{9,13},{10,... | collective-permute-start | bytes 12296 | tf_op jit(solution)/shard_map/ppermute | solution.py:168
  76.4 13.8 %collective-permute-start.5 = (f32[128,512]{0,1:T(8,128)S(1)}, f32[128,512]{0,1:T(8,128)S(1)}, u32[]{:S(2)}, u32[]{:S(2)}) collective-permute-start(f32[128,512]{0,1:T(8,128)S(1)} %constant_dynamic-slice_fusion.3), channel_id=1, source_target_pairs={{0,4},{1,5},{2,6},{3,7},{4,0},{5,1},{6,2},{7,3},{8,12},{9,13},{10,... | collective-permute-start | bytes 786440 | tf_op jit(solution)/shard_map/ppermute | solution.py:168
  90.3 4.6 %collective-permute-start.12 = (f32[16,128]{1,0:T(8,128)S(1)}, f32[16,128]{1,0:T(8,128)S(1)}, u32[]{:S(2)}, u32[]{:S(2)}) collective-permute-start(f32[16,128]{1,0:T(8,128)S(1)} %pad_maximum_fusion.8), channel_id=1, source_target_pairs={{0,4},{1,5},{2,6},{3,7},{4,0},{5,1},{6,2},{7,3},{8,12},{9,13},{10,... | collective-permute-start | bytes 24584 | tf_op jit(solution)/shard_map/ppermute | solution.py:202
  94.9 3.8 %collective-permute-start.13 = (f32[16,256]{1,0:T(8,128)S(1)}, f32[16,256]{1,0:T(8,128)S(1)}, u32[]{:S(2)}, u32[]{:S(2)}) collective-permute-start(f32[16,256]{1,0:T(8,128)S(1)} %pad_maximum_fusion.7), channel_id=1, source_target_pairs={{0,2},{1,3},{2,0},{3,1},{4,6},{5,7},{6,4},{7,5},{8,10},{9,11},{10,... | collective-permute-start | bytes 49160 | tf_op jit(solution)/shard_map/ppermute | solution.py:202
  98.7 3.5 %collective-permute-start.14 = (f32[16,512]{1,0:T(8,128)S(1)}, f32[16,512]{1,0:T(8,128)S(1)}, u32[]{:S(2)}, u32[]{:S(2)}) collective-permute-start(f32[16,512]{1,0:T(8,128)S(1)} %pad_maximum_fusion.6), channel_id=1, source_target_pairs={{0,1},{1,0},{2,3},{3,2},{4,5},{5,4},{6,7},{7,6},{8,9},{9,8},{10,11... | collective-permute-start | bytes 98312 | tf_op jit(solution)/shard_map/ppermute | solution.py:202
  100.6 66.7 %collective-permute-start.9 = (bf16[128,512]{0,1:T(8,128)(2,1)S(1)}, bf16[128,512]{0,1:T(8,128)(2,1)S(1)}, u32[]{:S(2)}, u32[]{:S(2)}) collective-permute-start(bf16[128,512]{0,1:T(8,128)(2,1)S(1)} %get-tuple-element.55), channel_id=1, source_target_pairs={{0,4},{1,5},{2,6},{3,7},{4,0},{5,1},{6,2},{7,3},{8,12},{9,13},{10,... | collective-permute-start | bytes 393224 | tf_op jit(solution)/shard_map/ppermute | solution.py:202
  158.9 2.6 %copy-start.1 = (bf16[1024,8,64]{0,2,1:T(8,128)(2,1)S(1)}, bf16[1024,8,64]{0,2,1:T(8,128)(2,1)}, u32[]{:S(2)}) copy-start(bf16[1024,8,64]{0,2,1:T(8,128)(2,1)} %copy.52) | copy-start | bytes 3145732
  167.4 8.8 %collective-permute-start.10 = (bf16[256,512]{0,1:T(8,128)(2,1)S(1)}, bf16[256,512]{0,1:T(8,128)(2,1)S(1)}, u32[]{:S(2)}, u32[]{:S(2)}) collective-permute-start(bf16[256,512]{0,1:T(8,128)(2,1)S(1)} %pad_maximum_fusion.4), channel_id=1, source_target_pairs={{0,2},{1,3},{2,0},{3,1},{4,6},{5,7},{6,4},{7,5},{8,10},{9,11},{10,... | collective-permute-start | bytes 786440 | tf_op jit(solution)/shard_map/ppermute | solution.py:202
  172.2 4.2 %copy-start.2 = (bf16[1024,8,64]{0,2,1:T(8,128)(2,1)S(1)}, bf16[1024,8,64]{0,2,1:T(8,128)(2,1)}, u32[]{:S(2)}) copy-start(bf16[1024,8,64]{0,2,1:T(8,128)(2,1)} %copy.52) | copy-start | bytes 3145732
  172.2 4.2 %copy-start.6 = (bf16[512,512]{1,0:T(8,128)(2,1)S(1)}, bf16[512,512]{1,0:T(8,128)(2,1)}, u32[]{:S(2)}) copy-start(bf16[512,512]{1,0:T(8,128)(2,1)} %param.11) | copy-start | bytes 1572868
  176.3 3.1 %collective-permute-start.11 = (bf16[512,512]{0,1:T(8,128)(2,1)S(1)}, bf16[512,512]{0,1:T(8,128)(2,1)S(1)}, u32[]{:S(2)}, u32[]{:S(2)}) collective-permute-start(bf16[512,512]{0,1:T(8,128)(2,1)S(1)} %pad_maximum_fusion.3), channel_id=1, source_target_pairs={{0,1},{1,0},{2,3},{3,2},{4,5},{5,4},{6,7},{7,6},{8,9},{9,8},{10,11... | collective-permute-start | bytes 1572872 | tf_op jit(solution)/shard_map/ppermute | solution.py:202
  179.6 2.7 %copy-start.11 = (bf16[1024,512]{1,0:T(8,128)(2,1)S(1)}, bf16[1024,512]{1,0:T(8,128)(2,1)}, u32[]{:S(2)}) copy-start(bf16[1024,512]{1,0:T(8,128)(2,1)} %param.8) | copy-start | bytes 3145732
  179.6 2.7 %copy-start.17 = (bf16[512,512]{1,0:T(8,128)(2,1)S(1)}, bf16[512,512]{1,0:T(8,128)(2,1)}, u32[]{:S(2)}) copy-start(bf16[512,512]{1,0:T(8,128)(2,1)} %param.13) | copy-start | bytes 1572868
  236.1 2.1 copy-start.14
  236.1 2.1 copy-start.15
  236.1 2.1 copy-start.18
  238.3 3.1 %copy-start.10 = (bf16[512,512]{0,1:T(8,128)(2,1)S(1)}, bf16[512,512]{0,1:T(8,128)(2,1)}, u32[]{:S(2)}) copy-start(bf16[512,512]{0,1:T(8,128)(2,1)} %get-tuple-element.51) | copy-start | bytes 1572868
  240.0 2.5 copy-start.9
  (3 other events, 3.8 us)
Sparse Core Ops, SparseCore 0:
  172.3 63.7 all-reduce.2

commit v6 on v5

--- a/solution.py
+++ b/solution.py
@@ -13,28 +13,43 @@
 TQ = 256
 
 
-def _fwd_kernel(q_ref, k_ref, v_ref, cm_ref, numer_ref, m_ref, l_ref, *, scale):
+def _fwd_kernel(need_ref, q_ref, k_ref, v_ref, cm_ref, numer_ref, m_ref, l_ref, s_scr, m_scr, l_scr, acc_scr, *, scale):
+    i = pl.program_id(1)
+    n_tiles = pl.num_programs(1)
     q = q_ref[0]
-    k = k_ref[0]
-    v = v_ref[0]
-    s = lax.dot_general(q, k, (((1,), (1,)), ((), ())), preferred_element_type=jnp.float32) * scale
-    tq, nk = s.shape
+    tq = q.shape[0]
+    nk = k_ref.shape[1]
     nb = tq // BLOCK
-    s3 = s.reshape(nb, BLOCK, nk)
-    allowed = cm_ref[...] > 0.5
-    masked = jnp.where(allowed, s3, -1e30)
-    mx = jnp.max(masked, axis=2, keepdims=True)
-    e = jnp.where(allowed, jnp.exp(masked - mx), 0.0)
-    tot = jnp.sum(e, axis=2, keepdims=True)
-    numer = jnp.dot(
-        e.reshape(tq, nk).astype(jnp.bfloat16), v, preferred_element_type=jnp.float32
-    )
-    numer_ref[0] = numer
-    m_ref[0] = mx.reshape(tq, 1)
-    l_ref[0] = tot.reshape(tq, 1)
-
-
-def _bwd_kernel(q_ref, k_ref, v_ref, ga_ref, lt_ref, dl_ref, cm_ref, dq_ref, dk_ref, dv_ref, *, scale):
+    chunks = nk // BLOCK
+    m_scr[...] = jnp.full(m_scr.shape, -1e30, jnp.float32)
+    l_scr[...] = jnp.zeros(l_scr.shape, jnp.float32)
+    acc_scr[...] = jnp.zeros(acc_scr.shape, jnp.float32)
+    for c in range(chunks):
+        @pl.when(need_ref[i * chunks + c] != 0)
+        def _():
+            k = k_ref[0, c * BLOCK : (c + 1) * BLOCK, :]
+            s = lax.dot_general(q, k, (((1,), (1,)), ((), ())), preferred_element_type=jnp.float32) * scale
+            allowed = cm_ref[:, :, c * BLOCK : (c + 1) * BLOCK] > 0.5
+            masked = jnp.where(allowed, s.reshape(nb, BLOCK, BLOCK), -1e30)
+            s_scr[c] = masked.reshape(tq, BLOCK)
+            m_scr[...] = jnp.maximum(m_scr[...], jnp.max(masked, axis=2, keepdims=True).reshape(tq, 1))
+
+    for c in range(chunks):
+        @pl.when(need_ref[i * chunks + c] != 0)
+        def _():
+            allowed = cm_ref[:, :, c * BLOCK : (c + 1) * BLOCK] > 0.5
+            mx = m_scr[...].reshape(nb, BLOCK, 1)
+            e = jnp.where(allowed, jnp.exp(s_scr[c].reshape(nb, BLOCK, BLOCK) - mx), 0.0).reshape(tq, BLOCK)
+            l_scr[...] += jnp.sum(e, axis=1, keepdims=True)
+            v = v_ref[0, c * BLOCK : (c + 1) * BLOCK, :]
+            acc_scr[...] += jnp.dot(e.astype(jnp.bfloat16), v, preferred_element_type=jnp.float32)
+
+    numer_ref[0] = acc_scr[...]
+    m_ref[0] = m_scr[...]
+    l_ref[0] = l_scr[...]
+
+
+def _bwd_kernel(need_ref, q_ref, k_ref, v_ref, ga_ref, lt_ref, dl_ref, cm_ref, dq_ref, dk_ref, dv_ref, dq_scr, *, scale):
     i = pl.program_id(1)
 
     @pl.when(i == 0)
@@ -43,83 +58,105 @@
         dv_ref[...] = jnp.zeros_like(dv_ref)
 
     q = q_ref[0]
-    k = k_ref[0]
-    v = v_ref[0]
     ga = ga_ref[0]
-    s = lax.dot_general(q, k, (((1,), (1,)), ((), ())), preferred_element_type=jnp.float32) * scale
-    tq, nk = s.shape
+    tq = q.shape[0]
+    nk = k_ref.shape[1]
     nb = tq // BLOCK
-    s3 = s.reshape(nb, BLOCK, nk)
-    allowed = cm_ref[...] > 0.5
-    lt = lt_ref[0].reshape(nb, BLOCK, 1)
-    p = jnp.where(allowed, jnp.exp(s3 - lt), 0.0).reshape(tq, nk)
-    dv_ref[0] += lax.dot_general(
-        p.astype(jnp.bfloat16), ga, (((0,), (0,)), ((), ())), preferred_element_type=jnp.float32
-    )
-    dp = lax.dot_general(ga, v, (((1,), (1,)), ((), ())), preferred_element_type=jnp.float32)
-    ds = (p * (dp - dl_ref[0]) * scale).astype(jnp.bfloat16)
-    dq_ref[0] = jnp.dot(ds, k, preferred_element_type=jnp.float32)
-    dk_ref[0] += lax.dot_general(
-        ds, q, (((0,), (0,)), ((), ())), preferred_element_type=jnp.float32
-    )
-
-
-def _forward(qT, kT, vT, cm, scale):
+    chunks = nk // BLOCK
+    dq_scr[...] = jnp.zeros(dq_scr.shape, jnp.float32)
+    for c in range(chunks):
+        @pl.when(need_ref[i * chunks + c] != 0)
+        def _():
+            k = k_ref[0, c * BLOCK : (c + 1) * BLOCK, :]
+            v = v_ref[0, c * BLOCK : (c + 1) * BLOCK, :]
+            s = lax.dot_general(q, k, (((1,), (1,)), ((), ())), preferred_element_type=jnp.float32) * scale
+            allowed = cm_ref[:, :, c * BLOCK : (c + 1) * BLOCK] > 0.5
+            lt = lt_ref[0].reshape(nb, BLOCK, 1)
+            p = jnp.where(allowed, jnp.exp(s.reshape(nb, BLOCK, BLOCK) - lt), 0.0).reshape(tq, BLOCK)
+            dv_ref[0, c * BLOCK : (c + 1) * BLOCK, :] += lax.dot_general(
+                p.astype(jnp.bfloat16), ga, (((0,), (0,)), ((), ())), preferred_element_type=jnp.float32
+            )
+            dp = lax.dot_general(ga, v, (((1,), (1,)), ((), ())), preferred_element_type=jnp.float32)
+            ds = (p * (dp - dl_ref[0]) * scale).astype(jnp.bfloat16)
+            dq_scr[...] += jnp.dot(ds, k, preferred_element_type=jnp.float32)
+            dk_ref[0, c * BLOCK : (c + 1) * BLOCK, :] += lax.dot_general(
+                ds, q, (((0,), (0,)), ((), ())), preferred_element_type=jnp.float32
+            )
+
+    dq_ref[0] = dq_scr[...]
+
+
+def _forward(need, qT, kT, vT, cm, scale):
     heads, nq, hd = qT.shape
     nk = kT.shape[1]
     nb = TQ // BLOCK
     f32 = jnp.float32
+    grid_spec = pltpu.PrefetchScalarGridSpec(
+        num_scalar_prefetch=1,
+        grid=(heads, nq // TQ),
+        in_specs=[
+            pl.BlockSpec((1, TQ, hd), lambda h, i, n: (h, i, 0)),
+            pl.BlockSpec((1, nk, hd), lambda h, i, n: (h, 0, 0)),
+            pl.BlockSpec((1, nk, hd), lambda h, i, n: (h, 0, 0)),
+            pl.BlockSpec((nb, 1, nk), lambda h, i, n: (i, 0, 0)),
+        ],
+        out_specs=[
+            pl.BlockSpec((1, TQ, hd), lambda h, i, n: (h, i, 0)),
+            pl.BlockSpec((1, TQ, 1), lambda h, i, n: (h, i, 0)),
+            pl.BlockSpec((1, TQ, 1), lambda h, i, n: (h, i, 0)),
+        ],
+        scratch_shapes=[
+            pltpu.VMEM((nk // BLOCK, TQ, BLOCK), f32),
+            pltpu.VMEM((TQ, 1), f32),
+            pltpu.VMEM((TQ, 1), f32),
+            pltpu.VMEM((TQ, hd), f32),
+        ],
+    )
     return pl.pallas_call(
         functools.partial(_fwd_kernel, scale=scale),
-        grid=(heads, nq // TQ),
-        in_specs=[
-            pl.BlockSpec((1, TQ, hd), lambda h, i: (h, i, 0)),
-            pl.BlockSpec((1, nk, hd), lambda h, i: (h, 0, 0)),
-            pl.BlockSpec((1, nk, hd), lambda h, i: (h, 0, 0)),
-            pl.BlockSpec((nb, 1, nk), lambda h, i: (i, 0, 0)),
-        ],
-        out_specs=[
-            pl.BlockSpec((1, TQ, hd), lambda h, i: (h, i, 0)),
-            pl.BlockSpec((1, TQ, 1), lambda h, i: (h, i, 0)),
-            pl.BlockSpec((1, TQ, 1), lambda h, i: (h, i, 0)),
-        ],
+        grid_spec=grid_spec,
         out_shape=[
             jax.ShapeDtypeStruct((heads, nq, hd), f32),
             jax.ShapeDtypeStruct((heads, nq, 1), f32),
             jax.ShapeDtypeStruct((heads, nq, 1), f32),
         ],
-    )(qT, kT, vT, cm)
-
-
-def _backward(qT, kT, vT, gaT, lt, dl, cm, scale):
+    )(need, qT, kT, vT, cm)
+
+
+def _backward(need, qT, kT, vT, gaT, lt, dl, cm, scale):
     heads, nq, hd = qT.shape
     nk = kT.shape[1]
     nb = TQ // BLOCK
     f32 = jnp.float32
+    grid_spec = pltpu.PrefetchScalarGridSpec(
+        num_scalar_prefetch=1,
+        grid=(heads, nq // TQ),
+        in_specs=[
+            pl.BlockSpec((1, TQ, hd), lambda h, i, n: (h, i, 0)),
+            pl.BlockSpec((1, nk, hd), lambda h, i, n: (h, 0, 0)),
+            pl.BlockSpec((1, nk, hd), lambda h, i, n: (h, 0, 0)),
+            pl.BlockSpec((1, TQ, hd), lambda h, i, n: (h, i, 0)),
+            pl.BlockSpec((1, TQ, 1), lambda h, i, n: (h, i, 0)),
+            pl.BlockSpec((1, TQ, 1), lambda h, i, n: (h, i, 0)),
+            pl.BlockSpec((nb, 1, nk), lambda h, i, n: (i, 0, 0)),
+        ],
+        out_specs=[
+            pl.BlockSpec((1, TQ, hd), lambda h, i, n: (h, i, 0)),
+            pl.BlockSpec((1, nk, hd), lambda h, i, n: (h, 0, 0)),
+            pl.BlockSpec((1, nk, hd), lambda h, i, n: (h, 0, 0)),
+        ],
+        scratch_shapes=[pltpu.VMEM((TQ, hd), f32)],
+    )
     return pl.pallas_call(
         functools.partial(_bwd_kernel, scale=scale),
-        grid=(heads, nq // TQ),
-        in_specs=[
-            pl.BlockSpec((1, TQ, hd), lambda h, i: (h, i, 0)),
-            pl.BlockSpec((1, nk, hd), lambda h, i: (h, 0, 0)),
-            pl.BlockSpec((1, nk, hd), lambda h, i: (h, 0, 0)),
-            pl.BlockSpec((1, TQ, hd), lambda h, i: (h, i, 0)),
-            pl.BlockSpec((1, TQ, 1), lambda h, i: (h, i, 0)),
-            pl.BlockSpec((1, TQ, 1), lambda h, i: (h, i, 0)),
-            pl.BlockSpec((nb, 1, nk), lambda h, i: (i, 0, 0)),
-        ],
-        out_specs=[
-            pl.BlockSpec((1, TQ, hd), lambda h, i: (h, i, 0)),
-            pl.BlockSpec((1, nk, hd), lambda h, i: (h, 0, 0)),
-            pl.BlockSpec((1, nk, hd), lambda h, i: (h, 0, 0)),
-        ],
+        grid_spec=grid_spec,
         out_shape=[
             jax.ShapeDtypeStruct((heads, nq, hd), f32),
             jax.ShapeDtypeStruct((heads, nk, hd), f32),
             jax.ShapeDtypeStruct((heads, nk, hd), f32),
         ],
         compiler_params=pltpu.CompilerParams(dimension_semantics=("parallel", "arbitrary")),
-    )(qT, kT, vT, gaT, lt, dl, cm)
+    )(need, qT, kT, vT, gaT, lt, dl, cm)
 
 
 def on_device(queries_in, hits_in, w_query, w_key, w_value, w_out, mask_list, grad_out):
@@ -135,6 +172,7 @@
     local_ids = region_index * hit_blocks + jnp.arange(hit_blocks, dtype=jnp.int32)
     blockmask = jnp.any(mask_list[:, :, None] == local_ids[None, None, :], axis=1)
     cm = jnp.repeat(blockmask.astype(f32), BLOCK, axis=1).reshape(q_blocks, 1, n_hits)
+    need = jnp.any(blockmask.reshape(n_queries // TQ, TQ // BLOCK, hit_blocks), axis=1).astype(jnp.int32).reshape(-1)
 
     def heads(x):
         return x.reshape(x.shape[0], HEADS, head_dim).transpose(1, 0, 2)
@@ -148,7 +186,7 @@
     qT, kT, vT = heads(query), heads(keys), heads(vals)
 
     regions = lax.axis_size("region")
-    numer_r, max_r, total_r = _forward(qT, kT, vT, cm, scale)
+    numer_r, max_r, total_r = _forward(need, qT, kT, vT, cm, scale)
     numer = joined(numer_r)
     peak = max_r.reshape(HEADS, n_queries)
     total = total_r.reshape(HEADS, n_queries)
@@ -215,7 +253,7 @@
     grad_wo = jnp.einsum("qa,qb->ab", attended, grad_out, preferred_element_type=f32)
     gaT = heads(grad_att)
 
-    dq_r, dk, dv = _backward(qT, kT, vT, gaT, log_total, deltas, cm, scale)
+    dq_r, dk, dv = _backward(need, qT, kT, vT, gaT, log_total, deltas, cm, scale)
     keys_grad = joined(dk).astype(bf16)
     vals_grad = joined(dv).astype(bf16)
     wk_part = jnp.einsum("ka,kb->ab", hits_in, keys_grad, preferred_element_type=f32)

time: 252 us -> 359 us (1.42)
  Pallas kernels: 72.9 us -> 173 us
  waiting for transfers between devices: 83.7 us -> 101 us
  starting transfers between devices: 16.6 us -> 7.01 us
    pallas_call x2, Pallas kernels: 72.9 us -> 173 us  [the longest x1 95.8 us: _backward(): pl.pallas_call(functools.partial(_bwd_kernel, scale=scale), grid_spec=gri...]
    psum x1, waiting for transfers between devices: 52.1 us -> 65.6 us  [on_device(): lax.psum((joined(dq_r).astype(bf16), wk_part.astype(bf16), wv_part.astype...]
    ppermute x9, starting transfers between devices: 11.8 us -> 6.56 us  [on_device(): lax.ppermute((lax.dynamic_slice_in_dim(numer, (1 - bit) * half, half, 0),...]
    ppermute x6, starting transfers between devices: 4.74 us -> 0.42 us  [on_device(): other = lax.ppermute(gathered, 'region', pairs)]
  transfers between devices with their start and end apart: 16 -> 16, of which waited for: 7 -> 7; matrix products, arithmetic and copies ran while one was open for 15% -> 11% of each run, Pallas kernels for 18% -> 27%
where the time goes in v6:
time: 359 us
  Pallas kernels  173 us (48%)
  waiting for transfers between devices  101 us (28%)
  local copies, waits for them, and re-layouts  33.7 us (9%)
  matrix products  18.3 us (5%)
  between operations  14.5 us (4%)
  other arithmetic  11.4 us (3%)
  starting transfers between devices  7.01 us (2%)
    pallas_call x1, Pallas kernels, _backward(): pl.pallas_call(functools.partial(_bwd_kernel, scale=scale), grid_spec=gri...  95.8 us
    pallas_call x1, Pallas kernels, _forward(): pl.pallas_call(functools.partial(_fwd_kernel, scale=scale), grid_spec=gri...  77.4 us
    psum x1, waiting for transfers between devices, on_device(): lax.psum((joined(dq_r).astype(bf16), wk_part.astype(bf16), wv_part.astype...  65.6 us
    ppermute x9, waiting for transfers between devices, on_device(): lax.ppermute((lax.dynamic_slice_in_dim(numer, (1 - bit) * half, half, 0),...  23.6 us
    ppermute x6, waiting for transfers between devices, on_device(): other = lax.ppermute(gathered, 'region', pairs)  11.9 us
    reshape x4, local copies, waits for them, and re-layouts, heads(): return x.reshape(x.shape[0], HEADS, head_dim).transpose(1, 0, 2)  7.3 us
  transfers between devices with their start and end apart: 16, of which 7 were waited for; matrix products, arithmetic and copies ran while one was open for 11% of the time, Pallas kernels for 27%

profile of v6, /device:TPU:0, one launch (start us, length us, event | category | flops | bytes accessed | tf_op | source)
XLA Modules:
  0.0 359.1 jit_solution(11715765536016544517)
XLA Ops:
  9.0 2.1 convolution_convert_fusion.3
  11.1 1.8 copy.44
  13.7 1.9 copy.45
  16.3 1.8 copy.46
  18.8 77.4 %shard_map.135 = (f32[8,1024,64]{2,1,0:T(8,128)}, f32[8,1024,1]{2,1,0:T(8,128)}, f32[8,1024,1]{2,1,0:T(8,128)}) custom-call(s32[32]{0:T(128)} %reshape.99.need_ref, bf16[8,1024,64]{2,1,0:T(8,128)(2,1)} %bitcast.102, bf16[8,1024,64]{2,1,0:T(8,128)(2,1)} %bitcast.104, bf16[8,1024,64]{2,1,0:T(8,128)(2,1)} %bitcast.106, f32[8,1,1024]{2,1,0:T(1,128)} %bitcast.121), custom_call_target="tpu_custom_call" | custom-call | tf_op jit(solution)/shard_map/pallas_call | solution.py:115
  96.2 2.8 copy.47
  100.1 3.5 dynamic-slice_reduce_fusion.3
  106.8 2.0 collective-permute-start.7
  108.8 1.5 fusion.2
  111.3 2.2 collective-permute-start.4
  113.6 10.5 %collective-permute-done.3 = f32[256,512]{0,1:T(8,128)S(1)} collective-permute-done((f32[256,512]{0,1:T(8,128)S(1)}, f32[256,512]{0,1:T(8,128)S(1)}, u32[]{:S(2)}, u32[]{:S(2)}) %collective-permute-start.3) | collective-permute-done | bytes 524320 | tf_op jit(solution)/shard_map/ppermute | solution.py:206
  125.7 12.0 %collective-permute-done.5 = f32[128,512]{0,1:T(8,128)S(1)} collective-permute-done((f32[128,512]{0,1:T(8,128)S(1)}, f32[128,512]{0,1:T(8,128)S(1)}, u32[]{:S(2)}, u32[]{:S(2)}) %collective-permute-start.5) | collective-permute-done | bytes 262176 | tf_op jit(solution)/shard_map/ppermute | solution.py:206
  137.9 4.5 %collective-permute-done.12 = f32[16,128]{1,0:T(8,128)S(1)} collective-permute-done((f32[16,128]{1,0:T(8,128)S(1)}, f32[16,128]{1,0:T(8,128)S(1)}, u32[]{:S(2)}, u32[]{:S(2)}) %collective-permute-start.12) | collective-permute-done | bytes 8224 | tf_op jit(solution)/shard_map/ppermute | solution.py:240
  142.5 3.7 %collective-permute-done.13 = f32[16,256]{1,0:T(8,128)S(1)} collective-permute-done((f32[16,256]{1,0:T(8,128)S(1)}, f32[16,256]{1,0:T(8,128)S(1)}, u32[]{:S(2)}, u32[]{:S(2)}) %collective-permute-start.13) | collective-permute-done | bytes 16416 | tf_op jit(solution)/shard_map/ppermute | solution.py:240
  146.3 1.8 copy.48
  148.2 2.7 copy.49.lt_ref
  150.9 2.7 copy.50.dl_ref
  153.5 95.8 %shard_map.136 = (f32[8,1024,64]{2,1,0:T(8,128)}, f32[8,1024,64]{2,1,0:T(8,128)}, f32[8,1024,64]{2,1,0:T(8,128)}) custom-call(s32[32]{0:T(128)} %reshape.99.need_ref, bf16[8,1024,64]{2,1,0:T(8,128)(2,1)} %bitcast.103, bf16[8,1024,64]{2,1,0:T(8,128)(2,1)} %bitcast.105, bf16[8,1024,64]{2,1,0:T(8,128)(2,1)} %bitcast.107, bf16[8,1024,64]{2,1,0:T(8,128)(2,1)} %bitcast.110, ...), custom_call_target="tpu_custom_call" | custom-call | tf_op jit(solution)/shard_map/pallas_call | solution.py:150
  249.3 5.5 %convert_bitcast_fusion = (bf16[1024,8,64]{2,0,1:T(8,128)(2,1)}, bf16[1024,8,64]{2,0,1:T(8,128)(2,1)S(1)}) fusion(f32[8,1024,64]{2,1,0:T(8,128)} %get-tuple-element.18, f32[8,1024,64]{2,1,0:T(8,128)} %get-tuple-element.17), kind=kLoop, calls=%fused_computation.1 | loop fusion | flops 1048576 | bytes 6291456 | tf_op jit(solution)/shard_map/convert_element_type | solution.py:258
  254.8 1.6 copy.52
  256.4 2.6 convert_bitcast_fusion.2
  259.0 1.5 fusion
  260.5 2.7 copy.53
  263.2 1.6 copy.51
  265.0 2.7 fusion.1
  267.7 3.6 %collective-permute-done.10 = bf16[256,512]{0,1:T(8,128)(2,1)S(1)} collective-permute-done((bf16[256,512]{0,1:T(8,128)(2,1)S(1)}, bf16[256,512]{0,1:T(8,128)(2,1)S(1)}, u32[]{:S(2)}, u32[]{:S(2)}) %collective-permute-start.10) | collective-permute-done | bytes 262176 | tf_op jit(solution)/shard_map/ppermute | solution.py:240
  272.8 1.7 add_convert_fusion
  275.8 1.7 fusion.3
  277.5 1.7 add_convert_fusion.2
  279.2 65.6 %all-reduce.3.cloned.1.call-done = (bf16[512,512]{0,1:T(8,128)(2,1)}, bf16[512,512]{0,1:T(8,128)(2,1)}, bf16[1024,512]{0,1:T(8,128)(2,1)}) async-done(((bf16[512,512]{0,1:T(8,128)(2,1)}, bf16[512,512]{0,1:T(8,128)(2,1)}, bf16[1024,512]{0,1:T(8,128)(2,1)}), (bf16[512,512]{0,1:T(8,128)(2,1)}, bf16[512,512]{0,1:T(8,128)(2,1)}, bf16[1024,512]{0,1:T(8,128)(2,1)})) %all-reduce.3.cloned.1.call-update) | async-done | bytes 2097168 | tf_op jit(solution)/shard_map/psum | solution.py:261
  344.8 2.1 convolution_bitcast_fusion
  346.9 1.7 add_convert_fusion.1
  (105 shorter events, 17.6 us)
Async XLA Ops:
  7.2 5.7 %copy-start = (bf16[1024,512]{1,0:T(8,128)(2,1)S(1)}, bf16[1024,512]{1,0:T(8,128)(2,1)}, u32[]{:S(2)}) copy-start(bf16[1024,512]{1,0:T(8,128)(2,1)} %param.9) | copy-start | bytes 3145732
  7.2 337.6 %all-reduce.3.cloned.1.call-start = ((), (), s32[]{:S(2)}) async-start(), calls=%async_computation | async-start | bytes 4194304 | tf_op jit(solution)/shard_map/psum | solution.py:261
  11.1 1.8 copy-start.5
  13.7 1.9 copy-start.7
  100.1 8.7 %collective-permute-start.1 = (f32[512,512]{0,1:T(8,128)}, f32[512,512]{0,1:T(8,128)}, u32[]{:S(2)}, u32[]{:S(2)}) collective-permute-start(f32[512,512]{0,1:T(8,128)} %constant_dynamic-slice_fusion.8), channel_id=1, source_target_pairs={{0,1},{1,0},{2,3},{3,2},{4,5},{5,4},{6,7},{7,6},{8,9},{9,8},{10,11... | collective-permute-start | bytes 3145736 | tf_op jit(solution)/shard_map/ppermute | solution.py:206
  100.1 4.1 %copy-start.3 = (f32[8,1024,1]{2,1,0:T(8,128)S(1)}, f32[8,1024,1]{2,1,0:T(8,128)}, u32[]{:S(2)}) copy-start(f32[8,1024,1]{2,1,0:T(8,128)} %get-tuple-element.15) | copy-start | bytes 98308
  103.7 1.8 collective-permute-start
  105.4 1.2 collective-permute-start.6
  106.7 3.9 %collective-permute-start.2 = (f32[8,256]{1,0:T(8,128)S(1)}, f32[8,256]{1,0:T(8,128)S(1)}, u32[]{:S(2)}, u32[]{:S(2)}) collective-permute-start(f32[8,256]{1,0:T(8,128)S(1)} %constant_dynamic-slice_fusion.7), channel_id=1, source_target_pairs={{0,2},{1,3},{2,0},{3,1},{4,6},{5,7},{6,4},{7,5},{8,10},{9,11},{10,... | collective-permute-start | bytes 24584 | tf_op jit(solution)/shard_map/ppermute | solution.py:206
  106.8 3.8 %collective-permute-start.7 = (f32[8,256]{1,0:T(8,128)S(1)}, f32[8,256]{1,0:T(8,128)S(1)}, u32[]{:S(2)}, u32[]{:S(2)}) collective-permute-start(f32[8,256]{1,0:T(8,128)S(1)} %constant_dynamic-slice_fusion.2), channel_id=1, source_target_pairs={{0,2},{1,3},{2,0},{3,1},{4,6},{5,7},{6,4},{7,5},{8,10},{9,11},{10,... | collective-permute-start | bytes 24584 | tf_op jit(solution)/shard_map/ppermute | solution.py:206
  110.3 14.6 %copy-start.12 = (bf16[1024,512]{1,0:T(8,128)(2,1)S(1)}, bf16[1024,512]{1,0:T(8,128)(2,1)}, u32[]{:S(2)}) copy-start(bf16[1024,512]{1,0:T(8,128)(2,1)} %param.15) | copy-start | bytes 3145732
  110.3 14.6 %copy-start.16 = (bf16[512,512]{1,0:T(8,128)(2,1)S(1)}, bf16[512,512]{1,0:T(8,128)(2,1)}, u32[]{:S(2)}) copy-start(bf16[512,512]{1,0:T(8,128)(2,1)} %param.13) | copy-start | bytes 1572868
  110.4 13.7 %collective-permute-start.3 = (f32[256,512]{0,1:T(8,128)S(1)}, f32[256,512]{0,1:T(8,128)S(1)}, u32[]{:S(2)}, u32[]{:S(2)}) collective-permute-start(f32[256,512]{0,1:T(8,128)S(1)} %constant_dynamic-slice_fusion.6), channel_id=1, source_target_pairs={{0,2},{1,3},{2,0},{3,1},{4,6},{5,7},{6,4},{7,5},{8,10},{9,11},{10,... | collective-permute-start | bytes 1572872 | tf_op jit(solution)/shard_map/ppermute | solution.py:206
  110.6 15.1 %collective-permute-start.8 = (f32[8,128]{1,0:T(8,128)S(1)}, f32[8,128]{1,0:T(8,128)S(1)}, u32[]{:S(2)}, u32[]{:S(2)}) collective-permute-start(f32[8,128]{1,0:T(8,128)S(1)} %constant_dynamic-slice_fusion), channel_id=1, source_target_pairs={{0,4},{1,5},{2,6},{3,7},{4,0},{5,1},{6,2},{7,3},{8,12},{9,13},{10,... | collective-permute-start | bytes 12296 | tf_op jit(solution)/shard_map/ppermute | solution.py:206
  111.3 14.3 %collective-permute-start.4 = (f32[8,128]{1,0:T(8,128)S(1)}, f32[8,128]{1,0:T(8,128)S(1)}, u32[]{:S(2)}, u32[]{:S(2)}) collective-permute-start(f32[8,128]{1,0:T(8,128)S(1)} %constant_dynamic-slice_fusion.4), channel_id=1, source_target_pairs={{0,4},{1,5},{2,6},{3,7},{4,0},{5,1},{6,2},{7,3},{8,12},{9,13},{10,... | collective-permute-start | bytes 12296 | tf_op jit(solution)/shard_map/ppermute | solution.py:206
  124.2 13.5 %collective-permute-start.5 = (f32[128,512]{0,1:T(8,128)S(1)}, f32[128,512]{0,1:T(8,128)S(1)}, u32[]{:S(2)}, u32[]{:S(2)}) collective-permute-start(f32[128,512]{0,1:T(8,128)S(1)} %constant_dynamic-slice_fusion.3), channel_id=1, source_target_pairs={{0,4},{1,5},{2,6},{3,7},{4,0},{5,1},{6,2},{7,3},{8,12},{9,13},{10,... | collective-permute-start | bytes 786440 | tf_op jit(solution)/shard_map/ppermute | solution.py:206
  137.8 4.6 %collective-permute-start.12 = (f32[16,128]{1,0:T(8,128)S(1)}, f32[16,128]{1,0:T(8,128)S(1)}, u32[]{:S(2)}, u32[]{:S(2)}) collective-permute-start(f32[16,128]{1,0:T(8,128)S(1)} %pad_maximum_fusion.8), channel_id=1, source_target_pairs={{0,4},{1,5},{2,6},{3,7},{4,0},{5,1},{6,2},{7,3},{8,12},{9,13},{10,... | collective-permute-start | bytes 24584 | tf_op jit(solution)/shard_map/ppermute | solution.py:240
  142.4 3.8 %collective-permute-start.13 = (f32[16,256]{1,0:T(8,128)S(1)}, f32[16,256]{1,0:T(8,128)S(1)}, u32[]{:S(2)}, u32[]{:S(2)}) collective-permute-start(f32[16,256]{1,0:T(8,128)S(1)} %pad_maximum_fusion.7), channel_id=1, source_target_pairs={{0,2},{1,3},{2,0},{3,1},{4,6},{5,7},{6,4},{7,5},{8,10},{9,11},{10,... | collective-permute-start | bytes 49160 | tf_op jit(solution)/shard_map/ppermute | solution.py:240
  146.2 2.0 collective-permute-start.14
  148.1 116.7 %collective-permute-start.9 = (bf16[128,512]{0,1:T(8,128)(2,1)S(1)}, bf16[128,512]{0,1:T(8,128)(2,1)S(1)}, u32[]{:S(2)}, u32[]{:S(2)}) collective-permute-start(bf16[128,512]{0,1:T(8,128)(2,1)S(1)} %get-tuple-element.55), channel_id=1, source_target_pairs={{0,4},{1,5},{2,6},{3,7},{4,0},{5,1},{6,2},{7,3},{8,12},{9,13},{10,... | collective-permute-start | bytes 393224 | tf_op jit(solution)/shard_map/ppermute | solution.py:240
  256.4 2.6 copy-start.1
  264.9 6.4 %collective-permute-start.10 = (bf16[256,512]{0,1:T(8,128)(2,1)S(1)}, bf16[256,512]{0,1:T(8,128)(2,1)S(1)}, u32[]{:S(2)}, u32[]{:S(2)}) collective-permute-start(bf16[256,512]{0,1:T(8,128)(2,1)S(1)} %pad_maximum_fusion.4), channel_id=1, source_target_pairs={{0,2},{1,3},{2,0},{3,1},{4,6},{5,7},{6,4},{7,5},{8,10},{9,11},{10,... | collective-permute-start | bytes 786440 | tf_op jit(solution)/shard_map/ppermute | solution.py:240
  267.7 3.9 %copy-start.2 = (bf16[1024,8,64]{0,2,1:T(8,128)(2,1)S(1)}, bf16[1024,8,64]{0,2,1:T(8,128)(2,1)}, u32[]{:S(2)}) copy-start(bf16[1024,8,64]{0,2,1:T(8,128)(2,1)} %copy.52) | copy-start | bytes 3145732
  267.7 3.9 %copy-start.6 = (bf16[512,512]{1,0:T(8,128)(2,1)S(1)}, bf16[512,512]{1,0:T(8,128)(2,1)}, u32[]{:S(2)}) copy-start(bf16[512,512]{1,0:T(8,128)(2,1)} %param.11) | copy-start | bytes 1572868
  271.5 3.1 collective-permute-start.11
  274.8 2.7 copy-start.11
  274.8 2.7 copy-start.17
  344.8 2.1 copy-start.14
  344.8 2.1 copy-start.15
  344.8 2.1 copy-start.18
  346.9 3.1 copy-start.10
  348.6 2.5 copy-start.9
  (3 other events, 3.8 us)
Sparse Core Ops, SparseCore 0:
  267.8 76.8 all-reduce.2

commit v7 on v5

--- a/solution.py
+++ b/solution.py
@@ -10,7 +10,7 @@
 
 HEADS = 8
 BLOCK = 128
-TQ = 256
+TQ = 512
 
 
 def _fwd_kernel(q_ref, k_ref, v_ref, cm_ref, numer_ref, m_ref, l_ref, *, scale):

time: 252 us -> 237 us (0.940)
  Pallas kernels: 72.9 us -> 59.2 us
    pallas_call x1, Pallas kernels: 44.1 us -> 31.2 us  [_backward(): pl.pallas_call(functools.partial(_bwd_kernel, scale=scale), grid=(heads,...]
  transfers between devices with their start and end apart: 16 -> 16, of which waited for: 7 -> 7; matrix products, arithmetic and copies ran while one was open for 15% -> 16% of each run, Pallas kernels for 18% -> 13%
where the time goes in v7:
time: 237 us
  waiting for transfers between devices  83.8 us (35%)
  Pallas kernels  59.2 us (25%)
  local copies, waits for them, and re-layouts  33.2 us (14%)
  matrix products  18.3 us (8%)
  starting transfers between devices  16.6 us (7%)
  between operations  14.5 us (6%)
  other arithmetic  11.4 us (5%)
    psum x1, waiting for transfers between devices, on_device(): lax.psum((joined(dq_r).astype(bf16), wk_part.astype(bf16), wv_part.astype...  52.2 us
    pallas_call x1, Pallas kernels, _backward(): pl.pallas_call(functools.partial(_bwd_kernel, scale=scale), grid=(heads,...  31.2 us
    pallas_call x1, Pallas kernels, _forward(): pl.pallas_call(functools.partial(_fwd_kernel, scale=scale), grid=(heads,...  28 us
    ppermute x9, waiting for transfers between devices, on_device(): lax.ppermute((lax.dynamic_slice_in_dim(numer, (1 - bit) * half, half, 0),...  20.1 us
    ppermute x9, starting transfers between devices, on_device(): lax.ppermute((lax.dynamic_slice_in_dim(numer, (1 - bit) * half, half, 0),...  11.8 us
    ppermute x6, waiting for transfers between devices, on_device(): other = lax.ppermute(gathered, 'region', pairs)  11.4 us
    reshape x4, local copies, waits for them, and re-layouts, heads(): return x.reshape(x.shape[0], HEADS, head_dim).transpose(1, 0, 2)  7.33 us
    convert_element_type x1, other arithmetic, on_device(): vals_grad = joined(dv).astype(bf16)  5.5 us
  transfers between devices with their start and end apart: 16, of which 7 were waited for; matrix products, arithmetic and copies ran while one was open for 16% of the time, Pallas kernels for 13%

profile of v7, /device:TPU:0, one launch (start us, length us, event | category | flops | bytes accessed | tf_op | source)
XLA Modules:
  0.0 236.9 jit_solution(6902999920499356116)
XLA Ops:
  8.3 2.1 convolution_convert_fusion.3
  10.4 1.8 copy.44
  13.0 1.9 copy.45
  15.7 1.8 copy.46
  18.2 28.0 %shard_map.135 = (f32[8,1024,64]{2,1,0:T(8,128)}, f32[8,1024,1]{2,1,0:T(8,128)}, f32[8,1024,1]{2,1,0:T(8,128)}) custom-call(bf16[8,1024,64]{2,1,0:T(8,128)(2,1)} %bitcast.102, bf16[8,1024,64]{2,1,0:T(8,128)(2,1)} %bitcast.104, bf16[8,1024,64]{2,1,0:T(8,128)(2,1)} %bitcast.106, f32[8,1,1024]{2,1,0:T(1,128)} %bitcast.121), custom_call_target="tpu_custom_call" | custom-call | tf_op jit(solution)/shard_map/pallas_call | solution.py:72
  46.2 2.8 %copy.47 = f32[1024,8,64]{0,2,1:T(8,128)S(1)} copy(f32[1024,8,64]{2,0,1:T(8,128)} %bitcast.114) | data formatting | bytes 4194304 | tf_op jit(solution)/shard_map/transpose | solution.py:143
  50.6 3.5 %dynamic-slice_reduce_fusion.3 = (f32[8,512]{1,0:T(8,128)S(1)}, f32[8,512]{1,0:T(8,128)S(1)}) fusion(f32[8,1024,1]{2,1,0:T(8,128)} %get-tuple-element.14, s32[]{:T(128)S(6)} %select_n.108, s32[]{:T(128)S(6)} %select_n.109), kind=kLoop, calls=%fused_computation.9 | loop fusion | bytes 65544 | tf_op jit(solution)/shard_map/dynamic_slice | solution.py:165
  56.8 3.0 %collective-permute-start.2 = (f32[8,256]{1,0:T(8,128)S(1)}, f32[8,256]{1,0:T(8,128)S(1)}, u32[]{:S(2)}, u32[]{:S(2)}) collective-permute-start(f32[8,256]{1,0:T(8,128)S(1)} %constant_dynamic-slice_fusion.7), channel_id=1, source_target_pairs={{0,2},{1,3},{2,0},{3,1},{4,6},{5,7},{6,4},{7,5},{8,10},{9,11},{10,... | collective-permute-start | bytes 24584 | tf_op jit(solution)/shard_map/ppermute | solution.py:168
  61.5 2.0 collective-permute-start.3
  63.5 2.6 %collective-permute-start.8 = (f32[8,128]{1,0:T(8,128)S(1)}, f32[8,128]{1,0:T(8,128)S(1)}, u32[]{:S(2)}, u32[]{:S(2)}) collective-permute-start(f32[8,128]{1,0:T(8,128)S(1)} %constant_dynamic-slice_fusion), channel_id=1, source_target_pairs={{0,4},{1,5},{2,6},{3,7},{4,0},{5,1},{6,2},{7,3},{8,12},{9,13},{10,... | collective-permute-start | bytes 12296 | tf_op jit(solution)/shard_map/ppermute | solution.py:168
  66.5 8.9 %collective-permute-done.3 = f32[256,512]{0,1:T(8,128)S(1)} collective-permute-done((f32[256,512]{0,1:T(8,128)S(1)}, f32[256,512]{0,1:T(8,128)S(1)}, u32[]{:S(2)}, u32[]{:S(2)}) %collective-permute-start.3) | collective-permute-done | bytes 524320 | tf_op jit(solution)/shard_map/ppermute | solution.py:168
  75.6 2.6 %collective-permute-start.5 = (f32[128,512]{0,1:T(8,128)S(1)}, f32[128,512]{0,1:T(8,128)S(1)}, u32[]{:S(2)}, u32[]{:S(2)}) collective-permute-start(f32[128,512]{0,1:T(8,128)S(1)} %constant_dynamic-slice_fusion.3), channel_id=1, source_target_pairs={{0,4},{1,5},{2,6},{3,7},{4,0},{5,1},{6,2},{7,3},{8,12},{9,13},{10,... | collective-permute-start | bytes 786440 | tf_op jit(solution)/shard_map/ppermute | solution.py:168
  79.0 10.4 %collective-permute-done.5 = f32[128,512]{0,1:T(8,128)S(1)} collective-permute-done((f32[128,512]{0,1:T(8,128)S(1)}, f32[128,512]{0,1:T(8,128)S(1)}, u32[]{:S(2)}, u32[]{:S(2)}) %collective-permute-start.5) | collective-permute-done | bytes 262176 | tf_op jit(solution)/shard_map/ppermute | solution.py:168
  89.6 4.5 %collective-permute-done.12 = f32[16,128]{1,0:T(8,128)S(1)} collective-permute-done((f32[16,128]{1,0:T(8,128)S(1)}, f32[16,128]{1,0:T(8,128)S(1)}, u32[]{:S(2)}, u32[]{:S(2)}) %collective-permute-start.12) | collective-permute-done | bytes 8224 | tf_op jit(solution)/shard_map/ppermute | solution.py:202
  95.0 3.0 %collective-permute-done.13 = f32[16,256]{1,0:T(8,128)S(1)} collective-permute-done((f32[16,256]{1,0:T(8,128)S(1)}, f32[16,256]{1,0:T(8,128)S(1)}, u32[]{:S(2)}, u32[]{:S(2)}) %collective-permute-start.13) | collective-permute-done | bytes 16416 | tf_op jit(solution)/shard_map/ppermute | solution.py:202
  98.0 1.8 copy.48
  99.9 1.7 collective-permute-start.9
  101.5 2.7 %copy.49.lt_ref = f32[8,1024,1]{2,1,0:T(8,128)} copy(f32[8,1024,1]{1,0,2:T(8,128)S(1)} %get-tuple-element.67) | data formatting | bytes 65536 | tf_op jit(solution)/shard_map/reshape | solution.py:210
  104.2 2.7 %copy.50.dl_ref = f32[8,1024,1]{2,1,0:T(8,128)} copy(f32[8,1024,1]{1,0,2:T(8,128)S(1)} %get-tuple-element.66) | data formatting | bytes 65536 | tf_op jit(solution)/shard_map/reshape | solution.py:211
  106.9 31.2 %shard_map.136 = (f32[8,1024,64]{2,1,0:T(8,128)}, f32[8,1024,64]{2,1,0:T(8,128)}, f32[8,1024,64]{2,1,0:T(8,128)}) custom-call(bf16[8,1024,64]{2,1,0:T(8,128)(2,1)} %bitcast.103, bf16[8,1024,64]{2,1,0:T(8,128)(2,1)} %bitcast.105, bf16[8,1024,64]{2,1,0:T(8,128)(2,1)} %bitcast.107, bf16[8,1024,64]{2,1,0:T(8,128)(2,1)} %bitcast.110, f32[8,1024,1]{2,1,0:T(8,128)} %copy.49.lt_ref, ...), custom_call_target="tpu_custom_call" | custom-call | tf_op jit(solution)/shard_map/pallas_call | solution.py:99
  138.1 5.5 %convert_bitcast_fusion = (bf16[1024,8,64]{2,0,1:T(8,128)(2,1)}, bf16[1024,8,64]{2,0,1:T(8,128)(2,1)S(1)}) fusion(f32[8,1024,64]{2,1,0:T(8,128)} %get-tuple-element.18, f32[8,1024,64]{2,1,0:T(8,128)} %get-tuple-element.17), kind=kLoop, calls=%fused_computation.1 | loop fusion | flops 1048576 | bytes 6291456 | tf_op jit(solution)/shard_map/convert_element_type | solution.py:220
  145.2 2.6 %convert_bitcast_fusion.2 = bf16[1024,8,64]{2,0,1:T(8,128)(2,1)S(1)} fusion(f32[8,1024,64]{2,1,0:T(8,128)} %get-tuple-element.16), kind=kLoop, calls=%fused_computation.4 | loop fusion | flops 524288 | bytes 3145728 | tf_op jit(solution)/shard_map/convert_element_type | solution.py:224
  149.3 2.7 %copy.53 = bf16[1024,8,64]{0,2,1:T(8,128)(2,1)} copy(bf16[1024,8,64]{2,0,1:T(8,128)(2,1)} %get-tuple-element.82) | data formatting | bytes 2097152 | tf_op jit(solution)/shard_map/convert_element_type | solution.py:220
  153.7 2.1 collective-permute-start.10
  155.8 2.7 %fusion.1 = bf16[512,512]{0,1:T(8,128)(2,1)} fusion(bf16[1024,512]{0,1:T(8,128)(2,1)} %bitcast.115, bf16[1024,512]{1,0:T(8,128)(2,1)S(1)} %copy-done), kind=kOutput, calls=%fused_computation.18 | convolution fusion | flops 537133056 | bytes 2621440 | tf_op jit(solution)/shard_map/ka,kb->ab/dot_general | solution.py:222
  158.5 3.9 %collective-permute-done.10 = bf16[256,512]{0,1:T(8,128)(2,1)S(1)} collective-permute-done((bf16[256,512]{0,1:T(8,128)(2,1)S(1)}, bf16[256,512]{0,1:T(8,128)(2,1)S(1)}, u32[]{:S(2)}, u32[]{:S(2)}) %collective-permute-start.10) | collective-permute-done | bytes 262176 | tf_op jit(solution)/shard_map/ppermute | solution.py:202
  164.0 1.7 add_convert_fusion
  166.9 1.7 fusion.3
  168.6 1.7 add_convert_fusion.2
  170.3 52.2 %all-reduce.3.cloned.1.call-done = (bf16[512,512]{0,1:T(8,128)(2,1)}, bf16[512,512]{0,1:T(8,128)(2,1)}, bf16[1024,512]{0,1:T(8,128)(2,1)}) async-done(((bf16[512,512]{0,1:T(8,128)(2,1)}, bf16[512,512]{0,1:T(8,128)(2,1)}, bf16[1024,512]{0,1:T(8,128)(2,1)}), (bf16[512,512]{0,1:T(8,128)(2,1)}, bf16[512,512]{0,1:T(8,128)(2,1)}, bf16[1024,512]{0,1:T(8,128)(2,1)})) %all-reduce.3.cloned.1.call-update) | async-done | bytes 2097168 | tf_op jit(solution)/shard_map/psum | solution.py:223
  222.5 2.1 convolution_bitcast_fusion
  224.7 1.7 add_convert_fusion.1
  (101 shorter events, 22.7 us)
Async XLA Ops:
  7.2 5.1 %copy-start = (bf16[1024,512]{1,0:T(8,128)(2,1)S(1)}, bf16[1024,512]{1,0:T(8,128)(2,1)}, u32[]{:S(2)}) copy-start(bf16[1024,512]{1,0:T(8,128)(2,1)} %param.9) | copy-start | bytes 3145732
  7.2 215.4 %all-reduce.3.cloned.1.call-start = ((), (), s32[]{:S(2)}) async-start(), calls=%async_computation | async-start | bytes 4194304 | tf_op jit(solution)/shard_map/psum | solution.py:223
  10.4 1.8 copy-start.5
  13.0 1.9 copy-start.7
  50.1 9.8 %collective-permute-start.1 = (f32[512,512]{0,1:T(8,128)}, f32[512,512]{0,1:T(8,128)}, u32[]{:S(2)}, u32[]{:S(2)}) collective-permute-start(f32[512,512]{0,1:T(8,128)} %constant_dynamic-slice_fusion.8), channel_id=1, source_target_pairs={{0,1},{1,0},{2,3},{3,2},{4,5},{5,4},{6,7},{7,6},{8,9},{9,8},{10,11... | collective-permute-start | bytes 3145736 | tf_op jit(solution)/shard_map/ppermute | solution.py:168
  50.6 3.6 %copy-start.3 = (f32[8,1024,1]{2,1,0:T(8,128)S(1)}, f32[8,1024,1]{2,1,0:T(8,128)}, u32[]{:S(2)}) copy-start(f32[8,1024,1]{2,1,0:T(8,128)} %get-tuple-element.15) | copy-start | bytes 98308
  54.1 1.8 collective-permute-start
  55.4 1.4 collective-permute-start.6
  56.8 6.7 %collective-permute-start.2 = (f32[8,256]{1,0:T(8,128)S(1)}, f32[8,256]{1,0:T(8,128)S(1)}, u32[]{:S(2)}, u32[]{:S(2)}) collective-permute-start(f32[8,256]{1,0:T(8,128)S(1)} %constant_dynamic-slice_fusion.7), channel_id=1, source_target_pairs={{0,2},{1,3},{2,0},{3,1},{4,6},{5,7},{6,4},{7,5},{8,10},{9,11},{10,... | collective-permute-start | bytes 24584 | tf_op jit(solution)/shard_map/ppermute | solution.py:168
  59.8 3.7 %collective-permute-start.7 = (f32[8,256]{1,0:T(8,128)S(1)}, f32[8,256]{1,0:T(8,128)S(1)}, u32[]{:S(2)}, u32[]{:S(2)}) collective-permute-start(f32[8,256]{1,0:T(8,128)S(1)} %constant_dynamic-slice_fusion.2), channel_id=1, source_target_pairs={{0,2},{1,3},{2,0},{3,1},{4,6},{5,7},{6,4},{7,5},{8,10},{9,11},{10,... | collective-permute-start | bytes 24584 | tf_op jit(solution)/shard_map/ppermute | solution.py:168
  61.4 16.8 %copy-start.12 = (bf16[1024,512]{1,0:T(8,128)(2,1)S(1)}, bf16[1024,512]{1,0:T(8,128)(2,1)}, u32[]{:S(2)}) copy-start(bf16[1024,512]{1,0:T(8,128)(2,1)} %param.15) | copy-start | bytes 3145732
  61.4 16.8 %copy-start.16 = (bf16[512,512]{1,0:T(8,128)(2,1)S(1)}, bf16[512,512]{1,0:T(8,128)(2,1)}, u32[]{:S(2)}) copy-start(bf16[512,512]{1,0:T(8,128)(2,1)} %param.13) | copy-start | bytes 1572868
  61.5 14.0 %collective-permute-start.3 = (f32[256,512]{0,1:T(8,128)S(1)}, f32[256,512]{0,1:T(8,128)S(1)}, u32[]{:S(2)}, u32[]{:S(2)}) collective-permute-start(f32[256,512]{0,1:T(8,128)S(1)} %constant_dynamic-slice_fusion.6), channel_id=1, source_target_pairs={{0,2},{1,3},{2,0},{3,1},{4,6},{5,7},{6,4},{7,5},{8,10},{9,11},{10,... | collective-permute-start | bytes 1572872 | tf_op jit(solution)/shard_map/ppermute | solution.py:168
  63.5 15.5 %collective-permute-start.8 = (f32[8,128]{1,0:T(8,128)S(1)}, f32[8,128]{1,0:T(8,128)S(1)}, u32[]{:S(2)}, u32[]{:S(2)}) collective-permute-start(f32[8,128]{1,0:T(8,128)S(1)} %constant_dynamic-slice_fusion), channel_id=1, source_target_pairs={{0,4},{1,5},{2,6},{3,7},{4,0},{5,1},{6,2},{7,3},{8,12},{9,13},{10,... | collective-permute-start | bytes 12296 | tf_op jit(solution)/shard_map/ppermute | solution.py:168
  66.2 12.8 %collective-permute-start.4 = (f32[8,128]{1,0:T(8,128)S(1)}, f32[8,128]{1,0:T(8,128)S(1)}, u32[]{:S(2)}, u32[]{:S(2)}) collective-permute-start(f32[8,128]{1,0:T(8,128)S(1)} %constant_dynamic-slice_fusion.4), channel_id=1, source_target_pairs={{0,4},{1,5},{2,6},{3,7},{4,0},{5,1},{6,2},{7,3},{8,12},{9,13},{10,... | collective-permute-start | bytes 12296 | tf_op jit(solution)/shard_map/ppermute | solution.py:168
  75.6 13.8 %collective-permute-start.5 = (f32[128,512]{0,1:T(8,128)S(1)}, f32[128,512]{0,1:T(8,128)S(1)}, u32[]{:S(2)}, u32[]{:S(2)}) collective-permute-start(f32[128,512]{0,1:T(8,128)S(1)} %constant_dynamic-slice_fusion.3), channel_id=1, source_target_pairs={{0,4},{1,5},{2,6},{3,7},{4,0},{5,1},{6,2},{7,3},{8,12},{9,13},{10,... | collective-permute-start | bytes 786440 | tf_op jit(solution)/shard_map/ppermute | solution.py:168
  89.5 4.6 %collective-permute-start.12 = (f32[16,128]{1,0:T(8,128)S(1)}, f32[16,128]{1,0:T(8,128)S(1)}, u32[]{:S(2)}, u32[]{:S(2)}) collective-permute-start(f32[16,128]{1,0:T(8,128)S(1)} %pad_maximum_fusion.8), channel_id=1, source_target_pairs={{0,4},{1,5},{2,6},{3,7},{4,0},{5,1},{6,2},{7,3},{8,12},{9,13},{10,... | collective-permute-start | bytes 24584 | tf_op jit(solution)/shard_map/ppermute | solution.py:202
  94.2 3.8 %collective-permute-start.13 = (f32[16,256]{1,0:T(8,128)S(1)}, f32[16,256]{1,0:T(8,128)S(1)}, u32[]{:S(2)}, u32[]{:S(2)}) collective-permute-start(f32[16,256]{1,0:T(8,128)S(1)} %pad_maximum_fusion.7), channel_id=1, source_target_pairs={{0,2},{1,3},{2,0},{3,1},{4,6},{5,7},{6,4},{7,5},{8,10},{9,11},{10,... | collective-permute-start | bytes 49160 | tf_op jit(solution)/shard_map/ppermute | solution.py:202
  98.0 3.5 %collective-permute-start.14 = (f32[16,512]{1,0:T(8,128)S(1)}, f32[16,512]{1,0:T(8,128)S(1)}, u32[]{:S(2)}, u32[]{:S(2)}) collective-permute-start(f32[16,512]{1,0:T(8,128)S(1)} %pad_maximum_fusion.6), channel_id=1, source_target_pairs={{0,1},{1,0},{2,3},{3,2},{4,5},{5,4},{6,7},{7,6},{8,9},{9,8},{10,11... | collective-permute-start | bytes 98312 | tf_op jit(solution)/shard_map/ppermute | solution.py:202
  99.9 53.8 %collective-permute-start.9 = (bf16[128,512]{0,1:T(8,128)(2,1)S(1)}, bf16[128,512]{0,1:T(8,128)(2,1)S(1)}, u32[]{:S(2)}, u32[]{:S(2)}) collective-permute-start(bf16[128,512]{0,1:T(8,128)(2,1)S(1)} %get-tuple-element.55), channel_id=1, source_target_pairs={{0,4},{1,5},{2,6},{3,7},{4,0},{5,1},{6,2},{7,3},{8,12},{9,13},{10,... | collective-permute-start | bytes 393224 | tf_op jit(solution)/shard_map/ppermute | solution.py:202
  145.2 2.6 %copy-start.1 = (bf16[1024,8,64]{0,2,1:T(8,128)(2,1)S(1)}, bf16[1024,8,64]{0,2,1:T(8,128)(2,1)}, u32[]{:S(2)}) copy-start(bf16[1024,8,64]{0,2,1:T(8,128)(2,1)} %copy.52) | copy-start | bytes 3145732
  153.7 8.8 %collective-permute-start.10 = (bf16[256,512]{0,1:T(8,128)(2,1)S(1)}, bf16[256,512]{0,1:T(8,128)(2,1)S(1)}, u32[]{:S(2)}, u32[]{:S(2)}) collective-permute-start(bf16[256,512]{0,1:T(8,128)(2,1)S(1)} %pad_maximum_fusion.4), channel_id=1, source_target_pairs={{0,2},{1,3},{2,0},{3,1},{4,6},{5,7},{6,4},{7,5},{8,10},{9,11},{10,... | collective-permute-start | bytes 786440 | tf_op jit(solution)/shard_map/ppermute | solution.py:202
  158.5 4.2 %copy-start.2 = (bf16[1024,8,64]{0,2,1:T(8,128)(2,1)S(1)}, bf16[1024,8,64]{0,2,1:T(8,128)(2,1)}, u32[]{:S(2)}) copy-start(bf16[1024,8,64]{0,2,1:T(8,128)(2,1)} %copy.52) | copy-start | bytes 3145732
  158.5 4.2 %copy-start.6 = (bf16[512,512]{1,0:T(8,128)(2,1)S(1)}, bf16[512,512]{1,0:T(8,128)(2,1)}, u32[]{:S(2)}) copy-start(bf16[512,512]{1,0:T(8,128)(2,1)} %param.11) | copy-start | bytes 1572868
  162.6 3.1 %collective-permute-start.11 = (bf16[512,512]{0,1:T(8,128)(2,1)S(1)}, bf16[512,512]{0,1:T(8,128)(2,1)S(1)}, u32[]{:S(2)}, u32[]{:S(2)}) collective-permute-start(bf16[512,512]{0,1:T(8,128)(2,1)S(1)} %pad_maximum_fusion.3), channel_id=1, source_target_pairs={{0,1},{1,0},{2,3},{3,2},{4,5},{5,4},{6,7},{7,6},{8,9},{9,8},{10,11... | collective-permute-start | bytes 1572872 | tf_op jit(solution)/shard_map/ppermute | solution.py:202
  165.9 2.7 %copy-start.11 = (bf16[1024,512]{1,0:T(8,128)(2,1)S(1)}, bf16[1024,512]{1,0:T(8,128)(2,1)}, u32[]{:S(2)}) copy-start(bf16[1024,512]{1,0:T(8,128)(2,1)} %param.8) | copy-start | bytes 3145732
  165.9 2.7 %copy-start.17 = (bf16[512,512]{1,0:T(8,128)(2,1)S(1)}, bf16[512,512]{1,0:T(8,128)(2,1)}, u32[]{:S(2)}) copy-start(bf16[512,512]{1,0:T(8,128)(2,1)} %param.13) | copy-start | bytes 1572868
  222.5 2.1 copy-start.14
  222.5 2.1 copy-start.15
  222.5 2.1 copy-start.18
  224.7 3.1 %copy-start.10 = (bf16[512,512]{0,1:T(8,128)(2,1)S(1)}, bf16[512,512]{0,1:T(8,128)(2,1)}, u32[]{:S(2)}) copy-start(bf16[512,512]{0,1:T(8,128)(2,1)} %get-tuple-element.51) | copy-start | bytes 1572868
  226.4 2.5 %copy-start.9 = (bf16[512,512]{0,1:T(8,128)(2,1)S(1)}, bf16[512,512]{0,1:T(8,128)(2,1)}, u32[]{:S(2)}) copy-start(bf16[512,512]{0,1:T(8,128)(2,1)} %get-tuple-element.52) | copy-start | bytes 1572868
  (3 other events, 3.8 us)
Sparse Core Ops, SparseCore 0:
  158.6 63.8 all-reduce.2

commit v8 on v7

--- a/solution.py
+++ b/solution.py
@@ -142,10 +142,12 @@
     def joined(x):
         return x.transpose(1, 0, 2).reshape(x.shape[1], width)
 
-    query = jnp.dot(queries_in, w_query, preferred_element_type=f32).astype(bf16)
-    keys = jnp.dot(hits_in, w_key, preferred_element_type=f32).astype(bf16)
-    vals = jnp.dot(hits_in, w_value, preferred_element_type=f32).astype(bf16)
-    qT, kT, vT = heads(query), heads(keys), heads(vals)
+    def project(x, w):
+        return jnp.einsum(
+            "nd,dhe->hne", x, w.reshape(width, HEADS, head_dim), preferred_element_type=f32
+        ).astype(bf16)
+
+    qT, kT, vT = project(queries_in, w_query), project(hits_in, w_key), project(hits_in, w_value)
 
     regions = lax.axis_size("region")
     numer_r, max_r, total_r = _forward(qT, kT, vT, cm, scale)
@@ -213,13 +215,15 @@
         queries_in.astype(f32) + jnp.dot(attended, w_out, preferred_element_type=f32)
     ).astype(bf16)
     grad_wo = jnp.einsum("qa,qb->ab", attended, grad_out, preferred_element_type=f32)
-    gaT = heads(grad_att)
+    gaT = jnp.einsum(
+        "nd,hed->hne", grad_out, w_out.reshape(HEADS, head_dim, width), preferred_element_type=f32
+    ).astype(bf16)
 
     dq_r, dk, dv = _backward(qT, kT, vT, gaT, log_total, deltas, cm, scale)
-    keys_grad = joined(dk).astype(bf16)
-    vals_grad = joined(dv).astype(bf16)
-    wk_part = jnp.einsum("ka,kb->ab", hits_in, keys_grad, preferred_element_type=f32)
-    wv_part = jnp.einsum("ka,kb->ab", hits_in, vals_grad, preferred_element_type=f32)
+    keys_grad = dk.astype(bf16)
+    vals_grad = dv.astype(bf16)
+    wk_part = jnp.einsum("nd,hne->dhe", hits_in, keys_grad, preferred_element_type=f32).reshape(width, width)
+    wv_part = jnp.einsum("nd,hne->dhe", hits_in, vals_grad, preferred_element_type=f32).reshape(width, width)
     query_grad_sum, grad_wk, grad_wv = lax.psum(
         (joined(dq_r).astype(bf16), wk_part.astype(bf16), wv_part.astype(bf16)), "region"
     )
@@ -232,8 +236,8 @@
         + lax.dot_general(grad_q, w_query, (((1,), (1,)), ((), ())), preferred_element_type=f32)
     ).astype(bf16)
     grad_hits = (
-        lax.dot_general(keys_grad, w_key, (((1,), (1,)), ((), ())), preferred_element_type=f32)
-        + lax.dot_general(vals_grad, w_value, (((1,), (1,)), ((), ())), preferred_element_type=f32)
+        jnp.einsum("hne,dhe->nd", keys_grad, w_key.reshape(width, HEADS, head_dim), preferred_element_type=f32)
+        + jnp.einsum("hne,dhe->nd", vals_grad, w_value.reshape(width, HEADS, head_dim), preferred_element_type=f32)
     ).astype(bf16)
     return (layer_out, grad_queries, grad_hits, grad_wq, grad_wk, grad_wv, grad_wo)
 

time: 237 us -> 248 us (1.046)
  matrix products: 18.3 us -> 26.2 us
  waiting for transfers between devices: 83.8 us -> 88.4 us
  other arithmetic: 11.4 us -> 8.87 us
    dot_general x7 -> x8, matrix products: 10.3 us -> 17.9 us  [the longest x1 4.64 us: on_device(): jnp.einsum('hne,dhe->nd', vals_grad, w_value.reshape(width, HEADS, head_d...]
    reshape x4 -> x0, local copies, waits for them, and re-layouts: 7.33 us -> none  [heads(): return x.reshape(x.shape[0], HEADS, head_dim).transpose(1, 0, 2)]
    convert_element_type x2 -> x6, local copies, waits for them, and re-layouts: 4.29 us -> 11.5 us  [the longest x3 5.5 us: project(): return jnp.einsum('nd,dhe->hne', x, w.reshape(width, HEADS, head_dim), pr...]
    psum x1, waiting for transfers between devices: 52.2 us -> 55.6 us  [on_device(): lax.psum((joined(dq_r).astype(bf16), wk_part.astype(bf16), wv_part.astype...]
    convert_element_type x1 -> x2, other arithmetic: 5.5 us -> 2.2 us  [the longest x1 1.1 us: on_device(): grad_wk = grad_wk.astype(f32)]
    unnamed x41 -> x48, local copies, waits for them, and re-layouts: 5.23 us -> 5.85 us
where the time goes in v8:
time: 248 us; the launch traced here: 247 us
  waiting for transfers between devices  88.4 us (36%)
  Pallas kernels  59.4 us (24%)
  local copies, waits for them, and re-layouts  33.6 us (14%)
  matrix products  26.2 us (11%)
  starting transfers between devices  16.6 us (7%)
  between operations  14.5 us (6%)
  other arithmetic  8.87 us (4%)
    psum x1, waiting for transfers between devices, on_device(): lax.psum((joined(dq_r).astype(bf16), wk_part.astype(bf16), wv_part.astype...  55.6 us
    pallas_call x1, Pallas kernels, _backward(): pl.pallas_call(functools.partial(_bwd_kernel, scale=scale), grid=(heads,...  31.4 us
    pallas_call x1, Pallas kernels, _forward(): pl.pallas_call(functools.partial(_fwd_kernel, scale=scale), grid=(heads,...  28 us
    ppermute x9, waiting for transfers between devices, on_device(): lax.ppermute((lax.dynamic_slice_in_dim(numer, (1 - bit) * half, half, 0),...  20.1 us
    ppermute x6, waiting for transfers between devices, on_device(): other = lax.ppermute(gathered, 'region', pairs)  12.6 us
    ppermute x9, starting transfers between devices, on_device(): lax.ppermute((lax.dynamic_slice_in_dim(numer, (1 - bit) * half, half, 0),...  11.8 us
    unnamed x48, local copies, waits for them, and re-layouts  5.85 us
    convert_element_type x3, local copies, waits for them, and re-layouts, project(): return jnp.einsum('nd,dhe->hne', x, w.reshape(width, HEADS, head_dim), pr...  5.5 us
  transfers between devices with their start and end apart: 16, of which 7 were waited for; matrix products, arithmetic and copies ran while one was open for 16% of the time, Pallas kernels for 13%

profile of v8, /device:TPU:0, one launch (start us, length us, event | category | flops | bytes accessed | tf_op | source)
XLA Modules:
  0.0 247.5 jit_solution(2041685905698117261)
XLA Ops:
  12.1 2.1 convolution_convert_fusion.3
  14.3 1.8 copy.86
  16.8 1.8 copy.90
  19.4 1.9 copy.88
  22.0 28.0 %shard_map.135 = (f32[8,1024,64]{2,1,0:T(8,128)}, f32[8,1024,1]{2,1,0:T(8,128)}, f32[8,1024,1]{2,1,0:T(8,128)}) custom-call(bf16[8,1024,64]{2,1,0:T(8,128)(2,1)} %bitcast.111, bf16[8,1024,64]{2,1,0:T(8,128)(2,1)} %bitcast.115, bf16[8,1024,64]{2,1,0:T(8,128)(2,1)} %bitcast.113, f32[8,1,1024]{2,1,0:T(1,128)} %bitcast.129), custom_call_target="tpu_custom_call" | custom-call | tf_op jit(solution)/shard_map/pallas_call | solution.py:72
  50.0 2.8 %copy.91 = f32[1024,8,64]{0,2,1:T(8,128)S(1)} copy(f32[1024,8,64]{2,0,1:T(8,128)} %bitcast.121) | data formatting | bytes 4194304 | tf_op jit(solution)/shard_map/transpose | solution.py:143
  54.4 3.5 %dynamic-slice_reduce_fusion.3 = (f32[8,512]{1,0:T(8,128)S(1)}, f32[8,512]{1,0:T(8,128)S(1)}) fusion(f32[8,1024,1]{2,1,0:T(8,128)} %get-tuple-element.14, s32[]{:T(128)S(6)} %select_n.108, s32[]{:T(128)S(6)} %select_n.109), kind=kLoop, calls=%fused_computation.8 | loop fusion | bytes 65544 | tf_op jit(solution)/shard_map/dynamic_slice | solution.py:167
  60.6 3.0 %collective-permute-start.2 = (f32[8,256]{1,0:T(8,128)S(1)}, f32[8,256]{1,0:T(8,128)S(1)}, u32[]{:S(2)}, u32[]{:S(2)}) collective-permute-start(f32[8,256]{1,0:T(8,128)S(1)} %constant_dynamic-slice_fusion.7), channel_id=1, source_target_pairs={{0,2},{1,3},{2,0},{3,1},{4,6},{5,7},{6,4},{7,5},{8,10},{9,11},{10,... | collective-permute-start | bytes 24584 | tf_op jit(solution)/shard_map/ppermute | solution.py:170
  65.3 2.0 collective-permute-start.3
  67.3 2.7 %collective-permute-start.4 = (f32[8,128]{1,0:T(8,128)S(1)}, f32[8,128]{1,0:T(8,128)S(1)}, u32[]{:S(2)}, u32[]{:S(2)}) collective-permute-start(f32[8,128]{1,0:T(8,128)S(1)} %constant_dynamic-slice_fusion.4), channel_id=1, source_target_pairs={{0,4},{1,5},{2,6},{3,7},{4,0},{5,1},{6,2},{7,3},{8,12},{9,13},{10,... | collective-permute-start | bytes 12296 | tf_op jit(solution)/shard_map/ppermute | solution.py:170
  70.3 8.9 %collective-permute-done.3 = f32[256,512]{0,1:T(8,128)S(1)} collective-permute-done((f32[256,512]{0,1:T(8,128)S(1)}, f32[256,512]{0,1:T(8,128)S(1)}, u32[]{:S(2)}, u32[]{:S(2)}) %collective-permute-start.3) | collective-permute-done | bytes 524320 | tf_op jit(solution)/shard_map/ppermute | solution.py:170
  79.4 2.6 %collective-permute-start.5 = (f32[128,512]{0,1:T(8,128)S(1)}, f32[128,512]{0,1:T(8,128)S(1)}, u32[]{:S(2)}, u32[]{:S(2)}) collective-permute-start(f32[128,512]{0,1:T(8,128)S(1)} %constant_dynamic-slice_fusion.3), channel_id=1, source_target_pairs={{0,4},{1,5},{2,6},{3,7},{4,0},{5,1},{6,2},{7,3},{8,12},{9,13},{10,... | collective-permute-start | bytes 786440 | tf_op jit(solution)/shard_map/ppermute | solution.py:170
  82.8 10.4 %collective-permute-done.5 = f32[128,512]{0,1:T(8,128)S(1)} collective-permute-done((f32[128,512]{0,1:T(8,128)S(1)}, f32[128,512]{0,1:T(8,128)S(1)}, u32[]{:S(2)}, u32[]{:S(2)}) %collective-permute-start.5) | collective-permute-done | bytes 262176 | tf_op jit(solution)/shard_map/ppermute | solution.py:170
  93.4 4.5 %collective-permute-done.12 = f32[16,128]{1,0:T(8,128)S(1)} collective-permute-done((f32[16,128]{1,0:T(8,128)S(1)}, f32[16,128]{1,0:T(8,128)S(1)}, u32[]{:S(2)}, u32[]{:S(2)}) %collective-permute-start.12) | collective-permute-done | bytes 8224 | tf_op jit(solution)/shard_map/ppermute | solution.py:204
  98.8 3.0 %collective-permute-done.13 = f32[16,256]{1,0:T(8,128)S(1)} collective-permute-done((f32[16,256]{1,0:T(8,128)S(1)}, f32[16,256]{1,0:T(8,128)S(1)}, u32[]{:S(2)}, u32[]{:S(2)}) %collective-permute-start.13) | collective-permute-done | bytes 16416 | tf_op jit(solution)/shard_map/ppermute | solution.py:204
  101.8 2.1 convolution_convert_fusion
  104.0 1.8 copy.92
  105.8 1.7 collective-permute-start.9
  107.5 2.7 %copy.94.dl_ref = f32[8,1024,1]{2,1,0:T(8,128)} copy(f32[8,1024,1]{1,0,2:T(8,128)S(1)} %get-tuple-element.73) | data formatting | bytes 65536 | tf_op jit(solution)/shard_map/reshape | solution.py:213
  110.1 2.7 %copy.93.lt_ref = f32[8,1024,1]{2,1,0:T(8,128)} copy(f32[8,1024,1]{1,0,2:T(8,128)S(1)} %get-tuple-element.74) | data formatting | bytes 65536 | tf_op jit(solution)/shard_map/reshape | solution.py:212
  112.8 31.4 %shard_map.136 = (f32[8,1024,64]{2,1,0:T(8,128)}, f32[8,1024,64]{2,1,0:T(8,128)}, f32[8,1024,64]{2,1,0:T(8,128)}) custom-call(bf16[8,1024,64]{2,1,0:T(8,128)(2,1)} %bitcast.112, bf16[8,1024,64]{2,1,0:T(8,128)(2,1)} %bitcast.116, bf16[8,1024,64]{2,1,0:T(8,128)(2,1)} %bitcast.114, bf16[8,1024,64]{2,1,0:T(8,128)(2,1)} %bitcast.119, f32[8,1024,1]{2,1,0:T(8,128)} %copy.93.lt_ref, ...), custom_call_target="tpu_custom_call" | custom-call | tf_op jit(solution)/shard_map/pallas_call | solution.py:99
  144.2 4.4 %fusion.11 = f32[1024,512,1]{1,0,2:T(8,128)} fusion(bf16[512,8,64]{0,2,1:T(8,128)(2,1)S(1)} %bitcast.127, f32[8,1024,64]{2,1,0:T(8,128)} %get-tuple-element.17), kind=kOutput, calls=%fused_computation.29 | convolution fusion | flops 537395200 | bytes 4718592 | tf_op jit(solution)/shard_map/hne,dhe->nd/dot_general | solution.py:239
  150.1 2.1 collective-permute-start.10
  153.7 5.1 %collective-permute-done.10 = bf16[256,512]{0,1:T(8,128)(2,1)S(1)} collective-permute-done((bf16[256,512]{0,1:T(8,128)(2,1)S(1)}, bf16[256,512]{0,1:T(8,128)(2,1)S(1)}, u32[]{:S(2)}, u32[]{:S(2)}) %collective-permute-start.10) | collective-permute-done | bytes 262176 | tf_op jit(solution)/shard_map/ppermute | solution.py:204
  163.7 2.1 copy.101
  165.8 2.0 copy.99
  167.9 4.6 %fusion = bf16[1024,512]{1,0:T(8,128)(2,1)} fusion(f32[1024,512,1]{1,0,2:T(8,128)} %fusion.11, bf16[512,8,64]{0,2,1:T(8,128)(2,1)S(1)} %bitcast.125, f32[8,1024,64]{2,1,0:T(8,128)} %get-tuple-element.18), kind=kOutput, calls=%fused_computation.1 | convolution fusion | flops 538443776 | bytes 5767168 | tf_op jit(solution)/shard_map/hne,dhe->nd/dot_general | solution.py:240
  173.9 1.7 fusion.13
  175.6 1.7 add_convert_fusion.1
  177.3 55.6 %all-reduce.3.cloned.1.call-done = (bf16[1024,512]{0,1:T(8,128)(2,1)}, bf16[512,512]{1,0:T(8,128)(2,1)}, bf16[512,512]{1,0:T(8,128)(2,1)}) async-done(((bf16[1024,512]{0,1:T(8,128)(2,1)}, bf16[512,512]{1,0:T(8,128)(2,1)}, bf16[512,512]{1,0:T(8,128)(2,1)}), (bf16[1024,512]{0,1:T(8,128)(2,1)}, bf16[512,512]{1,0:T(8,128)(2,1)}, bf16[512,512]{1,0:T(8,128)(2,1)})) %all-reduce.3.cloned.1.call-update) | async-done | bytes 2097168 | tf_op jit(solution)/shard_map/psum | solution.py:227
  232.9 2.4 convolution_bitcast_fusion
  235.4 1.7 add_convert_fusion
  (110 shorter events, 28.1 us)
Async XLA Ops:
  7.2 8.9 %copy-start = (bf16[1024,512]{1,0:T(8,128)(2,1)S(1)}, bf16[1024,512]{1,0:T(8,128)(2,1)}, u32[]{:S(2)}) copy-start(bf16[1024,512]{1,0:T(8,128)(2,1)} %param.9) | copy-start | bytes 3145732
  7.2 3.9 %copy-start.9 = (bf16[512,512]{1,0:T(8,128)(2,1)S(1)}, bf16[512,512]{1,0:T(8,128)(2,1)}, u32[]{:S(2)}) copy-start(bf16[512,512]{1,0:T(8,128)(2,1)} %param.10) | copy-start | bytes 1572868
  7.2 225.7 %all-reduce.3.cloned.1.call-start = ((), (), s32[]{:S(2)}) async-start(), calls=%async_computation | async-start | bytes 4194304 | tf_op jit(solution)/shard_map/psum | solution.py:227
  9.6 9.0 %copy-start.13 = (bf16[512,512]{0,1:T(8,128)(2,1)}, bf16[512,512]{0,1:T(8,128)(2,1)S(1)}, u32[]{:S(2)}) copy-start(bf16[512,512]{0,1:T(8,128)(2,1)S(1)} %copy.87) | copy-start | bytes 1572868
  11.1 5.0 %copy-start.11 = (bf16[512,512]{0,1:T(8,128)(2,1)}, bf16[512,512]{0,1:T(8,128)(2,1)S(1)}, u32[]{:S(2)}) copy-start(bf16[512,512]{0,1:T(8,128)(2,1)S(1)} %copy.89) | copy-start | bytes 1572868
  53.9 9.8 %collective-permute-start.1 = (f32[512,512]{0,1:T(8,128)}, f32[512,512]{0,1:T(8,128)}, u32[]{:S(2)}, u32[]{:S(2)}) collective-permute-start(f32[512,512]{0,1:T(8,128)} %constant_dynamic-slice_fusion.8), channel_id=1, source_target_pairs={{0,1},{1,0},{2,3},{3,2},{4,5},{5,4},{6,7},{7,6},{8,9},{9,8},{10,11... | collective-permute-start | bytes 3145736 | tf_op jit(solution)/shard_map/ppermute | solution.py:170
  54.4 3.6 %copy-start.1 = (f32[8,1024,1]{2,1,0:T(8,128)S(1)}, f32[8,1024,1]{2,1,0:T(8,128)}, u32[]{:S(2)}) copy-start(f32[8,1024,1]{2,1,0:T(8,128)} %get-tuple-element.15) | copy-start | bytes 98308
  57.9 1.8 collective-permute-start
  59.2 1.4 collective-permute-start.6
  60.6 6.7 %collective-permute-start.2 = (f32[8,256]{1,0:T(8,128)S(1)}, f32[8,256]{1,0:T(8,128)S(1)}, u32[]{:S(2)}, u32[]{:S(2)}) collective-permute-start(f32[8,256]{1,0:T(8,128)S(1)} %constant_dynamic-slice_fusion.7), channel_id=1, source_target_pairs={{0,2},{1,3},{2,0},{3,1},{4,6},{5,7},{6,4},{7,5},{8,10},{9,11},{10,... | collective-permute-start | bytes 24584 | tf_op jit(solution)/shard_map/ppermute | solution.py:170
  63.6 3.7 %collective-permute-start.7 = (f32[8,256]{1,0:T(8,128)S(1)}, f32[8,256]{1,0:T(8,128)S(1)}, u32[]{:S(2)}, u32[]{:S(2)}) collective-permute-start(f32[8,256]{1,0:T(8,128)S(1)} %constant_dynamic-slice_fusion.2), channel_id=1, source_target_pairs={{0,2},{1,3},{2,0},{3,1},{4,6},{5,7},{6,4},{7,5},{8,10},{9,11},{10,... | collective-permute-start | bytes 24584 | tf_op jit(solution)/shard_map/ppermute | solution.py:170
  65.2 16.8 %copy-start.16 = (bf16[1024,512]{1,0:T(8,128)(2,1)S(1)}, bf16[1024,512]{1,0:T(8,128)(2,1)}, u32[]{:S(2)}) copy-start(bf16[1024,512]{1,0:T(8,128)(2,1)} %param.15) | copy-start | bytes 3145732
  65.2 16.8 %copy-start.20 = (bf16[512,512]{1,0:T(8,128)(2,1)S(1)}, bf16[512,512]{1,0:T(8,128)(2,1)}, u32[]{:S(2)}) copy-start(bf16[512,512]{1,0:T(8,128)(2,1)} %param.13) | copy-start | bytes 1572868
  65.3 14.0 %collective-permute-start.3 = (f32[256,512]{0,1:T(8,128)S(1)}, f32[256,512]{0,1:T(8,128)S(1)}, u32[]{:S(2)}, u32[]{:S(2)}) collective-permute-start(f32[256,512]{0,1:T(8,128)S(1)} %constant_dynamic-slice_fusion.6), channel_id=1, source_target_pairs={{0,2},{1,3},{2,0},{3,1},{4,6},{5,7},{6,4},{7,5},{8,10},{9,11},{10,... | collective-permute-start | bytes 1572872 | tf_op jit(solution)/shard_map/ppermute | solution.py:170
  67.3 15.5 %collective-permute-start.4 = (f32[8,128]{1,0:T(8,128)S(1)}, f32[8,128]{1,0:T(8,128)S(1)}, u32[]{:S(2)}, u32[]{:S(2)}) collective-permute-start(f32[8,128]{1,0:T(8,128)S(1)} %constant_dynamic-slice_fusion.4), channel_id=1, source_target_pairs={{0,4},{1,5},{2,6},{3,7},{4,0},{5,1},{6,2},{7,3},{8,12},{9,13},{10,... | collective-permute-start | bytes 12296 | tf_op jit(solution)/shard_map/ppermute | solution.py:170
  70.0 12.8 %collective-permute-start.8 = (f32[8,128]{1,0:T(8,128)S(1)}, f32[8,128]{1,0:T(8,128)S(1)}, u32[]{:S(2)}, u32[]{:S(2)}) collective-permute-start(f32[8,128]{1,0:T(8,128)S(1)} %constant_dynamic-slice_fusion), channel_id=1, source_target_pairs={{0,4},{1,5},{2,6},{3,7},{4,0},{5,1},{6,2},{7,3},{8,12},{9,13},{10,... | collective-permute-start | bytes 12296 | tf_op jit(solution)/shard_map/ppermute | solution.py:170
  79.4 13.8 %collective-permute-start.5 = (f32[128,512]{0,1:T(8,128)S(1)}, f32[128,512]{0,1:T(8,128)S(1)}, u32[]{:S(2)}, u32[]{:S(2)}) collective-permute-start(f32[128,512]{0,1:T(8,128)S(1)} %constant_dynamic-slice_fusion.3), channel_id=1, source_target_pairs={{0,4},{1,5},{2,6},{3,7},{4,0},{5,1},{6,2},{7,3},{8,12},{9,13},{10,... | collective-permute-start | bytes 786440 | tf_op jit(solution)/shard_map/ppermute | solution.py:170
  93.3 4.6 %collective-permute-start.12 = (f32[16,128]{1,0:T(8,128)S(1)}, f32[16,128]{1,0:T(8,128)S(1)}, u32[]{:S(2)}, u32[]{:S(2)}) collective-permute-start(f32[16,128]{1,0:T(8,128)S(1)} %pad_maximum_fusion.8), channel_id=1, source_target_pairs={{0,4},{1,5},{2,6},{3,7},{4,0},{5,1},{6,2},{7,3},{8,12},{9,13},{10,... | collective-permute-start | bytes 24584 | tf_op jit(solution)/shard_map/ppermute | solution.py:204
  97.9 3.8 %collective-permute-start.13 = (f32[16,256]{1,0:T(8,128)S(1)}, f32[16,256]{1,0:T(8,128)S(1)}, u32[]{:S(2)}, u32[]{:S(2)}) collective-permute-start(f32[16,256]{1,0:T(8,128)S(1)} %pad_maximum_fusion.7), channel_id=1, source_target_pairs={{0,2},{1,3},{2,0},{3,1},{4,6},{5,7},{6,4},{7,5},{8,10},{9,11},{10,... | collective-permute-start | bytes 49160 | tf_op jit(solution)/shard_map/ppermute | solution.py:204
  101.7 5.7 %collective-permute-start.14 = (f32[16,512]{1,0:T(8,128)S(1)}, f32[16,512]{1,0:T(8,128)S(1)}, u32[]{:S(2)}, u32[]{:S(2)}) collective-permute-start(f32[16,512]{1,0:T(8,128)S(1)} %pad_maximum_fusion.6), channel_id=1, source_target_pairs={{0,1},{1,0},{2,3},{3,2},{4,5},{5,4},{6,7},{7,6},{8,9},{9,8},{10,11... | collective-permute-start | bytes 98312 | tf_op jit(solution)/shard_map/ppermute | solution.py:204
  105.8 43.2 %collective-permute-start.9 = (bf16[128,512]{0,1:T(8,128)(2,1)S(1)}, bf16[128,512]{0,1:T(8,128)(2,1)}, u32[]{:S(2)}, u32[]{:S(2)}) collective-permute-start(bf16[128,512]{0,1:T(8,128)(2,1)S(1)} %get-tuple-element.62), channel_id=1, source_target_pairs={{0,4},{1,5},{2,6},{3,7},{4,0},{5,1},{6,2},{7,3},{8,12},{9,13},{10,... | collective-permute-start | bytes 393224 | tf_op jit(solution)/shard_map/ppermute | solution.py:204
  112.8 31.4 %copy-start.14 = (bf16[512,512]{0,1:T(8,128)(2,1)S(1)}, bf16[512,512]{0,1:T(8,128)(2,1)}, u32[]{:S(2)}) copy-start(bf16[512,512]{0,1:T(8,128)(2,1)} %copy-done.13) | copy-start | bytes 1572868
  144.2 4.4 %copy-start.2 = (f32[8,1024,64]{2,1,0:T(8,128)S(1)}, f32[8,1024,64]{2,1,0:T(8,128)}, u32[]{:S(2)}) copy-start(f32[8,1024,64]{2,1,0:T(8,128)} %get-tuple-element.16) | copy-start | bytes 6291460
  148.6 3.6 %copy-start.4 = (f32[8,1024,64]{2,1,0:T(8,128)S(1)}, f32[8,1024,64]{2,1,0:T(8,128)}, u32[]{:S(2)}) copy-start(f32[8,1024,64]{2,1,0:T(8,128)} %get-tuple-element.17) | copy-start | bytes 6291460
  150.1 8.8 %collective-permute-start.10 = (bf16[256,512]{0,1:T(8,128)(2,1)S(1)}, bf16[256,512]{0,1:T(8,128)(2,1)S(1)}, u32[]{:S(2)}, u32[]{:S(2)}) collective-permute-start(bf16[256,512]{0,1:T(8,128)(2,1)S(1)} %pad_maximum_fusion.4), channel_id=1, source_target_pairs={{0,2},{1,3},{2,0},{3,1},{4,6},{5,7},{6,4},{7,5},{8,10},{9,11},{10,... | collective-permute-start | bytes 786440 | tf_op jit(solution)/shard_map/ppermute | solution.py:204
  152.2 8.3 %copy-start.3 = (f32[8,1024,64]{2,1,0:T(8,128)S(1)}, f32[8,1024,64]{2,1,0:T(8,128)}, u32[]{:S(2)}) copy-start(f32[8,1024,64]{2,1,0:T(8,128)} %get-tuple-element.18) | copy-start | bytes 6291460
  160.5 12.0 %collective-permute-start.11 = (bf16[512,512]{0,1:T(8,128)(2,1)}, bf16[512,512]{0,1:T(8,128)(2,1)}, u32[]{:S(2)}, u32[]{:S(2)}) collective-permute-start(bf16[512,512]{0,1:T(8,128)(2,1)} %pad_maximum_fusion.3), channel_id=1, source_target_pairs={{0,1},{1,0},{2,3},{3,2},{4,5},{5,4},{6,7},{7,6},{8,9},{9,8},{10,11... | collective-permute-start | bytes 1572872 | tf_op jit(solution)/shard_map/ppermute | solution.py:204
  163.7 4.2 %copy-start.12 = (bf16[512,512]{0,1:T(8,128)(2,1)S(1)}, bf16[512,512]{0,1:T(8,128)(2,1)}, u32[]{:S(2)}) copy-start(bf16[512,512]{0,1:T(8,128)(2,1)} %copy-done.11) | copy-start | bytes 1572868
  167.9 4.7 %copy-start.6 = (bf16[256,512]{0,1:T(8,128)(2,1)S(1)}, bf16[256,512]{0,1:T(8,128)(2,1)}, u32[]{:S(2)}) copy-start(bf16[256,512]{0,1:T(8,128)(2,1)} %copy-done.5) | copy-start | bytes 786436
  177.3 58.0 %copy-start.10 = (bf16[512,512]{1,0:T(8,128)(2,1)S(1)}, bf16[512,512]{1,0:T(8,128)(2,1)}, u32[]{:S(2)}) copy-start(bf16[512,512]{1,0:T(8,128)(2,1)} %param.10) | copy-start | bytes 1572868
  232.9 2.4 copy-start.19
  235.4 2.9 %copy-start.7 = (bf16[512,512]{1,0:T(8,128)(2,1)S(1)}, bf16[512,512]{1,0:T(8,128)(2,1)}, u32[]{:S(2)}) copy-start(bf16[512,512]{1,0:T(8,128)(2,1)} %get-tuple-element.60) | copy-start | bytes 1572868
  (6 other events, 9.8 us)
Sparse Core Ops, SparseCore 0:
  168.0 64.9 all-reduce.2

commit v9 on v7

--- a/solution.py
+++ b/solution.py
@@ -94,22 +94,23 @@
 def _backward(qT, kT, vT, gaT, lt, dl, cm, scale):
     heads, nq, hd = qT.shape
     nk = kT.shape[1]
-    nb = TQ // BLOCK
+    tile = min(nq, 2 * TQ)
+    nb = tile // BLOCK
     f32 = jnp.float32
     return pl.pallas_call(
         functools.partial(_bwd_kernel, scale=scale),
-        grid=(heads, nq // TQ),
+        grid=(heads, nq // tile),
         in_specs=[
-            pl.BlockSpec((1, TQ, hd), lambda h, i: (h, i, 0)),
-            pl.BlockSpec((1, nk, hd), lambda h, i: (h, 0, 0)),
-            pl.BlockSpec((1, nk, hd), lambda h, i: (h, 0, 0)),
-            pl.BlockSpec((1, TQ, hd), lambda h, i: (h, i, 0)),
-            pl.BlockSpec((1, TQ, 1), lambda h, i: (h, i, 0)),
-            pl.BlockSpec((1, TQ, 1), lambda h, i: (h, i, 0)),
+            pl.BlockSpec((1, tile, hd), lambda h, i: (h, i, 0)),
+            pl.BlockSpec((1, nk, hd), lambda h, i: (h, 0, 0)),
+            pl.BlockSpec((1, nk, hd), lambda h, i: (h, 0, 0)),
+            pl.BlockSpec((1, tile, hd), lambda h, i: (h, i, 0)),
+            pl.BlockSpec((1, tile, 1), lambda h, i: (h, i, 0)),
+            pl.BlockSpec((1, tile, 1), lambda h, i: (h, i, 0)),
             pl.BlockSpec((nb, 1, nk), lambda h, i: (i, 0, 0)),
         ],
         out_specs=[
-            pl.BlockSpec((1, TQ, hd), lambda h, i: (h, i, 0)),
+            pl.BlockSpec((1, tile, hd), lambda h, i: (h, i, 0)),
             pl.BlockSpec((1, nk, hd), lambda h, i: (h, 0, 0)),
             pl.BlockSpec((1, nk, hd), lambda h, i: (h, 0, 0)),
         ],
@@ -118,7 +119,9 @@
             jax.ShapeDtypeStruct((heads, nk, hd), f32),
             jax.ShapeDtypeStruct((heads, nk, hd), f32),
         ],
-        compiler_params=pltpu.CompilerParams(dimension_semantics=("parallel", "arbitrary")),
+        compiler_params=pltpu.CompilerParams(
+            dimension_semantics=("parallel", "arbitrary"), vmem_limit_bytes=48 * 1024 * 1024
+        ),
     )(qT, kT, vT, gaT, lt, dl, cm)
 
 
@@ -167,7 +170,7 @@
         )
         theirs = lax.ppermute(
             (
-                lax.dynamic_slice_in_dim(numer, (1 - bit) * half, half, 0),
+                lax.dynamic_slice_in_dim(numer, (1 - bit) * half, half, 0).astype(bf16),
                 lax.dynamic_slice_in_dim(peak, (1 - bit) * half, half, 1),
                 lax.dynamic_slice_in_dim(total, (1 - bit) * half, half, 1),
             ),
@@ -177,7 +180,7 @@
         top = jnp.maximum(mine[1], theirs[1])
         scale_a = jnp.exp(mine[1] - top)
         scale_b = jnp.exp(theirs[1] - top)
-        numer = mine[0] * jnp.repeat(scale_a.T, head_dim, axis=1) + theirs[0] * jnp.repeat(
+        numer = mine[0] * jnp.repeat(scale_a.T, head_dim, axis=1) + theirs[0].astype(f32) * jnp.repeat(
             scale_b.T, head_dim, axis=1
         )
         total = mine[2] * scale_a + theirs[2] * scale_b

time: 237 us -> 232 us (0.979)
  starting transfers between devices: 16.6 us -> 8.8 us
    ppermute x9, starting transfers between devices: 11.8 us -> 7.42 us  [on_device(): lax.ppermute((lax.dynamic_slice_in_dim(numer, (1 - bit) * half, half, 0)....]
    ppermute x6, starting transfers between devices: 4.75 us -> 1.33 us  [on_device(): other = lax.ppermute(gathered, 'region', pairs)]
    ppermute x9, waiting for transfers between devices: 20.1 us -> 17 us  [on_device(): lax.ppermute((lax.dynamic_slice_in_dim(numer, (1 - bit) * half, half, 0)....]
    unnamed x41 -> x45, local copies, waits for them, and re-layouts: 5.23 us -> 6.82 us
  transfers between devices with their start and end apart: 16 -> 16, of which waited for: 7 -> 8; matrix products, arithmetic and copies ran while one was open for 16% -> 18% of each run, Pallas kernels for 13% -> 13%
where the time goes in v9:
time: 232 us
  waiting for transfers between devices  84.2 us (36%)
  Pallas kernels  57.2 us (25%)
  local copies, waits for them, and re-layouts  34.5 us (15%)
  matrix products  20.6 us (9%)
  between operations  14.4 us (6%)
  other arithmetic  12.1 us (5%)
  starting transfers between devices  8.8 us (4%)
    psum x1, waiting for transfers between devices, on_device(): lax.psum((joined(dq_r).astype(bf16), wk_part.astype(bf16), wv_part.astype...  54 us
    pallas_call x1, Pallas kernels, _backward(): pl.pallas_call(functools.partial(_bwd_kernel, scale=scale), grid=(heads,...  29.2 us
    pallas_call x1, Pallas kernels, _forward(): pl.pallas_call(functools.partial(_fwd_kernel, scale=scale), grid=(heads,...  28 us
    ppermute x9, waiting for transfers between devices, on_device(): lax.ppermute((lax.dynamic_slice_in_dim(numer, (1 - bit) * half, half, 0)....  17 us
    ppermute x6, waiting for transfers between devices, on_device(): other = lax.ppermute(gathered, 'region', pairs)  13.2 us
    ppermute x9, starting transfers between devices, on_device(): lax.ppermute((lax.dynamic_slice_in_dim(numer, (1 - bit) * half, half, 0)....  7.42 us
    reshape x4, local copies, waits for them, and re-layouts, heads(): return x.reshape(x.shape[0], HEADS, head_dim).transpose(1, 0, 2)  7.23 us
    unnamed x45, local copies, waits for them, and re-layouts  6.82 us
  transfers between devices with their start and end apart: 16, of which 8 were waited for; matrix products, arithmetic and copies ran while one was open for 18% of the time, Pallas kernels for 13%

profile of v9, /device:TPU:0, one launch (start us, length us, event | category | flops | bytes accessed | tf_op | source)
XLA Modules:
  0.0 231.7 jit_solution(7972858137804062061)
XLA Ops:
  8.3 2.1 convolution_convert_fusion.3
  10.4 1.8 copy.44
  13.0 1.8 copy.45
  15.5 1.8 copy.46
  18.0 28.0 %shard_map.135 = (f32[8,1024,64]{2,1,0:T(8,128)}, f32[8,1024,1]{2,1,0:T(8,128)}, f32[8,1024,1]{2,1,0:T(8,128)}) custom-call(bf16[8,1024,64]{2,1,0:T(8,128)(2,1)} %bitcast.102, bf16[8,1024,64]{2,1,0:T(8,128)(2,1)} %bitcast.104, bf16[8,1024,64]{2,1,0:T(8,128)(2,1)} %bitcast.108, f32[8,1,1024]{2,1,0:T(1,128)} %bitcast.106), custom_call_target="tpu_custom_call" | custom-call | tf_op jit(solution)/shard_map/pallas_call | solution.py:72
  46.1 3.5 %dynamic-slice_reduce_fusion.3 = (f32[8,512]{1,0:T(8,128)S(1)}, f32[8,512]{1,0:T(8,128)S(1)}) fusion(f32[8,1024,1]{2,1,0:T(8,128)} %get-tuple-element.14, s32[]{:T(128)S(6)} %select_n.108, s32[]{:T(128)S(6)} %select_n.109), kind=kLoop, calls=%fused_computation.9 | loop fusion | bytes 65544 | tf_op jit(solution)/shard_map/dynamic_slice | solution.py:168
  51.4 2.8 %copy.47 = f32[1024,8,64]{0,2,1:T(8,128)S(1)} copy(f32[1024,8,64]{2,0,1:T(8,128)} %bitcast.116) | data formatting | bytes 4194304 | tf_op jit(solution)/shard_map/transpose | solution.py:146
  55.6 3.1 %convolution_convert_fusion = bf16[1024,512]{0,1:T(8,128)(2,1)} fusion(bf16[1024,512]{1,0:T(8,128)(2,1)} %param.15, bf16[512,512]{1,0:T(8,128)(2,1)} %param.13), kind=kOutput, calls=%fused_computation.10 | convolution fusion | flops 537395200 | bytes 2621440 | tf_op jit(solution)/shard_map/dot_general | solution.py:194
  58.7 2.6 %collective-permute-start.2 = (f32[8,256]{1,0:T(8,128)S(1)}, f32[8,256]{1,0:T(8,128)S(1)}, u32[]{:S(2)}, u32[]{:S(2)}) collective-permute-start(f32[8,256]{1,0:T(8,128)S(1)} %constant_dynamic-slice_fusion.5), channel_id=1, source_target_pairs={{0,2},{1,3},{2,0},{3,1},{4,6},{5,7},{6,4},{7,5},{8,10},{9,11},{10,... | collective-permute-start | bytes 24584 | tf_op jit(solution)/shard_map/ppermute | solution.py:171
  63.0 2.0 collective-permute-done.7
  65.1 2.7 %collective-permute-start.8 = (f32[8,128]{1,0:T(8,128)S(1)}, f32[8,128]{1,0:T(8,128)S(1)}, u32[]{:S(2)}, u32[]{:S(2)}) collective-permute-start(f32[8,128]{1,0:T(8,128)S(1)} %constant_dynamic-slice_fusion), channel_id=1, source_target_pairs={{0,4},{1,5},{2,6},{3,7},{4,0},{5,1},{6,2},{7,3},{8,12},{9,13},{10,... | collective-permute-start | bytes 12296 | tf_op jit(solution)/shard_map/ppermute | solution.py:171
  69.6 6.6 %collective-permute-done.3 = bf16[256,512]{0,1:T(8,128)(2,1)S(1)} collective-permute-done((bf16[256,512]{0,1:T(8,128)(2,1)S(1)}, bf16[256,512]{0,1:T(8,128)(2,1)S(1)}, u32[]{:S(2)}, u32[]{:S(2)}) %collective-permute-start.3) | collective-permute-done | bytes 262176 | tf_op jit(solution)/shard_map/ppermute | solution.py:171
  76.7 6.8 %collective-permute-done.5 = bf16[128,512]{0,1:T(8,128)(2,1)S(1)} collective-permute-done((bf16[128,512]{0,1:T(8,128)(2,1)S(1)}, bf16[128,512]{0,1:T(8,128)(2,1)S(1)}, u32[]{:S(2)}, u32[]{:S(2)}) %collective-permute-start.5) | collective-permute-done | bytes 131104 | tf_op jit(solution)/shard_map/ppermute | solution.py:171
  84.6 4.5 %collective-permute-done.12 = f32[16,128]{1,0:T(8,128)S(1)} collective-permute-done((f32[16,128]{1,0:T(8,128)S(1)}, f32[16,128]{1,0:T(8,128)S(1)}, u32[]{:S(2)}, u32[]{:S(2)}) %collective-permute-start.12) | collective-permute-done | bytes 8224 | tf_op jit(solution)/shard_map/ppermute | solution.py:205
  89.2 3.7 %collective-permute-done.13 = f32[16,256]{1,0:T(8,128)S(1)} collective-permute-done((f32[16,256]{1,0:T(8,128)S(1)}, f32[16,256]{1,0:T(8,128)S(1)}, u32[]{:S(2)}, u32[]{:S(2)}) %collective-permute-start.13) | collective-permute-done | bytes 16416 | tf_op jit(solution)/shard_map/ppermute | solution.py:205
  93.1 1.9 copy.48
  95.0 2.7 %copy.49.lt_ref = f32[8,1024,1]{2,1,0:T(8,128)} copy(f32[8,1024,1]{1,0,2:T(8,128)S(1)} %get-tuple-element.67) | data formatting | bytes 65536 | tf_op jit(solution)/shard_map/reshape | solution.py:213
  97.6 2.7 %copy.50.dl_ref = f32[8,1024,1]{2,1,0:T(8,128)} copy(f32[8,1024,1]{1,0,2:T(8,128)S(1)} %get-tuple-element.66) | data formatting | bytes 65536 | tf_op jit(solution)/shard_map/reshape | solution.py:214
  101.9 29.2 %shard_map.136 = (f32[8,1024,64]{2,1,0:T(8,128)}, f32[8,1024,64]{2,1,0:T(8,128)}, f32[8,1024,64]{2,1,0:T(8,128)}) custom-call(bf16[8,1024,64]{2,1,0:T(8,128)(2,1)S(1)} %bitcast.103, bf16[8,1024,64]{2,1,0:T(8,128)(2,1)S(1)} %bitcast.105, bf16[8,1024,64]{2,1,0:T(8,128)(2,1)} %bitcast.109, bf16[8,1024,64]{2,1,0:T(8,128)(2,1)} %bitcast.110, ...), custom_call_target="tpu_custom_call" | custom-call | tf_op jit(solution)/shard_map/pallas_call | solution.py:100
  131.1 5.6 %convert_bitcast_fusion = (bf16[1024,8,64]{2,0,1:T(8,128)(2,1)}, bf16[1024,8,64]{2,0,1:T(8,128)(2,1)S(1)}) fusion(f32[8,1024,64]{2,1,0:T(8,128)} %get-tuple-element.18, f32[8,1024,64]{2,1,0:T(8,128)} %get-tuple-element.17), kind=kLoop, calls=%fused_computation.1 | loop fusion | flops 1048576 | bytes 6291456 | tf_op jit(solution)/shard_map/convert_element_type | solution.py:223
  136.6 1.6 copy.52
  138.3 2.6 %convert_bitcast_fusion.2 = bf16[1024,8,64]{2,0,1:T(8,128)(2,1)S(1)} fusion(f32[8,1024,64]{2,1,0:T(8,128)} %get-tuple-element.16), kind=kLoop, calls=%fused_computation.4 | loop fusion | flops 524288 | bytes 3145728 | tf_op jit(solution)/shard_map/convert_element_type | solution.py:227
  142.4 2.7 %copy.53 = bf16[1024,8,64]{0,2,1:T(8,128)(2,1)} copy(bf16[1024,8,64]{2,0,1:T(8,128)(2,1)} %get-tuple-element.82) | data formatting | bytes 2097152 | tf_op jit(solution)/shard_map/convert_element_type | solution.py:223
  145.1 1.6 copy.51
  147.8 2.7 %fusion.1 = bf16[512,512]{0,1:T(8,128)(2,1)} fusion(bf16[1024,512]{0,1:T(8,128)(2,1)} %bitcast.117, bf16[1024,512]{1,0:T(8,128)(2,1)S(1)} %copy-done), kind=kOutput, calls=%fused_computation.18 | convolution fusion | flops 537133056 | bytes 2621440 | tf_op jit(solution)/shard_map/ka,kb->ab/dot_general | solution.py:225
  150.5 4.9 %collective-permute-done.10 = bf16[256,512]{0,1:T(8,128)(2,1)S(1)} collective-permute-done((bf16[256,512]{0,1:T(8,128)(2,1)S(1)}, bf16[256,512]{0,1:T(8,128)(2,1)S(1)}, u32[]{:S(2)}, u32[]{:S(2)}) %collective-permute-start.10) | collective-permute-done | bytes 262176 | tf_op jit(solution)/shard_map/ppermute | solution.py:205
  157.0 1.7 add_convert_fusion
  160.0 1.7 fusion.3
  161.7 1.7 add_convert_fusion.2
  163.4 54.0 %all-reduce.3.cloned.1.call-done = (bf16[512,512]{0,1:T(8,128)(2,1)}, bf16[512,512]{0,1:T(8,128)(2,1)}, bf16[1024,512]{0,1:T(8,128)(2,1)}) async-done(((bf16[512,512]{0,1:T(8,128)(2,1)}, bf16[512,512]{0,1:T(8,128)(2,1)}, bf16[1024,512]{0,1:T(8,128)(2,1)}), (bf16[512,512]{0,1:T(8,128)(2,1)}, bf16[512,512]{0,1:T(8,128)(2,1)}, bf16[1024,512]{0,1:T(8,128)(2,1)})) %all-reduce.3.cloned.1.call-update) | async-done | bytes 2097168 | tf_op jit(solution)/shard_map/psum | solution.py:226
  217.3 2.1 convolution_bitcast_fusion
  219.5 1.7 add_convert_fusion.1
  (105 shorter events, 22.3 us)
Async XLA Ops:
  7.2 5.1 %copy-start = (bf16[1024,512]{1,0:T(8,128)(2,1)S(1)}, bf16[1024,512]{1,0:T(8,128)(2,1)}, u32[]{:S(2)}) copy-start(bf16[1024,512]{1,0:T(8,128)(2,1)} %param.9) | copy-start | bytes 3145732
  7.2 210.1 %all-reduce.3.cloned.1.call-start = ((), (), s32[]{:S(2)}) async-start(), calls=%async_computation | async-start | bytes 4194304 | tf_op jit(solution)/shard_map/psum | solution.py:226
  10.4 1.8 copy-start.9
  46.1 4.1 %copy-start.6 = (f32[8,1024,1]{2,1,0:T(8,128)S(1)}, f32[8,1024,1]{2,1,0:T(8,128)}, u32[]{:S(2)}) copy-start(f32[8,1024,1]{2,1,0:T(8,128)} %get-tuple-element.15) | copy-start | bytes 98308
  49.6 9.1 %collective-permute-start = (f32[8,512]{1,0:T(8,128)S(1)}, f32[8,512]{1,0:T(8,128)S(1)}, u32[]{:S(2)}, u32[]{:S(2)}) collective-permute-start(f32[8,512]{1,0:T(8,128)S(1)} %get-tuple-element.50), channel_id=1, source_target_pairs={{0,1},{1,0},{2,3},{3,2},{4,5},{5,4},{6,7},{7,6},{8,9},{9,8},{10,11... | collective-permute-start | bytes 49160 | tf_op jit(solution)/shard_map/ppermute | solution.py:171
  51.3 7.4 %collective-permute-start.6 = (f32[8,512]{1,0:T(8,128)S(1)}, f32[8,512]{1,0:T(8,128)S(1)}, u32[]{:S(2)}, u32[]{:S(2)}) collective-permute-start(f32[8,512]{1,0:T(8,128)S(1)} %get-tuple-element.48), channel_id=1, source_target_pairs={{0,1},{1,0},{2,3},{3,2},{4,5},{5,4},{6,7},{7,6},{8,9},{9,8},{10,11... | collective-permute-start | bytes 49160 | tf_op jit(solution)/shard_map/ppermute | solution.py:171
  55.1 12.6 %collective-permute-start.1 = (bf16[512,512]{0,1:T(8,128)(2,1)}, bf16[512,512]{0,1:T(8,128)(2,1)}, u32[]{:S(2)}, u32[]{:S(2)}) collective-permute-start(bf16[512,512]{0,1:T(8,128)(2,1)} %dynamic-slice_convert_fusion), channel_id=1, source_target_pairs={{0,1},{1,0},{2,3},{3,2},{4,5},{5,4},{6,7},{7,6},{8,9},{9,8},{10,11... | collective-permute-start | bytes 1572872 | tf_op jit(solution)/shard_map/ppermute | solution.py:171
  58.7 4.3 %collective-permute-start.2 = (f32[8,256]{1,0:T(8,128)S(1)}, f32[8,256]{1,0:T(8,128)S(1)}, u32[]{:S(2)}, u32[]{:S(2)}) collective-permute-start(f32[8,256]{1,0:T(8,128)S(1)} %constant_dynamic-slice_fusion.5), channel_id=1, source_target_pairs={{0,2},{1,3},{2,0},{3,1},{4,6},{5,7},{6,4},{7,5},{8,10},{9,11},{10,... | collective-permute-start | bytes 24584 | tf_op jit(solution)/shard_map/ppermute | solution.py:171
  61.4 3.7 %collective-permute-start.7 = (f32[8,256]{1,0:T(8,128)S(1)}, f32[8,256]{1,0:T(8,128)S(1)}, u32[]{:S(2)}, u32[]{:S(2)}) collective-permute-start(f32[8,256]{1,0:T(8,128)S(1)} %constant_dynamic-slice_fusion.2), channel_id=1, source_target_pairs={{0,2},{1,3},{2,0},{3,1},{4,6},{5,7},{6,4},{7,5},{8,10},{9,11},{10,... | collective-permute-start | bytes 24584 | tf_op jit(solution)/shard_map/ppermute | solution.py:171
  65.1 11.6 %collective-permute-start.8 = (f32[8,128]{1,0:T(8,128)S(1)}, f32[8,128]{1,0:T(8,128)S(1)}, u32[]{:S(2)}, u32[]{:S(2)}) collective-permute-start(f32[8,128]{1,0:T(8,128)S(1)} %constant_dynamic-slice_fusion), channel_id=1, source_target_pairs={{0,4},{1,5},{2,6},{3,7},{4,0},{5,1},{6,2},{7,3},{8,12},{9,13},{10,... | collective-permute-start | bytes 12296 | tf_op jit(solution)/shard_map/ppermute | solution.py:171
  69.0 24.1 %copy-start.8 = (bf16[1024,512]{0,1:T(8,128)(2,1)S(1)}, bf16[1024,512]{0,1:T(8,128)(2,1)}, u32[]{:S(2)}) copy-start(bf16[1024,512]{0,1:T(8,128)(2,1)} %convolution_convert_fusion) | copy-start | bytes 3145732
  69.0 7.1 %collective-permute-start.3 = (bf16[256,512]{0,1:T(8,128)(2,1)S(1)}, bf16[256,512]{0,1:T(8,128)(2,1)S(1)}, u32[]{:S(2)}, u32[]{:S(2)}) collective-permute-start(bf16[256,512]{0,1:T(8,128)(2,1)S(1)} %dynamic-slice_convert_fusion.1), channel_id=1, source_target_pairs={{0,2},{1,3},{2,0},{3,1},{4,6},{5,7},{6,4},{7,5},{8,10},{9,11},{10,... | collective-permute-start | bytes 786440 | tf_op jit(solution)/shard_map/ppermute | solution.py:171
  69.5 7.1 %collective-permute-start.4 = (f32[8,128]{1,0:T(8,128)S(1)}, f32[8,128]{1,0:T(8,128)S(1)}, u32[]{:S(2)}, u32[]{:S(2)}) collective-permute-start(f32[8,128]{1,0:T(8,128)S(1)} %constant_dynamic-slice_fusion.3), channel_id=1, source_target_pairs={{0,4},{1,5},{2,6},{3,7},{4,0},{5,1},{6,2},{7,3},{8,12},{9,13},{10,... | collective-permute-start | bytes 12296 | tf_op jit(solution)/shard_map/ppermute | solution.py:171
  76.3 7.2 %collective-permute-start.5 = (bf16[128,512]{0,1:T(8,128)(2,1)S(1)}, bf16[128,512]{0,1:T(8,128)(2,1)S(1)}, u32[]{:S(2)}, u32[]{:S(2)}) collective-permute-start(bf16[128,512]{0,1:T(8,128)(2,1)S(1)} %dynamic-slice_convert_fusion.2), channel_id=1, source_target_pairs={{0,4},{1,5},{2,6},{3,7},{4,0},{5,1},{6,2},{7,3},{8,12},{9,13},{10,... | collective-permute-start | bytes 393224 | tf_op jit(solution)/shard_map/ppermute | solution.py:171
  84.5 4.6 %collective-permute-start.12 = (f32[16,128]{1,0:T(8,128)S(1)}, f32[16,128]{1,0:T(8,128)S(1)}, u32[]{:S(2)}, u32[]{:S(2)}) collective-permute-start(f32[16,128]{1,0:T(8,128)S(1)} %pad_maximum_fusion.8), channel_id=1, source_target_pairs={{0,4},{1,5},{2,6},{3,7},{4,0},{5,1},{6,2},{7,3},{8,12},{9,13},{10,... | collective-permute-start | bytes 24584 | tf_op jit(solution)/shard_map/ppermute | solution.py:205
  89.2 3.8 %collective-permute-start.13 = (f32[16,256]{1,0:T(8,128)S(1)}, f32[16,256]{1,0:T(8,128)S(1)}, u32[]{:S(2)}, u32[]{:S(2)}) collective-permute-start(f32[16,256]{1,0:T(8,128)S(1)} %pad_maximum_fusion.7), channel_id=1, source_target_pairs={{0,2},{1,3},{2,0},{3,1},{4,6},{5,7},{6,4},{7,5},{8,10},{9,11},{10,... | collective-permute-start | bytes 49160 | tf_op jit(solution)/shard_map/ppermute | solution.py:205
  93.0 2.0 collective-permute-start.14
  94.9 51.7 %collective-permute-start.9 = (bf16[128,512]{0,1:T(8,128)(2,1)S(1)}, bf16[128,512]{0,1:T(8,128)(2,1)S(1)}, u32[]{:S(2)}, u32[]{:S(2)}) collective-permute-start(bf16[128,512]{0,1:T(8,128)(2,1)S(1)} %get-tuple-element.55), channel_id=1, source_target_pairs={{0,4},{1,5},{2,6},{3,7},{4,0},{5,1},{6,2},{7,3},{8,12},{9,13},{10,... | collective-permute-start | bytes 393224 | tf_op jit(solution)/shard_map/ppermute | solution.py:205
  97.6 2.7 %copy-start.1 = (bf16[1024,8,64]{2,0,1:T(8,128)(2,1)S(1)}, bf16[1024,8,64]{2,0,1:T(8,128)(2,1)}, u32[]{:S(2)}) copy-start(bf16[1024,8,64]{2,0,1:T(8,128)(2,1)} %copy.44) | copy-start | bytes 3145732
  97.6 2.7 %copy-start.3 = (f32[8,8,128]{2,1,0:T(8,128)S(1)}, f32[8,8,128]{2,1,0:T(8,128)}, u32[]{:S(2)}) copy-start(f32[8,8,128]{2,1,0:T(8,128)} %broadcast_in_dim.26) | copy-start | bytes 98308
  138.3 2.6 %copy-start.4 = (bf16[1024,8,64]{0,2,1:T(8,128)(2,1)S(1)}, bf16[1024,8,64]{0,2,1:T(8,128)(2,1)}, u32[]{:S(2)}) copy-start(bf16[1024,8,64]{0,2,1:T(8,128)(2,1)} %copy.52) | copy-start | bytes 3145732
  146.7 8.8 %collective-permute-start.10 = (bf16[256,512]{0,1:T(8,128)(2,1)S(1)}, bf16[256,512]{0,1:T(8,128)(2,1)S(1)}, u32[]{:S(2)}, u32[]{:S(2)}) collective-permute-start(bf16[256,512]{0,1:T(8,128)(2,1)S(1)} %pad_maximum_fusion.4), channel_id=1, source_target_pairs={{0,2},{1,3},{2,0},{3,1},{4,6},{5,7},{6,4},{7,5},{8,10},{9,11},{10,... | collective-permute-start | bytes 786440 | tf_op jit(solution)/shard_map/ppermute | solution.py:205
  150.5 5.2 %copy-start.5 = (bf16[1024,8,64]{0,2,1:T(8,128)(2,1)S(1)}, bf16[1024,8,64]{0,2,1:T(8,128)(2,1)}, u32[]{:S(2)}) copy-start(bf16[1024,8,64]{0,2,1:T(8,128)(2,1)} %copy.52) | copy-start | bytes 3145732
  150.5 5.2 %copy-start.10 = (bf16[512,512]{1,0:T(8,128)(2,1)S(1)}, bf16[512,512]{1,0:T(8,128)(2,1)}, u32[]{:S(2)}) copy-start(bf16[512,512]{1,0:T(8,128)(2,1)} %param.11) | copy-start | bytes 1572868
  155.7 3.1 %collective-permute-start.11 = (bf16[512,512]{0,1:T(8,128)(2,1)S(1)}, bf16[512,512]{0,1:T(8,128)(2,1)S(1)}, u32[]{:S(2)}, u32[]{:S(2)}) collective-permute-start(bf16[512,512]{0,1:T(8,128)(2,1)S(1)} %pad_maximum_fusion.3), channel_id=1, source_target_pairs={{0,1},{1,0},{2,3},{3,2},{4,5},{5,4},{6,7},{7,6},{8,9},{9,8},{10,11... | collective-permute-start | bytes 1572872 | tf_op jit(solution)/shard_map/ppermute | solution.py:205
  159.0 2.7 %copy-start.15 = (bf16[1024,512]{1,0:T(8,128)(2,1)S(1)}, bf16[1024,512]{1,0:T(8,128)(2,1)}, u32[]{:S(2)}) copy-start(bf16[1024,512]{1,0:T(8,128)(2,1)} %param.8) | copy-start | bytes 3145732
  159.0 2.7 %copy-start.19 = (bf16[512,512]{1,0:T(8,128)(2,1)S(1)}, bf16[512,512]{1,0:T(8,128)(2,1)}, u32[]{:S(2)}) copy-start(bf16[512,512]{1,0:T(8,128)(2,1)} %param.13) | copy-start | bytes 1572868
  217.3 2.1 copy-start.17
  217.3 2.1 copy-start.18
  217.3 2.1 copy-start.20
  219.4 3.1 %copy-start.14 = (bf16[512,512]{0,1:T(8,128)(2,1)S(1)}, bf16[512,512]{0,1:T(8,128)(2,1)}, u32[]{:S(2)}) copy-start(bf16[512,512]{0,1:T(8,128)(2,1)} %get-tuple-element.51) | copy-start | bytes 1572868
  221.2 2.5 %copy-start.13 = (bf16[512,512]{0,1:T(8,128)(2,1)S(1)}, bf16[512,512]{0,1:T(8,128)(2,1)}, u32[]{:S(2)}) copy-start(bf16[512,512]{0,1:T(8,128)(2,1)} %get-tuple-element.52) | copy-start | bytes 1572868
  (5 other events, 7.2 us)
Sparse Core Ops, SparseCore 0:
  150.7 66.6 all-reduce.2

commit v10 on v9

--- a/solution.py
+++ b/solution.py
@@ -13,28 +13,27 @@
 TQ = 512
 
 
-def _fwd_kernel(q_ref, k_ref, v_ref, cm_ref, numer_ref, m_ref, l_ref, *, scale):
+def _fwd_kernel(q_ref, k_ref, vt_ref, cm_ref, numer_ref, m_ref, l_ref, *, scale):
     q = q_ref[0]
     k = k_ref[0]
-    v = v_ref[0]
-    s = lax.dot_general(q, k, (((1,), (1,)), ((), ())), preferred_element_type=jnp.float32) * scale
-    tq, nk = s.shape
-    nb = tq // BLOCK
-    s3 = s.reshape(nb, BLOCK, nk)
+    vt = vt_ref[0]
+    s = lax.dot_general(k, q, (((1,), (1,)), ((), ())), preferred_element_type=jnp.float32) * scale
+    nk, tq = s.shape
+    hb = nk // BLOCK
+    s3 = s.reshape(hb, BLOCK, tq)
     allowed = cm_ref[...] > 0.5
     masked = jnp.where(allowed, s3, -1e30)
-    mx = jnp.max(masked, axis=2, keepdims=True)
-    e = jnp.where(allowed, jnp.exp(masked - mx), 0.0)
-    tot = jnp.sum(e, axis=2, keepdims=True)
-    numer = jnp.dot(
-        e.reshape(tq, nk).astype(jnp.bfloat16), v, preferred_element_type=jnp.float32
-    )
-    numer_ref[0] = numer
-    m_ref[0] = mx.reshape(tq, 1)
-    l_ref[0] = tot.reshape(tq, 1)
-
-
-def _bwd_kernel(q_ref, k_ref, v_ref, ga_ref, lt_ref, dl_ref, cm_ref, dq_ref, dk_ref, dv_ref, *, scale):
+    mx = jnp.max(jnp.max(masked, axis=0), axis=0, keepdims=True)
+    e = jnp.where(allowed, jnp.exp(masked - mx[None]), 0.0)
+    tot = jnp.sum(jnp.sum(e, axis=0), axis=0, keepdims=True)
+    numer_ref[0] = jnp.dot(
+        vt, e.reshape(nk, tq).astype(jnp.bfloat16), preferred_element_type=jnp.float32
+    )
+    m_ref[0] = mx
+    l_ref[0] = tot
+
+
+def _bwd_kernel(q_ref, k_ref, v_ref, kt_ref, ga_ref, lt_ref, dl_ref, cm_ref, dq_ref, dk_ref, dv_ref, *, scale):
     i = pl.program_id(1)
 
     @pl.when(i == 0)
@@ -46,28 +45,23 @@
     k = k_ref[0]
     v = v_ref[0]
     ga = ga_ref[0]
-    s = lax.dot_general(q, k, (((1,), (1,)), ((), ())), preferred_element_type=jnp.float32) * scale
-    tq, nk = s.shape
-    nb = tq // BLOCK
-    s3 = s.reshape(nb, BLOCK, nk)
+    s = lax.dot_general(k, q, (((1,), (1,)), ((), ())), preferred_element_type=jnp.float32) * scale
+    nk, tq = s.shape
+    hb = nk // BLOCK
+    s3 = s.reshape(hb, BLOCK, tq)
     allowed = cm_ref[...] > 0.5
-    lt = lt_ref[0].reshape(nb, BLOCK, 1)
-    p = jnp.where(allowed, jnp.exp(s3 - lt), 0.0).reshape(tq, nk)
-    dv_ref[0] += lax.dot_general(
-        p.astype(jnp.bfloat16), ga, (((0,), (0,)), ((), ())), preferred_element_type=jnp.float32
-    )
-    dp = lax.dot_general(ga, v, (((1,), (1,)), ((), ())), preferred_element_type=jnp.float32)
+    p = jnp.where(allowed, jnp.exp(s3 - lt_ref[...]), 0.0).reshape(nk, tq)
+    dv_ref[0] += jnp.dot(p.astype(jnp.bfloat16), ga, preferred_element_type=jnp.float32)
+    dp = lax.dot_general(v, ga, (((1,), (1,)), ((), ())), preferred_element_type=jnp.float32)
     ds = (p * (dp - dl_ref[0]) * scale).astype(jnp.bfloat16)
-    dq_ref[0] = jnp.dot(ds, k, preferred_element_type=jnp.float32)
-    dk_ref[0] += lax.dot_general(
-        ds, q, (((0,), (0,)), ((), ())), preferred_element_type=jnp.float32
-    )
-
-
-def _forward(qT, kT, vT, cm, scale):
+    dk_ref[0] += jnp.dot(ds, q, preferred_element_type=jnp.float32)
+    dq_ref[0] = jnp.dot(kt_ref[0], ds, preferred_element_type=jnp.float32)
+
+
+def _forward(qT, kT, vTT, cm, scale):
     heads, nq, hd = qT.shape
     nk = kT.shape[1]
-    nb = TQ // BLOCK
+    hb = nk // BLOCK
     f32 = jnp.float32
     return pl.pallas_call(
         functools.partial(_fwd_kernel, scale=scale),
@@ -75,27 +69,28 @@
         in_specs=[
             pl.BlockSpec((1, TQ, hd), lambda h, i: (h, i, 0)),
             pl.BlockSpec((1, nk, hd), lambda h, i: (h, 0, 0)),
-            pl.BlockSpec((1, nk, hd), lambda h, i: (h, 0, 0)),
-            pl.BlockSpec((nb, 1, nk), lambda h, i: (i, 0, 0)),
+            pl.BlockSpec((1, hd, nk), lambda h, i: (h, 0, 0)),
+            pl.BlockSpec((hb, 1, TQ), lambda h, i: (0, 0, i)),
         ],
         out_specs=[
-            pl.BlockSpec((1, TQ, hd), lambda h, i: (h, i, 0)),
-            pl.BlockSpec((1, TQ, 1), lambda h, i: (h, i, 0)),
-            pl.BlockSpec((1, TQ, 1), lambda h, i: (h, i, 0)),
+            pl.BlockSpec((1, hd, TQ), lambda h, i: (h, 0, i)),
+            pl.BlockSpec((1, 1, TQ), lambda h, i: (h, 0, i)),
+            pl.BlockSpec((1, 1, TQ), lambda h, i: (h, 0, i)),
         ],
         out_shape=[
-            jax.ShapeDtypeStruct((heads, nq, hd), f32),
-            jax.ShapeDtypeStruct((heads, nq, 1), f32),
-            jax.ShapeDtypeStruct((heads, nq, 1), f32),
-        ],
-    )(qT, kT, vT, cm)
-
-
-def _backward(qT, kT, vT, gaT, lt, dl, cm, scale):
+            jax.ShapeDtypeStruct((heads, hd, nq), f32),
+            jax.ShapeDtypeStruct((heads, 1, nq), f32),
+            jax.ShapeDtypeStruct((heads, 1, nq), f32),
+        ],
+        compiler_params=pltpu.CompilerParams(vmem_limit_bytes=48 * 1024 * 1024),
+    )(qT, kT, vTT, cm)
+
+
+def _backward(qT, kT, vT, kTT, gaT, lt, dl, cm, scale):
     heads, nq, hd = qT.shape
     nk = kT.shape[1]
+    hb = nk // BLOCK
     tile = min(nq, 2 * TQ)
-    nb = tile // BLOCK
     f32 = jnp.float32
     return pl.pallas_call(
         functools.partial(_bwd_kernel, scale=scale),
@@ -104,25 +99,26 @@
             pl.BlockSpec((1, tile, hd), lambda h, i: (h, i, 0)),
             pl.BlockSpec((1, nk, hd), lambda h, i: (h, 0, 0)),
             pl.BlockSpec((1, nk, hd), lambda h, i: (h, 0, 0)),
+            pl.BlockSpec((1, hd, nk), lambda h, i: (h, 0, 0)),
             pl.BlockSpec((1, tile, hd), lambda h, i: (h, i, 0)),
-            pl.BlockSpec((1, tile, 1), lambda h, i: (h, i, 0)),
-            pl.BlockSpec((1, tile, 1), lambda h, i: (h, i, 0)),
-            pl.BlockSpec((nb, 1, nk), lambda h, i: (i, 0, 0)),
+            pl.BlockSpec((1, 1, tile), lambda h, i: (h, 0, i)),
+            pl.BlockSpec((1, 1, tile), lambda h, i: (h, 0, i)),
+            pl.BlockSpec((hb, 1, tile), lambda h, i: (0, 0, i)),
         ],
         out_specs=[
-            pl.BlockSpec((1, tile, hd), lambda h, i: (h, i, 0)),
+            pl.BlockSpec((1, hd, tile), lambda h, i: (h, 0, i)),
             pl.BlockSpec((1, nk, hd), lambda h, i: (h, 0, 0)),
             pl.BlockSpec((1, nk, hd), lambda h, i: (h, 0, 0)),
         ],
         out_shape=[
-            jax.ShapeDtypeStruct((heads, nq, hd), f32),
+            jax.ShapeDtypeStruct((heads, hd, nq), f32),
             jax.ShapeDtypeStruct((heads, nk, hd), f32),
             jax.ShapeDtypeStruct((heads, nk, hd), f32),
         ],
         compiler_params=pltpu.CompilerParams(
             dimension_semantics=("parallel", "arbitrary"), vmem_limit_bytes=48 * 1024 * 1024
         ),
-    )(qT, kT, vT, gaT, lt, dl, cm)
+    )(qT, kT, vT, kTT, gaT, lt, dl, cm)
 
 
 def on_device(queries_in, hits_in, w_query, w_key, w_value, w_out, mask_list, grad_out):
@@ -137,7 +133,7 @@
     q_blocks = n_queries // BLOCK
     local_ids = region_index * hit_blocks + jnp.arange(hit_blocks, dtype=jnp.int32)
     blockmask = jnp.any(mask_list[:, :, None] == local_ids[None, None, :], axis=1)
-    cm = jnp.repeat(blockmask.astype(f32), BLOCK, axis=1).reshape(q_blocks, 1, n_hits)
+    cm = jnp.repeat(blockmask.T.astype(f32), BLOCK, axis=1).reshape(hit_blocks, 1, n_queries)
 
     def heads(x):
         return x.reshape(x.shape[0], HEADS, head_dim).transpose(1, 0, 2)
@@ -151,8 +147,8 @@
     qT, kT, vT = heads(query), heads(keys), heads(vals)
 
     regions = lax.axis_size("region")
-    numer_r, max_r, total_r = _forward(qT, kT, vT, cm, scale)
-    numer = joined(numer_r)
+    numer_r, max_r, total_r = _forward(qT, kT, vT.transpose(0, 2, 1), cm, scale)
+    numer = numer_r.transpose(2, 0, 1).reshape(n_queries, width)
     peak = max_r.reshape(HEADS, n_queries)
     total = total_r.reshape(HEADS, n_queries)
     rows = n_queries
@@ -210,21 +206,21 @@
             jnp.concatenate([lo[1], hi[1]], axis=1),
         )
     attended = gathered[0]
-    log_total = gathered[1][:HEADS].reshape(HEADS, n_queries, 1)
-    deltas = gathered[1][HEADS:].reshape(HEADS, n_queries, 1)
+    log_total = gathered[1][:HEADS].reshape(HEADS, 1, n_queries)
+    deltas = gathered[1][HEADS:].reshape(HEADS, 1, n_queries)
     layer_out = (
         queries_in.astype(f32) + jnp.dot(attended, w_out, preferred_element_type=f32)
     ).astype(bf16)
     grad_wo = jnp.einsum("qa,qb->ab", attended, grad_out, preferred_element_type=f32)
     gaT = heads(grad_att)
 
-    dq_r, dk, dv = _backward(qT, kT, vT, gaT, log_total, deltas, cm, scale)
+    dq_r, dk, dv = _backward(qT, kT, vT, kT.transpose(0, 2, 1), gaT, log_total, deltas, cm, scale)
     keys_grad = joined(dk).astype(bf16)
     vals_grad = joined(dv).astype(bf16)
     wk_part = jnp.einsum("ka,kb->ab", hits_in, keys_grad, preferred_element_type=f32)
     wv_part = jnp.einsum("ka,kb->ab", hits_in, vals_grad, preferred_element_type=f32)
     query_grad_sum, grad_wk, grad_wv = lax.psum(
-        (joined(dq_r).astype(bf16), wk_part.astype(bf16), wv_part.astype(bf16)), "region"
+        (dq_r.transpose(2, 0, 1).reshape(n_queries, width).astype(bf16), wk_part.astype(bf16), wv_part.astype(bf16)), "region"
     )
     grad_wk = grad_wk.astype(f32)
     grad_wv = grad_wv.astype(f32)

time: 232 us -> 212 us (0.914)
  local copies, waits for them, and re-layouts: 34.5 us -> 23.5 us
  Pallas kernels: 57.2 us -> 46.3 us
  matrix products: 20.6 us -> 24.4 us
  waiting for transfers between devices: 84.2 us -> 80.4 us
    pallas_call x1, Pallas kernels: 28 us -> 20.4 us  [_forward(): pl.pallas_call(functools.partial(_fwd_kernel, scale=scale), grid=(heads,...]
    reshape x2, local copies, waits for them, and re-layouts: 5.36 us -> 0.06 us  [the longest x1 0.04 us: on_device(): log_total = gathered[1][:HEADS].reshape(HEADS, 1, n_queries)]
    dynamic_slice x1, local copies, waits for them, and re-layouts: 3.53 us -> 0.02 us  [on_device(): lax.dynamic_slice_in_dim(peak, bit * half, half, 1)]
    pallas_call x1, Pallas kernels: 29.2 us -> 26 us  [_backward(): pl.pallas_call(functools.partial(_bwd_kernel, scale=scale), grid=(heads,...]
    ppermute x9, waiting for transfers between devices: 17 us -> 14 us  [on_device(): lax.ppermute((lax.dynamic_slice_in_dim(numer, (1 - bit) * half, half, 0)....]
    unnamed x45 -> x47, local copies, waits for them, and re-layouts: 6.82 us -> 8.58 us
    reshape x4 -> x3, local copies, waits for them, and re-layouts: 7.23 us -> 7.54 us  [heads(): return x.reshape(x.shape[0], HEADS, head_dim).transpose(1, 0, 2)]
  transfers between devices with their start and end apart: 16 -> 16, of which waited for: 8 -> 7; matrix products, arithmetic and copies ran while one was open for 18% -> 16% of each run, Pallas kernels for 13% -> 12%
where the time goes in v10:
time: 212 us
  waiting for transfers between devices  80.4 us (38%)
  Pallas kernels  46.3 us (22%)
  matrix products  24.4 us (12%)
  local copies, waits for them, and re-layouts  23.5 us (11%)
  between operations  14.4 us (7%)
  other arithmetic  11.7 us (6%)
  starting transfers between devices  10.9 us (5%)
    psum x1, waiting for transfers between devices, on_device(): lax.psum((dq_r.transpose(2, 0, 1).reshape(n_queries, width).astype(bf16),...  52.7 us
    pallas_call x1, Pallas kernels, _backward(): pl.pallas_call(functools.partial(_bwd_kernel, scale=scale), grid=(heads,...  26 us
    pallas_call x1, Pallas kernels, _forward(): pl.pallas_call(functools.partial(_fwd_kernel, scale=scale), grid=(heads,...  20.4 us
    ppermute x9, waiting for transfers between devices, on_device(): lax.ppermute((lax.dynamic_slice_in_dim(numer, (1 - bit) * half, half, 0)....  14 us
    ppermute x6, waiting for transfers between devices, on_device(): other = lax.ppermute(gathered, 'region', pairs)  13.6 us
    ppermute x9, starting transfers between devices, on_device(): lax.ppermute((lax.dynamic_slice_in_dim(numer, (1 - bit) * half, half, 0)....  8.72 us
    unnamed x47, local copies, waits for them, and re-layouts  8.58 us
    reshape x3, local copies, waits for them, and re-layouts, heads(): return x.reshape(x.shape[0], HEADS, head_dim).transpose(1, 0, 2)  7.54 us
  transfers between devices with their start and end apart: 16, of which 7 were waited for; matrix products, arithmetic and copies ran while one was open for 16% of the time, Pallas kernels for 12%

profile of v10, /device:TPU:0, one launch (start us, length us, event | category | flops | bytes accessed | tf_op | source)
XLA Modules:
  0.0 211.6 jit_solution(5586796573530888811)
XLA Ops:
  8.4 1.8 convolution_convert_fusion.2
  10.2 1.8 copy.35.k_ref
  12.2 2.8 %convolution_convert_fusion.3 = bf16[1024,512]{0,1:T(8,128)(2,1)} fusion(bf16[1024,512]{1,0:T(8,128)(2,1)S(1)} %copy-done.14, bf16[512,512]{1,0:T(8,128)(2,1)} %param.10), kind=kOutput, calls=%fused_computation.8 | convolution fusion | flops 537395200 | bytes 2621440 | tf_op jit(solution)/shard_map/dot_general | solution.py:144
  15.0 2.0 copy.33
  17.0 2.8 %convolution_convert_fusion.1 = bf16[1024,512]{0,1:T(8,128)(2,1)} fusion(bf16[1024,512]{1,0:T(8,128)(2,1)S(1)} %copy-done, bf16[512,512]{1,0:T(8,128)(2,1)} %param.12), kind=kOutput, calls=%fused_computation.6 | convolution fusion | flops 537395200 | bytes 2621440 | tf_op jit(solution)/shard_map/dot_general | solution.py:146
  21.1 20.4 %shard_map.135 = (f32[8,64,1024]{2,1,0:T(8,128)S(1)}, f32[8,1,1024]{2,1,0:T(1,128)S(1)}, f32[8,1,1024]{2,1,0:T(1,128)S(1)}) custom-call(bf16[8,1024,64]{2,1,0:T(8,128)(2,1)S(1)} %bitcast.133, bf16[8,1024,64]{2,1,0:T(8,128)(2,1)} %copy.35.k_ref, bf16[8,64,1024]{2,1,0:T(8,128)(2,1)S(1)} %bitcast.138, f32[8,1,1024]{2,1,0:T(1,128)S(1)} %bitcast.141), custom_call_target="tpu_custom_call" | custom-call | tf_op jit(solution)/shard_map/pallas_call | solution.py:66
  44.2 2.6 %collective-permute-start.2 = (f32[8,256]{1,0:T(8,128)S(1)}, f32[8,256]{1,0:T(8,128)S(1)}, u32[]{:S(2)}, u32[]{:S(2)}) collective-permute-start(f32[8,256]{1,0:T(8,128)S(1)} %constant_dynamic-slice_fusion.7), channel_id=1, source_target_pairs={{0,2},{1,3},{2,0},{3,1},{4,6},{5,7},{6,4},{7,5},{8,10},{9,11},{10,... | collective-permute-start | bytes 24584 | tf_op jit(solution)/shard_map/ppermute | solution.py:167
  46.9 3.1 %convolution_convert_fusion = bf16[1024,512]{0,1:T(8,128)(2,1)} fusion(bf16[1024,512]{1,0:T(8,128)(2,1)} %param.15, bf16[512,512]{1,0:T(8,128)(2,1)} %param.13), kind=kOutput, calls=%fused_computation.5 | convolution fusion | flops 537395200 | bytes 2621440 | tf_op jit(solution)/shard_map/dot_general | solution.py:190
  50.5 2.6 %collective-permute-start.8 = (f32[8,128]{1,0:T(8,128)S(1)}, f32[8,128]{1,0:T(8,128)S(1)}, u32[]{:S(2)}, u32[]{:S(2)}) collective-permute-start(f32[8,128]{1,0:T(8,128)S(1)} %constant_dynamic-slice_fusion), channel_id=1, source_target_pairs={{0,4},{1,5},{2,6},{3,7},{4,0},{5,1},{6,2},{7,3},{8,12},{9,13},{10,... | collective-permute-start | bytes 12296 | tf_op jit(solution)/shard_map/ppermute | solution.py:167
  53.2 1.6 fusion.2
  54.8 1.5 collective-permute-start.3
  56.7 6.0 %collective-permute-done.3 = bf16[256,512]{0,1:T(8,128)(2,1)S(1)} collective-permute-done((bf16[256,512]{0,1:T(8,128)(2,1)S(1)}, bf16[256,512]{0,1:T(8,128)(2,1)S(1)}, u32[]{:S(2)}, u32[]{:S(2)}) %collective-permute-start.3) | collective-permute-done | bytes 262176 | tf_op jit(solution)/shard_map/ppermute | solution.py:167
  63.2 7.5 %collective-permute-done.5 = bf16[128,512]{0,1:T(8,128)(2,1)S(1)} collective-permute-done((bf16[128,512]{0,1:T(8,128)(2,1)S(1)}, bf16[128,512]{0,1:T(8,128)(2,1)S(1)}, u32[]{:S(2)}, u32[]{:S(2)}) %collective-permute-start.5) | collective-permute-done | bytes 131104 | tf_op jit(solution)/shard_map/ppermute | solution.py:167
  71.8 4.5 %collective-permute-done.12 = f32[16,128]{1,0:T(8,128)S(1)} collective-permute-done((f32[16,128]{1,0:T(8,128)S(1)}, f32[16,128]{1,0:T(8,128)S(1)}, u32[]{:S(2)}, u32[]{:S(2)}) %collective-permute-start.12) | collective-permute-done | bytes 8224 | tf_op jit(solution)/shard_map/ppermute | solution.py:201
  76.4 3.7 %collective-permute-done.13 = f32[16,256]{1,0:T(8,128)S(1)} collective-permute-done((f32[16,256]{1,0:T(8,128)S(1)}, f32[16,256]{1,0:T(8,128)S(1)}, u32[]{:S(2)}, u32[]{:S(2)}) %collective-permute-start.13) | collective-permute-done | bytes 16416 | tf_op jit(solution)/shard_map/ppermute | solution.py:201
  80.3 2.8 %copy.36 = bf16[1024,8,64]{2,0,1:T(8,128)(2,1)} copy(bf16[1024,8,64]{0,2,1:T(8,128)(2,1)} %bitcast.137) | data formatting | bytes 2097152 | tf_op jit(solution)/shard_map/reshape | solution.py:139
  83.1 2.7 %copy.37 = bf16[1024,8,64]{2,0,1:T(8,128)(2,1)} copy(bf16[1024,8,64]{0,2,1:T(8,128)(2,1)} %bitcast.150) | data formatting | bytes 2097152 | tf_op jit(solution)/shard_map/reshape | solution.py:139
  87.1 26.0 %shard_map.136 = (f32[8,64,1024]{2,1,0:T(8,128)S(1)}, f32[8,1024,64]{2,1,0:T(8,128)}, f32[8,1024,64]{2,1,0:T(8,128)}) custom-call(bf16[8,1024,64]{2,1,0:T(8,128)(2,1)S(1)} %bitcast.134, bf16[8,1024,64]{2,1,0:T(8,128)(2,1)} %copy.35.k_ref, bf16[8,1024,64]{2,1,0:T(8,128)(2,1)} %bitcast.143, bf16[8,64,1024]{2,1,0:T(8,128)(2,1)S(1)} %bitcast.136, ...), custom_call_target="tpu_custom_call" | custom-call | tf_op jit(solution)/shard_map/pallas_call | solution.py:95
  113.1 6.4 %convert_bitcast_fusion = (bf16[1024,8,64]{2,0,1:T(8,128)(2,1)}, bf16[1024,8,64]{2,0,1:T(8,128)(2,1)S(1)}) fusion(f32[8,1024,64]{2,1,0:T(8,128)} %get-tuple-element.18, f32[8,1024,64]{2,1,0:T(8,128)} %get-tuple-element.17), kind=kLoop, calls=%fused_computation.1 | loop fusion | flops 1048576 | bytes 6291456 | tf_op jit(solution)/shard_map/convert_element_type | solution.py:219
  119.5 1.6 copy.40
  121.1 2.7 %fusion = bf16[512,512]{0,1:T(8,128)(2,1)} fusion(bf16[1024,512]{0,1:T(8,128)(2,1)} %bitcast.145, bf16[1024,512]{1,0:T(8,128)(2,1)S(1)} %copy-done), kind=kOutput, calls=%fused_computation.12 | convolution fusion | flops 537133056 | bytes 2621440 | tf_op jit(solution)/shard_map/ka,kb->ab/dot_general | solution.py:220
  123.8 2.8 %copy.41 = bf16[1024,8,64]{0,2,1:T(8,128)(2,1)} copy(bf16[1024,8,64]{2,0,1:T(8,128)(2,1)} %get-tuple-element.75) | data formatting | bytes 2097152 | tf_op jit(solution)/shard_map/convert_element_type | solution.py:219
  127.8 1.8 collective-permute-start.10
  129.7 1.5 fusion.1
  131.2 5.4 %collective-permute-done.10 = bf16[256,512]{0,1:T(8,128)(2,1)S(1)} collective-permute-done((bf16[256,512]{0,1:T(8,128)(2,1)S(1)}, bf16[256,512]{0,1:T(8,128)(2,1)S(1)}, u32[]{:S(2)}, u32[]{:S(2)}) %collective-permute-start.10) | collective-permute-done | bytes 262176 | tf_op jit(solution)/shard_map/ppermute | solution.py:201
  138.1 1.7 add_convert_fusion
  141.1 1.7 fusion.3
  142.8 1.7 add_convert_fusion.2
  144.5 52.7 %all-reduce.3.cloned.1.call-done = (bf16[512,512]{0,1:T(8,128)(2,1)}, bf16[512,512]{0,1:T(8,128)(2,1)}, bf16[1024,512]{0,1:T(8,128)(2,1)}) async-done(((bf16[512,512]{0,1:T(8,128)(2,1)}, bf16[512,512]{0,1:T(8,128)(2,1)}, bf16[1024,512]{0,1:T(8,128)(2,1)}), (bf16[512,512]{0,1:T(8,128)(2,1)}, bf16[512,512]{0,1:T(8,128)(2,1)}, bf16[1024,512]{0,1:T(8,128)(2,1)})) %all-reduce.3.cloned.1.call-update) | async-done | bytes 2097168 | tf_op jit(solution)/shard_map/psum | solution.py:222
  197.3 2.1 convolution_bitcast_fusion
  199.4 1.7 add_convert_fusion.1
  201.1 1.3 copy.42
  (105 shorter events, 15.8 us)
Async XLA Ops:
  7.2 190.1 %all-reduce.3.cloned.1.call-start = ((), (), s32[]{:S(2)}) async-start(), calls=%async_computation | async-start | bytes 4194304 | tf_op jit(solution)/shard_map/psum | solution.py:222
  10.2 4.8 %copy-start.1 = (bf16[1024,512]{0,1:T(8,128)(2,1)}, bf16[1024,512]{0,1:T(8,128)(2,1)S(1)}, u32[]{:S(2)}) copy-start(bf16[1024,512]{0,1:T(8,128)(2,1)S(1)} %convolution_convert_fusion.2) | copy-start | bytes 3145732
  10.2 2.0 copy-start.14
  41.5 1.3 copy-start.6
  41.5 2.7 %collective-permute-start = (f32[8,512]{1,0:T(8,128)S(1)}, f32[8,512]{1,0:T(8,128)S(1)}, u32[]{:S(2)}, u32[]{:S(2)}) collective-permute-start(f32[8,512]{1,0:T(8,128)S(1)} %bitcast.154), channel_id=1, source_target_pairs={{0,1},{1,0},{2,3},{3,2},{4,5},{5,4},{6,7},{7,6},{8,9},{9,8},{10,11... | collective-permute-start | bytes 49160 | tf_op jit(solution)/shard_map/ppermute | solution.py:167
  42.1 2.1 collective-permute-start.6
  43.7 9.5 %collective-permute-start.1 = (bf16[512,512]{0,1:T(8,128)(2,1)}, bf16[512,512]{0,1:T(8,128)(2,1)}, u32[]{:S(2)}, u32[]{:S(2)}) collective-permute-start(bf16[512,512]{0,1:T(8,128)(2,1)} %dynamic-slice_convert_fusion), channel_id=1, source_target_pairs={{0,1},{1,0},{2,3},{3,2},{4,5},{5,4},{6,7},{7,6},{8,9},{9,8},{10,11... | collective-permute-start | bytes 1572872 | tf_op jit(solution)/shard_map/ppermute | solution.py:167
  44.2 5.8 %collective-permute-start.2 = (f32[8,256]{1,0:T(8,128)S(1)}, f32[8,256]{1,0:T(8,128)S(1)}, u32[]{:S(2)}, u32[]{:S(2)}) collective-permute-start(f32[8,256]{1,0:T(8,128)S(1)} %constant_dynamic-slice_fusion.7), channel_id=1, source_target_pairs={{0,2},{1,3},{2,0},{3,1},{4,6},{5,7},{6,4},{7,5},{8,10},{9,11},{10,... | collective-permute-start | bytes 24584 | tf_op jit(solution)/shard_map/ppermute | solution.py:167
  46.8 3.7 %collective-permute-start.7 = (f32[8,256]{1,0:T(8,128)S(1)}, f32[8,256]{1,0:T(8,128)S(1)}, u32[]{:S(2)}, u32[]{:S(2)}) collective-permute-start(f32[8,256]{1,0:T(8,128)S(1)} %constant_dynamic-slice_fusion.2), channel_id=1, source_target_pairs={{0,2},{1,3},{2,0},{3,1},{4,6},{5,7},{6,4},{7,5},{8,10},{9,11},{10,... | collective-permute-start | bytes 24584 | tf_op jit(solution)/shard_map/ppermute | solution.py:167
  50.5 12.6 %collective-permute-start.8 = (f32[8,128]{1,0:T(8,128)S(1)}, f32[8,128]{1,0:T(8,128)S(1)}, u32[]{:S(2)}, u32[]{:S(2)}) collective-permute-start(f32[8,128]{1,0:T(8,128)S(1)} %constant_dynamic-slice_fusion), channel_id=1, source_target_pairs={{0,4},{1,5},{2,6},{3,7},{4,0},{5,1},{6,2},{7,3},{8,12},{9,13},{10,... | collective-permute-start | bytes 12296 | tf_op jit(solution)/shard_map/ppermute | solution.py:167
  54.8 7.9 %collective-permute-start.3 = (bf16[256,512]{0,1:T(8,128)(2,1)S(1)}, bf16[256,512]{0,1:T(8,128)(2,1)S(1)}, u32[]{:S(2)}, u32[]{:S(2)}) collective-permute-start(bf16[256,512]{0,1:T(8,128)(2,1)S(1)} %dynamic-slice_convert_fusion.1), channel_id=1, source_target_pairs={{0,2},{1,3},{2,0},{3,1},{4,6},{5,7},{6,4},{7,5},{8,10},{9,11},{10,... | collective-permute-start | bytes 786440 | tf_op jit(solution)/shard_map/ppermute | solution.py:167
  56.3 6.9 %collective-permute-start.4 = (f32[8,128]{1,0:T(8,128)S(1)}, f32[8,128]{1,0:T(8,128)S(1)}, u32[]{:S(2)}, u32[]{:S(2)}) collective-permute-start(f32[8,128]{1,0:T(8,128)S(1)} %constant_dynamic-slice_fusion.5), channel_id=1, source_target_pairs={{0,4},{1,5},{2,6},{3,7},{4,0},{5,1},{6,2},{7,3},{8,12},{9,13},{10,... | collective-permute-start | bytes 12296 | tf_op jit(solution)/shard_map/ppermute | solution.py:167
  62.8 7.9 %collective-permute-start.5 = (bf16[128,512]{0,1:T(8,128)(2,1)S(1)}, bf16[128,512]{0,1:T(8,128)(2,1)S(1)}, u32[]{:S(2)}, u32[]{:S(2)}) collective-permute-start(bf16[128,512]{0,1:T(8,128)(2,1)S(1)} %dynamic-slice_convert_fusion.2), channel_id=1, source_target_pairs={{0,4},{1,5},{2,6},{3,7},{4,0},{5,1},{6,2},{7,3},{8,12},{9,13},{10,... | collective-permute-start | bytes 393224 | tf_op jit(solution)/shard_map/ppermute | solution.py:167
  71.7 4.6 %collective-permute-start.12 = (f32[16,128]{1,0:T(8,128)S(1)}, f32[16,128]{1,0:T(8,128)S(1)}, u32[]{:S(2)}, u32[]{:S(2)}) collective-permute-start(f32[16,128]{1,0:T(8,128)S(1)} %pad_maximum_fusion.8), channel_id=1, source_target_pairs={{0,4},{1,5},{2,6},{3,7},{4,0},{5,1},{6,2},{7,3},{8,12},{9,13},{10,... | collective-permute-start | bytes 24584 | tf_op jit(solution)/shard_map/ppermute | solution.py:201
  76.4 3.8 %collective-permute-start.13 = (f32[16,256]{1,0:T(8,128)S(1)}, f32[16,256]{1,0:T(8,128)S(1)}, u32[]{:S(2)}, u32[]{:S(2)}) collective-permute-start(f32[16,256]{1,0:T(8,128)S(1)} %pad_maximum_fusion.7), channel_id=1, source_target_pairs={{0,2},{1,3},{2,0},{3,1},{4,6},{5,7},{6,4},{7,5},{8,10},{9,11},{10,... | collective-permute-start | bytes 49160 | tf_op jit(solution)/shard_map/ppermute | solution.py:201
  80.2 5.6 %collective-permute-start.14 = (f32[16,512]{1,0:T(8,128)S(1)}, f32[16,512]{1,0:T(8,128)S(1)}, u32[]{:S(2)}, u32[]{:S(2)}) collective-permute-start(f32[16,512]{1,0:T(8,128)S(1)} %pad_maximum_fusion.6), channel_id=1, source_target_pairs={{0,1},{1,0},{2,3},{3,2},{4,5},{5,4},{6,7},{7,6},{8,9},{9,8},{10,11... | collective-permute-start | bytes 98312 | tf_op jit(solution)/shard_map/ppermute | solution.py:201
  85.8 42.0 %collective-permute-start.9 = (bf16[128,512]{0,1:T(8,128)(2,1)S(1)}, bf16[128,512]{0,1:T(8,128)(2,1)S(1)}, u32[]{:S(2)}, u32[]{:S(2)}) collective-permute-start(bf16[128,512]{0,1:T(8,128)(2,1)S(1)} %get-tuple-element.44), channel_id=1, source_target_pairs={{0,4},{1,5},{2,6},{3,7},{4,0},{5,1},{6,2},{7,3},{8,12},{9,13},{10,... | collective-permute-start | bytes 393224 | tf_op jit(solution)/shard_map/ppermute | solution.py:201
  113.1 6.4 %copy-start.4 = (f32[8,64,1024]{2,1,0:T(8,128)}, f32[8,64,1024]{2,1,0:T(8,128)S(1)}, u32[]{:S(2)}) copy-start(f32[8,64,1024]{2,1,0:T(8,128)S(1)} %get-tuple-element.16) | copy-start | bytes 6291460
  123.8 2.8 %copy-start.5 = (f32[8,64,1024]{2,1,0:T(8,128)S(1)}, f32[8,64,1024]{2,1,0:T(8,128)}, u32[]{:S(2)}) copy-start(f32[8,64,1024]{2,1,0:T(8,128)} %copy-done.4) | copy-start | bytes 6291460
  126.6 3.0 %copy-start.8 = (bf16[1024,8,64]{0,2,1:T(8,128)(2,1)S(1)}, bf16[1024,8,64]{0,2,1:T(8,128)(2,1)}, u32[]{:S(2)}) copy-start(bf16[1024,8,64]{0,2,1:T(8,128)(2,1)} %copy.41) | copy-start | bytes 3145732
  127.8 8.8 %collective-permute-start.10 = (bf16[256,512]{0,1:T(8,128)(2,1)S(1)}, bf16[256,512]{0,1:T(8,128)(2,1)S(1)}, u32[]{:S(2)}, u32[]{:S(2)}) collective-permute-start(bf16[256,512]{0,1:T(8,128)(2,1)S(1)} %pad_maximum_fusion.4), channel_id=1, source_target_pairs={{0,2},{1,3},{2,0},{3,1},{4,6},{5,7},{6,4},{7,5},{8,10},{9,11},{10,... | collective-permute-start | bytes 786440 | tf_op jit(solution)/shard_map/ppermute | solution.py:201
  131.2 5.7 %copy-start.7 = (bf16[1024,8,64]{0,2,1:T(8,128)(2,1)S(1)}, bf16[1024,8,64]{0,2,1:T(8,128)(2,1)}, u32[]{:S(2)}) copy-start(bf16[1024,8,64]{0,2,1:T(8,128)(2,1)} %copy.40) | copy-start | bytes 3145732
  131.2 5.7 %copy-start.10 = (bf16[512,512]{1,0:T(8,128)(2,1)S(1)}, bf16[512,512]{1,0:T(8,128)(2,1)}, u32[]{:S(2)}) copy-start(bf16[512,512]{1,0:T(8,128)(2,1)} %param.11) | copy-start | bytes 1572868
  136.8 1.4 copy-start.11
  136.8 3.1 %collective-permute-start.11 = (bf16[512,512]{0,1:T(8,128)(2,1)S(1)}, bf16[512,512]{0,1:T(8,128)(2,1)S(1)}, u32[]{:S(2)}, u32[]{:S(2)}) collective-permute-start(bf16[512,512]{0,1:T(8,128)(2,1)S(1)} %pad_maximum_fusion.3), channel_id=1, source_target_pairs={{0,1},{1,0},{2,3},{3,2},{4,5},{5,4},{6,7},{7,6},{8,9},{9,8},{10,11... | collective-permute-start | bytes 1572872 | tf_op jit(solution)/shard_map/ppermute | solution.py:201
  140.1 2.7 %copy-start.15 = (bf16[1024,512]{1,0:T(8,128)(2,1)S(1)}, bf16[1024,512]{1,0:T(8,128)(2,1)}, u32[]{:S(2)}) copy-start(bf16[1024,512]{1,0:T(8,128)(2,1)} %param.8) | copy-start | bytes 3145732
  140.1 2.7 %copy-start.19 = (bf16[512,512]{1,0:T(8,128)(2,1)S(1)}, bf16[512,512]{1,0:T(8,128)(2,1)}, u32[]{:S(2)}) copy-start(bf16[512,512]{1,0:T(8,128)(2,1)} %param.13) | copy-start | bytes 1572868
  197.3 2.1 copy-start.17
  197.3 2.1 copy-start.18
  197.3 2.1 copy-start.20
  199.4 3.1 %copy-start.13 = (bf16[512,512]{0,1:T(8,128)(2,1)S(1)}, bf16[512,512]{0,1:T(8,128)(2,1)}, u32[]{:S(2)}) copy-start(bf16[512,512]{0,1:T(8,128)(2,1)} %get-tuple-element.40) | copy-start | bytes 1572868
  201.1 2.5 %copy-start.12 = (bf16[512,512]{0,1:T(8,128)(2,1)S(1)}, bf16[512,512]{0,1:T(8,128)(2,1)}, u32[]{:S(2)}) copy-start(bf16[512,512]{0,1:T(8,128)(2,1)} %get-tuple-element.41) | copy-start | bytes 1572868
  (5 other events, 6.2 us)
Sparse Core Ops, SparseCore 0:
  131.3 65.8 all-reduce.2

commit v11 on v10

--- a/solution.py
+++ b/solution.py
@@ -62,20 +62,21 @@
     heads, nq, hd = qT.shape
     nk = kT.shape[1]
     hb = nk // BLOCK
+    tile = min(nq, 2 * TQ)
     f32 = jnp.float32
     return pl.pallas_call(
         functools.partial(_fwd_kernel, scale=scale),
-        grid=(heads, nq // TQ),
+        grid=(heads, nq // tile),
         in_specs=[
-            pl.BlockSpec((1, TQ, hd), lambda h, i: (h, i, 0)),
+            pl.BlockSpec((1, tile, hd), lambda h, i: (h, i, 0)),
             pl.BlockSpec((1, nk, hd), lambda h, i: (h, 0, 0)),
             pl.BlockSpec((1, hd, nk), lambda h, i: (h, 0, 0)),
-            pl.BlockSpec((hb, 1, TQ), lambda h, i: (0, 0, i)),
+            pl.BlockSpec((hb, 1, tile), lambda h, i: (0, 0, i)),
         ],
         out_specs=[
-            pl.BlockSpec((1, hd, TQ), lambda h, i: (h, 0, i)),
-            pl.BlockSpec((1, 1, TQ), lambda h, i: (h, 0, i)),
-            pl.BlockSpec((1, 1, TQ), lambda h, i: (h, 0, i)),
+            pl.BlockSpec((1, hd, tile), lambda h, i: (h, 0, i)),
+            pl.BlockSpec((1, 1, tile), lambda h, i: (h, 0, i)),
+            pl.BlockSpec((1, 1, tile), lambda h, i: (h, 0, i)),
         ],
         out_shape=[
             jax.ShapeDtypeStruct((heads, hd, nq), f32),
@@ -208,6 +209,7 @@
     attended = gathered[0]
     log_total = gathered[1][:HEADS].reshape(HEADS, 1, n_queries)
     deltas = gathered[1][HEADS:].reshape(HEADS, 1, n_queries)
+    attended, log_total, deltas = lax.optimization_barrier((attended, log_total, deltas))
     layer_out = (
         queries_in.astype(f32) + jnp.dot(attended, w_out, preferred_element_type=f32)
     ).astype(bf16)

time: 212 us -> 216 us (1.019)
  starting transfers between devices: 10.9 us -> 16.7 us
  Pallas kernels: 46.3 us -> 43.2 us
  other arithmetic: 11.7 us -> 14 us
    psum x1, waiting for transfers between devices: 52.7 us -> 60.2 us  [on_device(): lax.psum((dq_r.transpose(2, 0, 1).reshape(n_queries, width).astype(bf16),...]
    ppermute x9, waiting for transfers between devices: 14 us -> 9.52 us  [on_device(): lax.ppermute((lax.dynamic_slice_in_dim(numer, (1 - bit) * half, half, 0)....]
    ppermute x6, waiting for transfers between devices: 13.6 us -> 9.4 us  [on_device(): other = lax.ppermute(gathered, 'region', pairs)]
    ppermute x6, starting transfers between devices: 2.1 us -> 5.69 us  [on_device(): other = lax.ppermute(gathered, 'region', pairs)]
    pallas_call x1, Pallas kernels: 20.4 us -> 17.3 us  [_forward(): pl.pallas_call(functools.partial(_fwd_kernel, scale=scale), grid=(heads,...]
    ppermute x9, starting transfers between devices: 8.72 us -> 11 us  [on_device(): lax.ppermute((lax.dynamic_slice_in_dim(numer, (1 - bit) * half, half, 0)....]
    unnamed x47 -> x49, local copies, waits for them, and re-layouts: 8.58 us -> 7.22 us
  transfers between devices with their start and end apart: 16 -> 16, of which waited for: 7 -> 6; matrix products, arithmetic and copies ran while one was open for 16% -> 8% of each run, Pallas kernels for 12% -> 0%
where the time goes in v11:
time: 216 us; the launch traced here: 215 us
  waiting for transfers between devices  79.2 us (37%)
  Pallas kernels  43.2 us (20%)
  matrix products  24.9 us (12%)
  local copies, waits for them, and re-layouts  23 us (11%)
  starting transfers between devices  16.7 us (8%)
  between operations  14.4 us (7%)
  other arithmetic  14 us (6%)
    psum x1, waiting for transfers between devices, on_device(): lax.psum((dq_r.transpose(2, 0, 1).reshape(n_queries, width).astype(bf16),...  60.2 us
    pallas_call x1, Pallas kernels, _backward(): pl.pallas_call(functools.partial(_bwd_kernel, scale=scale), grid=(heads,...  26 us
    pallas_call x1, Pallas kernels, _forward(): pl.pallas_call(functools.partial(_fwd_kernel, scale=scale), grid=(heads,...  17.3 us
    ppermute x9, starting transfers between devices, on_device(): lax.ppermute((lax.dynamic_slice_in_dim(numer, (1 - bit) * half, half, 0)....  11 us
    ppermute x9, waiting for transfers between devices, on_device(): lax.ppermute((lax.dynamic_slice_in_dim(numer, (1 - bit) * half, half, 0)....  9.52 us
    ppermute x6, waiting for transfers between devices, on_device(): other = lax.ppermute(gathered, 'region', pairs)  9.4 us
    reshape x3, local copies, waits for them, and re-layouts, heads(): return x.reshape(x.shape[0], HEADS, head_dim).transpose(1, 0, 2)  7.53 us
    unnamed x49, local copies, waits for them, and re-layouts  7.22 us
  transfers between devices with their start and end apart: 16, of which 6 were waited for; matrix products, arithmetic and copies ran while one was open for 8% of the time, Pallas kernels for 0%

profile of v11, /device:TPU:0, one launch (start us, length us, event | category | flops | bytes accessed | tf_op | source)
XLA Modules:
  0.0 215.5 jit_solution(14958848544069928159)
XLA Ops:
  8.4 2.8 %convolution_convert_fusion.2 = bf16[1024,512]{0,1:T(8,128)(2,1)} fusion(bf16[1024,512]{1,0:T(8,128)(2,1)S(1)} %copy-done, bf16[512,512]{1,0:T(8,128)(2,1)} %param.11), kind=kOutput, calls=%fused_computation.7 | convolution fusion | flops 537395200 | bytes 2621440 | tf_op jit(solution)/shard_map/dot_general | solution.py:146
  11.2 1.7 convolution_convert_fusion.1
  12.9 1.7 convolution_convert_fusion.3
  14.7 2.0 copy.33
  16.7 2.7 %copy.35.k_ref = bf16[8,1024,64]{2,1,0:T(8,128)(2,1)} copy(bf16[8,1024,64]{1,2,0:T(8,128)(2,1)} %bitcast.137) | data formatting | bytes 2097152 | tf_op jit(solution)/shard_map/transpose | solution.py:140
  20.7 17.3 %shard_map.135 = (f32[8,64,1024]{2,1,0:T(8,128)S(1)}, f32[8,1,1024]{2,1,0:T(1,128)S(1)}, f32[8,1,1024]{2,1,0:T(1,128)S(1)}) custom-call(bf16[8,1024,64]{2,1,0:T(8,128)(2,1)S(1)} %bitcast.135, bf16[8,1024,64]{2,1,0:T(8,128)(2,1)} %copy.35.k_ref, bf16[8,64,1024]{2,1,0:T(8,128)(2,1)S(1)} %bitcast.140, f32[8,1,1024]{2,1,0:T(1,128)S(1)} %bitcast.143), custom_call_target="tpu_custom_call" | custom-call | tf_op jit(solution)/shard_map/pallas_call | solution.py:67
  40.7 2.7 %collective-permute-start.2 = (f32[8,256]{1,0:T(8,128)S(1)}, f32[8,256]{1,0:T(8,128)S(1)}, u32[]{:S(2)}, u32[]{:S(2)}) collective-permute-start(f32[8,256]{1,0:T(8,128)S(1)} %constant_dynamic-slice_fusion.7), channel_id=1, source_target_pairs={{0,2},{1,3},{2,0},{3,1},{4,6},{5,7},{6,4},{7,5},{8,10},{9,11},{10,... | collective-permute-start | bytes 24584 | tf_op jit(solution)/shard_map/ppermute | solution.py:168
  43.5 3.1 %convolution_convert_fusion = bf16[1024,512]{0,1:T(8,128)(2,1)} fusion(bf16[1024,512]{1,0:T(8,128)(2,1)} %param.15, bf16[512,512]{1,0:T(8,128)(2,1)} %param.13), kind=kOutput, calls=%fused_computation.5 | convolution fusion | flops 537395200 | bytes 2621440 | tf_op jit(solution)/shard_map/dot_general | solution.py:191
  47.1 1.6 fusion.2
  48.7 1.5 collective-permute-start.3
  50.2 2.6 %collective-permute-start.4 = (f32[8,128]{1,0:T(8,128)S(1)}, f32[8,128]{1,0:T(8,128)S(1)}, u32[]{:S(2)}, u32[]{:S(2)}) collective-permute-start(f32[8,128]{1,0:T(8,128)S(1)} %constant_dynamic-slice_fusion.5), channel_id=1, source_target_pairs={{0,4},{1,5},{2,6},{3,7},{4,0},{5,1},{6,2},{7,3},{8,12},{9,13},{10,... | collective-permute-start | bytes 12296 | tf_op jit(solution)/shard_map/ppermute | solution.py:168
  53.2 3.7 %collective-permute-done.3 = bf16[256,512]{0,1:T(8,128)(2,1)S(1)} collective-permute-done((bf16[256,512]{0,1:T(8,128)(2,1)S(1)}, bf16[256,512]{0,1:T(8,128)(2,1)S(1)}, u32[]{:S(2)}, u32[]{:S(2)}) %collective-permute-start.3) | collective-permute-done | bytes 262176 | tf_op jit(solution)/shard_map/ppermute | solution.py:168
  57.0 2.7 %collective-permute-start.5 = (bf16[128,512]{0,1:T(8,128)(2,1)S(1)}, bf16[128,512]{0,1:T(8,128)(2,1)S(1)}, u32[]{:S(2)}, u32[]{:S(2)}) collective-permute-start(bf16[128,512]{0,1:T(8,128)(2,1)S(1)} %dynamic-slice_convert_fusion.2), channel_id=1, source_target_pairs={{0,4},{1,5},{2,6},{3,7},{4,0},{5,1},{6,2},{7,3},{8,12},{9,13},{10,... | collective-permute-start | bytes 393224 | tf_op jit(solution)/shard_map/ppermute | solution.py:168
  59.7 5.3 %collective-permute-done.5 = bf16[128,512]{0,1:T(8,128)(2,1)S(1)} collective-permute-done((bf16[128,512]{0,1:T(8,128)(2,1)S(1)}, bf16[128,512]{0,1:T(8,128)(2,1)S(1)}, u32[]{:S(2)}, u32[]{:S(2)}) %collective-permute-start.5) | collective-permute-done | bytes 131104 | tf_op jit(solution)/shard_map/ppermute | solution.py:168
  66.7 2.3 %collective-permute-start.12 = (f32[16,128]{1,0:T(8,128)S(1)}, f32[16,128]{1,0:T(8,128)S(1)}, u32[]{:S(2)}, u32[]{:S(2)}) collective-permute-start(f32[16,128]{1,0:T(8,128)S(1)} %pad_maximum_fusion.6), channel_id=1, source_target_pairs={{0,4},{1,5},{2,6},{3,7},{4,0},{5,1},{6,2},{7,3},{8,12},{9,13},{10,... | collective-permute-start | bytes 24584 | tf_op jit(solution)/shard_map/ppermute | solution.py:202
  69.0 5.1 %collective-permute-done.9 = bf16[128,512]{0,1:T(8,128)(2,1)S(1)} collective-permute-done((bf16[128,512]{0,1:T(8,128)(2,1)S(1)}, bf16[128,512]{0,1:T(8,128)(2,1)S(1)}, u32[]{:S(2)}, u32[]{:S(2)}) %collective-permute-start.9) | collective-permute-done | bytes 131104 | tf_op jit(solution)/shard_map/ppermute | solution.py:202
  74.3 2.1 collective-permute-start.13
  76.4 4.3 %collective-permute-done.10 = bf16[256,512]{0,1:T(8,128)(2,1)S(1)} collective-permute-done((bf16[256,512]{0,1:T(8,128)(2,1)S(1)}, bf16[256,512]{0,1:T(8,128)(2,1)S(1)}, u32[]{:S(2)}, u32[]{:S(2)}) %collective-permute-start.10) | collective-permute-done | bytes 262176 | tf_op jit(solution)/shard_map/ppermute | solution.py:202
  82.9 2.7 %copy.37 = bf16[1024,8,64]{2,0,1:T(8,128)(2,1)} copy(bf16[1024,8,64]{0,2,1:T(8,128)(2,1)} %bitcast.152) | data formatting | bytes 2097152 | tf_op jit(solution)/shard_map/reshape | solution.py:140
  85.6 2.8 %copy.36 = bf16[1024,8,64]{2,0,1:T(8,128)(2,1)} copy(bf16[1024,8,64]{0,2,1:T(8,128)(2,1)} %bitcast.139) | data formatting | bytes 2097152 | tf_op jit(solution)/shard_map/reshape | solution.py:140
  91.1 26.0 %shard_map.136 = (f32[8,64,1024]{2,1,0:T(8,128)S(1)}, f32[8,1024,64]{2,1,0:T(8,128)}, f32[8,1024,64]{2,1,0:T(8,128)}) custom-call(bf16[8,1024,64]{2,1,0:T(8,128)(2,1)S(1)} %bitcast.136, bf16[8,1024,64]{2,1,0:T(8,128)(2,1)} %copy.35.k_ref, bf16[8,1024,64]{2,1,0:T(8,128)(2,1)} %bitcast.146, bf16[8,64,1024]{2,1,0:T(8,128)(2,1)S(1)} %bitcast.138, ...), custom_call_target="tpu_custom_call" | custom-call | tf_op jit(solution)/shard_map/pallas_call | solution.py:96
  118.2 5.5 %convert_bitcast_fusion = (bf16[1024,8,64]{2,0,1:T(8,128)(2,1)}, bf16[1024,8,64]{2,0,1:T(8,128)(2,1)S(1)}) fusion(f32[8,1024,64]{2,1,0:T(8,128)} %get-tuple-element.24, f32[8,1024,64]{2,1,0:T(8,128)} %get-tuple-element.23), kind=kLoop, calls=%fused_computation.1 | loop fusion | flops 1048576 | bytes 6291456 | tf_op jit(solution)/shard_map/convert_element_type | solution.py:221
  123.7 2.7 %copy.41 = bf16[1024,8,64]{0,2,1:T(8,128)(2,1)} copy(bf16[1024,8,64]{2,0,1:T(8,128)(2,1)} %get-tuple-element.81) | data formatting | bytes 2097152 | tf_op jit(solution)/shard_map/convert_element_type | solution.py:221
  126.4 2.7 %fusion.1 = bf16[512,512]{0,1:T(8,128)(2,1)} fusion(bf16[1024,512]{0,1:T(8,128)(2,1)} %bitcast.150, bf16[1024,512]{1,0:T(8,128)(2,1)S(1)} %copy-done), kind=kOutput, calls=%fused_computation.13 | convolution fusion | flops 537133056 | bytes 2621440 | tf_op jit(solution)/shard_map/ka,kb->ab/dot_general | solution.py:223
  129.1 1.6 copy.40
  130.7 2.9 %fusion = bf16[512,512]{0,1:T(8,128)(2,1)} fusion(bf16[1024,512]{0,1:T(8,128)(2,1)} %bitcast.147, bf16[1024,512]{1,0:T(8,128)(2,1)S(1)} %copy-done), kind=kOutput, calls=%fused_computation.12 | convolution fusion | flops 537133056 | bytes 2621440 | tf_op jit(solution)/shard_map/ka,kb->ab/dot_general | solution.py:222
  133.7 1.7 fusion.21
  137.1 1.7 add_convert_fusion.2
  138.8 1.7 add_convert_fusion
  140.5 60.2 %all-reduce.3.cloned.1.call-done = (bf16[512,512]{0,1:T(8,128)(2,1)}, bf16[512,512]{0,1:T(8,128)(2,1)}, bf16[1024,512]{0,1:T(8,128)(2,1)}) async-done(((bf16[512,512]{0,1:T(8,128)(2,1)}, bf16[512,512]{0,1:T(8,128)(2,1)}, bf16[1024,512]{0,1:T(8,128)(2,1)}), (bf16[512,512]{0,1:T(8,128)(2,1)}, bf16[512,512]{0,1:T(8,128)(2,1)}, bf16[1024,512]{0,1:T(8,128)(2,1)})) %all-reduce.3.cloned.1.call-update) | async-done | bytes 2097168 | tf_op jit(solution)/shard_map/psum | solution.py:224
  200.8 2.4 %convolution_bitcast_fusion = f32[512,512]{0,1:T(8,128)S(1)} fusion(bf16[1024,512]{0,1:T(8,128)(2,1)} %get-tuple-element.48, bf16[1024,512]{1,0:T(8,128)(2,1)} %param.8), kind=kOutput, calls=%fused_computation.9 | convolution fusion | flops 536870912 | bytes 3145728 | tf_op jit(solution)/shard_map/qa,qb->ab/dot_general | solution.py:230
  203.2 1.7 add_convert_fusion.1
  (108 shorter events, 19.5 us)
Async XLA Ops:
  7.2 4.0 %copy-start.10 = (bf16[512,512]{1,0:T(8,128)(2,1)S(1)}, bf16[512,512]{1,0:T(8,128)(2,1)}, u32[]{:S(2)}) copy-start(bf16[512,512]{1,0:T(8,128)(2,1)} %param.12) | copy-start | bytes 1572868
  7.2 193.6 %all-reduce.3.cloned.1.call-start = ((), (), s32[]{:S(2)}) async-start(), calls=%async_computation | async-start | bytes 4194304 | tf_op jit(solution)/shard_map/psum | solution.py:224
  11.2 1.7 copy-start.14
  11.2 1.7 copy-start.20
  38.0 2.6 %collective-permute-start = (f32[8,512]{1,0:T(8,128)S(1)}, f32[8,512]{1,0:T(8,128)S(1)}, u32[]{:S(2)}, u32[]{:S(2)}) collective-permute-start(f32[8,512]{1,0:T(8,128)S(1)} %bitcast.156), channel_id=1, source_target_pairs={{0,1},{1,0},{2,3},{3,2},{4,5},{5,4},{6,7},{7,6},{8,9},{9,8},{10,11... | collective-permute-start | bytes 49160 | tf_op jit(solution)/shard_map/ppermute | solution.py:168
  38.5 2.1 collective-permute-start.6
  40.2 6.9 %collective-permute-start.1 = (bf16[512,512]{0,1:T(8,128)(2,1)}, bf16[512,512]{0,1:T(8,128)(2,1)}, u32[]{:S(2)}, u32[]{:S(2)}) collective-permute-start(bf16[512,512]{0,1:T(8,128)(2,1)} %dynamic-slice_convert_fusion), channel_id=1, source_target_pairs={{0,1},{1,0},{2,3},{3,2},{4,5},{5,4},{6,7},{7,6},{8,9},{9,8},{10,11... | collective-permute-start | bytes 1572872 | tf_op jit(solution)/shard_map/ppermute | solution.py:168
  40.7 5.8 %collective-permute-start.2 = (f32[8,256]{1,0:T(8,128)S(1)}, f32[8,256]{1,0:T(8,128)S(1)}, u32[]{:S(2)}, u32[]{:S(2)}) collective-permute-start(f32[8,256]{1,0:T(8,128)S(1)} %constant_dynamic-slice_fusion.7), channel_id=1, source_target_pairs={{0,2},{1,3},{2,0},{3,1},{4,6},{5,7},{6,4},{7,5},{8,10},{9,11},{10,... | collective-permute-start | bytes 24584 | tf_op jit(solution)/shard_map/ppermute | solution.py:168
  43.4 3.7 %collective-permute-start.7 = (f32[8,256]{1,0:T(8,128)S(1)}, f32[8,256]{1,0:T(8,128)S(1)}, u32[]{:S(2)}, u32[]{:S(2)}) collective-permute-start(f32[8,256]{1,0:T(8,128)S(1)} %constant_dynamic-slice_fusion.2), channel_id=1, source_target_pairs={{0,2},{1,3},{2,0},{3,1},{4,6},{5,7},{6,4},{7,5},{8,10},{9,11},{10,... | collective-permute-start | bytes 24584 | tf_op jit(solution)/shard_map/ppermute | solution.py:168
  48.7 8.1 %collective-permute-start.3 = (bf16[256,512]{0,1:T(8,128)(2,1)S(1)}, bf16[256,512]{0,1:T(8,128)(2,1)S(1)}, u32[]{:S(2)}, u32[]{:S(2)}) collective-permute-start(bf16[256,512]{0,1:T(8,128)(2,1)S(1)} %dynamic-slice_convert_fusion.1), channel_id=1, source_target_pairs={{0,2},{1,3},{2,0},{3,1},{4,6},{5,7},{6,4},{7,5},{8,10},{9,11},{10,... | collective-permute-start | bytes 786440 | tf_op jit(solution)/shard_map/ppermute | solution.py:168
  50.2 9.5 %collective-permute-start.4 = (f32[8,128]{1,0:T(8,128)S(1)}, f32[8,128]{1,0:T(8,128)S(1)}, u32[]{:S(2)}, u32[]{:S(2)}) collective-permute-start(f32[8,128]{1,0:T(8,128)S(1)} %constant_dynamic-slice_fusion.5), channel_id=1, source_target_pairs={{0,4},{1,5},{2,6},{3,7},{4,0},{5,1},{6,2},{7,3},{8,12},{9,13},{10,... | collective-permute-start | bytes 12296 | tf_op jit(solution)/shard_map/ppermute | solution.py:168
  52.8 6.9 %collective-permute-start.8 = (f32[8,128]{1,0:T(8,128)S(1)}, f32[8,128]{1,0:T(8,128)S(1)}, u32[]{:S(2)}, u32[]{:S(2)}) collective-permute-start(f32[8,128]{1,0:T(8,128)S(1)} %constant_dynamic-slice_fusion), channel_id=1, source_target_pairs={{0,4},{1,5},{2,6},{3,7},{4,0},{5,1},{6,2},{7,3},{8,12},{9,13},{10,... | collective-permute-start | bytes 12296 | tf_op jit(solution)/shard_map/ppermute | solution.py:168
  57.0 8.1 %collective-permute-start.5 = (bf16[128,512]{0,1:T(8,128)(2,1)S(1)}, bf16[128,512]{0,1:T(8,128)(2,1)S(1)}, u32[]{:S(2)}, u32[]{:S(2)}) collective-permute-start(bf16[128,512]{0,1:T(8,128)(2,1)S(1)} %dynamic-slice_convert_fusion.2), channel_id=1, source_target_pairs={{0,4},{1,5},{2,6},{3,7},{4,0},{5,1},{6,2},{7,3},{8,12},{9,13},{10,... | collective-permute-start | bytes 393224 | tf_op jit(solution)/shard_map/ppermute | solution.py:168
  66.0 8.1 %collective-permute-start.9 = (bf16[128,512]{0,1:T(8,128)(2,1)S(1)}, bf16[128,512]{0,1:T(8,128)(2,1)S(1)}, u32[]{:S(2)}, u32[]{:S(2)}) collective-permute-start(bf16[128,512]{0,1:T(8,128)(2,1)S(1)} %get-tuple-element.50), channel_id=1, source_target_pairs={{0,4},{1,5},{2,6},{3,7},{4,0},{5,1},{6,2},{7,3},{8,12},{9,13},{10,... | collective-permute-start | bytes 393224 | tf_op jit(solution)/shard_map/ppermute | solution.py:202
  66.7 7.6 %collective-permute-start.12 = (f32[16,128]{1,0:T(8,128)S(1)}, f32[16,128]{1,0:T(8,128)S(1)}, u32[]{:S(2)}, u32[]{:S(2)}) collective-permute-start(f32[16,128]{1,0:T(8,128)S(1)} %pad_maximum_fusion.6), channel_id=1, source_target_pairs={{0,4},{1,5},{2,6},{3,7},{4,0},{5,1},{6,2},{7,3},{8,12},{9,13},{10,... | collective-permute-start | bytes 24584 | tf_op jit(solution)/shard_map/ppermute | solution.py:202
  74.2 6.4 %collective-permute-start.10 = (bf16[256,512]{0,1:T(8,128)(2,1)S(1)}, bf16[256,512]{0,1:T(8,128)(2,1)S(1)}, u32[]{:S(2)}, u32[]{:S(2)}) collective-permute-start(bf16[256,512]{0,1:T(8,128)(2,1)S(1)} %pad_maximum_fusion.2), channel_id=1, source_target_pairs={{0,2},{1,3},{2,0},{3,1},{4,6},{5,7},{6,4},{7,5},{8,10},{9,11},{10,... | collective-permute-start | bytes 786440 | tf_op jit(solution)/shard_map/ppermute | solution.py:202
  74.3 8.0 %collective-permute-start.13 = (f32[16,256]{1,0:T(8,128)S(1)}, f32[16,256]{1,0:T(8,128)S(1)}, u32[]{:S(2)}, u32[]{:S(2)}) collective-permute-start(f32[16,256]{1,0:T(8,128)S(1)} %pad_maximum_fusion.5), channel_id=1, source_target_pairs={{0,2},{1,3},{2,0},{3,1},{4,6},{5,7},{6,4},{7,5},{8,10},{9,11},{10,... | collective-permute-start | bytes 49160 | tf_op jit(solution)/shard_map/ppermute | solution.py:202
  82.3 6.2 %collective-permute-start.11 = (bf16[512,512]{0,1:T(8,128)(2,1)}, bf16[512,512]{0,1:T(8,128)(2,1)}, u32[]{:S(2)}, u32[]{:S(2)}) collective-permute-start(bf16[512,512]{0,1:T(8,128)(2,1)} %pad_maximum_fusion.1), channel_id=1, source_target_pairs={{0,1},{1,0},{2,3},{3,2},{4,5},{5,4},{6,7},{7,6},{8,9},{9,8},{10,11... | collective-permute-start | bytes 1572872 | tf_op jit(solution)/shard_map/ppermute | solution.py:202
  82.3 6.1 %collective-permute-start.14 = (f32[16,512]{1,0:T(8,128)S(1)}, f32[16,512]{1,0:T(8,128)S(1)}, u32[]{:S(2)}, u32[]{:S(2)}) collective-permute-start(f32[16,512]{1,0:T(8,128)S(1)} %pad_maximum_fusion.4), channel_id=1, source_target_pairs={{0,1},{1,0},{2,3},{3,2},{4,5},{5,4},{6,7},{7,6},{8,9},{9,8},{10,11... | collective-permute-start | bytes 98312 | tf_op jit(solution)/shard_map/ppermute | solution.py:202
  88.5 2.6 %copy-start.1 = (bf16[1024,512]{0,1:T(8,128)(2,1)S(1)}, bf16[1024,512]{0,1:T(8,128)(2,1)}, u32[]{:S(2)}) copy-start(bf16[1024,512]{0,1:T(8,128)(2,1)} %convolution_convert_fusion.2) | copy-start | bytes 3145732
  130.7 2.9 %copy-start.7 = (bf16[1024,512]{0,1:T(8,128)(2,1)S(1)}, bf16[1024,512]{0,1:T(8,128)(2,1)}, u32[]{:S(2)}) copy-start(bf16[1024,512]{0,1:T(8,128)(2,1)} %pad_maximum_fusion) | copy-start | bytes 3145732
  130.7 2.9 %copy-start.16 = (bf16[1024,512]{1,0:T(8,128)(2,1)S(1)}, bf16[1024,512]{1,0:T(8,128)(2,1)}, u32[]{:S(2)}) copy-start(bf16[1024,512]{1,0:T(8,128)(2,1)} %param.15) | copy-start | bytes 3145732
  133.7 1.7 copy-start.4
  133.7 1.7 copy-start.9
  135.4 1.7 copy-start.19
  137.0 1.7 copy-start.5
  137.1 1.7 copy-start.11
  200.7 2.4 %copy-start.17 = (bf16[1024,512]{1,0:T(8,128)(2,1)S(1)}, bf16[1024,512]{1,0:T(8,128)(2,1)}, u32[]{:S(2)}) copy-start(bf16[1024,512]{1,0:T(8,128)(2,1)} %param.15) | copy-start | bytes 3145732
  200.8 2.4 %copy-start.18 = (bf16[1024,512]{0,1:T(8,128)(2,1)S(1)}, bf16[1024,512]{0,1:T(8,128)(2,1)}, u32[]{:S(2)}) copy-start(bf16[1024,512]{0,1:T(8,128)(2,1)} %get-tuple-element.48) | copy-start | bytes 3145732
  200.8 2.4 %copy-start.21 = (bf16[512,512]{1,0:T(8,128)(2,1)S(1)}, bf16[512,512]{1,0:T(8,128)(2,1)}, u32[]{:S(2)}) copy-start(bf16[512,512]{1,0:T(8,128)(2,1)} %param.10) | copy-start | bytes 1572868
  203.2 1.8 copy-start.13
  203.2 2.9 %copy-start.12 = (bf16[512,512]{0,1:T(8,128)(2,1)S(1)}, bf16[512,512]{0,1:T(8,128)(2,1)}, u32[]{:S(2)}) copy-start(bf16[512,512]{0,1:T(8,128)(2,1)} %get-tuple-element.47) | copy-start | bytes 1572868
  (6 other events, 7.3 us)
Sparse Core Ops, SparseCore 0:
  133.8 66.9 all-reduce.2

commit v12 on v11

--- a/solution.py
+++ b/solution.py
@@ -209,7 +209,6 @@
     attended = gathered[0]
     log_total = gathered[1][:HEADS].reshape(HEADS, 1, n_queries)
     deltas = gathered[1][HEADS:].reshape(HEADS, 1, n_queries)
-    attended, log_total, deltas = lax.optimization_barrier((attended, log_total, deltas))
     layer_out = (
         queries_in.astype(f32) + jnp.dot(attended, w_out, preferred_element_type=f32)
     ).astype(bf16)

time: 216 us -> 209 us (0.968)
  starting transfers between devices: 16.7 us -> 10.9 us
  other arithmetic: 14 us -> 11.7 us
    psum x1, waiting for transfers between devices: 60.2 us -> 52.7 us  [on_device(): lax.psum((dq_r.transpose(2, 0, 1).reshape(n_queries, width).astype(bf16),...]
    ppermute x9, waiting for transfers between devices: 9.52 us -> 14 us  [on_device(): lax.ppermute((lax.dynamic_slice_in_dim(numer, (1 - bit) * half, half, 0)....]
    ppermute x6, waiting for transfers between devices: 9.4 us -> 13.6 us  [on_device(): other = lax.ppermute(gathered, 'region', pairs)]
    ppermute x6, starting transfers between devices: 5.69 us -> 2.09 us  [on_device(): other = lax.ppermute(gathered, 'region', pairs)]
    ppermute x9, starting transfers between devices: 11 us -> 8.73 us  [on_device(): lax.ppermute((lax.dynamic_slice_in_dim(numer, (1 - bit) * half, half, 0)....]
    unnamed x49 -> x47, local copies, waits for them, and re-layouts: 7.22 us -> 8.58 us
  transfers between devices with their start and end apart: 16 -> 16, of which waited for: 6 -> 7; matrix products, arithmetic and copies ran while one was open for 8% -> 16% of each run, Pallas kernels for 0% -> 12%
where the time goes in v12:
time: 209 us; the launch traced here: 208 us
  waiting for transfers between devices  80.4 us (38%)
  Pallas kernels  43.2 us (21%)
  matrix products  24.4 us (12%)
  local copies, waits for them, and re-layouts  23.5 us (11%)
  between operations  14.4 us (7%)
  other arithmetic  11.7 us (6%)
  starting transfers between devices  10.9 us (5%)
    psum x1, waiting for transfers between devices, on_device(): lax.psum((dq_r.transpose(2, 0, 1).reshape(n_queries, width).astype(bf16),...  52.7 us
    pallas_call x1, Pallas kernels, _backward(): pl.pallas_call(functools.partial(_bwd_kernel, scale=scale), grid=(heads,...  26 us
    pallas_call x1, Pallas kernels, _forward(): pl.pallas_call(functools.partial(_fwd_kernel, scale=scale), grid=(heads,...  17.3 us
    ppermute x9, waiting for transfers between devices, on_device(): lax.ppermute((lax.dynamic_slice_in_dim(numer, (1 - bit) * half, half, 0)....  14 us
    ppermute x6, waiting for transfers between devices, on_device(): other = lax.ppermute(gathered, 'region', pairs)  13.6 us
    ppermute x9, starting transfers between devices, on_device(): lax.ppermute((lax.dynamic_slice_in_dim(numer, (1 - bit) * half, half, 0)....  8.73 us
    unnamed x47, local copies, waits for them, and re-layouts  8.58 us
    reshape x3, local copies, waits for them, and re-layouts, heads(): return x.reshape(x.shape[0], HEADS, head_dim).transpose(1, 0, 2)  7.54 us
  transfers between devices with their start and end apart: 16, of which 7 were waited for; matrix products, arithmetic and copies ran while one was open for 16% of the time, Pallas kernels for 12%

profile of v12, /device:TPU:0, one launch (start us, length us, event | category | flops | bytes accessed | tf_op | source)
XLA Modules:
  0.0 208.5 jit_solution(12792254939419071610)
XLA Ops:
  8.4 1.8 convolution_convert_fusion.2
  10.2 1.8 copy.35.k_ref
  12.2 2.8 %convolution_convert_fusion.3 = bf16[1024,512]{0,1:T(8,128)(2,1)} fusion(bf16[1024,512]{1,0:T(8,128)(2,1)S(1)} %copy-done.14, bf16[512,512]{1,0:T(8,128)(2,1)} %param.10), kind=kOutput, calls=%fused_computation.8 | convolution fusion | flops 537395200 | bytes 2621440 | tf_op jit(solution)/shard_map/dot_general | solution.py:145
  15.0 2.0 copy.33
  17.0 2.8 %convolution_convert_fusion.1 = bf16[1024,512]{0,1:T(8,128)(2,1)} fusion(bf16[1024,512]{1,0:T(8,128)(2,1)S(1)} %copy-done, bf16[512,512]{1,0:T(8,128)(2,1)} %param.12), kind=kOutput, calls=%fused_computation.6 | convolution fusion | flops 537395200 | bytes 2621440 | tf_op jit(solution)/shard_map/dot_general | solution.py:147
  21.1 17.3 %shard_map.135 = (f32[8,64,1024]{2,1,0:T(8,128)S(1)}, f32[8,1,1024]{2,1,0:T(1,128)S(1)}, f32[8,1,1024]{2,1,0:T(1,128)S(1)}) custom-call(bf16[8,1024,64]{2,1,0:T(8,128)(2,1)S(1)} %bitcast.133, bf16[8,1024,64]{2,1,0:T(8,128)(2,1)} %copy.35.k_ref, bf16[8,64,1024]{2,1,0:T(8,128)(2,1)S(1)} %bitcast.138, f32[8,1,1024]{2,1,0:T(1,128)S(1)} %bitcast.141), custom_call_target="tpu_custom_call" | custom-call | tf_op jit(solution)/shard_map/pallas_call | solution.py:67
  41.1 2.6 %collective-permute-start.2 = (f32[8,256]{1,0:T(8,128)S(1)}, f32[8,256]{1,0:T(8,128)S(1)}, u32[]{:S(2)}, u32[]{:S(2)}) collective-permute-start(f32[8,256]{1,0:T(8,128)S(1)} %constant_dynamic-slice_fusion.7), channel_id=1, source_target_pairs={{0,2},{1,3},{2,0},{3,1},{4,6},{5,7},{6,4},{7,5},{8,10},{9,11},{10,... | collective-permute-start | bytes 24584 | tf_op jit(solution)/shard_map/ppermute | solution.py:168
  43.8 3.1 %convolution_convert_fusion = bf16[1024,512]{0,1:T(8,128)(2,1)} fusion(bf16[1024,512]{1,0:T(8,128)(2,1)} %param.15, bf16[512,512]{1,0:T(8,128)(2,1)} %param.13), kind=kOutput, calls=%fused_computation.5 | convolution fusion | flops 537395200 | bytes 2621440 | tf_op jit(solution)/shard_map/dot_general | solution.py:191
  47.4 2.6 %collective-permute-start.8 = (f32[8,128]{1,0:T(8,128)S(1)}, f32[8,128]{1,0:T(8,128)S(1)}, u32[]{:S(2)}, u32[]{:S(2)}) collective-permute-start(f32[8,128]{1,0:T(8,128)S(1)} %constant_dynamic-slice_fusion), channel_id=1, source_target_pairs={{0,4},{1,5},{2,6},{3,7},{4,0},{5,1},{6,2},{7,3},{8,12},{9,13},{10,... | collective-permute-start | bytes 12296 | tf_op jit(solution)/shard_map/ppermute | solution.py:168
  50.1 1.6 fusion.2
  51.7 1.5 collective-permute-start.3
  53.6 6.0 %collective-permute-done.3 = bf16[256,512]{0,1:T(8,128)(2,1)S(1)} collective-permute-done((bf16[256,512]{0,1:T(8,128)(2,1)S(1)}, bf16[256,512]{0,1:T(8,128)(2,1)S(1)}, u32[]{:S(2)}, u32[]{:S(2)}) %collective-permute-start.3) | collective-permute-done | bytes 262176 | tf_op jit(solution)/shard_map/ppermute | solution.py:168
  60.1 7.5 %collective-permute-done.5 = bf16[128,512]{0,1:T(8,128)(2,1)S(1)} collective-permute-done((bf16[128,512]{0,1:T(8,128)(2,1)S(1)}, bf16[128,512]{0,1:T(8,128)(2,1)S(1)}, u32[]{:S(2)}, u32[]{:S(2)}) %collective-permute-start.5) | collective-permute-done | bytes 131104 | tf_op jit(solution)/shard_map/ppermute | solution.py:168
  68.7 4.5 %collective-permute-done.12 = f32[16,128]{1,0:T(8,128)S(1)} collective-permute-done((f32[16,128]{1,0:T(8,128)S(1)}, f32[16,128]{1,0:T(8,128)S(1)}, u32[]{:S(2)}, u32[]{:S(2)}) %collective-permute-start.12) | collective-permute-done | bytes 8224 | tf_op jit(solution)/shard_map/ppermute | solution.py:202
  73.3 3.7 %collective-permute-done.13 = f32[16,256]{1,0:T(8,128)S(1)} collective-permute-done((f32[16,256]{1,0:T(8,128)S(1)}, f32[16,256]{1,0:T(8,128)S(1)}, u32[]{:S(2)}, u32[]{:S(2)}) %collective-permute-start.13) | collective-permute-done | bytes 16416 | tf_op jit(solution)/shard_map/ppermute | solution.py:202
  77.1 2.8 %copy.36 = bf16[1024,8,64]{2,0,1:T(8,128)(2,1)} copy(bf16[1024,8,64]{0,2,1:T(8,128)(2,1)} %bitcast.137) | data formatting | bytes 2097152 | tf_op jit(solution)/shard_map/reshape | solution.py:140
  79.9 2.7 %copy.37 = bf16[1024,8,64]{2,0,1:T(8,128)(2,1)} copy(bf16[1024,8,64]{0,2,1:T(8,128)(2,1)} %bitcast.150) | data formatting | bytes 2097152 | tf_op jit(solution)/shard_map/reshape | solution.py:140
  84.0 26.0 %shard_map.136 = (f32[8,64,1024]{2,1,0:T(8,128)S(1)}, f32[8,1024,64]{2,1,0:T(8,128)}, f32[8,1024,64]{2,1,0:T(8,128)}) custom-call(bf16[8,1024,64]{2,1,0:T(8,128)(2,1)S(1)} %bitcast.134, bf16[8,1024,64]{2,1,0:T(8,128)(2,1)} %copy.35.k_ref, bf16[8,1024,64]{2,1,0:T(8,128)(2,1)} %bitcast.143, bf16[8,64,1024]{2,1,0:T(8,128)(2,1)S(1)} %bitcast.136, ...), custom_call_target="tpu_custom_call" | custom-call | tf_op jit(solution)/shard_map/pallas_call | solution.py:96
  110.0 6.4 %convert_bitcast_fusion = (bf16[1024,8,64]{2,0,1:T(8,128)(2,1)}, bf16[1024,8,64]{2,0,1:T(8,128)(2,1)S(1)}) fusion(f32[8,1024,64]{2,1,0:T(8,128)} %get-tuple-element.18, f32[8,1024,64]{2,1,0:T(8,128)} %get-tuple-element.17), kind=kLoop, calls=%fused_computation.1 | loop fusion | flops 1048576 | bytes 6291456 | tf_op jit(solution)/shard_map/convert_element_type | solution.py:220
  116.4 1.6 copy.40
  118.0 2.7 %fusion = bf16[512,512]{0,1:T(8,128)(2,1)} fusion(bf16[1024,512]{0,1:T(8,128)(2,1)} %bitcast.145, bf16[1024,512]{1,0:T(8,128)(2,1)S(1)} %copy-done), kind=kOutput, calls=%fused_computation.12 | convolution fusion | flops 537133056 | bytes 2621440 | tf_op jit(solution)/shard_map/ka,kb->ab/dot_general | solution.py:221
  120.7 2.8 %copy.41 = bf16[1024,8,64]{0,2,1:T(8,128)(2,1)} copy(bf16[1024,8,64]{2,0,1:T(8,128)(2,1)} %get-tuple-element.75) | data formatting | bytes 2097152 | tf_op jit(solution)/shard_map/convert_element_type | solution.py:220
  124.7 1.8 collective-permute-start.10
  126.6 1.5 fusion.1
  128.1 5.4 %collective-permute-done.10 = bf16[256,512]{0,1:T(8,128)(2,1)S(1)} collective-permute-done((bf16[256,512]{0,1:T(8,128)(2,1)S(1)}, bf16[256,512]{0,1:T(8,128)(2,1)S(1)}, u32[]{:S(2)}, u32[]{:S(2)}) %collective-permute-start.10) | collective-permute-done | bytes 262176 | tf_op jit(solution)/shard_map/ppermute | solution.py:202
  135.0 1.7 add_convert_fusion
  138.0 1.7 fusion.3
  139.7 1.7 add_convert_fusion.2
  141.4 52.7 %all-reduce.3.cloned.1.call-done = (bf16[512,512]{0,1:T(8,128)(2,1)}, bf16[512,512]{0,1:T(8,128)(2,1)}, bf16[1024,512]{0,1:T(8,128)(2,1)}) async-done(((bf16[512,512]{0,1:T(8,128)(2,1)}, bf16[512,512]{0,1:T(8,128)(2,1)}, bf16[1024,512]{0,1:T(8,128)(2,1)}), (bf16[512,512]{0,1:T(8,128)(2,1)}, bf16[512,512]{0,1:T(8,128)(2,1)}, bf16[1024,512]{0,1:T(8,128)(2,1)})) %all-reduce.3.cloned.1.call-update) | async-done | bytes 2097168 | tf_op jit(solution)/shard_map/psum | solution.py:223
  194.1 2.1 convolution_bitcast_fusion
  196.2 1.7 add_convert_fusion.1
  198.0 1.3 copy.42
  (105 shorter events, 15.8 us)
Async XLA Ops:
  7.2 186.9 %all-reduce.3.cloned.1.call-start = ((), (), s32[]{:S(2)}) async-start(), calls=%async_computation | async-start | bytes 4194304 | tf_op jit(solution)/shard_map/psum | solution.py:223
  10.2 4.8 %copy-start.1 = (bf16[1024,512]{0,1:T(8,128)(2,1)}, bf16[1024,512]{0,1:T(8,128)(2,1)S(1)}, u32[]{:S(2)}) copy-start(bf16[1024,512]{0,1:T(8,128)(2,1)S(1)} %convolution_convert_fusion.2) | copy-start | bytes 3145732
  10.2 2.0 copy-start.14
  38.4 1.3 copy-start.6
  38.4 2.7 %collective-permute-start = (f32[8,512]{1,0:T(8,128)S(1)}, f32[8,512]{1,0:T(8,128)S(1)}, u32[]{:S(2)}, u32[]{:S(2)}) collective-permute-start(f32[8,512]{1,0:T(8,128)S(1)} %bitcast.154), channel_id=1, source_target_pairs={{0,1},{1,0},{2,3},{3,2},{4,5},{5,4},{6,7},{7,6},{8,9},{9,8},{10,11... | collective-permute-start | bytes 49160 | tf_op jit(solution)/shard_map/ppermute | solution.py:168
  39.0 2.1 %collective-permute-start.6 = (f32[8,512]{1,0:T(8,128)S(1)}, f32[8,512]{1,0:T(8,128)S(1)}, u32[]{:S(2)}, u32[]{:S(2)}) collective-permute-start(f32[8,512]{1,0:T(8,128)S(1)} %bitcast.155), channel_id=1, source_target_pairs={{0,1},{1,0},{2,3},{3,2},{4,5},{5,4},{6,7},{7,6},{8,9},{9,8},{10,11... | collective-permute-start | bytes 49160 | tf_op jit(solution)/shard_map/ppermute | solution.py:168
  40.6 9.5 %collective-permute-start.1 = (bf16[512,512]{0,1:T(8,128)(2,1)}, bf16[512,512]{0,1:T(8,128)(2,1)}, u32[]{:S(2)}, u32[]{:S(2)}) collective-permute-start(bf16[512,512]{0,1:T(8,128)(2,1)} %dynamic-slice_convert_fusion), channel_id=1, source_target_pairs={{0,1},{1,0},{2,3},{3,2},{4,5},{5,4},{6,7},{7,6},{8,9},{9,8},{10,11... | collective-permute-start | bytes 1572872 | tf_op jit(solution)/shard_map/ppermute | solution.py:168
  41.1 5.8 %collective-permute-start.2 = (f32[8,256]{1,0:T(8,128)S(1)}, f32[8,256]{1,0:T(8,128)S(1)}, u32[]{:S(2)}, u32[]{:S(2)}) collective-permute-start(f32[8,256]{1,0:T(8,128)S(1)} %constant_dynamic-slice_fusion.7), channel_id=1, source_target_pairs={{0,2},{1,3},{2,0},{3,1},{4,6},{5,7},{6,4},{7,5},{8,10},{9,11},{10,... | collective-permute-start | bytes 24584 | tf_op jit(solution)/shard_map/ppermute | solution.py:168
  43.7 3.7 %collective-permute-start.7 = (f32[8,256]{1,0:T(8,128)S(1)}, f32[8,256]{1,0:T(8,128)S(1)}, u32[]{:S(2)}, u32[]{:S(2)}) collective-permute-start(f32[8,256]{1,0:T(8,128)S(1)} %constant_dynamic-slice_fusion.2), channel_id=1, source_target_pairs={{0,2},{1,3},{2,0},{3,1},{4,6},{5,7},{6,4},{7,5},{8,10},{9,11},{10,... | collective-permute-start | bytes 24584 | tf_op jit(solution)/shard_map/ppermute | solution.py:168
  47.4 12.6 %collective-permute-start.8 = (f32[8,128]{1,0:T(8,128)S(1)}, f32[8,128]{1,0:T(8,128)S(1)}, u32[]{:S(2)}, u32[]{:S(2)}) collective-permute-start(f32[8,128]{1,0:T(8,128)S(1)} %constant_dynamic-slice_fusion), channel_id=1, source_target_pairs={{0,4},{1,5},{2,6},{3,7},{4,0},{5,1},{6,2},{7,3},{8,12},{9,13},{10,... | collective-permute-start | bytes 12296 | tf_op jit(solution)/shard_map/ppermute | solution.py:168
  51.7 7.9 %collective-permute-start.3 = (bf16[256,512]{0,1:T(8,128)(2,1)S(1)}, bf16[256,512]{0,1:T(8,128)(2,1)S(1)}, u32[]{:S(2)}, u32[]{:S(2)}) collective-permute-start(bf16[256,512]{0,1:T(8,128)(2,1)S(1)} %dynamic-slice_convert_fusion.1), channel_id=1, source_target_pairs={{0,2},{1,3},{2,0},{3,1},{4,6},{5,7},{6,4},{7,5},{8,10},{9,11},{10,... | collective-permute-start | bytes 786440 | tf_op jit(solution)/shard_map/ppermute | solution.py:168
  53.2 6.9 %collective-permute-start.4 = (f32[8,128]{1,0:T(8,128)S(1)}, f32[8,128]{1,0:T(8,128)S(1)}, u32[]{:S(2)}, u32[]{:S(2)}) collective-permute-start(f32[8,128]{1,0:T(8,128)S(1)} %constant_dynamic-slice_fusion.5), channel_id=1, source_target_pairs={{0,4},{1,5},{2,6},{3,7},{4,0},{5,1},{6,2},{7,3},{8,12},{9,13},{10,... | collective-permute-start | bytes 12296 | tf_op jit(solution)/shard_map/ppermute | solution.py:168
  59.7 7.9 %collective-permute-start.5 = (bf16[128,512]{0,1:T(8,128)(2,1)S(1)}, bf16[128,512]{0,1:T(8,128)(2,1)S(1)}, u32[]{:S(2)}, u32[]{:S(2)}) collective-permute-start(bf16[128,512]{0,1:T(8,128)(2,1)S(1)} %dynamic-slice_convert_fusion.2), channel_id=1, source_target_pairs={{0,4},{1,5},{2,6},{3,7},{4,0},{5,1},{6,2},{7,3},{8,12},{9,13},{10,... | collective-permute-start | bytes 393224 | tf_op jit(solution)/shard_map/ppermute | solution.py:168
  68.6 4.6 %collective-permute-start.12 = (f32[16,128]{1,0:T(8,128)S(1)}, f32[16,128]{1,0:T(8,128)S(1)}, u32[]{:S(2)}, u32[]{:S(2)}) collective-permute-start(f32[16,128]{1,0:T(8,128)S(1)} %pad_maximum_fusion.8), channel_id=1, source_target_pairs={{0,4},{1,5},{2,6},{3,7},{4,0},{5,1},{6,2},{7,3},{8,12},{9,13},{10,... | collective-permute-start | bytes 24584 | tf_op jit(solution)/shard_map/ppermute | solution.py:202
  73.2 3.8 %collective-permute-start.13 = (f32[16,256]{1,0:T(8,128)S(1)}, f32[16,256]{1,0:T(8,128)S(1)}, u32[]{:S(2)}, u32[]{:S(2)}) collective-permute-start(f32[16,256]{1,0:T(8,128)S(1)} %pad_maximum_fusion.7), channel_id=1, source_target_pairs={{0,2},{1,3},{2,0},{3,1},{4,6},{5,7},{6,4},{7,5},{8,10},{9,11},{10,... | collective-permute-start | bytes 49160 | tf_op jit(solution)/shard_map/ppermute | solution.py:202
  77.1 5.6 %collective-permute-start.14 = (f32[16,512]{1,0:T(8,128)S(1)}, f32[16,512]{1,0:T(8,128)S(1)}, u32[]{:S(2)}, u32[]{:S(2)}) collective-permute-start(f32[16,512]{1,0:T(8,128)S(1)} %pad_maximum_fusion.6), channel_id=1, source_target_pairs={{0,1},{1,0},{2,3},{3,2},{4,5},{5,4},{6,7},{7,6},{8,9},{9,8},{10,11... | collective-permute-start | bytes 98312 | tf_op jit(solution)/shard_map/ppermute | solution.py:202
  82.7 42.0 %collective-permute-start.9 = (bf16[128,512]{0,1:T(8,128)(2,1)S(1)}, bf16[128,512]{0,1:T(8,128)(2,1)S(1)}, u32[]{:S(2)}, u32[]{:S(2)}) collective-permute-start(bf16[128,512]{0,1:T(8,128)(2,1)S(1)} %get-tuple-element.44), channel_id=1, source_target_pairs={{0,4},{1,5},{2,6},{3,7},{4,0},{5,1},{6,2},{7,3},{8,12},{9,13},{10,... | collective-permute-start | bytes 393224 | tf_op jit(solution)/shard_map/ppermute | solution.py:202
  110.0 6.4 %copy-start.4 = (f32[8,64,1024]{2,1,0:T(8,128)}, f32[8,64,1024]{2,1,0:T(8,128)S(1)}, u32[]{:S(2)}) copy-start(f32[8,64,1024]{2,1,0:T(8,128)S(1)} %get-tuple-element.16) | copy-start | bytes 6291460
  120.7 2.8 %copy-start.5 = (f32[8,64,1024]{2,1,0:T(8,128)S(1)}, f32[8,64,1024]{2,1,0:T(8,128)}, u32[]{:S(2)}) copy-start(f32[8,64,1024]{2,1,0:T(8,128)} %copy-done.4) | copy-start | bytes 6291460
  123.5 3.0 %copy-start.8 = (bf16[1024,8,64]{0,2,1:T(8,128)(2,1)S(1)}, bf16[1024,8,64]{0,2,1:T(8,128)(2,1)}, u32[]{:S(2)}) copy-start(bf16[1024,8,64]{0,2,1:T(8,128)(2,1)} %copy.41) | copy-start | bytes 3145732
  124.7 8.8 %collective-permute-start.10 = (bf16[256,512]{0,1:T(8,128)(2,1)S(1)}, bf16[256,512]{0,1:T(8,128)(2,1)S(1)}, u32[]{:S(2)}, u32[]{:S(2)}) collective-permute-start(bf16[256,512]{0,1:T(8,128)(2,1)S(1)} %pad_maximum_fusion.4), channel_id=1, source_target_pairs={{0,2},{1,3},{2,0},{3,1},{4,6},{5,7},{6,4},{7,5},{8,10},{9,11},{10,... | collective-permute-start | bytes 786440 | tf_op jit(solution)/shard_map/ppermute | solution.py:202
  128.1 5.7 %copy-start.7 = (bf16[1024,8,64]{0,2,1:T(8,128)(2,1)S(1)}, bf16[1024,8,64]{0,2,1:T(8,128)(2,1)}, u32[]{:S(2)}) copy-start(bf16[1024,8,64]{0,2,1:T(8,128)(2,1)} %copy.40) | copy-start | bytes 3145732
  128.1 5.7 %copy-start.10 = (bf16[512,512]{1,0:T(8,128)(2,1)S(1)}, bf16[512,512]{1,0:T(8,128)(2,1)}, u32[]{:S(2)}) copy-start(bf16[512,512]{1,0:T(8,128)(2,1)} %param.11) | copy-start | bytes 1572868
  133.7 1.4 copy-start.11
  133.7 3.1 %collective-permute-start.11 = (bf16[512,512]{0,1:T(8,128)(2,1)S(1)}, bf16[512,512]{0,1:T(8,128)(2,1)S(1)}, u32[]{:S(2)}, u32[]{:S(2)}) collective-permute-start(bf16[512,512]{0,1:T(8,128)(2,1)S(1)} %pad_maximum_fusion.3), channel_id=1, source_target_pairs={{0,1},{1,0},{2,3},{3,2},{4,5},{5,4},{6,7},{7,6},{8,9},{9,8},{10,11... | collective-permute-start | bytes 1572872 | tf_op jit(solution)/shard_map/ppermute | solution.py:202
  137.0 2.7 %copy-start.15 = (bf16[1024,512]{1,0:T(8,128)(2,1)S(1)}, bf16[1024,512]{1,0:T(8,128)(2,1)}, u32[]{:S(2)}) copy-start(bf16[1024,512]{1,0:T(8,128)(2,1)} %param.8) | copy-start | bytes 3145732
  137.0 2.7 %copy-start.19 = (bf16[512,512]{1,0:T(8,128)(2,1)S(1)}, bf16[512,512]{1,0:T(8,128)(2,1)}, u32[]{:S(2)}) copy-start(bf16[512,512]{1,0:T(8,128)(2,1)} %param.13) | copy-start | bytes 1572868
  194.1 2.1 %copy-start.17 = (bf16[1024,512]{1,0:T(8,128)(2,1)S(1)}, bf16[1024,512]{1,0:T(8,128)(2,1)}, u32[]{:S(2)}) copy-start(bf16[1024,512]{1,0:T(8,128)(2,1)} %param.15) | copy-start | bytes 3145732
  194.1 2.1 %copy-start.18 = (bf16[1024,512]{0,1:T(8,128)(2,1)S(1)}, bf16[1024,512]{0,1:T(8,128)(2,1)}, u32[]{:S(2)}) copy-start(bf16[1024,512]{0,1:T(8,128)(2,1)} %get-tuple-element.42) | copy-start | bytes 3145732
  194.1 2.1 %copy-start.20 = (bf16[512,512]{1,0:T(8,128)(2,1)S(1)}, bf16[512,512]{1,0:T(8,128)(2,1)}, u32[]{:S(2)}) copy-start(bf16[512,512]{1,0:T(8,128)(2,1)} %param.10) | copy-start | bytes 1572868
  196.2 3.1 %copy-start.13 = (bf16[512,512]{0,1:T(8,128)(2,1)S(1)}, bf16[512,512]{0,1:T(8,128)(2,1)}, u32[]{:S(2)}) copy-start(bf16[512,512]{0,1:T(8,128)(2,1)} %get-tuple-element.40) | copy-start | bytes 1572868
  198.0 2.5 %copy-start.12 = (bf16[512,512]{0,1:T(8,128)(2,1)S(1)}, bf16[512,512]{0,1:T(8,128)(2,1)}, u32[]{:S(2)}) copy-start(bf16[512,512]{0,1:T(8,128)(2,1)} %get-tuple-element.41) | copy-start | bytes 1572868
  (5 other events, 6.2 us)
Sparse Core Ops, SparseCore 0:
  128.2 65.8 all-reduce.2

commit v13 on v12

--- a/solution.py
+++ b/solution.py
@@ -220,11 +220,27 @@
     vals_grad = joined(dv).astype(bf16)
     wk_part = jnp.einsum("ka,kb->ab", hits_in, keys_grad, preferred_element_type=f32)
     wv_part = jnp.einsum("ka,kb->ab", hits_in, vals_grad, preferred_element_type=f32)
-    query_grad_sum, grad_wk, grad_wv = lax.psum(
-        (dq_r.transpose(2, 0, 1).reshape(n_queries, width).astype(bf16), wk_part.astype(bf16), wv_part.astype(bf16)), "region"
-    )
-    grad_wk = grad_wk.astype(f32)
-    grad_wv = grad_wv.astype(f32)
+    query_grad_sum = lax.psum(
+        dq_r.transpose(2, 0, 1).reshape(n_queries, width).astype(bf16), "region"
+    )
+    summed = jnp.concatenate([wk_part, wv_part], axis=0)
+    for k, bit, half in steps:
+        half = summed.shape[0] // 2
+        pairs = [(i, i ^ (1 << k)) for i in range(regions)]
+        other = lax.ppermute(
+            lax.dynamic_slice_in_dim(summed, (1 - bit) * half, half, 0).astype(bf16), "region", pairs
+        )
+        summed = lax.dynamic_slice_in_dim(summed, bit * half, half, 0) + other.astype(f32)
+    summed = summed.astype(bf16)
+    for k, bit, half in reversed(steps):
+        pairs = [(i, i ^ (1 << k)) for i in range(regions)]
+        other = lax.ppermute(summed, "region", pairs)
+        summed = jnp.concatenate(
+            [jnp.where(bit == 0, summed, other), jnp.where(bit == 0, other, summed)], axis=0
+        )
+    summed = summed.astype(f32)
+    grad_wk = summed[:width]
+    grad_wv = summed[width:]
     grad_q = query_grad_sum
     grad_wq = jnp.einsum("qa,qb->ab", queries_in, grad_q, preferred_element_type=f32)
     grad_queries = (

time: 209 us -> 232 us (1.11)
  waiting for transfers between devices: 80.4 us -> 87.3 us
  starting transfers between devices: 10.9 us -> 17.7 us
  matrix products: 24.4 us -> 28.2 us
  other arithmetic: 11.7 us -> 14.9 us
    ppermute x0 -> x6, waiting for transfers between devices: none -> 17.8 us  [the longest x3 9 us: on_device(): lax.ppermute(lax.dynamic_slice_in_dim(summed, (1 - bit) * half, half, 0)....]
    psum x1, waiting for transfers between devices: 52.7 us -> 41.2 us  [on_device(): lax.psum(dq_r.transpose(2, 0, 1).reshape(n_queries, width).astype(bf16),...]
    ppermute x0 -> x6, starting transfers between devices: none -> 6.86 us  [the longest x3 5.2 us: on_device(): lax.ppermute(lax.dynamic_slice_in_dim(summed, (1 - bit) * half, half, 0)....]
    unnamed x47 -> x49, local copies, waits for them, and re-layouts: 8.58 us -> 9.31 us
  transfers between devices with their start and end apart: 16 -> 22, of which waited for: 7 -> 10; matrix products, arithmetic and copies ran while one was open for 16% -> 20% of each run, Pallas kernels for 12% -> 11%
where the time goes in v13:
time: 232 us; the launch traced here: 231 us
  waiting for transfers between devices  87.3 us (38%)
  Pallas kernels  43.2 us (19%)
  matrix products  28.2 us (12%)
  local copies, waits for them, and re-layouts  25.3 us (11%)
  starting transfers between devices  17.7 us (8%)
  other arithmetic  14.9 us (6%)
  between operations  14.5 us (6%)
    psum x1, waiting for transfers between devices, on_device(): lax.psum(dq_r.transpose(2, 0, 1).reshape(n_queries, width).astype(bf16),...  41.2 us
    pallas_call x1, Pallas kernels, _backward(): pl.pallas_call(functools.partial(_bwd_kernel, scale=scale), grid=(heads,...  26 us
    pallas_call x1, Pallas kernels, _forward(): pl.pallas_call(functools.partial(_fwd_kernel, scale=scale), grid=(heads,...  17.3 us
    ppermute x6, waiting for transfers between devices, on_device(): other = lax.ppermute(gathered, 'region', pairs)  14.3 us
    ppermute x9, waiting for transfers between devices, on_device(): lax.ppermute((lax.dynamic_slice_in_dim(numer, (1 - bit) * half, half, 0)....  14 us
    unnamed x49, local copies, waits for them, and re-layouts  9.31 us
    ppermute x3, waiting for transfers between devices, on_device(): lax.ppermute(lax.dynamic_slice_in_dim(summed, (1 - bit) * half, half, 0)....  9 us
    ppermute x3, waiting for transfers between devices, on_device(): other = lax.ppermute(summed, 'region', pairs)  8.76 us
  transfers between devices with their start and end apart: 22, of which 10 were waited for; matrix products, arithmetic and copies ran while one was open for 20% of the time, Pallas kernels for 11%

profile of v13, /device:TPU:0, one launch (start us, length us, event | category | flops | bytes accessed | tf_op | source)
XLA Modules:
  0.0 231.1 jit_solution(10058257657240305272)
XLA Ops:
  8.4 1.8 convolution_convert_fusion.2
  10.2 1.8 copy.39.k_ref
  12.2 2.8 %convolution_convert_fusion.3 = bf16[1024,512]{0,1:T(8,128)(2,1)} fusion(bf16[1024,512]{1,0:T(8,128)(2,1)S(1)} %copy-done.18, bf16[512,512]{1,0:T(8,128)(2,1)} %param.10), kind=kOutput, calls=%fused_computation.12 | convolution fusion | flops 537395200 | bytes 2621440 | tf_op jit(solution)/shard_map/dot_general | solution.py:145
  15.0 2.0 copy.37
  17.0 2.8 %convolution_convert_fusion.1 = bf16[1024,512]{0,1:T(8,128)(2,1)} fusion(bf16[1024,512]{1,0:T(8,128)(2,1)S(1)} %copy-done, bf16[512,512]{1,0:T(8,128)(2,1)} %param.12), kind=kOutput, calls=%fused_computation.10 | convolution fusion | flops 537395200 | bytes 2621440 | tf_op jit(solution)/shard_map/dot_general | solution.py:147
  21.1 17.3 %shard_map.135 = (f32[8,64,1024]{2,1,0:T(8,128)S(1)}, f32[8,1,1024]{2,1,0:T(1,128)S(1)}, f32[8,1,1024]{2,1,0:T(1,128)S(1)}) custom-call(bf16[8,1024,64]{2,1,0:T(8,128)(2,1)S(1)} %bitcast.133, bf16[8,1024,64]{2,1,0:T(8,128)(2,1)} %copy.39.k_ref, bf16[8,64,1024]{2,1,0:T(8,128)(2,1)S(1)} %bitcast.138, f32[8,1,1024]{2,1,0:T(1,128)S(1)} %bitcast.141), custom_call_target="tpu_custom_call" | custom-call | tf_op jit(solution)/shard_map/pallas_call | solution.py:67
  41.1 2.6 %collective-permute-start.2 = (f32[8,256]{1,0:T(8,128)S(1)}, f32[8,256]{1,0:T(8,128)S(1)}, u32[]{:S(2)}, u32[]{:S(2)}) collective-permute-start(f32[8,256]{1,0:T(8,128)S(1)} %constant_dynamic-slice_fusion.7), channel_id=1, source_target_pairs={{0,2},{1,3},{2,0},{3,1},{4,6},{5,7},{6,4},{7,5},{8,10},{9,11},{10,... | collective-permute-start | bytes 24584 | tf_op jit(solution)/shard_map/ppermute | solution.py:168
  43.8 3.1 %convolution_convert_fusion = bf16[1024,512]{0,1:T(8,128)(2,1)} fusion(bf16[1024,512]{1,0:T(8,128)(2,1)} %param.15, bf16[512,512]{1,0:T(8,128)(2,1)} %param.13), kind=kOutput, calls=%fused_computation.9 | convolution fusion | flops 537395200 | bytes 2621440 | tf_op jit(solution)/shard_map/dot_general | solution.py:191
  47.4 2.7 %collective-permute-start.8 = (f32[8,128]{1,0:T(8,128)S(1)}, f32[8,128]{1,0:T(8,128)S(1)}, u32[]{:S(2)}, u32[]{:S(2)}) collective-permute-start(f32[8,128]{1,0:T(8,128)S(1)} %constant_dynamic-slice_fusion), channel_id=1, source_target_pairs={{0,4},{1,5},{2,6},{3,7},{4,0},{5,1},{6,2},{7,3},{8,12},{9,13},{10,... | collective-permute-start | bytes 12296 | tf_op jit(solution)/shard_map/ppermute | solution.py:168
  53.6 6.0 %collective-permute-done.3 = bf16[256,512]{0,1:T(8,128)(2,1)S(1)} collective-permute-done((bf16[256,512]{0,1:T(8,128)(2,1)S(1)}, bf16[256,512]{0,1:T(8,128)(2,1)S(1)}, u32[]{:S(2)}, u32[]{:S(2)}) %collective-permute-start.3) | collective-permute-done | bytes 262176 | tf_op jit(solution)/shard_map/ppermute | solution.py:168
  60.1 7.5 %collective-permute-done.5 = bf16[128,512]{0,1:T(8,128)(2,1)S(1)} collective-permute-done((bf16[128,512]{0,1:T(8,128)(2,1)S(1)}, bf16[128,512]{0,1:T(8,128)(2,1)S(1)}, u32[]{:S(2)}, u32[]{:S(2)}) %collective-permute-start.5) | collective-permute-done | bytes 131104 | tf_op jit(solution)/shard_map/ppermute | solution.py:168
  68.7 4.5 %collective-permute-done.12 = f32[16,128]{1,0:T(8,128)S(1)} collective-permute-done((f32[16,128]{1,0:T(8,128)S(1)}, f32[16,128]{1,0:T(8,128)S(1)}, u32[]{:S(2)}, u32[]{:S(2)}) %collective-permute-start.12) | collective-permute-done | bytes 8224 | tf_op jit(solution)/shard_map/ppermute | solution.py:202
  73.3 3.7 %collective-permute-done.13 = f32[16,256]{1,0:T(8,128)S(1)} collective-permute-done((f32[16,256]{1,0:T(8,128)S(1)}, f32[16,256]{1,0:T(8,128)S(1)}, u32[]{:S(2)}, u32[]{:S(2)}) %collective-permute-start.13) | collective-permute-done | bytes 16416 | tf_op jit(solution)/shard_map/ppermute | solution.py:202
  77.2 2.8 %copy.40 = bf16[1024,8,64]{2,0,1:T(8,128)(2,1)} copy(bf16[1024,8,64]{0,2,1:T(8,128)(2,1)} %bitcast.137) | data formatting | bytes 2097152 | tf_op jit(solution)/shard_map/reshape | solution.py:140
  80.0 2.7 %copy.41 = bf16[1024,8,64]{2,0,1:T(8,128)(2,1)} copy(bf16[1024,8,64]{0,2,1:T(8,128)(2,1)} %bitcast.150) | data formatting | bytes 2097152 | tf_op jit(solution)/shard_map/reshape | solution.py:140
  84.0 26.0 %shard_map.136 = (f32[8,64,1024]{2,1,0:T(8,128)S(1)}, f32[8,1024,64]{2,1,0:T(8,128)}, f32[8,1024,64]{2,1,0:T(8,128)}) custom-call(bf16[8,1024,64]{2,1,0:T(8,128)(2,1)S(1)} %bitcast.134, bf16[8,1024,64]{2,1,0:T(8,128)(2,1)} %copy.39.k_ref, bf16[8,1024,64]{2,1,0:T(8,128)(2,1)} %bitcast.143, bf16[8,64,1024]{2,1,0:T(8,128)(2,1)S(1)} %bitcast.136, ...), custom_call_target="tpu_custom_call" | custom-call | tf_op jit(solution)/shard_map/pallas_call | solution.py:96
  110.0 6.4 %convert_bitcast_fusion = (bf16[1024,8,64]{2,0,1:T(8,128)(2,1)S(1)}, bf16[1024,8,64]{2,0,1:T(8,128)(2,1)}) fusion(f32[8,1024,64]{2,1,0:T(8,128)} %get-tuple-element.18, f32[8,1024,64]{2,1,0:T(8,128)} %get-tuple-element.17), kind=kLoop, calls=%fused_computation.5 | loop fusion | flops 1048576 | bytes 6291456 | tf_op jit(solution)/shard_map/convert_element_type | solution.py:220
  116.4 2.7 %copy.44 = bf16[1024,8,64]{0,2,1:T(8,128)(2,1)} copy(bf16[1024,8,64]{2,0,1:T(8,128)(2,1)} %get-tuple-element.81) | data formatting | bytes 2097152 | tf_op jit(solution)/shard_map/convert_element_type | solution.py:219
  119.1 3.0 %convolution_bitcast_fusion.1 = f32[512,512]{0,1:T(8,128)} fusion(bf16[1024,512]{0,1:T(8,128)(2,1)} %bitcast.145, bf16[1024,512]{1,0:T(8,128)(2,1)S(1)} %copy-done), kind=kOutput, calls=%fused_computation.14 | convolution fusion | flops 536870912 | bytes 3145728 | tf_op jit(solution)/shard_map/ka,kb->ab/dot_general | solution.py:221
  122.1 2.1 fusion.26
  125.8 2.1 convolution_bitcast_fusion
  130.1 1.7 add_convert_fusion
  133.1 1.8 collective-permute-start.10
  137.5 6.0 %collective-permute-done.10 = bf16[256,512]{0,1:T(8,128)(2,1)S(1)} collective-permute-done((bf16[256,512]{0,1:T(8,128)(2,1)S(1)}, bf16[256,512]{0,1:T(8,128)(2,1)S(1)}, u32[]{:S(2)}, u32[]{:S(2)}) %collective-permute-start.10) | collective-permute-done | bytes 262176 | tf_op jit(solution)/shard_map/ppermute | solution.py:202
  143.8 9.0 %collective-permute-done.16 = bf16[256,512]{0,1:T(8,128)(2,1)S(1)} collective-permute-done((bf16[256,512]{0,1:T(8,128)(2,1)S(1)}, bf16[256,512]{0,1:T(8,128)(2,1)S(1)}, u32[]{:S(2)}, u32[]{:S(2)}) %collective-permute-start.16) | collective-permute-done | bytes 262176 | tf_op jit(solution)/shard_map/ppermute | solution.py:230
  152.9 3.5 %collective-permute-start.17 = (bf16[128,512]{0,1:T(8,128)(2,1)S(1)}, bf16[128,512]{0,1:T(8,128)(2,1)S(1)}, u32[]{:S(2)}, u32[]{:S(2)}) collective-permute-start(bf16[128,512]{0,1:T(8,128)(2,1)S(1)} %dynamic-slice_convert_fusion.3), channel_id=1, source_target_pairs={{0,4},{1,5},{2,6},{3,7},{4,0},{5,1},{6,2},{7,3},{8,12},{9,13},{10,... | collective-permute-start | bytes 393224 | tf_op jit(solution)/shard_map/ppermute | solution.py:230
  156.4 41.2 %all-reduce.2.cloned.1.call-done = bf16[1024,512]{0,1:T(8,128)(2,1)} async-done(((bf16[1024,512]{0,1:T(8,128)(2,1)}), bf16[1024,512]{0,1:T(8,128)(2,1)}) %all-reduce.2.cloned.1.call-update) | async-done | bytes 1048592 | tf_op jit(solution)/shard_map/psum | solution.py:223
  197.6 3.5 %add_convert_fusion.1 = bf16[1024,512]{1,0:T(8,128)(2,1)} fusion(bf16[1024,512]{1,0:T(8,128)(2,1)} %param.15, bf16[1024,512]{0,1:T(8,128)(2,1)} %all-reduce.2.cloned.1.call-done, bf16[512,512]{1,0:T(8,128)(2,1)} %param.10), kind=kOutput, calls=%fused_computation.7 | convolution fusion | flops 538443776 | bytes 3670016 | tf_op jit(solution)/shard_map/dot_general | solution.py:248
  202.7 1.9 convolution_bitcast_fusion.2
  205.9 2.6 %collective-permute-done.18 = bf16[128,512]{0,1:T(8,128)(2,1)S(1)} collective-permute-done((bf16[128,512]{0,1:T(8,128)(2,1)S(1)}, bf16[128,512]{0,1:T(8,128)(2,1)S(1)}, u32[]{:S(2)}, u32[]{:S(2)}) %collective-permute-start.18) | collective-permute-done | bytes 131104 | tf_op jit(solution)/shard_map/ppermute | solution.py:237
  208.9 6.2 %collective-permute-done.19 = bf16[256,512]{0,1:T(8,128)(2,1)S(1)} collective-permute-done((bf16[256,512]{0,1:T(8,128)(2,1)S(1)}, bf16[256,512]{0,1:T(8,128)(2,1)S(1)}, u32[]{:S(2)}, u32[]{:S(2)}) %collective-permute-start.19) | collective-permute-done | bytes 262176 | tf_op jit(solution)/shard_map/ppermute | solution.py:237
  220.4 2.6 %copy.49 = f32[512,512]{1,0:T(8,128)} copy(f32[512,512]{0,1:T(8,128)} %get-tuple-element.45) | data formatting | bytes 2097152
  (132 shorter events, 30.3 us)
Async XLA Ops:
  7.2 190.4 %all-reduce.2.cloned.1.call-start = ((), (), s32[]{:S(2)}) async-start(), calls=%async_computation | async-start | bytes 2097152 | tf_op jit(solution)/shard_map/psum | solution.py:223
  10.2 4.8 %copy-start.2 = (bf16[1024,512]{0,1:T(8,128)(2,1)}, bf16[1024,512]{0,1:T(8,128)(2,1)S(1)}, u32[]{:S(2)}) copy-start(bf16[1024,512]{0,1:T(8,128)(2,1)S(1)} %convolution_convert_fusion.2) | copy-start | bytes 3145732
  38.4 2.7 %collective-permute-start = (f32[8,512]{1,0:T(8,128)S(1)}, f32[8,512]{1,0:T(8,128)S(1)}, u32[]{:S(2)}, u32[]{:S(2)}) collective-permute-start(f32[8,512]{1,0:T(8,128)S(1)} %bitcast.154), channel_id=1, source_target_pairs={{0,1},{1,0},{2,3},{3,2},{4,5},{5,4},{6,7},{7,6},{8,9},{9,8},{10,11... | collective-permute-start | bytes 49160 | tf_op jit(solution)/shard_map/ppermute | solution.py:168
  39.0 2.1 collective-permute-start.6
  40.6 9.5 %collective-permute-start.1 = (bf16[512,512]{0,1:T(8,128)(2,1)}, bf16[512,512]{0,1:T(8,128)(2,1)}, u32[]{:S(2)}, u32[]{:S(2)}) collective-permute-start(bf16[512,512]{0,1:T(8,128)(2,1)} %dynamic-slice_convert_fusion), channel_id=1, source_target_pairs={{0,1},{1,0},{2,3},{3,2},{4,5},{5,4},{6,7},{7,6},{8,9},{9,8},{10,11... | collective-permute-start | bytes 1572872 | tf_op jit(solution)/shard_map/ppermute | solution.py:168
  41.1 5.8 %collective-permute-start.2 = (f32[8,256]{1,0:T(8,128)S(1)}, f32[8,256]{1,0:T(8,128)S(1)}, u32[]{:S(2)}, u32[]{:S(2)}) collective-permute-start(f32[8,256]{1,0:T(8,128)S(1)} %constant_dynamic-slice_fusion.7), channel_id=1, source_target_pairs={{0,2},{1,3},{2,0},{3,1},{4,6},{5,7},{6,4},{7,5},{8,10},{9,11},{10,... | collective-permute-start | bytes 24584 | tf_op jit(solution)/shard_map/ppermute | solution.py:168
  43.7 3.7 %collective-permute-start.7 = (f32[8,256]{1,0:T(8,128)S(1)}, f32[8,256]{1,0:T(8,128)S(1)}, u32[]{:S(2)}, u32[]{:S(2)}) collective-permute-start(f32[8,256]{1,0:T(8,128)S(1)} %constant_dynamic-slice_fusion.2), channel_id=1, source_target_pairs={{0,2},{1,3},{2,0},{3,1},{4,6},{5,7},{6,4},{7,5},{8,10},{9,11},{10,... | collective-permute-start | bytes 24584 | tf_op jit(solution)/shard_map/ppermute | solution.py:168
  47.4 12.7 %collective-permute-start.8 = (f32[8,128]{1,0:T(8,128)S(1)}, f32[8,128]{1,0:T(8,128)S(1)}, u32[]{:S(2)}, u32[]{:S(2)}) collective-permute-start(f32[8,128]{1,0:T(8,128)S(1)} %constant_dynamic-slice_fusion), channel_id=1, source_target_pairs={{0,4},{1,5},{2,6},{3,7},{4,0},{5,1},{6,2},{7,3},{8,12},{9,13},{10,... | collective-permute-start | bytes 12296 | tf_op jit(solution)/shard_map/ppermute | solution.py:168
  51.7 7.9 %collective-permute-start.3 = (bf16[256,512]{0,1:T(8,128)(2,1)S(1)}, bf16[256,512]{0,1:T(8,128)(2,1)S(1)}, u32[]{:S(2)}, u32[]{:S(2)}) collective-permute-start(bf16[256,512]{0,1:T(8,128)(2,1)S(1)} %dynamic-slice_convert_fusion.2), channel_id=1, source_target_pairs={{0,2},{1,3},{2,0},{3,1},{4,6},{5,7},{6,4},{7,5},{8,10},{9,11},{10,... | collective-permute-start | bytes 786440 | tf_op jit(solution)/shard_map/ppermute | solution.py:168
  53.2 6.9 %collective-permute-start.4 = (f32[8,128]{1,0:T(8,128)S(1)}, f32[8,128]{1,0:T(8,128)S(1)}, u32[]{:S(2)}, u32[]{:S(2)}) collective-permute-start(f32[8,128]{1,0:T(8,128)S(1)} %constant_dynamic-slice_fusion.5), channel_id=1, source_target_pairs={{0,4},{1,5},{2,6},{3,7},{4,0},{5,1},{6,2},{7,3},{8,12},{9,13},{10,... | collective-permute-start | bytes 12296 | tf_op jit(solution)/shard_map/ppermute | solution.py:168
  59.8 7.9 %collective-permute-start.5 = (bf16[128,512]{0,1:T(8,128)(2,1)S(1)}, bf16[128,512]{0,1:T(8,128)(2,1)S(1)}, u32[]{:S(2)}, u32[]{:S(2)}) collective-permute-start(bf16[128,512]{0,1:T(8,128)(2,1)S(1)} %dynamic-slice_convert_fusion.4), channel_id=1, source_target_pairs={{0,4},{1,5},{2,6},{3,7},{4,0},{5,1},{6,2},{7,3},{8,12},{9,13},{10,... | collective-permute-start | bytes 393224 | tf_op jit(solution)/shard_map/ppermute | solution.py:168
  68.6 4.6 %collective-permute-start.12 = (f32[16,128]{1,0:T(8,128)S(1)}, f32[16,128]{1,0:T(8,128)S(1)}, u32[]{:S(2)}, u32[]{:S(2)}) collective-permute-start(f32[16,128]{1,0:T(8,128)S(1)} %pad_maximum_fusion.10), channel_id=1, source_target_pairs={{0,4},{1,5},{2,6},{3,7},{4,0},{5,1},{6,2},{7,3},{8,12},{9,13},{10,... | collective-permute-start | bytes 24584 | tf_op jit(solution)/shard_map/ppermute | solution.py:202
  73.3 3.8 %collective-permute-start.13 = (f32[16,256]{1,0:T(8,128)S(1)}, f32[16,256]{1,0:T(8,128)S(1)}, u32[]{:S(2)}, u32[]{:S(2)}) collective-permute-start(f32[16,256]{1,0:T(8,128)S(1)} %pad_maximum_fusion.9), channel_id=1, source_target_pairs={{0,2},{1,3},{2,0},{3,1},{4,6},{5,7},{6,4},{7,5},{8,10},{9,11},{10,... | collective-permute-start | bytes 49160 | tf_op jit(solution)/shard_map/ppermute | solution.py:202
  77.1 5.6 %collective-permute-start.14 = (f32[16,512]{1,0:T(8,128)S(1)}, f32[16,512]{1,0:T(8,128)S(1)}, u32[]{:S(2)}, u32[]{:S(2)}) collective-permute-start(f32[16,512]{1,0:T(8,128)S(1)} %pad_maximum_fusion.8), channel_id=1, source_target_pairs={{0,1},{1,0},{2,3},{3,2},{4,5},{5,4},{6,7},{7,6},{8,9},{9,8},{10,11... | collective-permute-start | bytes 98312 | tf_op jit(solution)/shard_map/ppermute | solution.py:202
  82.7 50.4 %collective-permute-start.9 = (bf16[128,512]{0,1:T(8,128)(2,1)S(1)}, bf16[128,512]{0,1:T(8,128)(2,1)S(1)}, u32[]{:S(2)}, u32[]{:S(2)}) collective-permute-start(bf16[128,512]{0,1:T(8,128)(2,1)S(1)} %get-tuple-element.41), channel_id=1, source_target_pairs={{0,4},{1,5},{2,6},{3,7},{4,0},{5,1},{6,2},{7,3},{8,12},{9,13},{10,... | collective-permute-start | bytes 393224 | tf_op jit(solution)/shard_map/ppermute | solution.py:202
  110.0 6.4 %copy-start.5 = (f32[8,64,1024]{2,1,0:T(8,128)}, f32[8,64,1024]{2,1,0:T(8,128)S(1)}, u32[]{:S(2)}) copy-start(f32[8,64,1024]{2,1,0:T(8,128)S(1)} %get-tuple-element.16) | copy-start | bytes 6291460
  119.1 3.0 %copy-start.9 = (bf16[1024,8,64]{0,2,1:T(8,128)(2,1)S(1)}, bf16[1024,8,64]{0,2,1:T(8,128)(2,1)}, u32[]{:S(2)}) copy-start(bf16[1024,8,64]{0,2,1:T(8,128)(2,1)} %copy.44) | copy-start | bytes 3145732
  119.1 3.0 %copy-start.15 = (bf16[512,512]{1,0:T(8,128)(2,1)S(1)}, bf16[512,512]{1,0:T(8,128)(2,1)}, u32[]{:S(2)}) copy-start(bf16[512,512]{1,0:T(8,128)(2,1)} %param.11) | copy-start | bytes 1572868
  125.8 3.7 %copy-start.10 = (bf16[1024,8,64]{0,2,1:T(8,128)(2,1)S(1)}, bf16[1024,8,64]{0,2,1:T(8,128)(2,1)}, u32[]{:S(2)}) copy-start(bf16[1024,8,64]{0,2,1:T(8,128)(2,1)} %copy.45) | copy-start | bytes 3145732
  129.0 2.9 %copy-start.6 = (f32[8,64,1024]{2,1,0:T(8,128)S(1)}, f32[8,64,1024]{2,1,0:T(8,128)}, u32[]{:S(2)}) copy-start(f32[8,64,1024]{2,1,0:T(8,128)} %copy-done.5) | copy-start | bytes 6291460
  129.0 5.9 %collective-permute-start.15 = (bf16[512,512]{0,1:T(8,128)(2,1)}, bf16[512,512]{0,1:T(8,128)(2,1)}, u32[]{:S(2)}, u32[]{:S(2)}) collective-permute-start(bf16[512,512]{0,1:T(8,128)(2,1)} %fusion.1), channel_id=1, source_target_pairs={{0,1},{1,0},{2,3},{3,2},{4,5},{5,4},{6,7},{7,6},{8,9},{9,8},{10,11... | collective-permute-start | bytes 1572872 | tf_op jit(solution)/shard_map/ppermute | solution.py:230
  131.9 3.1 %copy-start.12 = (f32[512,512]{0,1:T(8,128)S(1)}, f32[512,512]{0,1:T(8,128)}, u32[]{:S(2)}) copy-start(f32[512,512]{0,1:T(8,128)} %convolution_bitcast_fusion.1) | copy-start | bytes 3145732
  133.1 10.4 %collective-permute-start.10 = (bf16[256,512]{0,1:T(8,128)(2,1)S(1)}, bf16[256,512]{0,1:T(8,128)(2,1)S(1)}, u32[]{:S(2)}, u32[]{:S(2)}) collective-permute-start(bf16[256,512]{0,1:T(8,128)(2,1)S(1)} %pad_maximum_fusion.5), channel_id=1, source_target_pairs={{0,2},{1,3},{2,0},{3,1},{4,6},{5,7},{6,4},{7,5},{8,10},{9,11},{10,... | collective-permute-start | bytes 786440 | tf_op jit(solution)/shard_map/ppermute | solution.py:202
  136.4 16.4 %collective-permute-start.16 = (bf16[256,512]{0,1:T(8,128)(2,1)S(1)}, bf16[256,512]{0,1:T(8,128)(2,1)S(1)}, u32[]{:S(2)}, u32[]{:S(2)}) collective-permute-start(bf16[256,512]{0,1:T(8,128)(2,1)S(1)} %dynamic-slice_convert_fusion.1), channel_id=1, source_target_pairs={{0,2},{1,3},{2,0},{3,1},{4,6},{5,7},{6,4},{7,5},{8,10},{9,11},{10,... | collective-permute-start | bytes 786440 | tf_op jit(solution)/shard_map/ppermute | solution.py:230
  143.7 65.0 %collective-permute-start.11 = (bf16[512,512]{0,1:T(8,128)(2,1)S(1)}, bf16[512,512]{0,1:T(8,128)(2,1)S(1)}, u32[]{:S(2)}, u32[]{:S(2)}) collective-permute-start(bf16[512,512]{0,1:T(8,128)(2,1)S(1)} %pad_maximum_fusion.3), channel_id=1, source_target_pairs={{0,1},{1,0},{2,3},{3,2},{4,5},{5,4},{6,7},{7,6},{8,9},{9,8},{10,11... | collective-permute-start | bytes 1572872 | tf_op jit(solution)/shard_map/ppermute | solution.py:202
  152.9 48.2 %collective-permute-start.17 = (bf16[128,512]{0,1:T(8,128)(2,1)S(1)}, bf16[128,512]{0,1:T(8,128)(2,1)S(1)}, u32[]{:S(2)}, u32[]{:S(2)}) collective-permute-start(bf16[128,512]{0,1:T(8,128)(2,1)S(1)} %dynamic-slice_convert_fusion.3), channel_id=1, source_target_pairs={{0,4},{1,5},{2,6},{3,7},{4,0},{5,1},{6,2},{7,3},{8,12},{9,13},{10,... | collective-permute-start | bytes 393224 | tf_op jit(solution)/shard_map/ppermute | solution.py:230
  197.6 5.1 %copy-start.20 = (bf16[1024,512]{0,1:T(8,128)(2,1)S(1)}, bf16[1024,512]{0,1:T(8,128)(2,1)}, u32[]{:S(2)}) copy-start(bf16[1024,512]{0,1:T(8,128)(2,1)} %all-reduce.2.cloned.1.call-done) | copy-start | bytes 3145732
  201.2 7.4 %collective-permute-start.18 = (bf16[128,512]{0,1:T(8,128)(2,1)S(1)}, bf16[128,512]{0,1:T(8,128)(2,1)S(1)}, u32[]{:S(2)}, u32[]{:S(2)}) collective-permute-start(bf16[128,512]{0,1:T(8,128)(2,1)S(1)} %add_convert_fusion.3), channel_id=1, source_target_pairs={{0,4},{1,5},{2,6},{3,7},{4,0},{5,1},{6,2},{7,3},{8,12},{9,13},{10,... | collective-permute-start | bytes 393224 | tf_op jit(solution)/shard_map/ppermute | solution.py:237
  208.6 6.7 %copy-start.17 = (bf16[1024,512]{1,0:T(8,128)(2,1)S(1)}, bf16[1024,512]{1,0:T(8,128)(2,1)}, u32[]{:S(2)}) copy-start(bf16[1024,512]{1,0:T(8,128)(2,1)} %param.15) | copy-start | bytes 3145732
  208.6 6.4 %collective-permute-start.19 = (bf16[256,512]{0,1:T(8,128)(2,1)S(1)}, bf16[256,512]{0,1:T(8,128)(2,1)S(1)}, u32[]{:S(2)}, u32[]{:S(2)}) collective-permute-start(bf16[256,512]{0,1:T(8,128)(2,1)S(1)} %pad_maximum_fusion.6), channel_id=1, source_target_pairs={{0,2},{1,3},{2,0},{3,1},{4,6},{5,7},{6,4},{7,5},{8,10},{9,11},{10,... | collective-permute-start | bytes 786440 | tf_op jit(solution)/shard_map/ppermute | solution.py:237
  215.2 3.5 %collective-permute-start.20 = (bf16[512,512]{0,1:T(8,128)(2,1)S(1)}, bf16[512,512]{0,1:T(8,128)(2,1)S(1)}, u32[]{:S(2)}, u32[]{:S(2)}) collective-permute-start(bf16[512,512]{0,1:T(8,128)(2,1)S(1)} %pad_maximum_fusion.4), channel_id=1, source_target_pairs={{0,1},{1,0},{2,3},{3,2},{4,5},{5,4},{6,7},{7,6},{8,9},{9,8},{10,11... | collective-permute-start | bytes 1572872 | tf_op jit(solution)/shard_map/ppermute | solution.py:237
  220.4 3.9 %copy-start.1 = (bf16[1024,512]{1,0:T(8,128)(2,1)S(1)}, bf16[1024,512]{1,0:T(8,128)(2,1)}, u32[]{:S(2)}) copy-start(bf16[1024,512]{1,0:T(8,128)(2,1)} %param.9) | copy-start | bytes 3145732
  (12 other events, 20.2 us)
Sparse Core Ops, SparseCore 0:
  133.2 64.3 all-reduce.1

commit v14 on v12

--- a/solution.py
+++ b/solution.py
@@ -35,11 +35,13 @@
 
 def _bwd_kernel(q_ref, k_ref, v_ref, kt_ref, ga_ref, lt_ref, dl_ref, cm_ref, dq_ref, dk_ref, dv_ref, *, scale):
     i = pl.program_id(1)
-
-    @pl.when(i == 0)
-    def _():
-        dk_ref[...] = jnp.zeros_like(dk_ref)
-        dv_ref[...] = jnp.zeros_like(dv_ref)
+    single = dk_ref.dtype == jnp.bfloat16
+
+    if not single:
+        @pl.when(i == 0)
+        def _():
+            dk_ref[...] = jnp.zeros_like(dk_ref)
+            dv_ref[...] = jnp.zeros_like(dv_ref)
 
     q = q_ref[0]
     k = k_ref[0]
@@ -51,11 +53,17 @@
     s3 = s.reshape(hb, BLOCK, tq)
     allowed = cm_ref[...] > 0.5
     p = jnp.where(allowed, jnp.exp(s3 - lt_ref[...]), 0.0).reshape(nk, tq)
-    dv_ref[0] += jnp.dot(p.astype(jnp.bfloat16), ga, preferred_element_type=jnp.float32)
+    dv = jnp.dot(p.astype(jnp.bfloat16), ga, preferred_element_type=jnp.float32)
     dp = lax.dot_general(v, ga, (((1,), (1,)), ((), ())), preferred_element_type=jnp.float32)
     ds = (p * (dp - dl_ref[0]) * scale).astype(jnp.bfloat16)
-    dk_ref[0] += jnp.dot(ds, q, preferred_element_type=jnp.float32)
-    dq_ref[0] = jnp.dot(kt_ref[0], ds, preferred_element_type=jnp.float32)
+    dk = jnp.dot(ds, q, preferred_element_type=jnp.float32)
+    if single:
+        dv_ref[0] = dv.astype(dv_ref.dtype)
+        dk_ref[0] = dk.astype(dk_ref.dtype)
+    else:
+        dv_ref[0] += dv
+        dk_ref[0] += dk
+    dq_ref[0] = jnp.dot(kt_ref[0], ds, preferred_element_type=jnp.float32).astype(dq_ref.dtype)
 
 
 def _forward(qT, kT, vTT, cm, scale):
@@ -93,6 +101,7 @@
     hb = nk // BLOCK
     tile = min(nq, 2 * TQ)
     f32 = jnp.float32
+    grad_type = jnp.bfloat16 if tile == nq else f32
     return pl.pallas_call(
         functools.partial(_bwd_kernel, scale=scale),
         grid=(heads, nq // tile),
@@ -112,9 +121,9 @@
             pl.BlockSpec((1, nk, hd), lambda h, i: (h, 0, 0)),
         ],
         out_shape=[
-            jax.ShapeDtypeStruct((heads, hd, nq), f32),
-            jax.ShapeDtypeStruct((heads, nk, hd), f32),
-            jax.ShapeDtypeStruct((heads, nk, hd), f32),
+            jax.ShapeDtypeStruct((heads, hd, nq), jnp.bfloat16),
+            jax.ShapeDtypeStruct((heads, nk, hd), grad_type),
+            jax.ShapeDtypeStruct((heads, nk, hd), grad_type),
         ],
         compiler_params=pltpu.CompilerParams(
             dimension_semantics=("parallel", "arbitrary"), vmem_limit_bytes=48 * 1024 * 1024

time: 209 us -> 196 us (0.938)
  waiting for transfers between devices: 80.4 us -> 71.2 us
  starting transfers between devices: 10.9 us -> 17.2 us
  other arithmetic: 11.7 us -> 6.54 us
  matrix products: 24.4 us -> 22 us
    convert_element_type x2 -> x0, other arithmetic: 7.51 us -> none  [the longest x1 6.37 us: on_device(): vals_grad = joined(dv).astype(bf16)]
    ppermute x9, waiting for transfers between devices: 14 us -> 9.5 us  [on_device(): lax.ppermute((lax.dynamic_slice_in_dim(numer, (1 - bit) * half, half, 0)....]
    convert_element_type x2 -> x0, local copies, waits for them, and re-layouts: 4.44 us -> none  [the longest x1 2.83 us: on_device(): vals_grad = joined(dv).astype(bf16)]
    ppermute x6, starting transfers between devices: 2.09 us -> 6.18 us  [on_device(): other = lax.ppermute(gathered, 'region', pairs)]
    psum x1, waiting for transfers between devices: 52.7 us -> 48.7 us  [on_device(): lax.psum((dq_r.transpose(2, 0, 1).reshape(n_queries, width).astype(bf16),...]
    transpose x0 -> x2, local copies, waits for them, and re-layouts: none -> 3.98 us  [joined(): return x.transpose(1, 0, 2).reshape(x.shape[1], width)]
    ppermute x9, starting transfers between devices: 8.73 us -> 11 us  [on_device(): lax.ppermute((lax.dynamic_slice_in_dim(numer, (1 - bit) * half, half, 0)....]
    unnamed x47 -> x51, local copies, waits for them, and re-layouts: 8.58 us -> 8.16 us
  transfers between devices with their start and end apart: 16 -> 16, of which waited for: 7 -> 7; matrix products, arithmetic and copies ran while one was open for 16% -> 11% of each run, Pallas kernels for 12% -> 12%
where the time goes in v14:
time: 196 us; the launch traced here: 195 us
  waiting for transfers between devices  71.2 us (36%)
  Pallas kernels  41.2 us (21%)
  local copies, waits for them, and re-layouts  22.2 us (11%)
  matrix products  22 us (11%)
  starting transfers between devices  17.2 us (9%)
  between operations  14.5 us (7%)
  other arithmetic  6.54 us (3%)
    psum x1, waiting for transfers between devices, on_device(): lax.psum((dq_r.transpose(2, 0, 1).reshape(n_queries, width).astype(bf16),...  48.7 us
    pallas_call x1, Pallas kernels, _backward(): pl.pallas_call(functools.partial(_bwd_kernel, scale=scale), grid=(heads,...  24 us
    pallas_call x1, Pallas kernels, _forward(): pl.pallas_call(functools.partial(_fwd_kernel, scale=scale), grid=(heads,...  17.3 us
    ppermute x6, waiting for transfers between devices, on_device(): other = lax.ppermute(gathered, 'region', pairs)  13.1 us
    ppermute x9, starting transfers between devices, on_device(): lax.ppermute((lax.dynamic_slice_in_dim(numer, (1 - bit) * half, half, 0)....  11 us
    ppermute x9, waiting for transfers between devices, on_device(): lax.ppermute((lax.dynamic_slice_in_dim(numer, (1 - bit) * half, half, 0)....  9.5 us
    unnamed x51, local copies, waits for them, and re-layouts  8.16 us
    ppermute x6, starting transfers between devices, on_device(): other = lax.ppermute(gathered, 'region', pairs)  6.18 us
  transfers between devices with their start and end apart: 16, of which 7 were waited for; matrix products, arithmetic and copies ran while one was open for 11% of the time, Pallas kernels for 12%

profile of v14, /device:TPU:0, one launch (start us, length us, event | category | flops | bytes accessed | tf_op | source)
XLA Modules:
  0.0 194.9 jit_solution(12916603524050159887)
XLA Ops:
  8.4 2.8 %convolution_convert_fusion.2 = bf16[1024,512]{0,1:T(8,128)(2,1)} fusion(bf16[1024,512]{1,0:T(8,128)(2,1)S(1)} %copy-done, bf16[512,512]{1,0:T(8,128)(2,1)} %param.11), kind=kOutput, calls=%fused_computation.5 | convolution fusion | flops 537395200 | bytes 2621440 | tf_op jit(solution)/shard_map/dot_general | solution.py:155
  11.2 1.7 convolution_convert_fusion.1
  12.9 1.7 convolution_convert_fusion.3
  14.7 2.0 %copy.33 = bf16[1024,8,64]{2,0,1:T(8,128)(2,1)S(1)} copy(bf16[1024,8,64]{0,2,1:T(8,128)(2,1)} %bitcast.150) | data formatting | bytes 2097152 | tf_op jit(solution)/shard_map/reshape | solution.py:149
  16.7 3.3 %copy.35.k_ref = bf16[8,1024,64]{2,1,0:T(8,128)(2,1)} copy(bf16[8,1024,64]{1,2,0:T(8,128)(2,1)} %bitcast.133) | data formatting | bytes 2097152 | tf_op jit(solution)/shard_map/transpose | solution.py:149
  21.3 17.3 %shard_map.135 = (f32[8,64,1024]{2,1,0:T(8,128)S(1)}, f32[8,1,1024]{2,1,0:T(1,128)S(1)}, f32[8,1,1024]{2,1,0:T(1,128)S(1)}) custom-call(bf16[8,1024,64]{2,1,0:T(8,128)(2,1)S(1)} %bitcast.131, bf16[8,1024,64]{2,1,0:T(8,128)(2,1)} %copy.35.k_ref, bf16[8,64,1024]{2,1,0:T(8,128)(2,1)S(1)} %bitcast.135, f32[8,1,1024]{2,1,0:T(1,128)S(1)} %bitcast.140), custom_call_target="tpu_custom_call" | custom-call | tf_op jit(solution)/shard_map/pallas_call | solution.py:75
  41.4 2.6 %collective-permute-start.2 = (f32[8,256]{1,0:T(8,128)S(1)}, f32[8,256]{1,0:T(8,128)S(1)}, u32[]{:S(2)}, u32[]{:S(2)}) collective-permute-start(f32[8,256]{1,0:T(8,128)S(1)} %constant_dynamic-slice_fusion.7), channel_id=1, source_target_pairs={{0,2},{1,3},{2,0},{3,1},{4,6},{5,7},{6,4},{7,5},{8,10},{9,11},{10,... | collective-permute-start | bytes 24584 | tf_op jit(solution)/shard_map/ppermute | solution.py:177
  44.0 3.1 %convolution_convert_fusion = bf16[1024,512]{0,1:T(8,128)(2,1)} fusion(bf16[1024,512]{1,0:T(8,128)(2,1)} %param.15, bf16[512,512]{1,0:T(8,128)(2,1)} %param.13), kind=kOutput, calls=%fused_computation.3 | convolution fusion | flops 537395200 | bytes 2621440 | tf_op jit(solution)/shard_map/dot_general | solution.py:200
  49.0 1.5 collective-permute-start.3
  50.5 2.7 %collective-permute-start.4 = (f32[8,128]{1,0:T(8,128)S(1)}, f32[8,128]{1,0:T(8,128)S(1)}, u32[]{:S(2)}, u32[]{:S(2)}) collective-permute-start(f32[8,128]{1,0:T(8,128)S(1)} %constant_dynamic-slice_fusion.5), channel_id=1, source_target_pairs={{0,4},{1,5},{2,6},{3,7},{4,0},{5,1},{6,2},{7,3},{8,12},{9,13},{10,... | collective-permute-start | bytes 12296 | tf_op jit(solution)/shard_map/ppermute | solution.py:177
  53.4 3.7 %collective-permute-done.3 = bf16[256,512]{0,1:T(8,128)(2,1)S(1)} collective-permute-done((bf16[256,512]{0,1:T(8,128)(2,1)S(1)}, bf16[256,512]{0,1:T(8,128)(2,1)S(1)}, u32[]{:S(2)}, u32[]{:S(2)}) %collective-permute-start.3) | collective-permute-done | bytes 262176 | tf_op jit(solution)/shard_map/ppermute | solution.py:177
  57.2 2.8 %collective-permute-start.5 = (bf16[128,512]{0,1:T(8,128)(2,1)S(1)}, bf16[128,512]{0,1:T(8,128)(2,1)S(1)}, u32[]{:S(2)}, u32[]{:S(2)}) collective-permute-start(bf16[128,512]{0,1:T(8,128)(2,1)S(1)} %dynamic-slice_convert_fusion.2), channel_id=1, source_target_pairs={{0,4},{1,5},{2,6},{3,7},{4,0},{5,1},{6,2},{7,3},{8,12},{9,13},{10,... | collective-permute-start | bytes 393224 | tf_op jit(solution)/shard_map/ppermute | solution.py:177
  60.0 5.3 %collective-permute-done.5 = bf16[128,512]{0,1:T(8,128)(2,1)S(1)} collective-permute-done((bf16[128,512]{0,1:T(8,128)(2,1)S(1)}, bf16[128,512]{0,1:T(8,128)(2,1)S(1)}, u32[]{:S(2)}, u32[]{:S(2)}) %collective-permute-start.5) | collective-permute-done | bytes 131104 | tf_op jit(solution)/shard_map/ppermute | solution.py:177
  67.1 3.9 %collective-permute-done.12 = f32[16,128]{1,0:T(8,128)S(1)} collective-permute-done((f32[16,128]{1,0:T(8,128)S(1)}, f32[16,128]{1,0:T(8,128)S(1)}, u32[]{:S(2)}, u32[]{:S(2)}) %collective-permute-start.12) | collective-permute-done | bytes 8224 | tf_op jit(solution)/shard_map/ppermute | solution.py:211
  72.2 2.6 %collective-permute-done.13 = f32[16,256]{1,0:T(8,128)S(1)} collective-permute-done((f32[16,256]{1,0:T(8,128)S(1)}, f32[16,256]{1,0:T(8,128)S(1)}, u32[]{:S(2)}, u32[]{:S(2)}) %collective-permute-start.13) | collective-permute-done | bytes 16416 | tf_op jit(solution)/shard_map/ppermute | solution.py:211
  74.9 1.8 copy.37
  76.7 1.8 copy.36
  78.5 2.1 %collective-permute-start.9 = (bf16[128,512]{0,1:T(8,128)(2,1)S(1)}, bf16[128,512]{0,1:T(8,128)(2,1)}, u32[]{:S(2)}, u32[]{:S(2)}) collective-permute-start(bf16[128,512]{0,1:T(8,128)(2,1)S(1)} %get-tuple-element.44), channel_id=1, source_target_pairs={{0,4},{1,5},{2,6},{3,7},{4,0},{5,1},{6,2},{7,3},{8,12},{9,13},{10,... | collective-permute-start | bytes 393224 | tf_op jit(solution)/shard_map/ppermute | solution.py:211
  80.7 24.0 %shard_map.136 = (bf16[8,64,1024]{2,1,0:T(8,128)(2,1)}, bf16[8,1024,64]{2,1,0:T(8,128)(2,1)S(1)}, bf16[8,1024,64]{2,1,0:T(8,128)(2,1)}) custom-call(bf16[8,1024,64]{2,1,0:T(8,128)(2,1)} %bitcast.132, bf16[8,1024,64]{2,1,0:T(8,128)(2,1)} %copy.35.k_ref, bf16[8,1024,64]{2,1,0:T(8,128)(2,1)} %bitcast.143, bf16[8,64,1024]{2,1,0:T(8,128)(2,1)S(1)} %bitcast.134, ...), custom_call_target="tpu_custom_call" | custom-call | tf_op jit(solution)/shard_map/pallas_call | solution.py:105
  104.7 1.3 copy-done.5
  106.0 1.9 copy.40
  107.9 1.5 fusion
  109.4 2.1 %copy.41 = bf16[1024,8,64]{0,2,1:T(8,128)(2,1)S(1)} copy(bf16[1024,8,64]{2,0,1:T(8,128)(2,1)} %bitcast.148) | data formatting | bytes 2097152 | tf_op jit(solution)/shard_map/transpose | solution.py:152
  113.2 2.0 %collective-permute-start.10 = (bf16[256,512]{0,1:T(8,128)(2,1)}, bf16[256,512]{0,1:T(8,128)(2,1)}, u32[]{:S(2)}, u32[]{:S(2)}) collective-permute-start(bf16[256,512]{0,1:T(8,128)(2,1)} %pad_maximum_fusion.4), channel_id=1, source_target_pairs={{0,2},{1,3},{2,0},{3,1},{4,6},{5,7},{6,4},{7,5},{8,10},{9,11},{10,... | collective-permute-start | bytes 786440 | tf_op jit(solution)/shard_map/ppermute | solution.py:211
  115.2 1.5 fusion.1
  116.8 6.6 %collective-permute-done.10 = bf16[256,512]{0,1:T(8,128)(2,1)} collective-permute-done((bf16[256,512]{0,1:T(8,128)(2,1)}, bf16[256,512]{0,1:T(8,128)(2,1)}, u32[]{:S(2)}, u32[]{:S(2)}) %collective-permute-start.10) | collective-permute-done | bytes 262176 | tf_op jit(solution)/shard_map/ppermute | solution.py:211
  125.5 1.7 add_convert_fusion
  128.5 1.7 fusion.3
  130.2 1.7 add_convert_fusion.2
  131.9 48.7 %all-reduce.3.cloned.1.call-done = (bf16[512,512]{0,1:T(8,128)(2,1)}, bf16[512,512]{0,1:T(8,128)(2,1)}, bf16[1024,512]{0,1:T(8,128)(2,1)}) async-done(((bf16[512,512]{0,1:T(8,128)(2,1)}, bf16[512,512]{0,1:T(8,128)(2,1)}, bf16[1024,512]{0,1:T(8,128)(2,1)}), (bf16[512,512]{0,1:T(8,128)(2,1)}, bf16[512,512]{0,1:T(8,128)(2,1)}, bf16[1024,512]{0,1:T(8,128)(2,1)})) %all-reduce.3.cloned.1.call-update) | async-done | bytes 2097168 | tf_op jit(solution)/shard_map/psum | solution.py:232
  180.6 2.1 %convolution_bitcast_fusion = f32[512,512]{0,1:T(8,128)S(1)} fusion(bf16[1024,512]{0,1:T(8,128)(2,1)} %get-tuple-element.42, bf16[1024,512]{1,0:T(8,128)(2,1)S(1)} %copy-done.16), kind=kOutput, calls=%fused_computation.7 | convolution fusion | flops 536870912 | bytes 3145728 | tf_op jit(solution)/shard_map/qa,qb->ab/dot_general | solution.py:238
  182.7 1.7 add_convert_fusion.1
  (107 shorter events, 19.5 us)
Async XLA Ops:
  7.2 4.0 %copy-start.10 = (bf16[512,512]{1,0:T(8,128)(2,1)S(1)}, bf16[512,512]{1,0:T(8,128)(2,1)}, u32[]{:S(2)}) copy-start(bf16[512,512]{1,0:T(8,128)(2,1)} %param.12) | copy-start | bytes 1572868
  7.2 173.4 %all-reduce.3.cloned.1.call-start = ((), (), s32[]{:S(2)}) async-start(), calls=%async_computation | async-start | bytes 4194304 | tf_op jit(solution)/shard_map/psum | solution.py:232
  11.2 1.7 copy-start.21
  16.7 21.9 %copy-start.1 = (bf16[1024,8,64]{2,0,1:T(8,128)(2,1)}, bf16[1024,8,64]{2,0,1:T(8,128)(2,1)S(1)}, u32[]{:S(2)}) copy-start(bf16[1024,8,64]{2,0,1:T(8,128)(2,1)S(1)} %copy.33) | copy-start | bytes 3145732
  38.6 2.7 %collective-permute-start = (f32[8,512]{1,0:T(8,128)S(1)}, f32[8,512]{1,0:T(8,128)S(1)}, u32[]{:S(2)}, u32[]{:S(2)}) collective-permute-start(f32[8,512]{1,0:T(8,128)S(1)} %bitcast.153), channel_id=1, source_target_pairs={{0,1},{1,0},{2,3},{3,2},{4,5},{5,4},{6,7},{7,6},{8,9},{9,8},{10,11... | collective-permute-start | bytes 49160 | tf_op jit(solution)/shard_map/ppermute | solution.py:177
  39.2 2.1 %collective-permute-start.6 = (f32[8,512]{1,0:T(8,128)S(1)}, f32[8,512]{1,0:T(8,128)S(1)}, u32[]{:S(2)}, u32[]{:S(2)}) collective-permute-start(f32[8,512]{1,0:T(8,128)S(1)} %bitcast.154), channel_id=1, source_target_pairs={{0,1},{1,0},{2,3},{3,2},{4,5},{5,4},{6,7},{7,6},{8,9},{9,8},{10,11... | collective-permute-start | bytes 49160 | tf_op jit(solution)/shard_map/ppermute | solution.py:177
  40.8 6.8 %copy-start.7 = (f32[8,64,1024]{2,1,0:T(8,128)S(1)}, f32[8,64,1024]{2,1,0:T(8,128)}, u32[]{:S(2)}) copy-start(f32[8,64,1024]{2,1,0:T(8,128)} %copy-done.6) | copy-start | bytes 6291460
  40.8 6.8 %collective-permute-start.1 = (bf16[512,512]{0,1:T(8,128)(2,1)}, bf16[512,512]{0,1:T(8,128)(2,1)}, u32[]{:S(2)}, u32[]{:S(2)}) collective-permute-start(bf16[512,512]{0,1:T(8,128)(2,1)} %dynamic-slice_convert_fusion), channel_id=1, source_target_pairs={{0,1},{1,0},{2,3},{3,2},{4,5},{5,4},{6,7},{7,6},{8,9},{9,8},{10,11... | collective-permute-start | bytes 1572872 | tf_op jit(solution)/shard_map/ppermute | solution.py:177
  41.4 5.7 %collective-permute-start.2 = (f32[8,256]{1,0:T(8,128)S(1)}, f32[8,256]{1,0:T(8,128)S(1)}, u32[]{:S(2)}, u32[]{:S(2)}) collective-permute-start(f32[8,256]{1,0:T(8,128)S(1)} %constant_dynamic-slice_fusion.7), channel_id=1, source_target_pairs={{0,2},{1,3},{2,0},{3,1},{4,6},{5,7},{6,4},{7,5},{8,10},{9,11},{10,... | collective-permute-start | bytes 24584 | tf_op jit(solution)/shard_map/ppermute | solution.py:177
  43.9 3.7 %collective-permute-start.7 = (f32[8,256]{1,0:T(8,128)S(1)}, f32[8,256]{1,0:T(8,128)S(1)}, u32[]{:S(2)}, u32[]{:S(2)}) collective-permute-start(f32[8,256]{1,0:T(8,128)S(1)} %constant_dynamic-slice_fusion.2), channel_id=1, source_target_pairs={{0,2},{1,3},{2,0},{3,1},{4,6},{5,7},{6,4},{7,5},{8,10},{9,11},{10,... | collective-permute-start | bytes 24584 | tf_op jit(solution)/shard_map/ppermute | solution.py:177
  48.9 26.0 %copy-start.8 = (bf16[1024,512]{0,1:T(8,128)(2,1)S(1)}, bf16[1024,512]{0,1:T(8,128)(2,1)}, u32[]{:S(2)}) copy-start(bf16[1024,512]{0,1:T(8,128)(2,1)} %convolution_convert_fusion) | copy-start | bytes 3145732
  49.0 8.1 %collective-permute-start.3 = (bf16[256,512]{0,1:T(8,128)(2,1)S(1)}, bf16[256,512]{0,1:T(8,128)(2,1)S(1)}, u32[]{:S(2)}, u32[]{:S(2)}) collective-permute-start(bf16[256,512]{0,1:T(8,128)(2,1)S(1)} %dynamic-slice_convert_fusion.1), channel_id=1, source_target_pairs={{0,2},{1,3},{2,0},{3,1},{4,6},{5,7},{6,4},{7,5},{8,10},{9,11},{10,... | collective-permute-start | bytes 786440 | tf_op jit(solution)/shard_map/ppermute | solution.py:177
  50.5 9.5 %collective-permute-start.4 = (f32[8,128]{1,0:T(8,128)S(1)}, f32[8,128]{1,0:T(8,128)S(1)}, u32[]{:S(2)}, u32[]{:S(2)}) collective-permute-start(f32[8,128]{1,0:T(8,128)S(1)} %constant_dynamic-slice_fusion.5), channel_id=1, source_target_pairs={{0,4},{1,5},{2,6},{3,7},{4,0},{5,1},{6,2},{7,3},{8,12},{9,13},{10,... | collective-permute-start | bytes 12296 | tf_op jit(solution)/shard_map/ppermute | solution.py:177
  53.1 6.9 %collective-permute-start.8 = (f32[8,128]{1,0:T(8,128)S(1)}, f32[8,128]{1,0:T(8,128)S(1)}, u32[]{:S(2)}, u32[]{:S(2)}) collective-permute-start(f32[8,128]{1,0:T(8,128)S(1)} %constant_dynamic-slice_fusion), channel_id=1, source_target_pairs={{0,4},{1,5},{2,6},{3,7},{4,0},{5,1},{6,2},{7,3},{8,12},{9,13},{10,... | collective-permute-start | bytes 12296 | tf_op jit(solution)/shard_map/ppermute | solution.py:177
  57.2 19.4 %copy-start.4 = (bf16[1024,512]{0,1:T(8,128)(2,1)S(1)}, bf16[1024,512]{0,1:T(8,128)(2,1)}, u32[]{:S(2)}) copy-start(bf16[1024,512]{0,1:T(8,128)(2,1)} %convolution_convert_fusion.1) | copy-start | bytes 3145732
  57.2 8.1 %collective-permute-start.5 = (bf16[128,512]{0,1:T(8,128)(2,1)S(1)}, bf16[128,512]{0,1:T(8,128)(2,1)S(1)}, u32[]{:S(2)}, u32[]{:S(2)}) collective-permute-start(bf16[128,512]{0,1:T(8,128)(2,1)S(1)} %dynamic-slice_convert_fusion.2), channel_id=1, source_target_pairs={{0,4},{1,5},{2,6},{3,7},{4,0},{5,1},{6,2},{7,3},{8,12},{9,13},{10,... | collective-permute-start | bytes 393224 | tf_op jit(solution)/shard_map/ppermute | solution.py:177
  66.3 12.1 %copy-start.14 = (bf16[128,512]{0,1:T(8,128)(2,1)}, bf16[128,512]{0,1:T(8,128)(2,1)S(1)}, u32[]{:S(2)}) copy-start(bf16[128,512]{0,1:T(8,128)(2,1)S(1)} %get-tuple-element.44) | copy-start | bytes 393220
  66.4 4.6 %collective-permute-start.12 = (f32[16,128]{1,0:T(8,128)S(1)}, f32[16,128]{1,0:T(8,128)S(1)}, u32[]{:S(2)}, u32[]{:S(2)}) collective-permute-start(f32[16,128]{1,0:T(8,128)S(1)} %pad_maximum_fusion.8), channel_id=1, source_target_pairs={{0,4},{1,5},{2,6},{3,7},{4,0},{5,1},{6,2},{7,3},{8,12},{9,13},{10,... | collective-permute-start | bytes 24584 | tf_op jit(solution)/shard_map/ppermute | solution.py:211
  71.0 3.8 %collective-permute-start.13 = (f32[16,256]{1,0:T(8,128)S(1)}, f32[16,256]{1,0:T(8,128)S(1)}, u32[]{:S(2)}, u32[]{:S(2)}) collective-permute-start(f32[16,256]{1,0:T(8,128)S(1)} %pad_maximum_fusion.7), channel_id=1, source_target_pairs={{0,2},{1,3},{2,0},{3,1},{4,6},{5,7},{6,4},{7,5},{8,10},{9,11},{10,... | collective-permute-start | bytes 49160 | tf_op jit(solution)/shard_map/ppermute | solution.py:211
  74.8 5.8 %collective-permute-start.14 = (f32[16,512]{1,0:T(8,128)S(1)}, f32[16,512]{1,0:T(8,128)S(1)}, u32[]{:S(2)}, u32[]{:S(2)}) collective-permute-start(f32[16,512]{1,0:T(8,128)S(1)} %pad_maximum_fusion.6), channel_id=1, source_target_pairs={{0,1},{1,0},{2,3},{3,2},{4,5},{5,4},{6,7},{7,6},{8,9},{9,8},{10,11... | collective-permute-start | bytes 98312 | tf_op jit(solution)/shard_map/ppermute | solution.py:211
  76.7 4.0 %copy-start.2 = (bf16[1024,512]{0,1:T(8,128)(2,1)S(1)}, bf16[1024,512]{0,1:T(8,128)(2,1)}, u32[]{:S(2)}) copy-start(bf16[1024,512]{0,1:T(8,128)(2,1)} %convolution_convert_fusion.2) | copy-start | bytes 3145732
  78.5 33.0 %collective-permute-start.9 = (bf16[128,512]{0,1:T(8,128)(2,1)S(1)}, bf16[128,512]{0,1:T(8,128)(2,1)}, u32[]{:S(2)}, u32[]{:S(2)}) collective-permute-start(bf16[128,512]{0,1:T(8,128)(2,1)S(1)} %get-tuple-element.44), channel_id=1, source_target_pairs={{0,4},{1,5},{2,6},{3,7},{4,0},{5,1},{6,2},{7,3},{8,12},{9,13},{10,... | collective-permute-start | bytes 393224 | tf_op jit(solution)/shard_map/ppermute | solution.py:211
  113.2 10.1 %collective-permute-start.10 = (bf16[256,512]{0,1:T(8,128)(2,1)}, bf16[256,512]{0,1:T(8,128)(2,1)}, u32[]{:S(2)}, u32[]{:S(2)}) collective-permute-start(bf16[256,512]{0,1:T(8,128)(2,1)} %pad_maximum_fusion.4), channel_id=1, source_target_pairs={{0,2},{1,3},{2,0},{3,1},{4,6},{5,7},{6,4},{7,5},{8,10},{9,11},{10,... | collective-permute-start | bytes 786440 | tf_op jit(solution)/shard_map/ppermute | solution.py:211
  116.8 7.8 %copy-start.9 = (bf16[512,512]{1,0:T(8,128)(2,1)S(1)}, bf16[512,512]{1,0:T(8,128)(2,1)}, u32[]{:S(2)}) copy-start(bf16[512,512]{1,0:T(8,128)(2,1)} %param.11) | copy-start | bytes 1572868
  124.5 2.8 %collective-permute-start.11 = (bf16[512,512]{0,1:T(8,128)(2,1)S(1)}, bf16[512,512]{0,1:T(8,128)(2,1)S(1)}, u32[]{:S(2)}, u32[]{:S(2)}) collective-permute-start(bf16[512,512]{0,1:T(8,128)(2,1)S(1)} %pad_maximum_fusion.3), channel_id=1, source_target_pairs={{0,1},{1,0},{2,3},{3,2},{4,5},{5,4},{6,7},{7,6},{8,9},{9,8},{10,11... | collective-permute-start | bytes 1572872 | tf_op jit(solution)/shard_map/ppermute | solution.py:211
  127.5 2.7 %copy-start.16 = (bf16[1024,512]{1,0:T(8,128)(2,1)S(1)}, bf16[1024,512]{1,0:T(8,128)(2,1)}, u32[]{:S(2)}) copy-start(bf16[1024,512]{1,0:T(8,128)(2,1)} %param.8) | copy-start | bytes 3145732
  127.5 2.7 %copy-start.20 = (bf16[512,512]{1,0:T(8,128)(2,1)S(1)}, bf16[512,512]{1,0:T(8,128)(2,1)}, u32[]{:S(2)}) copy-start(bf16[512,512]{1,0:T(8,128)(2,1)} %param.13) | copy-start | bytes 1572868
  180.5 2.1 %copy-start.18 = (bf16[1024,512]{1,0:T(8,128)(2,1)S(1)}, bf16[1024,512]{1,0:T(8,128)(2,1)}, u32[]{:S(2)}) copy-start(bf16[1024,512]{1,0:T(8,128)(2,1)} %param.15) | copy-start | bytes 3145732
  180.6 2.1 %copy-start.19 = (bf16[1024,512]{0,1:T(8,128)(2,1)S(1)}, bf16[1024,512]{0,1:T(8,128)(2,1)}, u32[]{:S(2)}) copy-start(bf16[1024,512]{0,1:T(8,128)(2,1)} %get-tuple-element.42) | copy-start | bytes 3145732
  180.6 2.1 %copy-start.22 = (bf16[512,512]{1,0:T(8,128)(2,1)S(1)}, bf16[512,512]{1,0:T(8,128)(2,1)}, u32[]{:S(2)}) copy-start(bf16[512,512]{1,0:T(8,128)(2,1)} %param.10) | copy-start | bytes 1572868
  182.7 1.8 copy-start.13
  182.7 2.9 %copy-start.12 = (bf16[512,512]{0,1:T(8,128)(2,1)S(1)}, bf16[512,512]{0,1:T(8,128)(2,1)}, u32[]{:S(2)}) copy-start(bf16[512,512]{0,1:T(8,128)(2,1)} %get-tuple-element.41) | copy-start | bytes 1572868
  (7 other events, 9.2 us)
Sparse Core Ops, SparseCore 0:
  116.9 63.6 all-reduce.2

commit v15 on v14

--- a/solution.py
+++ b/solution.py
@@ -159,8 +159,7 @@
     regions = lax.axis_size("region")
     numer_r, max_r, total_r = _forward(qT, kT, vT.transpose(0, 2, 1), cm, scale)
     numer = numer_r.transpose(2, 0, 1).reshape(n_queries, width)
-    peak = max_r.reshape(HEADS, n_queries)
-    total = total_r.reshape(HEADS, n_queries)
+    stats = jnp.concatenate([max_r.reshape(HEADS, n_queries), total_r.reshape(HEADS, n_queries)], axis=0)
     rows = n_queries
     base = 0
     steps = []
@@ -169,32 +168,29 @@
         bit = (region_index >> k) & 1
         half = rows // 2
         pairs = [(i, i ^ (1 << k)) for i in range(regions)]
-        mine = (
-            lax.dynamic_slice_in_dim(numer, bit * half, half, 0),
-            lax.dynamic_slice_in_dim(peak, bit * half, half, 1),
-            lax.dynamic_slice_in_dim(total, bit * half, half, 1),
-        )
-        theirs = lax.ppermute(
+        mine_n = lax.dynamic_slice_in_dim(numer, bit * half, half, 0)
+        mine_s = lax.dynamic_slice_in_dim(stats, bit * half, half, 1)
+        theirs_n, theirs_s = lax.ppermute(
             (
                 lax.dynamic_slice_in_dim(numer, (1 - bit) * half, half, 0).astype(bf16),
-                lax.dynamic_slice_in_dim(peak, (1 - bit) * half, half, 1),
-                lax.dynamic_slice_in_dim(total, (1 - bit) * half, half, 1),
+                lax.dynamic_slice_in_dim(stats, (1 - bit) * half, half, 1),
             ),
             "region",
             pairs,
         )
-        top = jnp.maximum(mine[1], theirs[1])
-        scale_a = jnp.exp(mine[1] - top)
-        scale_b = jnp.exp(theirs[1] - top)
-        numer = mine[0] * jnp.repeat(scale_a.T, head_dim, axis=1) + theirs[0].astype(f32) * jnp.repeat(
+        top = jnp.maximum(mine_s[:HEADS], theirs_s[:HEADS])
+        scale_a = jnp.exp(mine_s[:HEADS] - top)
+        scale_b = jnp.exp(theirs_s[:HEADS] - top)
+        numer = mine_n * jnp.repeat(scale_a.T, head_dim, axis=1) + theirs_n.astype(f32) * jnp.repeat(
             scale_b.T, head_dim, axis=1
         )
-        total = mine[2] * scale_a + theirs[2] * scale_b
-        peak = top
+        stats = jnp.concatenate([top, mine_s[HEADS:] * scale_a + theirs_s[HEADS:] * scale_b], axis=0)
         base = base + bit * half
         steps.append((k, bit, half))
         rows = half
         k += 1
+    peak = stats[:HEADS]
+    total = stats[HEADS:]
     attended_part = (numer / jnp.repeat(total.T, head_dim, axis=1)).astype(bf16)
     log_part = peak + jnp.log(total)
     grad_att = lax.dot_general(

time: 196 us -> 197 us (level)
  waiting for transfers between devices: 71.2 us -> 79.4 us
  starting transfers between devices: 17.2 us -> 11.4 us
    ppermute x9 -> x6, waiting for transfers between devices: 9.5 us -> 14.3 us  [on_device(): lax.ppermute((lax.dynamic_slice_in_dim(numer, (1 - bit) * half, half, 0)....]
    ppermute x6, starting transfers between devices: 6.18 us -> 2.6 us  [on_device(): other = lax.ppermute(gathered, 'region', pairs)]
    psum x1, waiting for transfers between devices: 48.7 us -> 51.6 us  [on_device(): lax.psum((dq_r.transpose(2, 0, 1).reshape(n_queries, width).astype(bf16),...]
    ppermute x9 -> x6, starting transfers between devices: 11 us -> 8.81 us  [on_device(): lax.ppermute((lax.dynamic_slice_in_dim(numer, (1 - bit) * half, half, 0)....]
    unnamed x51 -> x54, local copies, waits for them, and re-layouts: 8.16 us -> 8.35 us
  transfers between devices with their start and end apart: 16 -> 13, of which waited for: 7 -> 7; matrix products, arithmetic and copies ran while one was open for 11% -> 11% of each run, Pallas kernels for 12% -> 12%
where the time goes in v15:
time: 197 us; the launch traced here: 196 us
  waiting for transfers between devices  79.4 us (40%)
  Pallas kernels  41.3 us (21%)
  local copies, waits for them, and re-layouts  22.4 us (11%)
  matrix products  20.7 us (11%)
  between operations  14.5 us (7%)
  starting transfers between devices  11.4 us (6%)
  other arithmetic  6.59 us (3%)
    psum x1, waiting for transfers between devices, on_device(): lax.psum((dq_r.transpose(2, 0, 1).reshape(n_queries, width).astype(bf16),...  51.6 us
    pallas_call x1, Pallas kernels, _backward(): pl.pallas_call(functools.partial(_bwd_kernel, scale=scale), grid=(heads,...  24 us
    pallas_call x1, Pallas kernels, _forward(): pl.pallas_call(functools.partial(_fwd_kernel, scale=scale), grid=(heads,...  17.4 us
    ppermute x6, waiting for transfers between devices, on_device(): lax.ppermute((lax.dynamic_slice_in_dim(numer, (1 - bit) * half, half, 0)....  14.3 us
    ppermute x6, waiting for transfers between devices, on_device(): other = lax.ppermute(gathered, 'region', pairs)  13.5 us
    ppermute x6, starting transfers between devices, on_device(): lax.ppermute((lax.dynamic_slice_in_dim(numer, (1 - bit) * half, half, 0)....  8.81 us
    unnamed x54, local copies, waits for them, and re-layouts  8.35 us
    reshape x3, local copies, waits for them, and re-layouts, heads(): return x.reshape(x.shape[0], HEADS, head_dim).transpose(1, 0, 2)  5.6 us
  transfers between devices with their start and end apart: 13, of which 7 were waited for; matrix products, arithmetic and copies ran while one was open for 11% of the time, Pallas kernels for 12%

profile of v15, /device:TPU:0, one launch (start us, length us, event | category | flops | bytes accessed | tf_op | source)
XLA Modules:
  0.0 196.3 jit_solution(15783653342198788966)
XLA Ops:
  8.4 2.8 %convolution_convert_fusion.2 = bf16[1024,512]{0,1:T(8,128)(2,1)} fusion(bf16[1024,512]{1,0:T(8,128)(2,1)S(1)} %copy-done, bf16[512,512]{1,0:T(8,128)(2,1)} %param.11), kind=kOutput, calls=%fused_computation.5 | convolution fusion | flops 537395200 | bytes 2621440 | tf_op jit(solution)/shard_map/dot_general | solution.py:155
  11.2 1.7 convolution_convert_fusion.1
  12.9 1.7 convolution_convert_fusion.3
  14.7 2.0 %copy.33 = bf16[1024,8,64]{2,0,1:T(8,128)(2,1)S(1)} copy(bf16[1024,8,64]{0,2,1:T(8,128)(2,1)} %bitcast.128) | data formatting | bytes 2097152 | tf_op jit(solution)/shard_map/reshape | solution.py:149
  16.7 3.3 %copy.35.k_ref = bf16[8,1024,64]{2,1,0:T(8,128)(2,1)} copy(bf16[8,1024,64]{1,2,0:T(8,128)(2,1)} %bitcast.111) | data formatting | bytes 2097152 | tf_op jit(solution)/shard_map/transpose | solution.py:149
  21.3 17.4 %shard_map.135 = (f32[8,64,1024]{2,1,0:T(8,128)S(1)}, f32[8,1,1024]{2,1,0:T(1,128)S(1)}, f32[8,1,1024]{2,1,0:T(1,128)S(1)}) custom-call(bf16[8,1024,64]{2,1,0:T(8,128)(2,1)S(1)} %bitcast.109, bf16[8,1024,64]{2,1,0:T(8,128)(2,1)} %copy.35.k_ref, bf16[8,64,1024]{2,1,0:T(8,128)(2,1)S(1)} %bitcast.113, f32[8,1,1024]{2,1,0:T(1,128)S(1)} %bitcast.118), custom_call_target="tpu_custom_call" | custom-call | tf_op jit(solution)/shard_map/pallas_call | solution.py:75
  41.3 1.7 convolution_convert_fusion
  43.1 2.6 %collective-permute-start.2 = (f32[16,256]{1,0:T(8,128)S(1)}, f32[16,256]{1,0:T(8,128)S(1)}, u32[]{:S(2)}, u32[]{:S(2)}) collective-permute-start(f32[16,256]{1,0:T(8,128)S(1)} %get-tuple-element.67), channel_id=1, source_target_pairs={{0,2},{1,3},{2,0},{3,1},{4,6},{5,7},{6,4},{7,5},{8,10},{9,11},{10,... | collective-permute-start | bytes 49160 | tf_op jit(solution)/shard_map/ppermute | solution.py:173
  45.7 1.7 collective-permute-done.2
  47.5 3.2 %collective-permute-start.4 = (f32[16,128]{1,0:T(8,128)S(1)}, f32[16,128]{1,0:T(8,128)S(1)}, u32[]{:S(2)}, u32[]{:S(2)}) collective-permute-start(f32[16,128]{1,0:T(8,128)S(1)} %get-tuple-element.73), channel_id=1, source_target_pairs={{0,4},{1,5},{2,6},{3,7},{4,0},{5,1},{6,2},{7,3},{8,12},{9,13},{10,... | collective-permute-start | bytes 24584 | tf_op jit(solution)/shard_map/ppermute | solution.py:173
  52.0 1.6 collective-permute-start.3
  53.6 5.7 %collective-permute-done.3 = bf16[256,512]{0,1:T(8,128)(2,1)S(1)} collective-permute-done((bf16[256,512]{0,1:T(8,128)(2,1)S(1)}, bf16[256,512]{0,1:T(8,128)(2,1)S(1)}, u32[]{:S(2)}, u32[]{:S(2)}) %collective-permute-start.3) | collective-permute-done | bytes 262176 | tf_op jit(solution)/shard_map/ppermute | solution.py:173
  59.9 6.9 %collective-permute-done.5 = bf16[128,512]{0,1:T(8,128)(2,1)S(1)} collective-permute-done((bf16[128,512]{0,1:T(8,128)(2,1)S(1)}, bf16[128,512]{0,1:T(8,128)(2,1)S(1)}, u32[]{:S(2)}, u32[]{:S(2)}) %collective-permute-start.5) | collective-permute-done | bytes 131104 | tf_op jit(solution)/shard_map/ppermute | solution.py:173
  68.0 4.5 %collective-permute-done.9 = f32[16,128]{1,0:T(8,128)S(1)} collective-permute-done((f32[16,128]{1,0:T(8,128)S(1)}, f32[16,128]{1,0:T(8,128)S(1)}, u32[]{:S(2)}, u32[]{:S(2)}) %collective-permute-start.9) | collective-permute-done | bytes 8224 | tf_op jit(solution)/shard_map/ppermute | solution.py:207
  72.8 3.5 %collective-permute-done.10 = f32[16,256]{1,0:T(8,128)S(1)} collective-permute-done((f32[16,256]{1,0:T(8,128)S(1)}, f32[16,256]{1,0:T(8,128)S(1)}, u32[]{:S(2)}, u32[]{:S(2)}) %collective-permute-start.10) | collective-permute-done | bytes 16416 | tf_op jit(solution)/shard_map/ppermute | solution.py:207
  76.4 1.8 copy.37
  78.2 1.8 copy.36
  80.2 24.0 %shard_map.136 = (bf16[8,64,1024]{2,1,0:T(8,128)(2,1)}, bf16[8,1024,64]{2,1,0:T(8,128)(2,1)S(1)}, bf16[8,1024,64]{2,1,0:T(8,128)(2,1)}) custom-call(bf16[8,1024,64]{2,1,0:T(8,128)(2,1)} %bitcast.110, bf16[8,1024,64]{2,1,0:T(8,128)(2,1)} %copy.35.k_ref, bf16[8,1024,64]{2,1,0:T(8,128)(2,1)} %bitcast.121, bf16[8,64,1024]{2,1,0:T(8,128)(2,1)S(1)} %bitcast.112, ...), custom_call_target="tpu_custom_call" | custom-call | tf_op jit(solution)/shard_map/pallas_call | solution.py:105
  104.2 1.3 copy-done.5
  105.5 1.9 copy.40
  107.4 1.5 fusion
  108.9 2.1 %copy.41 = bf16[1024,8,64]{0,2,1:T(8,128)(2,1)S(1)} copy(bf16[1024,8,64]{2,0,1:T(8,128)(2,1)} %bitcast.126) | data formatting | bytes 2097152 | tf_op jit(solution)/shard_map/transpose | solution.py:152
  112.8 2.0 %collective-permute-start.7 = (bf16[256,512]{0,1:T(8,128)(2,1)}, bf16[256,512]{0,1:T(8,128)(2,1)}, u32[]{:S(2)}, u32[]{:S(2)}) collective-permute-start(bf16[256,512]{0,1:T(8,128)(2,1)} %pad_maximum_fusion.4), channel_id=1, source_target_pairs={{0,2},{1,3},{2,0},{3,1},{4,6},{5,7},{6,4},{7,5},{8,10},{9,11},{10,... | collective-permute-start | bytes 786440 | tf_op jit(solution)/shard_map/ppermute | solution.py:207
  114.8 1.5 fusion.1
  116.3 5.4 %collective-permute-done.7 = bf16[256,512]{0,1:T(8,128)(2,1)} collective-permute-done((bf16[256,512]{0,1:T(8,128)(2,1)}, bf16[256,512]{0,1:T(8,128)(2,1)}, u32[]{:S(2)}, u32[]{:S(2)}) %collective-permute-start.7) | collective-permute-done | bytes 262176 | tf_op jit(solution)/shard_map/ppermute | solution.py:207
  123.9 1.7 add_convert_fusion
  126.9 1.7 fusion.3
  128.6 1.7 add_convert_fusion.2
  130.3 51.6 %all-reduce.3.cloned.1.call-done = (bf16[512,512]{0,1:T(8,128)(2,1)}, bf16[512,512]{0,1:T(8,128)(2,1)}, bf16[1024,512]{0,1:T(8,128)(2,1)}) async-done(((bf16[512,512]{0,1:T(8,128)(2,1)}, bf16[512,512]{0,1:T(8,128)(2,1)}, bf16[1024,512]{0,1:T(8,128)(2,1)}), (bf16[512,512]{0,1:T(8,128)(2,1)}, bf16[512,512]{0,1:T(8,128)(2,1)}, bf16[1024,512]{0,1:T(8,128)(2,1)})) %all-reduce.3.cloned.1.call-update) | async-done | bytes 2097168 | tf_op jit(solution)/shard_map/psum | solution.py:228
  181.9 2.1 %convolution_bitcast_fusion = f32[512,512]{0,1:T(8,128)S(1)} fusion(bf16[1024,512]{0,1:T(8,128)(2,1)} %get-tuple-element.42, bf16[1024,512]{1,0:T(8,128)(2,1)S(1)} %copy-done.16), kind=kOutput, calls=%fused_computation.7 | convolution fusion | flops 536870912 | bytes 3145728 | tf_op jit(solution)/shard_map/qa,qb->ab/dot_general | solution.py:234
  184.1 1.7 add_convert_fusion.1
  188.2 1.3 copy.42
  (103 shorter events, 16.2 us)
Async XLA Ops:
  7.2 4.0 %copy-start.10 = (bf16[512,512]{1,0:T(8,128)(2,1)S(1)}, bf16[512,512]{1,0:T(8,128)(2,1)}, u32[]{:S(2)}) copy-start(bf16[512,512]{1,0:T(8,128)(2,1)} %param.12) | copy-start | bytes 1572868
  7.2 174.7 %all-reduce.3.cloned.1.call-start = ((), (), s32[]{:S(2)}) async-start(), calls=%async_computation | async-start | bytes 4194304 | tf_op jit(solution)/shard_map/psum | solution.py:228
  11.2 1.7 copy-start.15
  11.2 1.7 copy-start.23
  16.7 22.0 %copy-start.1 = (bf16[1024,8,64]{2,0,1:T(8,128)(2,1)}, bf16[1024,8,64]{2,0,1:T(8,128)(2,1)S(1)}, u32[]{:S(2)}) copy-start(bf16[1024,8,64]{2,0,1:T(8,128)(2,1)S(1)} %copy.33) | copy-start | bytes 3145732
  21.3 20.0 %copy-start.17 = (bf16[1024,512]{1,0:T(8,128)(2,1)S(1)}, bf16[1024,512]{1,0:T(8,128)(2,1)}, u32[]{:S(2)}) copy-start(bf16[1024,512]{1,0:T(8,128)(2,1)} %param.15) | copy-start | bytes 3145732
  21.3 20.0 %copy-start.21 = (bf16[512,512]{1,0:T(8,128)(2,1)S(1)}, bf16[512,512]{1,0:T(8,128)(2,1)}, u32[]{:S(2)}) copy-start(bf16[512,512]{1,0:T(8,128)(2,1)} %param.13) | copy-start | bytes 1572868
  38.7 4.3 %collective-permute-start = (f32[16,512]{1,0:T(8,128)S(1)}, f32[16,512]{1,0:T(8,128)S(1)}, u32[]{:S(2)}, u32[]{:S(2)}) collective-permute-start(f32[16,512]{1,0:T(8,128)S(1)} %get-tuple-element.63), channel_id=1, source_target_pairs={{0,1},{1,0},{2,3},{3,2},{4,5},{5,4},{6,7},{7,6},{8,9},{9,8},{10,11... | collective-permute-start | bytes 98312 | tf_op jit(solution)/shard_map/ppermute | solution.py:173
  40.9 9.7 %copy-start.7 = (f32[8,64,1024]{2,1,0:T(8,128)S(1)}, f32[8,64,1024]{2,1,0:T(8,128)}, u32[]{:S(2)}) copy-start(f32[8,64,1024]{2,1,0:T(8,128)} %copy-done.6) | copy-start | bytes 6291460
  40.9 9.7 %collective-permute-start.1 = (bf16[512,512]{0,1:T(8,128)(2,1)}, bf16[512,512]{0,1:T(8,128)(2,1)}, u32[]{:S(2)}, u32[]{:S(2)}) collective-permute-start(bf16[512,512]{0,1:T(8,128)(2,1)} %dynamic-slice_convert_fusion), channel_id=1, source_target_pairs={{0,1},{1,0},{2,3},{3,2},{4,5},{5,4},{6,7},{7,6},{8,9},{9,8},{10,11... | collective-permute-start | bytes 1572872 | tf_op jit(solution)/shard_map/ppermute | solution.py:173
  43.1 4.4 %collective-permute-start.2 = (f32[16,256]{1,0:T(8,128)S(1)}, f32[16,256]{1,0:T(8,128)S(1)}, u32[]{:S(2)}, u32[]{:S(2)}) collective-permute-start(f32[16,256]{1,0:T(8,128)S(1)} %get-tuple-element.67), channel_id=1, source_target_pairs={{0,2},{1,3},{2,0},{3,1},{4,6},{5,7},{6,4},{7,5},{8,10},{9,11},{10,... | collective-permute-start | bytes 49160 | tf_op jit(solution)/shard_map/ppermute | solution.py:173
  47.5 6.1 %collective-permute-start.4 = (f32[16,128]{1,0:T(8,128)S(1)}, f32[16,128]{1,0:T(8,128)S(1)}, u32[]{:S(2)}, u32[]{:S(2)}) collective-permute-start(f32[16,128]{1,0:T(8,128)S(1)} %get-tuple-element.73), channel_id=1, source_target_pairs={{0,4},{1,5},{2,6},{3,7},{4,0},{5,1},{6,2},{7,3},{8,12},{9,13},{10,... | collective-permute-start | bytes 24584 | tf_op jit(solution)/shard_map/ppermute | solution.py:173
  51.9 24.5 %copy-start.8 = (bf16[1024,512]{0,1:T(8,128)(2,1)S(1)}, bf16[1024,512]{0,1:T(8,128)(2,1)}, u32[]{:S(2)}) copy-start(bf16[1024,512]{0,1:T(8,128)(2,1)} %convolution_convert_fusion) | copy-start | bytes 3145732
  52.0 7.4 %collective-permute-start.3 = (bf16[256,512]{0,1:T(8,128)(2,1)S(1)}, bf16[256,512]{0,1:T(8,128)(2,1)S(1)}, u32[]{:S(2)}, u32[]{:S(2)}) collective-permute-start(bf16[256,512]{0,1:T(8,128)(2,1)S(1)} %dynamic-slice_convert_fusion.1), channel_id=1, source_target_pairs={{0,2},{1,3},{2,0},{3,1},{4,6},{5,7},{6,4},{7,5},{8,10},{9,11},{10,... | collective-permute-start | bytes 786440 | tf_op jit(solution)/shard_map/ppermute | solution.py:173
  59.5 18.7 %copy-start.4 = (bf16[1024,512]{0,1:T(8,128)(2,1)S(1)}, bf16[1024,512]{0,1:T(8,128)(2,1)}, u32[]{:S(2)}) copy-start(bf16[1024,512]{0,1:T(8,128)(2,1)} %convolution_convert_fusion.1) | copy-start | bytes 3145732
  59.5 7.4 %collective-permute-start.5 = (bf16[128,512]{0,1:T(8,128)(2,1)S(1)}, bf16[128,512]{0,1:T(8,128)(2,1)S(1)}, u32[]{:S(2)}, u32[]{:S(2)}) collective-permute-start(bf16[128,512]{0,1:T(8,128)(2,1)S(1)} %dynamic-slice_convert_fusion.2), channel_id=1, source_target_pairs={{0,4},{1,5},{2,6},{3,7},{4,0},{5,1},{6,2},{7,3},{8,12},{9,13},{10,... | collective-permute-start | bytes 393224 | tf_op jit(solution)/shard_map/ppermute | solution.py:173
  67.9 12.1 %copy-start.14 = (bf16[128,512]{0,1:T(8,128)(2,1)}, bf16[128,512]{0,1:T(8,128)(2,1)S(1)}, u32[]{:S(2)}) copy-start(bf16[128,512]{0,1:T(8,128)(2,1)S(1)} %get-tuple-element.47) | copy-start | bytes 393220
  67.9 4.6 %collective-permute-start.9 = (f32[16,128]{1,0:T(8,128)S(1)}, f32[16,128]{1,0:T(8,128)S(1)}, u32[]{:S(2)}, u32[]{:S(2)}) collective-permute-start(f32[16,128]{1,0:T(8,128)S(1)} %pad_maximum_fusion.8), channel_id=1, source_target_pairs={{0,4},{1,5},{2,6},{3,7},{4,0},{5,1},{6,2},{7,3},{8,12},{9,13},{10,... | collective-permute-start | bytes 24584 | tf_op jit(solution)/shard_map/ppermute | solution.py:207
  72.5 3.8 %collective-permute-start.10 = (f32[16,256]{1,0:T(8,128)S(1)}, f32[16,256]{1,0:T(8,128)S(1)}, u32[]{:S(2)}, u32[]{:S(2)}) collective-permute-start(f32[16,256]{1,0:T(8,128)S(1)} %pad_maximum_fusion.7), channel_id=1, source_target_pairs={{0,2},{1,3},{2,0},{3,1},{4,6},{5,7},{6,4},{7,5},{8,10},{9,11},{10,... | collective-permute-start | bytes 49160 | tf_op jit(solution)/shard_map/ppermute | solution.py:207
  76.3 3.8 %collective-permute-start.11 = (f32[16,512]{1,0:T(8,128)S(1)}, f32[16,512]{1,0:T(8,128)S(1)}, u32[]{:S(2)}, u32[]{:S(2)}) collective-permute-start(f32[16,512]{1,0:T(8,128)S(1)} %pad_maximum_fusion.6), channel_id=1, source_target_pairs={{0,1},{1,0},{2,3},{3,2},{4,5},{5,4},{6,7},{7,6},{8,9},{9,8},{10,11... | collective-permute-start | bytes 98312 | tf_op jit(solution)/shard_map/ppermute | solution.py:207
  78.2 2.0 %copy-start.2 = (bf16[1024,512]{0,1:T(8,128)(2,1)S(1)}, bf16[1024,512]{0,1:T(8,128)(2,1)}, u32[]{:S(2)}) copy-start(bf16[1024,512]{0,1:T(8,128)(2,1)} %convolution_convert_fusion.2) | copy-start | bytes 3145732
  80.0 31.0 %collective-permute-start.6 = (bf16[128,512]{0,1:T(8,128)(2,1)S(1)}, bf16[128,512]{0,1:T(8,128)(2,1)}, u32[]{:S(2)}, u32[]{:S(2)}) collective-permute-start(bf16[128,512]{0,1:T(8,128)(2,1)S(1)} %get-tuple-element.47), channel_id=1, source_target_pairs={{0,4},{1,5},{2,6},{3,7},{4,0},{5,1},{6,2},{7,3},{8,12},{9,13},{10,... | collective-permute-start | bytes 393224 | tf_op jit(solution)/shard_map/ppermute | solution.py:207
  112.8 9.0 %collective-permute-start.7 = (bf16[256,512]{0,1:T(8,128)(2,1)}, bf16[256,512]{0,1:T(8,128)(2,1)}, u32[]{:S(2)}, u32[]{:S(2)}) collective-permute-start(bf16[256,512]{0,1:T(8,128)(2,1)} %pad_maximum_fusion.4), channel_id=1, source_target_pairs={{0,2},{1,3},{2,0},{3,1},{4,6},{5,7},{6,4},{7,5},{8,10},{9,11},{10,... | collective-permute-start | bytes 786440 | tf_op jit(solution)/shard_map/ppermute | solution.py:207
  116.3 6.7 %copy-start.9 = (bf16[512,512]{1,0:T(8,128)(2,1)S(1)}, bf16[512,512]{1,0:T(8,128)(2,1)}, u32[]{:S(2)}) copy-start(bf16[512,512]{1,0:T(8,128)(2,1)} %param.11) | copy-start | bytes 1572868
  122.9 2.8 %collective-permute-start.8 = (bf16[512,512]{0,1:T(8,128)(2,1)S(1)}, bf16[512,512]{0,1:T(8,128)(2,1)S(1)}, u32[]{:S(2)}, u32[]{:S(2)}) collective-permute-start(bf16[512,512]{0,1:T(8,128)(2,1)S(1)} %pad_maximum_fusion.3), channel_id=1, source_target_pairs={{0,1},{1,0},{2,3},{3,2},{4,5},{5,4},{6,7},{7,6},{8,9},{9,8},{10,11... | collective-permute-start | bytes 1572872 | tf_op jit(solution)/shard_map/ppermute | solution.py:207
  125.9 2.7 %copy-start.16 = (bf16[1024,512]{1,0:T(8,128)(2,1)S(1)}, bf16[1024,512]{1,0:T(8,128)(2,1)}, u32[]{:S(2)}) copy-start(bf16[1024,512]{1,0:T(8,128)(2,1)} %param.8) | copy-start | bytes 3145732
  125.9 2.7 %copy-start.22 = (bf16[512,512]{1,0:T(8,128)(2,1)S(1)}, bf16[512,512]{1,0:T(8,128)(2,1)}, u32[]{:S(2)}) copy-start(bf16[512,512]{1,0:T(8,128)(2,1)} %param.13) | copy-start | bytes 1572868
  181.9 2.1 %copy-start.19 = (bf16[1024,512]{1,0:T(8,128)(2,1)S(1)}, bf16[1024,512]{1,0:T(8,128)(2,1)}, u32[]{:S(2)}) copy-start(bf16[1024,512]{1,0:T(8,128)(2,1)} %param.15) | copy-start | bytes 3145732
  181.9 2.1 %copy-start.20 = (bf16[1024,512]{0,1:T(8,128)(2,1)S(1)}, bf16[1024,512]{0,1:T(8,128)(2,1)}, u32[]{:S(2)}) copy-start(bf16[1024,512]{0,1:T(8,128)(2,1)} %get-tuple-element.42) | copy-start | bytes 3145732
  181.9 2.1 %copy-start.24 = (bf16[512,512]{1,0:T(8,128)(2,1)S(1)}, bf16[512,512]{1,0:T(8,128)(2,1)}, u32[]{:S(2)}) copy-start(bf16[512,512]{1,0:T(8,128)(2,1)} %param.10) | copy-start | bytes 1572868
  184.0 1.8 copy-start.13
  184.0 2.9 %copy-start.12 = (bf16[512,512]{0,1:T(8,128)(2,1)S(1)}, bf16[512,512]{0,1:T(8,128)(2,1)}, u32[]{:S(2)}) copy-start(bf16[512,512]{0,1:T(8,128)(2,1)} %get-tuple-element.41) | copy-start | bytes 1572868
  (6 other events, 7.5 us)
Sparse Core Ops, SparseCore 0:
  116.4 65.4 all-reduce.2

commit v16 on v14

--- a/solution.py
+++ b/solution.py
@@ -159,6 +159,7 @@
     regions = lax.axis_size("region")
     numer_r, max_r, total_r = _forward(qT, kT, vT.transpose(0, 2, 1), cm, scale)
     numer = numer_r.transpose(2, 0, 1).reshape(n_queries, width)
+    k_late = lax.optimization_barrier((kT, numer_r))[0]
     peak = max_r.reshape(HEADS, n_queries)
     total = total_r.reshape(HEADS, n_queries)
     rows = n_queries
@@ -224,7 +225,7 @@
     grad_wo = jnp.einsum("qa,qb->ab", attended, grad_out, preferred_element_type=f32)
     gaT = heads(grad_att)
 
-    dq_r, dk, dv = _backward(qT, kT, vT, kT.transpose(0, 2, 1), gaT, log_total, deltas, cm, scale)
+    dq_r, dk, dv = _backward(qT, kT, vT, k_late.transpose(0, 2, 1), gaT, log_total, deltas, cm, scale)
     keys_grad = joined(dk).astype(bf16)
     vals_grad = joined(dv).astype(bf16)
     wk_part = jnp.einsum("ka,kb->ab", hits_in, keys_grad, preferred_element_type=f32)

time: 196 us -> 197 us (level)
    unnamed x51 -> x47, local copies, waits for them, and re-layouts: 8.16 us -> 8.16 us
where the time goes in v16:
time: 197 us; the launch traced here: 196 us
  waiting for transfers between devices  71.3 us (36%)
  Pallas kernels  41.2 us (21%)
  matrix products  23.8 us (12%)
  local copies, waits for them, and re-layouts  21.7 us (11%)
  starting transfers between devices  17.2 us (9%)
  between operations  14.5 us (7%)
  other arithmetic  6.51 us (3%)
    psum x1, waiting for transfers between devices, on_device(): lax.psum((dq_r.transpose(2, 0, 1).reshape(n_queries, width).astype(bf16),...  48.6 us
    pallas_call x1, Pallas kernels, _backward(): pl.pallas_call(functools.partial(_bwd_kernel, scale=scale), grid=(heads,...  24 us
    pallas_call x1, Pallas kernels, _forward(): pl.pallas_call(functools.partial(_fwd_kernel, scale=scale), grid=(heads,...  17.3 us
    ppermute x6, waiting for transfers between devices, on_device(): other = lax.ppermute(gathered, 'region', pairs)  13.1 us
    ppermute x9, starting transfers between devices, on_device(): lax.ppermute((lax.dynamic_slice_in_dim(numer, (1 - bit) * half, half, 0)....  11 us
    ppermute x9, waiting for transfers between devices, on_device(): lax.ppermute((lax.dynamic_slice_in_dim(numer, (1 - bit) * half, half, 0)....  9.51 us
    unnamed x47, local copies, waits for them, and re-layouts  8.16 us
    ppermute x6, starting transfers between devices, on_device(): other = lax.ppermute(gathered, 'region', pairs)  6.17 us
  transfers between devices with their start and end apart: 16, of which 7 were waited for; matrix products, arithmetic and copies ran while one was open for 11% of the time, Pallas kernels for 12%

profile of v16, /device:TPU:0, one launch (start us, length us, event | category | flops | bytes accessed | tf_op | source)
XLA Modules:
  0.0 196.2 jit_solution(7650199995080216937)
XLA Ops:
  8.4 3.1 %convolution_convert_fusion.3 = bf16[1024,512]{0,1:T(8,128)(2,1)} fusion(bf16[1024,512]{1,0:T(8,128)(2,1)} %param.8, bf16[512,512]{1,0:T(8,128)(2,1)} %param.10), kind=kOutput, calls=%fused_computation.6 | convolution fusion | flops 537395200 | bytes 2621440 | tf_op jit(solution)/shard_map/dot_general | solution.py:154
  11.5 2.0 %copy.33 = bf16[1024,8,64]{2,0,1:T(8,128)(2,1)S(1)} copy(bf16[1024,8,64]{0,2,1:T(8,128)(2,1)} %bitcast.149) | data formatting | bytes 2097152 | tf_op jit(solution)/shard_map/reshape | solution.py:149
  13.5 3.2 %convolution_convert_fusion.1 = bf16[1024,512]{0,1:T(8,128)(2,1)} fusion(bf16[1024,512]{1,0:T(8,128)(2,1)S(1)} %copy-done, bf16[512,512]{1,0:T(8,128)(2,1)} %param.12), kind=kOutput, calls=%fused_computation.4 | convolution fusion | flops 537395200 | bytes 2621440 | tf_op jit(solution)/shard_map/dot_general | solution.py:156
  16.7 1.7 convolution_convert_fusion.2
  18.5 2.7 %copy.35.k_ref = bf16[8,1024,64]{2,1,0:T(8,128)(2,1)} copy(bf16[8,1024,64]{1,2,0:T(8,128)(2,1)} %bitcast.132) | data formatting | bytes 2097152 | tf_op jit(solution)/shard_map/transpose | solution.py:149
  22.5 17.3 %shard_map.135 = (f32[8,64,1024]{2,1,0:T(8,128)S(1)}, f32[8,1,1024]{2,1,0:T(1,128)S(1)}, f32[8,1,1024]{2,1,0:T(1,128)S(1)}) custom-call(bf16[8,1024,64]{2,1,0:T(8,128)(2,1)S(1)} %bitcast.130, bf16[8,1024,64]{2,1,0:T(8,128)(2,1)} %copy.35.k_ref, bf16[8,64,1024]{2,1,0:T(8,128)(2,1)S(1)} %bitcast.134, f32[8,1,1024]{2,1,0:T(1,128)S(1)} %bitcast.139), custom_call_target="tpu_custom_call" | custom-call | tf_op jit(solution)/shard_map/pallas_call | solution.py:75
  42.6 2.6 %collective-permute-start.2 = (f32[8,256]{1,0:T(8,128)S(1)}, f32[8,256]{1,0:T(8,128)S(1)}, u32[]{:S(2)}, u32[]{:S(2)}) collective-permute-start(f32[8,256]{1,0:T(8,128)S(1)} %constant_dynamic-slice_fusion.7), channel_id=1, source_target_pairs={{0,2},{1,3},{2,0},{3,1},{4,6},{5,7},{6,4},{7,5},{8,10},{9,11},{10,... | collective-permute-start | bytes 24584 | tf_op jit(solution)/shard_map/ppermute | solution.py:178
  45.2 3.1 %convolution_convert_fusion = bf16[1024,512]{0,1:T(8,128)(2,1)} fusion(bf16[1024,512]{1,0:T(8,128)(2,1)} %param.15, bf16[512,512]{1,0:T(8,128)(2,1)} %param.13), kind=kOutput, calls=%fused_computation.3 | convolution fusion | flops 537395200 | bytes 2621440 | tf_op jit(solution)/shard_map/dot_general | solution.py:201
  50.2 1.5 collective-permute-start.3
  51.7 2.6 %collective-permute-start.4 = (f32[8,128]{1,0:T(8,128)S(1)}, f32[8,128]{1,0:T(8,128)S(1)}, u32[]{:S(2)}, u32[]{:S(2)}) collective-permute-start(f32[8,128]{1,0:T(8,128)S(1)} %constant_dynamic-slice_fusion.5), channel_id=1, source_target_pairs={{0,4},{1,5},{2,6},{3,7},{4,0},{5,1},{6,2},{7,3},{8,12},{9,13},{10,... | collective-permute-start | bytes 12296 | tf_op jit(solution)/shard_map/ppermute | solution.py:178
  54.6 3.7 %collective-permute-done.3 = bf16[256,512]{0,1:T(8,128)(2,1)S(1)} collective-permute-done((bf16[256,512]{0,1:T(8,128)(2,1)S(1)}, bf16[256,512]{0,1:T(8,128)(2,1)S(1)}, u32[]{:S(2)}, u32[]{:S(2)}) %collective-permute-start.3) | collective-permute-done | bytes 262176 | tf_op jit(solution)/shard_map/ppermute | solution.py:178
  58.5 2.8 %collective-permute-start.5 = (bf16[128,512]{0,1:T(8,128)(2,1)S(1)}, bf16[128,512]{0,1:T(8,128)(2,1)S(1)}, u32[]{:S(2)}, u32[]{:S(2)}) collective-permute-start(bf16[128,512]{0,1:T(8,128)(2,1)S(1)} %dynamic-slice_convert_fusion.2), channel_id=1, source_target_pairs={{0,4},{1,5},{2,6},{3,7},{4,0},{5,1},{6,2},{7,3},{8,12},{9,13},{10,... | collective-permute-start | bytes 393224 | tf_op jit(solution)/shard_map/ppermute | solution.py:178
  61.2 5.3 %collective-permute-done.5 = bf16[128,512]{0,1:T(8,128)(2,1)S(1)} collective-permute-done((bf16[128,512]{0,1:T(8,128)(2,1)S(1)}, bf16[128,512]{0,1:T(8,128)(2,1)S(1)}, u32[]{:S(2)}, u32[]{:S(2)}) %collective-permute-start.5) | collective-permute-done | bytes 131104 | tf_op jit(solution)/shard_map/ppermute | solution.py:178
  68.3 3.9 %collective-permute-done.12 = f32[16,128]{1,0:T(8,128)S(1)} collective-permute-done((f32[16,128]{1,0:T(8,128)S(1)}, f32[16,128]{1,0:T(8,128)S(1)}, u32[]{:S(2)}, u32[]{:S(2)}) %collective-permute-start.12) | collective-permute-done | bytes 8224 | tf_op jit(solution)/shard_map/ppermute | solution.py:212
  73.5 2.6 %collective-permute-done.13 = f32[16,256]{1,0:T(8,128)S(1)} collective-permute-done((f32[16,256]{1,0:T(8,128)S(1)}, f32[16,256]{1,0:T(8,128)S(1)}, u32[]{:S(2)}, u32[]{:S(2)}) %collective-permute-start.13) | collective-permute-done | bytes 16416 | tf_op jit(solution)/shard_map/ppermute | solution.py:212
  76.1 1.8 copy.37
  77.9 1.8 copy.36
  79.7 2.1 %collective-permute-start.9 = (bf16[128,512]{0,1:T(8,128)(2,1)S(1)}, bf16[128,512]{0,1:T(8,128)(2,1)}, u32[]{:S(2)}, u32[]{:S(2)}) collective-permute-start(bf16[128,512]{0,1:T(8,128)(2,1)S(1)} %get-tuple-element.46), channel_id=1, source_target_pairs={{0,4},{1,5},{2,6},{3,7},{4,0},{5,1},{6,2},{7,3},{8,12},{9,13},{10,... | collective-permute-start | bytes 393224 | tf_op jit(solution)/shard_map/ppermute | solution.py:212
  81.9 24.0 %shard_map.136 = (bf16[8,64,1024]{2,1,0:T(8,128)(2,1)}, bf16[8,1024,64]{2,1,0:T(8,128)(2,1)S(1)}, bf16[8,1024,64]{2,1,0:T(8,128)(2,1)}) custom-call(bf16[8,1024,64]{2,1,0:T(8,128)(2,1)} %bitcast.131, bf16[8,1024,64]{2,1,0:T(8,128)(2,1)} %copy.35.k_ref, bf16[8,1024,64]{2,1,0:T(8,128)(2,1)} %bitcast.142, bf16[8,64,1024]{2,1,0:T(8,128)(2,1)S(1)} %bitcast.133, ...), custom_call_target="tpu_custom_call" | custom-call | tf_op jit(solution)/shard_map/pallas_call | solution.py:105
  105.9 1.3 copy-done.5
  107.2 1.9 copy.40
  109.1 1.5 fusion
  110.6 2.1 %copy.41 = bf16[1024,8,64]{0,2,1:T(8,128)(2,1)S(1)} copy(bf16[1024,8,64]{2,0,1:T(8,128)(2,1)} %bitcast.147) | data formatting | bytes 2097152 | tf_op jit(solution)/shard_map/transpose | solution.py:152
  114.5 2.0 %collective-permute-start.10 = (bf16[256,512]{0,1:T(8,128)(2,1)}, bf16[256,512]{0,1:T(8,128)(2,1)}, u32[]{:S(2)}, u32[]{:S(2)}) collective-permute-start(bf16[256,512]{0,1:T(8,128)(2,1)} %pad_maximum_fusion.4), channel_id=1, source_target_pairs={{0,2},{1,3},{2,0},{3,1},{4,6},{5,7},{6,4},{7,5},{8,10},{9,11},{10,... | collective-permute-start | bytes 786440 | tf_op jit(solution)/shard_map/ppermute | solution.py:212
  116.5 1.5 fusion.1
  118.0 6.6 %collective-permute-done.10 = bf16[256,512]{0,1:T(8,128)(2,1)} collective-permute-done((bf16[256,512]{0,1:T(8,128)(2,1)}, bf16[256,512]{0,1:T(8,128)(2,1)}, u32[]{:S(2)}, u32[]{:S(2)}) %collective-permute-start.10) | collective-permute-done | bytes 262176 | tf_op jit(solution)/shard_map/ppermute | solution.py:212
  126.8 1.7 add_convert_fusion
  129.8 1.7 fusion.3
  131.5 1.7 add_convert_fusion.2
  133.2 48.6 %all-reduce.3.cloned.1.call-done = (bf16[512,512]{0,1:T(8,128)(2,1)}, bf16[512,512]{0,1:T(8,128)(2,1)}, bf16[1024,512]{0,1:T(8,128)(2,1)}) async-done(((bf16[512,512]{0,1:T(8,128)(2,1)}, bf16[512,512]{0,1:T(8,128)(2,1)}, bf16[1024,512]{0,1:T(8,128)(2,1)}), (bf16[512,512]{0,1:T(8,128)(2,1)}, bf16[512,512]{0,1:T(8,128)(2,1)}, bf16[1024,512]{0,1:T(8,128)(2,1)})) %all-reduce.3.cloned.1.call-update) | async-done | bytes 2097168 | tf_op jit(solution)/shard_map/psum | solution.py:233
  181.8 2.1 %convolution_bitcast_fusion = f32[512,512]{0,1:T(8,128)S(1)} fusion(bf16[1024,512]{0,1:T(8,128)(2,1)} %get-tuple-element.44, bf16[1024,512]{1,0:T(8,128)(2,1)S(1)} %copy-done.15), kind=kOutput, calls=%fused_computation.7 | convolution fusion | flops 536870912 | bytes 3145728 | tf_op jit(solution)/shard_map/qa,qb->ab/dot_general | solution.py:239
  183.9 1.7 add_convert_fusion.1
  (103 shorter events, 19.5 us)
Async XLA Ops:
  7.2 6.3 %copy-start = (bf16[1024,512]{1,0:T(8,128)(2,1)S(1)}, bf16[1024,512]{1,0:T(8,128)(2,1)}, u32[]{:S(2)}) copy-start(bf16[1024,512]{1,0:T(8,128)(2,1)} %param.9) | copy-start | bytes 3145732
  7.2 174.6 %all-reduce.3.cloned.1.call-start = ((), (), s32[]{:S(2)}) async-start(), calls=%async_computation | async-start | bytes 4194304 | tf_op jit(solution)/shard_map/psum | solution.py:233
  13.5 7.8 %copy-start.1 = (bf16[1024,8,64]{2,0,1:T(8,128)(2,1)}, bf16[1024,8,64]{2,0,1:T(8,128)(2,1)S(1)}, u32[]{:S(2)}) copy-start(bf16[1024,8,64]{2,0,1:T(8,128)(2,1)S(1)} %copy.33) | copy-start | bytes 3145732
  13.5 3.2 %copy-start.9 = (bf16[512,512]{1,0:T(8,128)(2,1)S(1)}, bf16[512,512]{1,0:T(8,128)(2,1)}, u32[]{:S(2)}) copy-start(bf16[512,512]{1,0:T(8,128)(2,1)} %param.11) | copy-start | bytes 1572868
  39.8 2.7 %collective-permute-start = (f32[8,512]{1,0:T(8,128)S(1)}, f32[8,512]{1,0:T(8,128)S(1)}, u32[]{:S(2)}, u32[]{:S(2)}) collective-permute-start(f32[8,512]{1,0:T(8,128)S(1)} %bitcast.152), channel_id=1, source_target_pairs={{0,1},{1,0},{2,3},{3,2},{4,5},{5,4},{6,7},{7,6},{8,9},{9,8},{10,11... | collective-permute-start | bytes 49160 | tf_op jit(solution)/shard_map/ppermute | solution.py:178
  40.4 2.1 %collective-permute-start.6 = (f32[8,512]{1,0:T(8,128)S(1)}, f32[8,512]{1,0:T(8,128)S(1)}, u32[]{:S(2)}, u32[]{:S(2)}) collective-permute-start(f32[8,512]{1,0:T(8,128)S(1)} %bitcast.153), channel_id=1, source_target_pairs={{0,1},{1,0},{2,3},{3,2},{4,5},{5,4},{6,7},{7,6},{8,9},{9,8},{10,11... | collective-permute-start | bytes 49160 | tf_op jit(solution)/shard_map/ppermute | solution.py:178
  42.0 6.8 %copy-start.7 = (f32[8,64,1024]{2,1,0:T(8,128)S(1)}, f32[8,64,1024]{2,1,0:T(8,128)}, u32[]{:S(2)}) copy-start(f32[8,64,1024]{2,1,0:T(8,128)} %copy-done.6) | copy-start | bytes 6291460
  42.0 6.8 %collective-permute-start.1 = (bf16[512,512]{0,1:T(8,128)(2,1)}, bf16[512,512]{0,1:T(8,128)(2,1)}, u32[]{:S(2)}, u32[]{:S(2)}) collective-permute-start(bf16[512,512]{0,1:T(8,128)(2,1)} %dynamic-slice_convert_fusion), channel_id=1, source_target_pairs={{0,1},{1,0},{2,3},{3,2},{4,5},{5,4},{6,7},{7,6},{8,9},{9,8},{10,11... | collective-permute-start | bytes 1572872 | tf_op jit(solution)/shard_map/ppermute | solution.py:178
  42.6 5.7 %collective-permute-start.2 = (f32[8,256]{1,0:T(8,128)S(1)}, f32[8,256]{1,0:T(8,128)S(1)}, u32[]{:S(2)}, u32[]{:S(2)}) collective-permute-start(f32[8,256]{1,0:T(8,128)S(1)} %constant_dynamic-slice_fusion.7), channel_id=1, source_target_pairs={{0,2},{1,3},{2,0},{3,1},{4,6},{5,7},{6,4},{7,5},{8,10},{9,11},{10,... | collective-permute-start | bytes 24584 | tf_op jit(solution)/shard_map/ppermute | solution.py:178
  45.2 3.7 %collective-permute-start.7 = (f32[8,256]{1,0:T(8,128)S(1)}, f32[8,256]{1,0:T(8,128)S(1)}, u32[]{:S(2)}, u32[]{:S(2)}) collective-permute-start(f32[8,256]{1,0:T(8,128)S(1)} %constant_dynamic-slice_fusion.2), channel_id=1, source_target_pairs={{0,2},{1,3},{2,0},{3,1},{4,6},{5,7},{6,4},{7,5},{8,10},{9,11},{10,... | collective-permute-start | bytes 24584 | tf_op jit(solution)/shard_map/ppermute | solution.py:178
  50.1 26.0 %copy-start.8 = (bf16[1024,512]{0,1:T(8,128)(2,1)S(1)}, bf16[1024,512]{0,1:T(8,128)(2,1)}, u32[]{:S(2)}) copy-start(bf16[1024,512]{0,1:T(8,128)(2,1)} %convolution_convert_fusion) | copy-start | bytes 3145732
  50.2 8.1 %collective-permute-start.3 = (bf16[256,512]{0,1:T(8,128)(2,1)S(1)}, bf16[256,512]{0,1:T(8,128)(2,1)S(1)}, u32[]{:S(2)}, u32[]{:S(2)}) collective-permute-start(bf16[256,512]{0,1:T(8,128)(2,1)S(1)} %dynamic-slice_convert_fusion.1), channel_id=1, source_target_pairs={{0,2},{1,3},{2,0},{3,1},{4,6},{5,7},{6,4},{7,5},{8,10},{9,11},{10,... | collective-permute-start | bytes 786440 | tf_op jit(solution)/shard_map/ppermute | solution.py:178
  51.7 9.5 %collective-permute-start.4 = (f32[8,128]{1,0:T(8,128)S(1)}, f32[8,128]{1,0:T(8,128)S(1)}, u32[]{:S(2)}, u32[]{:S(2)}) collective-permute-start(f32[8,128]{1,0:T(8,128)S(1)} %constant_dynamic-slice_fusion.5), channel_id=1, source_target_pairs={{0,4},{1,5},{2,6},{3,7},{4,0},{5,1},{6,2},{7,3},{8,12},{9,13},{10,... | collective-permute-start | bytes 12296 | tf_op jit(solution)/shard_map/ppermute | solution.py:178
  54.3 6.9 %collective-permute-start.8 = (f32[8,128]{1,0:T(8,128)S(1)}, f32[8,128]{1,0:T(8,128)S(1)}, u32[]{:S(2)}, u32[]{:S(2)}) collective-permute-start(f32[8,128]{1,0:T(8,128)S(1)} %constant_dynamic-slice_fusion), channel_id=1, source_target_pairs={{0,4},{1,5},{2,6},{3,7},{4,0},{5,1},{6,2},{7,3},{8,12},{9,13},{10,... | collective-permute-start | bytes 12296 | tf_op jit(solution)/shard_map/ppermute | solution.py:178
  58.4 19.4 %copy-start.4 = (bf16[1024,512]{0,1:T(8,128)(2,1)S(1)}, bf16[1024,512]{0,1:T(8,128)(2,1)}, u32[]{:S(2)}) copy-start(bf16[1024,512]{0,1:T(8,128)(2,1)} %convolution_convert_fusion.1) | copy-start | bytes 3145732
  58.5 8.1 %collective-permute-start.5 = (bf16[128,512]{0,1:T(8,128)(2,1)S(1)}, bf16[128,512]{0,1:T(8,128)(2,1)S(1)}, u32[]{:S(2)}, u32[]{:S(2)}) collective-permute-start(bf16[128,512]{0,1:T(8,128)(2,1)S(1)} %dynamic-slice_convert_fusion.2), channel_id=1, source_target_pairs={{0,4},{1,5},{2,6},{3,7},{4,0},{5,1},{6,2},{7,3},{8,12},{9,13},{10,... | collective-permute-start | bytes 393224 | tf_op jit(solution)/shard_map/ppermute | solution.py:178
  67.6 12.2 %copy-start.14 = (bf16[128,512]{0,1:T(8,128)(2,1)}, bf16[128,512]{0,1:T(8,128)(2,1)S(1)}, u32[]{:S(2)}) copy-start(bf16[128,512]{0,1:T(8,128)(2,1)S(1)} %get-tuple-element.46) | copy-start | bytes 393220
  67.6 4.6 %collective-permute-start.12 = (f32[16,128]{1,0:T(8,128)S(1)}, f32[16,128]{1,0:T(8,128)S(1)}, u32[]{:S(2)}, u32[]{:S(2)}) collective-permute-start(f32[16,128]{1,0:T(8,128)S(1)} %pad_maximum_fusion.8), channel_id=1, source_target_pairs={{0,4},{1,5},{2,6},{3,7},{4,0},{5,1},{6,2},{7,3},{8,12},{9,13},{10,... | collective-permute-start | bytes 24584 | tf_op jit(solution)/shard_map/ppermute | solution.py:212
  72.2 3.8 %collective-permute-start.13 = (f32[16,256]{1,0:T(8,128)S(1)}, f32[16,256]{1,0:T(8,128)S(1)}, u32[]{:S(2)}, u32[]{:S(2)}) collective-permute-start(f32[16,256]{1,0:T(8,128)S(1)} %pad_maximum_fusion.7), channel_id=1, source_target_pairs={{0,2},{1,3},{2,0},{3,1},{4,6},{5,7},{6,4},{7,5},{8,10},{9,11},{10,... | collective-permute-start | bytes 49160 | tf_op jit(solution)/shard_map/ppermute | solution.py:212
  76.0 5.8 %collective-permute-start.14 = (f32[16,512]{1,0:T(8,128)S(1)}, f32[16,512]{1,0:T(8,128)S(1)}, u32[]{:S(2)}, u32[]{:S(2)}) collective-permute-start(f32[16,512]{1,0:T(8,128)S(1)} %pad_maximum_fusion.6), channel_id=1, source_target_pairs={{0,1},{1,0},{2,3},{3,2},{4,5},{5,4},{6,7},{7,6},{8,9},{9,8},{10,11... | collective-permute-start | bytes 98312 | tf_op jit(solution)/shard_map/ppermute | solution.py:212
  77.9 4.0 %copy-start.2 = (bf16[1024,512]{0,1:T(8,128)(2,1)S(1)}, bf16[1024,512]{0,1:T(8,128)(2,1)}, u32[]{:S(2)}) copy-start(bf16[1024,512]{0,1:T(8,128)(2,1)} %convolution_convert_fusion.2) | copy-start | bytes 3145732
  79.7 33.0 %collective-permute-start.9 = (bf16[128,512]{0,1:T(8,128)(2,1)S(1)}, bf16[128,512]{0,1:T(8,128)(2,1)}, u32[]{:S(2)}, u32[]{:S(2)}) collective-permute-start(bf16[128,512]{0,1:T(8,128)(2,1)S(1)} %get-tuple-element.46), channel_id=1, source_target_pairs={{0,4},{1,5},{2,6},{3,7},{4,0},{5,1},{6,2},{7,3},{8,12},{9,13},{10,... | collective-permute-start | bytes 393224 | tf_op jit(solution)/shard_map/ppermute | solution.py:212
  114.5 10.2 %collective-permute-start.10 = (bf16[256,512]{0,1:T(8,128)(2,1)}, bf16[256,512]{0,1:T(8,128)(2,1)}, u32[]{:S(2)}, u32[]{:S(2)}) collective-permute-start(bf16[256,512]{0,1:T(8,128)(2,1)} %pad_maximum_fusion.4), channel_id=1, source_target_pairs={{0,2},{1,3},{2,0},{3,1},{4,6},{5,7},{6,4},{7,5},{8,10},{9,11},{10,... | collective-permute-start | bytes 786440 | tf_op jit(solution)/shard_map/ppermute | solution.py:212
  118.0 7.8 %copy-start.10 = (bf16[512,512]{1,0:T(8,128)(2,1)S(1)}, bf16[512,512]{1,0:T(8,128)(2,1)}, u32[]{:S(2)}) copy-start(bf16[512,512]{1,0:T(8,128)(2,1)} %param.11) | copy-start | bytes 1572868
  125.7 2.8 %collective-permute-start.11 = (bf16[512,512]{0,1:T(8,128)(2,1)S(1)}, bf16[512,512]{0,1:T(8,128)(2,1)S(1)}, u32[]{:S(2)}, u32[]{:S(2)}) collective-permute-start(bf16[512,512]{0,1:T(8,128)(2,1)S(1)} %pad_maximum_fusion.3), channel_id=1, source_target_pairs={{0,1},{1,0},{2,3},{3,2},{4,5},{5,4},{6,7},{7,6},{8,9},{9,8},{10,11... | collective-permute-start | bytes 1572872 | tf_op jit(solution)/shard_map/ppermute | solution.py:212
  128.8 2.7 %copy-start.15 = (bf16[1024,512]{1,0:T(8,128)(2,1)S(1)}, bf16[1024,512]{1,0:T(8,128)(2,1)}, u32[]{:S(2)}) copy-start(bf16[1024,512]{1,0:T(8,128)(2,1)} %param.8) | copy-start | bytes 3145732
  128.8 2.7 %copy-start.19 = (bf16[512,512]{1,0:T(8,128)(2,1)S(1)}, bf16[512,512]{1,0:T(8,128)(2,1)}, u32[]{:S(2)}) copy-start(bf16[512,512]{1,0:T(8,128)(2,1)} %param.13) | copy-start | bytes 1572868
  181.8 2.1 %copy-start.17 = (bf16[1024,512]{1,0:T(8,128)(2,1)S(1)}, bf16[1024,512]{1,0:T(8,128)(2,1)}, u32[]{:S(2)}) copy-start(bf16[1024,512]{1,0:T(8,128)(2,1)} %param.15) | copy-start | bytes 3145732
  181.8 2.1 %copy-start.18 = (bf16[1024,512]{0,1:T(8,128)(2,1)S(1)}, bf16[1024,512]{0,1:T(8,128)(2,1)}, u32[]{:S(2)}) copy-start(bf16[1024,512]{0,1:T(8,128)(2,1)} %get-tuple-element.44) | copy-start | bytes 3145732
  181.8 2.1 %copy-start.20 = (bf16[512,512]{1,0:T(8,128)(2,1)S(1)}, bf16[512,512]{1,0:T(8,128)(2,1)}, u32[]{:S(2)}) copy-start(bf16[512,512]{1,0:T(8,128)(2,1)} %param.10) | copy-start | bytes 1572868
  183.9 1.8 copy-start.13
  183.9 2.9 %copy-start.12 = (bf16[512,512]{0,1:T(8,128)(2,1)S(1)}, bf16[512,512]{0,1:T(8,128)(2,1)}, u32[]{:S(2)}) copy-start(bf16[512,512]{0,1:T(8,128)(2,1)} %get-tuple-element.43) | copy-start | bytes 1572868
  (5 other events, 6.2 us)
Sparse Core Ops, SparseCore 0:
  118.1 63.6 all-reduce.2

commit v17 on v14

--- a/solution.py
+++ b/solution.py
@@ -229,9 +229,20 @@
     vals_grad = joined(dv).astype(bf16)
     wk_part = jnp.einsum("ka,kb->ab", hits_in, keys_grad, preferred_element_type=f32)
     wv_part = jnp.einsum("ka,kb->ab", hits_in, vals_grad, preferred_element_type=f32)
-    query_grad_sum, grad_wk, grad_wv = lax.psum(
-        (dq_r.transpose(2, 0, 1).reshape(n_queries, width).astype(bf16), wk_part.astype(bf16), wv_part.astype(bf16)), "region"
-    )
+    summed = lax.psum(
+        jnp.concatenate(
+            [
+                dq_r.transpose(2, 0, 1).reshape(n_queries, width).astype(bf16),
+                wk_part.astype(bf16),
+                wv_part.astype(bf16),
+            ],
+            axis=0,
+        ),
+        "region",
+    )
+    query_grad_sum = summed[:n_queries]
+    grad_wk = summed[n_queries : n_queries + width]
+    grad_wv = summed[n_queries + width :]
     grad_wk = grad_wk.astype(f32)
     grad_wv = grad_wv.astype(f32)
     grad_q = query_grad_sum

time: 196 us -> 200 us (1.020)
  matrix products: 22 us -> 24.7 us
    psum x1, waiting for transfers between devices: 48.7 us -> 51.9 us  [on_device(): lax.psum(jnp.concatenate([dq_r.transpose(2, 0, 1).reshape(n_queries, widt...]
    concatenate x0 -> x1, other arithmetic: none -> 3.02 us  [on_device(): jnp.concatenate([dq_r.transpose(2, 0, 1).reshape(n_queries, width).astype...]
    ppermute x6, waiting for transfers between devices: 13.1 us -> 10.1 us  [on_device(): other = lax.ppermute(gathered, 'region', pairs)]
    unnamed x51 -> x43, local copies, waits for them, and re-layouts: 8.16 us -> 6.12 us
  transfers between devices with their start and end apart: 16 -> 16, of which waited for: 7 -> 7; matrix products, arithmetic and copies ran while one was open for 11% -> 14% of each run, Pallas kernels for 12% -> 12%
where the time goes in v17:
time: 200 us
  waiting for transfers between devices  71.6 us (36%)
  Pallas kernels  41 us (20%)
  matrix products  24.7 us (12%)
  local copies, waits for them, and re-layouts  22.1 us (11%)
  starting transfers between devices  17.3 us (9%)
  between operations  14.4 us (7%)
  other arithmetic  8.53 us (4%)
    psum x1, waiting for transfers between devices, on_device(): lax.psum(jnp.concatenate([dq_r.transpose(2, 0, 1).reshape(n_queries, widt...  51.9 us
    pallas_call x1, Pallas kernels, _backward(): pl.pallas_call(functools.partial(_bwd_kernel, scale=scale), grid=(heads,...  23.8 us
    pallas_call x1, Pallas kernels, _forward(): pl.pallas_call(functools.partial(_fwd_kernel, scale=scale), grid=(heads,...  17.3 us
    ppermute x9, starting transfers between devices, on_device(): lax.ppermute((lax.dynamic_slice_in_dim(numer, (1 - bit) * half, half, 0)....  11 us
    ppermute x6, waiting for transfers between devices, on_device(): other = lax.ppermute(gathered, 'region', pairs)  10.1 us
    ppermute x9, waiting for transfers between devices, on_device(): lax.ppermute((lax.dynamic_slice_in_dim(numer, (1 - bit) * half, half, 0)....  9.5 us
    ppermute x6, starting transfers between devices, on_device(): other = lax.ppermute(gathered, 'region', pairs)  6.23 us
    unnamed x43, local copies, waits for them, and re-layouts  6.12 us
  transfers between devices with their start and end apart: 16, of which 7 were waited for; matrix products, arithmetic and copies ran while one was open for 14% of the time, Pallas kernels for 12%

profile of v17, /device:TPU:0, one launch (start us, length us, event | category | flops | bytes accessed | tf_op | source)
XLA Modules:
  0.0 199.6 jit_solution(3640183375494216723)
XLA Ops:
  8.4 2.8 %convolution_convert_fusion.2 = bf16[1024,512]{0,1:T(8,128)(2,1)} fusion(bf16[1024,512]{1,0:T(8,128)(2,1)S(1)} %copy-done, bf16[512,512]{1,0:T(8,128)(2,1)} %param.11), kind=kOutput, calls=%fused_computation.6 | convolution fusion | flops 537395200 | bytes 2621440 | tf_op jit(solution)/shard_map/dot_general | solution.py:155
  11.2 1.7 convolution_convert_fusion.1
  12.9 1.7 convolution_convert_fusion.3
  14.7 2.0 %copy.31 = bf16[1024,8,64]{2,0,1:T(8,128)(2,1)S(1)} copy(bf16[1024,8,64]{0,2,1:T(8,128)(2,1)} %bitcast.149) | data formatting | bytes 2097152 | tf_op jit(solution)/shard_map/reshape | solution.py:149
  16.7 3.3 %copy.33.k_ref = bf16[8,1024,64]{2,1,0:T(8,128)(2,1)} copy(bf16[8,1024,64]{1,2,0:T(8,128)(2,1)} %bitcast.131) | data formatting | bytes 2097152 | tf_op jit(solution)/shard_map/transpose | solution.py:149
  21.3 17.3 %shard_map.135 = (f32[8,64,1024]{2,1,0:T(8,128)S(1)}, f32[8,1,1024]{2,1,0:T(1,128)S(1)}, f32[8,1,1024]{2,1,0:T(1,128)S(1)}) custom-call(bf16[8,1024,64]{2,1,0:T(8,128)(2,1)S(1)} %bitcast.129, bf16[8,1024,64]{2,1,0:T(8,128)(2,1)} %copy.33.k_ref, bf16[8,64,1024]{2,1,0:T(8,128)(2,1)S(1)} %bitcast.133, f32[8,1,1024]{2,1,0:T(1,128)S(1)} %bitcast.139), custom_call_target="tpu_custom_call" | custom-call | tf_op jit(solution)/shard_map/pallas_call | solution.py:75
  41.4 2.6 %collective-permute-start.2 = (f32[8,256]{1,0:T(8,128)S(1)}, f32[8,256]{1,0:T(8,128)S(1)}, u32[]{:S(2)}, u32[]{:S(2)}) collective-permute-start(f32[8,256]{1,0:T(8,128)S(1)} %constant_dynamic-slice_fusion.7), channel_id=1, source_target_pairs={{0,2},{1,3},{2,0},{3,1},{4,6},{5,7},{6,4},{7,5},{8,10},{9,11},{10,... | collective-permute-start | bytes 24584 | tf_op jit(solution)/shard_map/ppermute | solution.py:177
  44.0 3.1 %convolution_convert_fusion = bf16[1024,512]{0,1:T(8,128)(2,1)} fusion(bf16[1024,512]{1,0:T(8,128)(2,1)} %param.15, bf16[512,512]{1,0:T(8,128)(2,1)} %param.13), kind=kOutput, calls=%fused_computation.4 | convolution fusion | flops 537395200 | bytes 2621440 | tf_op jit(solution)/shard_map/dot_general | solution.py:200
  50.5 2.6 %collective-permute-start.4 = (f32[8,128]{1,0:T(8,128)S(1)}, f32[8,128]{1,0:T(8,128)S(1)}, u32[]{:S(2)}, u32[]{:S(2)}) collective-permute-start(f32[8,128]{1,0:T(8,128)S(1)} %constant_dynamic-slice_fusion.5), channel_id=1, source_target_pairs={{0,4},{1,5},{2,6},{3,7},{4,0},{5,1},{6,2},{7,3},{8,12},{9,13},{10,... | collective-permute-start | bytes 12296 | tf_op jit(solution)/shard_map/ppermute | solution.py:177
  53.4 3.7 %collective-permute-done.3 = bf16[256,512]{0,1:T(8,128)(2,1)S(1)} collective-permute-done((bf16[256,512]{0,1:T(8,128)(2,1)S(1)}, bf16[256,512]{0,1:T(8,128)(2,1)S(1)}, u32[]{:S(2)}, u32[]{:S(2)}) %collective-permute-start.3) | collective-permute-done | bytes 262176 | tf_op jit(solution)/shard_map/ppermute | solution.py:177
  57.2 2.8 %collective-permute-start.5 = (bf16[128,512]{0,1:T(8,128)(2,1)S(1)}, bf16[128,512]{0,1:T(8,128)(2,1)S(1)}, u32[]{:S(2)}, u32[]{:S(2)}) collective-permute-start(bf16[128,512]{0,1:T(8,128)(2,1)S(1)} %dynamic-slice_convert_fusion.2), channel_id=1, source_target_pairs={{0,4},{1,5},{2,6},{3,7},{4,0},{5,1},{6,2},{7,3},{8,12},{9,13},{10,... | collective-permute-start | bytes 393224 | tf_op jit(solution)/shard_map/ppermute | solution.py:177
  60.0 5.3 %collective-permute-done.5 = bf16[128,512]{0,1:T(8,128)(2,1)S(1)} collective-permute-done((bf16[128,512]{0,1:T(8,128)(2,1)S(1)}, bf16[128,512]{0,1:T(8,128)(2,1)S(1)}, u32[]{:S(2)}, u32[]{:S(2)}) %collective-permute-start.5) | collective-permute-done | bytes 131104 | tf_op jit(solution)/shard_map/ppermute | solution.py:177
  67.0 3.9 %collective-permute-done.12 = f32[16,128]{1,0:T(8,128)S(1)} collective-permute-done((f32[16,128]{1,0:T(8,128)S(1)}, f32[16,128]{1,0:T(8,128)S(1)}, u32[]{:S(2)}, u32[]{:S(2)}) %collective-permute-start.12) | collective-permute-done | bytes 8224 | tf_op jit(solution)/shard_map/ppermute | solution.py:211
  72.2 2.6 %collective-permute-done.13 = f32[16,256]{1,0:T(8,128)S(1)} collective-permute-done((f32[16,256]{1,0:T(8,128)S(1)}, f32[16,256]{1,0:T(8,128)S(1)}, u32[]{:S(2)}, u32[]{:S(2)}) %collective-permute-start.13) | collective-permute-done | bytes 16416 | tf_op jit(solution)/shard_map/ppermute | solution.py:211
  74.9 1.8 copy.35
  76.7 1.8 copy.34
  78.5 2.1 %collective-permute-start.9 = (bf16[128,512]{0,1:T(8,128)(2,1)S(1)}, bf16[128,512]{0,1:T(8,128)(2,1)S(1)}, u32[]{:S(2)}, u32[]{:S(2)}) collective-permute-start(bf16[128,512]{0,1:T(8,128)(2,1)S(1)} %get-tuple-element.41), channel_id=1, source_target_pairs={{0,4},{1,5},{2,6},{3,7},{4,0},{5,1},{6,2},{7,3},{8,12},{9,13},{10,... | collective-permute-start | bytes 393224 | tf_op jit(solution)/shard_map/ppermute | solution.py:211
  80.7 23.8 %shard_map.136 = (bf16[8,64,1024]{2,1,0:T(8,128)(2,1)S(1)}, bf16[8,1024,64]{2,1,0:T(8,128)(2,1)S(1)}, bf16[8,1024,64]{2,1,0:T(8,128)(2,1)}) custom-call(bf16[8,1024,64]{2,1,0:T(8,128)(2,1)} %bitcast.130, bf16[8,1024,64]{2,1,0:T(8,128)(2,1)} %copy.33.k_ref, bf16[8,1024,64]{2,1,0:T(8,128)(2,1)} %bitcast.142, bf16[8,64,1024]{2,1,0:T(8,128)(2,1)S(1)} %bitcast.132, ...), custom_call_target="tpu_custom_call" | custom-call | tf_op jit(solution)/shard_map/pallas_call | solution.py:105
  105.8 1.9 copy.38
  107.7 1.6 fusion
  109.2 2.7 %copy.39 = bf16[1024,8,64]{0,2,1:T(8,128)(2,1)} copy(bf16[1024,8,64]{2,0,1:T(8,128)(2,1)} %bitcast.147) | data formatting | bytes 2097152 | tf_op jit(solution)/shard_map/transpose | solution.py:152
  111.9 2.8 %fusion.1 = bf16[512,512]{1,0:T(8,128)(2,1)} fusion(bf16[1024,512]{0,1:T(8,128)(2,1)} %bitcast.145, bf16[1024,512]{1,0:T(8,128)(2,1)S(1)} %copy-done), kind=kOutput, calls=%fused_computation.12 | convolution fusion | flops 537133056 | bytes 2621440 | tf_op jit(solution)/shard_map/ka,kb->ab/dot_general | solution.py:231
  116.1 2.1 %collective-permute-start.10 = (bf16[256,512]{0,1:T(8,128)(2,1)S(1)}, bf16[256,512]{0,1:T(8,128)(2,1)S(1)}, u32[]{:S(2)}, u32[]{:S(2)}) collective-permute-start(bf16[256,512]{0,1:T(8,128)(2,1)S(1)} %pad_maximum_fusion.5), channel_id=1, source_target_pairs={{0,2},{1,3},{2,0},{3,1},{4,6},{5,7},{6,4},{7,5},{8,10},{9,11},{10,... | collective-permute-start | bytes 786440 | tf_op jit(solution)/shard_map/ppermute | solution.py:211
  118.1 3.0 %pad_maximum_fusion = bf16[2048,512]{1,0:T(8,128)(2,1)} fusion(bf16[512,512]{1,0:T(8,128)(2,1)} %fusion.1, bf16[512,512]{1,0:T(8,128)(2,1)} %fusion, bf16[1024,512]{1,0:T(8,128)(2,1)} %copy.40), kind=kLoop, calls=%fused_computation | loop fusion | flops 6291456 | bytes 4194304 | tf_op jit(solution)/shard_map/concatenate | solution.py:233
  121.2 3.6 %collective-permute-done.10 = bf16[256,512]{0,1:T(8,128)(2,1)S(1)} collective-permute-done((bf16[256,512]{0,1:T(8,128)(2,1)S(1)}, bf16[256,512]{0,1:T(8,128)(2,1)S(1)}, u32[]{:S(2)}, u32[]{:S(2)}) %collective-permute-start.10) | collective-permute-done | bytes 262176 | tf_op jit(solution)/shard_map/ppermute | solution.py:211
  126.3 1.7 add_convert_fusion
  129.3 1.7 fusion.5
  131.0 1.7 add_convert_fusion.2
  132.7 51.9 %all-reduce.2.cloned.1.call-done = bf16[2048,512]{1,0:T(8,128)(2,1)} async-done(((bf16[2048,512]{1,0:T(8,128)(2,1)}), bf16[2048,512]{1,0:T(8,128)(2,1)}) %all-reduce.2.cloned.1.call-update) | async-done | bytes 2097168 | tf_op jit(solution)/shard_map/psum | solution.py:232
  184.6 2.0 convolution_bitcast_fusion
  187.9 3.2 %add_convert_fusion.1 = bf16[1024,512]{1,0:T(8,128)(2,1)} fusion(bf16[1024,512]{1,0:T(8,128)(2,1)S(1)} %copy-done.17, bf16[512,512]{1,0:T(8,128)(2,1)} %param.10, bf16[2048,512]{1,0:T(8,128)(2,1)} %all-reduce.2.cloned.1.call-done), kind=kOutput, calls=%fused_computation.2 | convolution fusion | flops 538443776 | bytes 3670016 | tf_op jit(solution)/shard_map/dot_general | solution.py:252
  191.1 1.6 slice_convert_fusion
  (102 shorter events, 19.0 us)
Async XLA Ops:
  7.2 4.0 %copy-start.12 = (bf16[512,512]{1,0:T(8,128)(2,1)S(1)}, bf16[512,512]{1,0:T(8,128)(2,1)}, u32[]{:S(2)}) copy-start(bf16[512,512]{1,0:T(8,128)(2,1)} %param.12) | copy-start | bytes 1572868
  7.2 177.4 %all-reduce.2.cloned.1.call-start = ((), (), s32[]{:S(2)}) async-start(), calls=%async_computation | async-start | bytes 4194304 | tf_op jit(solution)/shard_map/psum | solution.py:232
  11.2 1.7 copy-start.14
  11.2 1.7 copy-start.19
  16.7 21.9 %copy-start.1 = (bf16[1024,8,64]{2,0,1:T(8,128)(2,1)}, bf16[1024,8,64]{2,0,1:T(8,128)(2,1)S(1)}, u32[]{:S(2)}) copy-start(bf16[1024,8,64]{2,0,1:T(8,128)(2,1)S(1)} %copy.31) | copy-start | bytes 3145732
  38.6 1.4 copy-start.6
  38.6 2.7 %collective-permute-start = (f32[8,512]{1,0:T(8,128)S(1)}, f32[8,512]{1,0:T(8,128)S(1)}, u32[]{:S(2)}, u32[]{:S(2)}) collective-permute-start(f32[8,512]{1,0:T(8,128)S(1)} %bitcast.152), channel_id=1, source_target_pairs={{0,1},{1,0},{2,3},{3,2},{4,5},{5,4},{6,7},{7,6},{8,9},{9,8},{10,11... | collective-permute-start | bytes 49160 | tf_op jit(solution)/shard_map/ppermute | solution.py:177
  39.2 2.1 %collective-permute-start.6 = (f32[8,512]{1,0:T(8,128)S(1)}, f32[8,512]{1,0:T(8,128)S(1)}, u32[]{:S(2)}, u32[]{:S(2)}) collective-permute-start(f32[8,512]{1,0:T(8,128)S(1)} %bitcast.153), channel_id=1, source_target_pairs={{0,1},{1,0},{2,3},{3,2},{4,5},{5,4},{6,7},{7,6},{8,9},{9,8},{10,11... | collective-permute-start | bytes 49160 | tf_op jit(solution)/shard_map/ppermute | solution.py:177
  40.8 6.8 %copy-start.7 = (f32[8,64,1024]{2,1,0:T(8,128)S(1)}, f32[8,64,1024]{2,1,0:T(8,128)}, u32[]{:S(2)}) copy-start(f32[8,64,1024]{2,1,0:T(8,128)} %copy-done.6) | copy-start | bytes 6291460
  40.8 6.8 %collective-permute-start.1 = (bf16[512,512]{0,1:T(8,128)(2,1)}, bf16[512,512]{0,1:T(8,128)(2,1)}, u32[]{:S(2)}, u32[]{:S(2)}) collective-permute-start(bf16[512,512]{0,1:T(8,128)(2,1)} %dynamic-slice_convert_fusion), channel_id=1, source_target_pairs={{0,1},{1,0},{2,3},{3,2},{4,5},{5,4},{6,7},{7,6},{8,9},{9,8},{10,11... | collective-permute-start | bytes 1572872 | tf_op jit(solution)/shard_map/ppermute | solution.py:177
  41.4 5.7 %collective-permute-start.2 = (f32[8,256]{1,0:T(8,128)S(1)}, f32[8,256]{1,0:T(8,128)S(1)}, u32[]{:S(2)}, u32[]{:S(2)}) collective-permute-start(f32[8,256]{1,0:T(8,128)S(1)} %constant_dynamic-slice_fusion.7), channel_id=1, source_target_pairs={{0,2},{1,3},{2,0},{3,1},{4,6},{5,7},{6,4},{7,5},{8,10},{9,11},{10,... | collective-permute-start | bytes 24584 | tf_op jit(solution)/shard_map/ppermute | solution.py:177
  43.9 3.7 %collective-permute-start.7 = (f32[8,256]{1,0:T(8,128)S(1)}, f32[8,256]{1,0:T(8,128)S(1)}, u32[]{:S(2)}, u32[]{:S(2)}) collective-permute-start(f32[8,256]{1,0:T(8,128)S(1)} %constant_dynamic-slice_fusion.2), channel_id=1, source_target_pairs={{0,2},{1,3},{2,0},{3,1},{4,6},{5,7},{6,4},{7,5},{8,10},{9,11},{10,... | collective-permute-start | bytes 24584 | tf_op jit(solution)/shard_map/ppermute | solution.py:177
  48.9 26.0 %copy-start.9 = (bf16[1024,512]{0,1:T(8,128)(2,1)S(1)}, bf16[1024,512]{0,1:T(8,128)(2,1)}, u32[]{:S(2)}) copy-start(bf16[1024,512]{0,1:T(8,128)(2,1)} %convolution_convert_fusion) | copy-start | bytes 3145732
  49.0 8.1 %collective-permute-start.3 = (bf16[256,512]{0,1:T(8,128)(2,1)S(1)}, bf16[256,512]{0,1:T(8,128)(2,1)S(1)}, u32[]{:S(2)}, u32[]{:S(2)}) collective-permute-start(bf16[256,512]{0,1:T(8,128)(2,1)S(1)} %dynamic-slice_convert_fusion.1), channel_id=1, source_target_pairs={{0,2},{1,3},{2,0},{3,1},{4,6},{5,7},{6,4},{7,5},{8,10},{9,11},{10,... | collective-permute-start | bytes 786440 | tf_op jit(solution)/shard_map/ppermute | solution.py:177
  50.5 9.5 %collective-permute-start.4 = (f32[8,128]{1,0:T(8,128)S(1)}, f32[8,128]{1,0:T(8,128)S(1)}, u32[]{:S(2)}, u32[]{:S(2)}) collective-permute-start(f32[8,128]{1,0:T(8,128)S(1)} %constant_dynamic-slice_fusion.5), channel_id=1, source_target_pairs={{0,4},{1,5},{2,6},{3,7},{4,0},{5,1},{6,2},{7,3},{8,12},{9,13},{10,... | collective-permute-start | bytes 12296 | tf_op jit(solution)/shard_map/ppermute | solution.py:177
  53.1 6.9 %collective-permute-start.8 = (f32[8,128]{1,0:T(8,128)S(1)}, f32[8,128]{1,0:T(8,128)S(1)}, u32[]{:S(2)}, u32[]{:S(2)}) collective-permute-start(f32[8,128]{1,0:T(8,128)S(1)} %constant_dynamic-slice_fusion), channel_id=1, source_target_pairs={{0,4},{1,5},{2,6},{3,7},{4,0},{5,1},{6,2},{7,3},{8,12},{9,13},{10,... | collective-permute-start | bytes 12296 | tf_op jit(solution)/shard_map/ppermute | solution.py:177
  57.2 19.4 %copy-start.4 = (bf16[1024,512]{0,1:T(8,128)(2,1)S(1)}, bf16[1024,512]{0,1:T(8,128)(2,1)}, u32[]{:S(2)}) copy-start(bf16[1024,512]{0,1:T(8,128)(2,1)} %convolution_convert_fusion.1) | copy-start | bytes 3145732
  57.2 8.1 %collective-permute-start.5 = (bf16[128,512]{0,1:T(8,128)(2,1)S(1)}, bf16[128,512]{0,1:T(8,128)(2,1)S(1)}, u32[]{:S(2)}, u32[]{:S(2)}) collective-permute-start(bf16[128,512]{0,1:T(8,128)(2,1)S(1)} %dynamic-slice_convert_fusion.2), channel_id=1, source_target_pairs={{0,4},{1,5},{2,6},{3,7},{4,0},{5,1},{6,2},{7,3},{8,12},{9,13},{10,... | collective-permute-start | bytes 393224 | tf_op jit(solution)/shard_map/ppermute | solution.py:177
  66.4 4.6 %collective-permute-start.12 = (f32[16,128]{1,0:T(8,128)S(1)}, f32[16,128]{1,0:T(8,128)S(1)}, u32[]{:S(2)}, u32[]{:S(2)}) collective-permute-start(f32[16,128]{1,0:T(8,128)S(1)} %pad_maximum_fusion.9), channel_id=1, source_target_pairs={{0,4},{1,5},{2,6},{3,7},{4,0},{5,1},{6,2},{7,3},{8,12},{9,13},{10,... | collective-permute-start | bytes 24584 | tf_op jit(solution)/shard_map/ppermute | solution.py:211
  71.0 3.8 %collective-permute-start.13 = (f32[16,256]{1,0:T(8,128)S(1)}, f32[16,256]{1,0:T(8,128)S(1)}, u32[]{:S(2)}, u32[]{:S(2)}) collective-permute-start(f32[16,256]{1,0:T(8,128)S(1)} %pad_maximum_fusion.8), channel_id=1, source_target_pairs={{0,2},{1,3},{2,0},{3,1},{4,6},{5,7},{6,4},{7,5},{8,10},{9,11},{10,... | collective-permute-start | bytes 49160 | tf_op jit(solution)/shard_map/ppermute | solution.py:211
  74.8 5.8 %collective-permute-start.14 = (f32[16,512]{1,0:T(8,128)S(1)}, f32[16,512]{1,0:T(8,128)S(1)}, u32[]{:S(2)}, u32[]{:S(2)}) collective-permute-start(f32[16,512]{1,0:T(8,128)S(1)} %pad_maximum_fusion.7), channel_id=1, source_target_pairs={{0,1},{1,0},{2,3},{3,2},{4,5},{5,4},{6,7},{7,6},{8,9},{9,8},{10,11... | collective-permute-start | bytes 98312 | tf_op jit(solution)/shard_map/ppermute | solution.py:211
  76.6 4.0 %copy-start.2 = (bf16[1024,512]{0,1:T(8,128)(2,1)S(1)}, bf16[1024,512]{0,1:T(8,128)(2,1)}, u32[]{:S(2)}) copy-start(bf16[1024,512]{0,1:T(8,128)(2,1)} %convolution_convert_fusion.2) | copy-start | bytes 3145732
  78.5 37.5 %collective-permute-start.9 = (bf16[128,512]{0,1:T(8,128)(2,1)S(1)}, bf16[128,512]{0,1:T(8,128)(2,1)S(1)}, u32[]{:S(2)}, u32[]{:S(2)}) collective-permute-start(bf16[128,512]{0,1:T(8,128)(2,1)S(1)} %get-tuple-element.41), channel_id=1, source_target_pairs={{0,4},{1,5},{2,6},{3,7},{4,0},{5,1},{6,2},{7,3},{8,12},{9,13},{10,... | collective-permute-start | bytes 393224 | tf_op jit(solution)/shard_map/ppermute | solution.py:211
  104.4 1.3 copy-start.5
  116.1 8.7 %collective-permute-start.10 = (bf16[256,512]{0,1:T(8,128)(2,1)S(1)}, bf16[256,512]{0,1:T(8,128)(2,1)S(1)}, u32[]{:S(2)}, u32[]{:S(2)}) collective-permute-start(bf16[256,512]{0,1:T(8,128)(2,1)S(1)} %pad_maximum_fusion.5), channel_id=1, source_target_pairs={{0,2},{1,3},{2,0},{3,1},{4,6},{5,7},{6,4},{7,5},{8,10},{9,11},{10,... | collective-permute-start | bytes 786440 | tf_op jit(solution)/shard_map/ppermute | solution.py:211
  121.2 3.9 %copy-start.11 = (bf16[512,512]{1,0:T(8,128)(2,1)S(1)}, bf16[512,512]{1,0:T(8,128)(2,1)}, u32[]{:S(2)}) copy-start(bf16[512,512]{1,0:T(8,128)(2,1)} %param.11) | copy-start | bytes 1572868
  125.0 1.4 copy-start.13
  125.0 3.1 %collective-permute-start.11 = (bf16[512,512]{0,1:T(8,128)(2,1)S(1)}, bf16[512,512]{0,1:T(8,128)(2,1)S(1)}, u32[]{:S(2)}, u32[]{:S(2)}) collective-permute-start(bf16[512,512]{0,1:T(8,128)(2,1)S(1)} %pad_maximum_fusion.4), channel_id=1, source_target_pairs={{0,1},{1,0},{2,3},{3,2},{4,5},{5,4},{6,7},{7,6},{8,9},{9,8},{10,11... | collective-permute-start | bytes 1572872 | tf_op jit(solution)/shard_map/ppermute | solution.py:211
  128.3 2.7 %copy-start.15 = (bf16[1024,512]{1,0:T(8,128)(2,1)S(1)}, bf16[1024,512]{1,0:T(8,128)(2,1)}, u32[]{:S(2)}) copy-start(bf16[1024,512]{1,0:T(8,128)(2,1)} %param.8) | copy-start | bytes 3145732
  128.3 2.7 %copy-start.18 = (bf16[512,512]{1,0:T(8,128)(2,1)S(1)}, bf16[512,512]{1,0:T(8,128)(2,1)}, u32[]{:S(2)}) copy-start(bf16[512,512]{1,0:T(8,128)(2,1)} %param.13) | copy-start | bytes 1572868
  186.6 1.3 copy-start.17
  187.9 3.2 %copy-start.10 = (bf16[2048,512]{1,0:T(8,128)(2,1)S(1)}, bf16[2048,512]{1,0:T(8,128)(2,1)}, u32[]{:S(2)}) copy-start(bf16[2048,512]{1,0:T(8,128)(2,1)} %all-reduce.2.cloned.1.call-done) | copy-start | bytes 6291460
  (4 other events, 4.9 us)
Sparse Core Ops, SparseCore 0:
  121.3 63.2 all-reduce.1
